TPU v7x, 256 devices: a whole 4x4x8 slice. The times are simulated.
256 devices in a mesh: ch: 64 (over z_lo, y, x), ta: 4 (over z_hi, core).
Axes of the slice: x: 4, y: 4, z: 8 (z_hi: 2, z_lo: 4; z = z_hi * 4 + z_lo), core: 2. Of those that a mesh axis runs over, the one named last changes fastest.
Arguments:
- raw: bfloat16 [16384, 20480], P('ch', 'ta'), may hold values from -40 to 40
- fir_taps: bfloat16 [129], replicated, may hold values from -0.5 to 0.5
- start_basis: float32 [512, 16], replicated, may hold values from -6 to 6
Outputs:
- cleaned: bfloat16 [16384, 20480], P('ch', 'ta')
All inputs are finite; a program needn't handle non-finite values.
Results may differ from a plain program's by a relative error of at most 0.008.
Values may be sent and summed in bfloat16 or wider, within the bound.
No kernel may reach another device: no remote copies, remote signals or barrier semaphores. Data moves between devices by JAX's collectives and lax.ppermute only.
A program may use at most 64 MiB of HBM per device.

v0:
```python
import math

import jax
import jax.numpy as jnp
from jax import lax
from jax.sharding import PartitionSpec as P

TAPS = 129
GAUGE = 4
STRIDE = 128
RANK = 16
ITERS = 6
WIN = 512


def with_halo(block, sides, width):
    for axis, dim in sides:
        count = lax.axis_size(axis)
        forward = [(i, i + 1) for i in range(count - 1)]
        backward = [(target, source) for source, target in forward]
        low = lax.ppermute(
            lax.slice_in_dim(block, block.shape[dim] - width, None, axis=dim), axis, forward
        )
        high = lax.ppermute(lax.slice_in_dim(block, 0, width, axis=dim), axis, backward)
        block = jnp.concatenate([low, block, high], axis=dim)
    return block


def shifted(value, axis, steps):
    count = lax.axis_size(axis)
    first, last = (max(0, -steps), min(count, count - steps))
    return lax.ppermute(value, axis, [(source, source + steps) for source in range(first, last)])


def toeplitz_band(taps, width):
    count = taps.shape[0]
    line = jnp.concatenate([taps, jnp.zeros((width,), taps.dtype)])
    flat = jnp.tile(line, width)[: width * (count + width - 1)]
    return flat.reshape(width, count + width - 1).T


def orthonormal(image):
    gram = jnp.einsum("wcr,wcs->wrs", image, image, precision=lax.Precision.HIGHEST)
    lower = jnp.linalg.cholesky(gram)
    return lax.linalg.triangular_solve(lower, image, left_side=False, lower=True, transpose_a=True)


def per_device(raw, fir_taps, start_basis):
    chans = raw.shape[0]
    samples = raw.shape[1]
    half = (TAPS - 1) // 2
    width = math.gcd(samples, 256)
    padded = with_halo(raw, (("ta", 1),), half)
    band_matrix = toeplitz_band(fir_taps, width)
    pieces = jnp.stack(
        [
            padded[:, number * width : number * width + width + TAPS - 1]
            for number in range(samples // width)
        ]
    )
    filtered = jnp.einsum(
        "bct,tu->cbu", pieces, band_matrix, preferred_element_type=jnp.float32
    ).reshape(chans, samples)
    extended = with_halo(filtered, (("ch", 0),), GAUGE)
    gauged = (extended[2 * GAUGE :] - extended[: -2 * GAUGE]).astype(jnp.bfloat16)
    lower_part = shifted(gauged, "ch", 1)
    upper_part = shifted(gauged[:STRIDE], "ch", -1)
    stacked = jnp.concatenate([lower_part, gauged, upper_part], axis=0)
    windows = chans // STRIDE
    total_time = samples * lax.axis_size("ta")
    basis = jnp.broadcast_to(start_basis, (windows, WIN, RANK))
    partial_mats = jnp.stack(
        [
            jnp.dot(
                stacked[number * STRIDE : number * STRIDE + WIN],
                stacked[number * STRIDE : number * STRIDE + WIN].T,
                preferred_element_type=jnp.float32,
            )
            for number in range(windows)
        ]
    )
    scatter_mat = lax.psum(partial_mats, "ta") / total_time
    for sweep in range(ITERS):
        basis = orthonormal(
            jnp.einsum("wcd,wdr->wcr", scatter_mat, basis, precision=lax.Precision.HIGHEST)
        )
    rounded = basis.astype(jnp.bfloat16)
    outputs = []
    for number in range(windows):
        frame = stacked[number * STRIDE : number * STRIDE + WIN]
        coeffs = jnp.dot(rounded[number].T, frame, preferred_element_type=jnp.float32).astype(
            jnp.bfloat16
        )
        fitted = jnp.dot(
            rounded[number, 2 * STRIDE : 3 * STRIDE], coeffs, preferred_element_type=jnp.float32
        )
        outputs.append(
            (frame[2 * STRIDE : 3 * STRIDE].astype(jnp.float32) - fitted).astype(jnp.bfloat16)
        )
    return jnp.concatenate(outputs, axis=0)


def solution(mesh):
    return jax.shard_map(
        per_device,
        mesh=mesh,
        in_specs=(P("ch", "ta"), P(), P()),
        out_specs=P("ch", "ta"),
        check_vma=False,
    )
```

profile of v0, /device:TPU:1, one launch (start us, length us, event | category | flops | bytes accessed | tf_op | source)
XLA Modules:
  0.0 292.5 jit_solution(11654293994104194249)
XLA Ops:
  6.5 1.1 fusion.57
  7.7 10.2 %collective-permute-start = (bf16[256,64]{1,0:T(8,128)(2,1)S(1)}, bf16[256,64]{1,0:T(8,128)(2,1)S(1)}, u32[]{:S(2)}, u32[]{:S(2)}) collective-permute-start(bf16[256,64]{1,0:T(8,128)(2,1)S(1)} %get-tuple-element.10), channel_id=1, source_target_pairs={{0,1},{1,2},{2,3},{4,5},{5,6},{6,7},{8,9},{9,10},{10,11},{12,13},{... | collective-permute-start | bytes 98312 | tf_op jit(solution)/shard_map/ppermute | solution.py:21
  17.9 1.9 collective-permute-start.1
  19.8 0.7 concatenate.26
  20.5 0.6 tile.10
  21.2 1.0 fusion.30
  24.8 2.6 collective-permute-done.1
  27.5 1.6 convolution_bitcast_fusion
  29.1 2.3 copy-done.3
  31.5 1.3 collective-permute-start.2
  32.8 4.0 %collective-permute-start.3 = (f32[4,5120]{1,0:T(4,128)S(1)}, f32[4,5120]{1,0:T(4,128)S(1)}, u32[]{:S(2)}, u32[]{:S(2)}) collective-permute-start(f32[4,5120]{1,0:T(4,128)S(1)} %bitcast.161), channel_id=1, source_target_pairs={{0,4},{4,8},{8,12},{12,16},{16,20},{20,24},{24,28},{28,32},{32,36}... | collective-permute-start | bytes 245768 | tf_op jit(solution)/shard_map/ppermute | solution.py:21
  36.8 5.9 %copy.21 = f32[256,20,256]{0,2,1:T(8,128)} copy(f32[256,20,256]{2,0,1:T(8,128)} %copy-done.3) | data formatting | bytes 10485760 | tf_op jit(solution)/shard_map/bct,tu->cbu/transpose | solution.py:61
  42.7 5.9 %copy.22 = f32[256,5120]{1,0:T(8,128)} copy(f32[256,5120]{0,1:T(8,128)} %bitcast.160) | data formatting | bytes 10485760 | tf_op jit(solution)/shard_map/reshape | solution.py:63
  48.6 4.7 %fusion.3 = bf16[256,5120]{1,0:T(8,128)(2,1)S(1)} fusion(f32[256,5120]{1,0:T(8,128)} %copy.22, f32[4,5120]{1,0:T(4,128)S(1)} %collective-permute-done.3, f32[4,5120]{1,0:T(4,128)S(1)} %collective-permute-done.2), kind=kLoop, calls=%fused_computation.10 | loop fusion | flops 5242880 | bytes 8028160 | tf_op jit(solution)/shard_map/convert_element_type | solution.py:65
  53.3 3.3 %collective-permute-start.4 = (bf16[256,5120]{1,0:T(8,128)(2,1)S(1)}, bf16[256,5120]{1,0:T(8,128)(2,1)S(1)}, u32[]{:S(2)}, u32[]{:S(2)}) collective-permute-start(bf16[256,5120]{1,0:T(8,128)(2,1)S(1)} %fusion.3), channel_id=1, source_target_pairs={{0,4},{4,8},{8,12},{12,16},{16,20},{20,24},{24,28},{28,32},{32,36}... | collective-permute-start | bytes 7864328 | tf_op jit(solution)/shard_map/ppermute | solution.py:32
  56.7 1.5 collective-permute-start.5
  58.2 49.6 %collective-permute-done.4 = bf16[256,5120]{1,0:T(8,128)(2,1)S(1)} collective-permute-done((bf16[256,5120]{1,0:T(8,128)(2,1)S(1)}, bf16[256,5120]{1,0:T(8,128)(2,1)S(1)}, u32[]{:S(2)}, u32[]{:S(2)}) %collective-permute-start.4) | collective-permute-done | bytes 2621472 | tf_op jit(solution)/shard_map/ppermute | solution.py:32
  107.8 2.9 fusion.19
  110.8 2.9 fusion.18
  113.7 1.5 pad_maximum_fusion.8
  115.3 105.3 %all-reduce.3.cloned.1.call-done = f32[2,512,512]{2,1,0:T(8,128)} async-done(((f32[2,512,512]{2,1,0:T(8,128)}), f32[2,512,512]{2,1,0:T(8,128)}) %all-reduce.3.cloned.1.call-update) | async-done | bytes 2097168 | tf_op jit(solution)/shard_map/psum | solution.py:82
  220.6 3.6 %fusion.16 = f32[2,512,16]{1,2,0:T(8,128)S(1)} fusion(f32[2,512,512]{2,1,0:T(8,128)} %all-reduce.3.cloned.1.call-done, f32[512,16]{0,1:T(8,128)S(1)} %copy-done), kind=kOutput, calls=%fused_computation.28 | convolution fusion | flops 101187584 | bytes 2195456 | tf_op jit(solution)/shard_map/wcd,wdr->wcr/dot_general | solution.py:85
  224.5 3.1 %custom-call.16 = f32[2,16,16]{2,1,0:T(8,128)S(1)} custom-call(f32[2,16,16]{2,1,0:T(8,128)S(1)} %fusion.43), custom_call_target="Cholesky" | custom-call | tf_op jit(solution)/shard_map/jit(cholesky)/cholesky | solution.py:44
  227.8 2.5 custom-call.17
  230.3 0.3 convolution_bitcast_fusion.6
  230.6 3.5 %fusion.14 = f32[2,512,16]{1,2,0:T(8,128)S(1)} fusion(f32[2,512,16]{1,2,0:T(8,128)S(1)} %convolution_bitcast_fusion.6, f32[2,512,512]{2,1,0:T(8,128)} %all-reduce.3.cloned.1.call-done), kind=kOutput, calls=%fused_computation.26 | convolution fusion | flops 101187584 | bytes 2228224 | tf_op jit(solution)/shard_map/wcd,wdr->wcr/dot_general | solution.py:85
  234.4 2.9 %custom-call.18 = f32[2,16,16]{2,1,0:T(8,128)S(1)} custom-call(f32[2,16,16]{2,1,0:T(8,128)S(1)} %fusion.41), custom_call_target="Cholesky" | custom-call | tf_op jit(solution)/shard_map/jit(cholesky)/cholesky | solution.py:44
  237.6 2.5 custom-call.19
  240.0 0.3 convolution_bitcast_fusion.5
  240.3 1.9 fusion.12
  242.5 2.9 %custom-call.20 = f32[2,16,16]{2,1,0:T(8,128)S(1)} custom-call(f32[2,16,16]{2,1,0:T(8,128)S(1)} %fusion.39), custom_call_target="Cholesky" | custom-call | tf_op jit(solution)/shard_map/jit(cholesky)/cholesky | solution.py:44
  245.7 2.5 custom-call.21
  248.2 0.3 convolution_bitcast_fusion.4
  248.4 1.9 fusion.10
  250.7 2.9 %custom-call.22 = f32[2,16,16]{2,1,0:T(8,128)S(1)} custom-call(f32[2,16,16]{2,1,0:T(8,128)S(1)} %fusion.37), custom_call_target="Cholesky" | custom-call | tf_op jit(solution)/shard_map/jit(cholesky)/cholesky | solution.py:44
  253.8 2.5 custom-call.23
  256.3 0.3 convolution_bitcast_fusion.3
  256.6 1.9 fusion.8
  258.8 2.9 %custom-call.24 = f32[2,16,16]{2,1,0:T(8,128)S(1)} custom-call(f32[2,16,16]{2,1,0:T(8,128)S(1)} %fusion.35), custom_call_target="Cholesky" | custom-call | tf_op jit(solution)/shard_map/jit(cholesky)/cholesky | solution.py:44
  262.0 2.5 custom-call.25
  264.4 0.3 convolution_bitcast_fusion.2
  264.7 1.9 fusion.6
  266.9 2.9 %custom-call.26 = f32[2,16,16]{2,1,0:T(8,128)S(1)} custom-call(f32[2,16,16]{2,1,0:T(8,128)S(1)} %fusion.33), custom_call_target="Cholesky" | custom-call | tf_op jit(solution)/shard_map/jit(cholesky)/cholesky | solution.py:44
  270.1 2.6 custom-call.27
  272.7 0.3 fusion.20
  273.0 5.3 %fusion = bf16[128,5120]{1,0:T(8,128)(2,1)} fusion(bf16[256,5120]{1,0:T(8,128)(2,1)} %copy-done.4, bf16[256,5120]{1,0:T(8,128)(2,1)} %copy-done.6, bf16[2,512,16]{1,2,0:T(8,128)(2,1)S(1)} %fusion.20), kind=kOutput, calls=%fused_computation.2 | convolution fusion | flops 117391360 | bytes 7884800 | tf_op jit(solution)/shard_map/dot_general | solution.py:94
  278.3 4.0 %fusion.1 = bf16[128,5120]{1,0:T(8,128)(2,1)} fusion(bf16[256,5120]{1,0:T(8,128)(2,1)S(1)} %copy-done.5, bf16[128,5120]{1,0:T(8,128)(2,1)} %copy-done.7, bf16[256,5120]{1,0:T(8,128)(2,1)} %copy-done.6, bf16[2,512,16]{1,2,0:T(8,128)(2,1)S(1)} %fusion.20), kind=kOutput, calls=%fused_computation.3 | convolution fusion | flops 122634240 | bytes 9195520 | tf_op jit(solution)/shard_map/dot_general | solution.py:94
  282.2 3.4 %pad_maximum_fusion.7 = bf16[256,5120]{1,0:T(8,128)(2,1)} fusion(bf16[128,5120]{1,0:T(8,128)(2,1)} %fusion.1, bf16[128,5120]{1,0:T(8,128)(2,1)} %fusion), kind=kLoop, calls=%fused_computation.14 | loop fusion | flops 5242880 | bytes 5242880 | tf_op jit(solution)/shard_map/concatenate | solution.py:100
  (83 shorter events, 6.0 us)
Async XLA Ops:
  6.5 214.0 %copy-start = (f32[512,16]{0,1:T(8,128)S(1)}, f32[512,16]{0,1:T(8,128)}, u32[]{:S(2)}) copy-start(f32[512,16]{0,1:T(8,128)} %param.8) | copy-start | bytes 98308
  6.5 15.7 %copy-start.2 = (bf16[256,5120]{1,0:T(8,128)(2,1)S(1)}, bf16[256,5120]{1,0:T(8,128)(2,1)}, u32[]{:S(2)}) copy-start(bf16[256,5120]{1,0:T(8,128)(2,1)} %param.6) | copy-start | bytes 7864324
  6.5 214.0 %all-reduce.3.cloned.1.call-start = ((), (), s32[]{:S(2)}) async-start(), calls=%async_computation | async-start | bytes 4194304 | tf_op jit(solution)/shard_map/psum | solution.py:82
  7.7 13.5 %collective-permute-start = (bf16[256,64]{1,0:T(8,128)(2,1)S(1)}, bf16[256,64]{1,0:T(8,128)(2,1)S(1)}, u32[]{:S(2)}, u32[]{:S(2)}) collective-permute-start(bf16[256,64]{1,0:T(8,128)(2,1)S(1)} %get-tuple-element.10), channel_id=1, source_target_pairs={{0,1},{1,2},{2,3},{4,5},{5,6},{6,7},{8,9},{9,10},{10,11},{12,13},{... | collective-permute-start | bytes 98312 | tf_op jit(solution)/shard_map/ppermute | solution.py:21
  17.9 9.5 %collective-permute-start.1 = (bf16[256,64]{1,0:T(8,128)(2,1)S(1)}, bf16[256,64]{1,0:T(8,128)(2,1)S(1)}, u32[]{:S(2)}, u32[]{:S(2)}) collective-permute-start(bf16[256,64]{1,0:T(8,128)(2,1)S(1)} %get-tuple-element.9), channel_id=1, source_target_pairs={{1,0},{2,1},{3,2},{5,4},{6,5},{7,6},{9,8},{10,9},{11,10},{13,12},{... | collective-permute-start | bytes 98312 | tf_op jit(solution)/shard_map/ppermute | solution.py:24
  29.1 2.3 copy-start.3
  31.5 17.2 %collective-permute-start.2 = (f32[4,5120]{1,0:T(4,128)S(1)}, f32[4,5120]{1,0:T(4,128)S(1)}, u32[]{:S(2)}, u32[]{:S(2)}) collective-permute-start(f32[4,5120]{1,0:T(4,128)S(1)} %bitcast.162), channel_id=1, source_target_pairs={{4,0},{8,4},{12,8},{16,12},{20,16},{24,20},{28,24},{32,28},{36,32}... | collective-permute-start | bytes 245768 | tf_op jit(solution)/shard_map/ppermute | solution.py:24
  32.8 15.9 %collective-permute-start.3 = (f32[4,5120]{1,0:T(4,128)S(1)}, f32[4,5120]{1,0:T(4,128)S(1)}, u32[]{:S(2)}, u32[]{:S(2)}) collective-permute-start(f32[4,5120]{1,0:T(4,128)S(1)} %bitcast.161), channel_id=1, source_target_pairs={{0,4},{4,8},{8,12},{12,16},{16,20},{20,24},{24,28},{28,32},{32,36}... | collective-permute-start | bytes 245768 | tf_op jit(solution)/shard_map/ppermute | solution.py:21
  53.3 57.4 %copy-start.4 = (bf16[256,5120]{1,0:T(8,128)(2,1)}, bf16[256,5120]{1,0:T(8,128)(2,1)S(1)}, u32[]{:S(2)}) copy-start(bf16[256,5120]{1,0:T(8,128)(2,1)S(1)} %fusion.3) | copy-start | bytes 7864324
  53.3 54.5 %collective-permute-start.4 = (bf16[256,5120]{1,0:T(8,128)(2,1)S(1)}, bf16[256,5120]{1,0:T(8,128)(2,1)S(1)}, u32[]{:S(2)}, u32[]{:S(2)}) collective-permute-start(bf16[256,5120]{1,0:T(8,128)(2,1)S(1)} %fusion.3), channel_id=1, source_target_pairs={{0,4},{4,8},{8,12},{12,16},{16,20},{20,24},{24,28},{28,32},{32,36}... | collective-permute-start | bytes 7864328 | tf_op jit(solution)/shard_map/ppermute | solution.py:32
  56.7 54.0 %collective-permute-start.5 = (bf16[128,5120]{1,0:T(8,128)(2,1)S(1)}, bf16[128,5120]{1,0:T(8,128)(2,1)S(1)}, u32[]{:S(2)}, u32[]{:S(2)}) collective-permute-start(bf16[128,5120]{1,0:T(8,128)(2,1)S(1)} %slice.168), channel_id=1, source_target_pairs={{4,0},{8,4},{12,8},{16,12},{20,16},{24,20},{28,24},{32,28},{36,32}... | collective-permute-start | bytes 3932168 | tf_op jit(solution)/shard_map/ppermute | solution.py:32
  107.8 2.9 %copy-start.6 = (bf16[256,5120]{1,0:T(8,128)(2,1)}, bf16[256,5120]{1,0:T(8,128)(2,1)S(1)}, u32[]{:S(2)}) copy-start(bf16[256,5120]{1,0:T(8,128)(2,1)S(1)} %collective-permute-done.4) | copy-start | bytes 7864324
  110.8 2.9 copy-start.7
  220.6 19.8 %copy-start.1 = (f32[2,512,512]{2,1,0:T(8,128)S(1)}, f32[2,512,512]{2,1,0:T(8,128)}, u32[]{:S(2)}) copy-start(f32[2,512,512]{2,1,0:T(8,128)} %all-reduce.3.cloned.1.call-done) | copy-start | bytes 6291460
  273.0 5.3 %copy-start.5 = (bf16[256,5120]{1,0:T(8,128)(2,1)S(1)}, bf16[256,5120]{1,0:T(8,128)(2,1)}, u32[]{:S(2)}) copy-start(bf16[256,5120]{1,0:T(8,128)(2,1)} %copy-done.4) | copy-start | bytes 7864324
Sparse Core Ops, SparseCore 0:
  115.4 105.1 all-reduce.2
where the time goes:
time: 293 us; the launch traced here: 292 us
  waiting for transfers between devices  158 us (54%)
  other arithmetic  45 us (15%)
  matrix products  34.3 us (12%)
  starting transfers between devices  22.2 us (8%)
  local copies, waits for them, and re-layouts  19.7 us (7%)
  between operations  13.8 us (5%)
    psum x1, waiting for transfers between devices, per_device(): scatter_mat = lax.psum(partial_mats, 'ta') / total_time  105 us
    ppermute x2, waiting for transfers between devices, shifted(): lax.ppermute(value, axis, [(source, source + steps) for source in range(f...  49.6 us
    another operation x19, other arithmetic, orthonormal(): lower = jnp.linalg.cholesky(gram)  18.7 us
    another operation x13, other arithmetic, orthonormal(): lax.linalg.triangular_solve(lower, image, left_side=False, lower=True, tr...  15.4 us
    dot_general x6, matrix products, per_device(): jnp.einsum('wcd,wdr->wcr', scatter_mat, basis, precision=lax.Precision.HI...  14.8 us
    ppermute x2, starting transfers between devices, with_halo(): lax.ppermute(lax.slice_in_dim(block, block.shape[dim] - width, None, axis...  14.2 us
    dot_general x2, matrix products, per_device(): jnp.dot(rounded[number, 2 * STRIDE:3 * STRIDE], coeffs, preferred_element...  9.23 us
    reshape x1, local copies, waits for them, and re-layouts, per_device(): filtered = jnp.einsum('bct,tu->cbu', pieces, band_matrix, preferred_eleme...  5.95 us
  transfers between devices with their start and end apart: 7, of which 3 were waited for; matrix products, arithmetic and copies ran while one was open for 7% of the time, Pallas kernels for 0%

commit v1 on v0

--- a/solution.py
+++ b/solution.py
@@ -3,6 +3,8 @@
 import jax
 import jax.numpy as jnp
 from jax import lax
+from jax.experimental import pallas as pl
+from jax.experimental.pallas import tpu as pltpu
 from jax.sharding import PartitionSpec as P
 
 TAPS = 129
@@ -39,10 +41,48 @@
     return flat.reshape(width, count + width - 1).T
 
 
-def orthonormal(image):
-    gram = jnp.einsum("wcr,wcs->wrs", image, image, precision=lax.Precision.HIGHEST)
-    lower = jnp.linalg.cholesky(gram)
-    return lax.linalg.triangular_solve(lower, image, left_side=False, lower=True, transpose_a=True)
+def gram(a, b):
+    return lax.dot_general(a, b, (((1,), (1,)), ((), ())), preferred_element_type=jnp.float32)
+
+
+def orthonormal_rows(image, rows):
+    result = image
+    for i in range(image.shape[0]):
+        row = result[i : i + 1, :]
+        unit = row / jnp.sqrt(jnp.sum(row * row, axis=1, keepdims=True))
+        proj = jnp.sum(result * unit, axis=1, keepdims=True)
+        result = jnp.where(rows > i, result - proj * unit, jnp.where(rows == i, unit, result))
+    return result
+
+
+def subspace_kernel(band_ref, start_ref, out_ref):
+    windows = out_ref.shape[0]
+    rank, win = start_ref.shape
+    rows = lax.broadcasted_iota(jnp.int32, (rank, 1), 0)
+    bases = [start_ref[...] for _ in range(windows)]
+    for sweep in range(ITERS):
+        for number in range(windows):
+            lo = number * STRIDE
+            scatter_mat = band_ref[lo : lo + win, lo : lo + win]
+            image = jnp.dot(
+                bases[number], scatter_mat, precision=lax.Precision.HIGHEST,
+                preferred_element_type=jnp.float32,
+            )
+            bases[number] = orthonormal_rows(image, rows)
+    for number in range(windows):
+        out_ref[number] = bases[number].astype(out_ref.dtype)
+
+
+def subspace(band, start_t, windows):
+    return pl.pallas_call(
+        subspace_kernel,
+        out_shape=jax.ShapeDtypeStruct((windows,) + start_t.shape, jnp.bfloat16),
+        in_specs=[
+            pl.BlockSpec(memory_space=pltpu.VMEM),
+            pl.BlockSpec(memory_space=pltpu.VMEM),
+        ],
+        out_specs=pl.BlockSpec(memory_space=pltpu.VMEM),
+    )(band, start_t)
 
 
 def per_device(raw, fir_taps, start_basis):
@@ -63,36 +103,46 @@
     ).reshape(chans, samples)
     extended = with_halo(filtered, (("ch", 0),), GAUGE)
     gauged = (extended[2 * GAUGE :] - extended[: -2 * GAUGE]).astype(jnp.bfloat16)
-    lower_part = shifted(gauged, "ch", 1)
+
+    tiles = chans // STRIDE
+    windows = tiles
+    total_time = samples * lax.axis_size("ta")
+    lower_part = shifted(gauged[chans - 2 * STRIDE :], "ch", 1)
     upper_part = shifted(gauged[:STRIDE], "ch", -1)
+
+    own = lax.psum(gram(gauged, gauged), "ta")
+    own_left = shifted(own[chans - 2 * STRIDE :, chans - 2 * STRIDE :], "ch", 1)
+    own_right = shifted(own[:STRIDE, :STRIDE], "ch", -1)
+
+    own, lower_part, upper_part = lax.optimization_barrier((own, lower_part, upper_part))
+    cross_left = gram(lower_part, gauged)
+    tail = jnp.concatenate([lower_part[STRIDE:], gauged], axis=0)
+    cross_right = gram(tail, upper_part)
+    cross_left, cross_right = lax.psum((cross_left, cross_right), "ta")
+
+    zeros = jnp.zeros((STRIDE, STRIDE), jnp.float32)
+    top = jnp.concatenate(
+        [own_left, cross_left, jnp.concatenate([zeros, cross_right[:STRIDE]], axis=0)], axis=1
+    )
+    middle = jnp.concatenate(
+        [cross_left.T, own, cross_right[STRIDE:]], axis=1
+    )
+    corner = jnp.concatenate([zeros, cross_right[:STRIDE].T], axis=1)
+    bottom = jnp.concatenate([corner, cross_right[STRIDE:].T, own_right], axis=1)
+    band = jnp.concatenate([top, middle, bottom], axis=0) / total_time
+
+    rounded = subspace(band, start_basis.T, windows)
+
     stacked = jnp.concatenate([lower_part, gauged, upper_part], axis=0)
-    windows = chans // STRIDE
-    total_time = samples * lax.axis_size("ta")
-    basis = jnp.broadcast_to(start_basis, (windows, WIN, RANK))
-    partial_mats = jnp.stack(
-        [
-            jnp.dot(
-                stacked[number * STRIDE : number * STRIDE + WIN],
-                stacked[number * STRIDE : number * STRIDE + WIN].T,
-                preferred_element_type=jnp.float32,
-            )
-            for number in range(windows)
-        ]
-    )
-    scatter_mat = lax.psum(partial_mats, "ta") / total_time
-    for sweep in range(ITERS):
-        basis = orthonormal(
-            jnp.einsum("wcd,wdr->wcr", scatter_mat, basis, precision=lax.Precision.HIGHEST)
-        )
-    rounded = basis.astype(jnp.bfloat16)
     outputs = []
     for number in range(windows):
         frame = stacked[number * STRIDE : number * STRIDE + WIN]
-        coeffs = jnp.dot(rounded[number].T, frame, preferred_element_type=jnp.float32).astype(
+        coeffs = jnp.dot(rounded[number], frame, preferred_element_type=jnp.float32).astype(
             jnp.bfloat16
         )
-        fitted = jnp.dot(
-            rounded[number, 2 * STRIDE : 3 * STRIDE], coeffs, preferred_element_type=jnp.float32
+        fitted = lax.dot_general(
+            rounded[number, :, 2 * STRIDE : 3 * STRIDE], coeffs, (((0,), (0,)), ((), ())),
+            preferred_element_type=jnp.float32,
         )
         outputs.append(
             (frame[2 * STRIDE : 3 * STRIDE].astype(jnp.float32) - fitted).astype(jnp.bfloat16)

time: 293 us -> 236 us (0.81)
  the two profiles are of different devices: /device:TPU:1 before, /device:TPU:97 now
where the time goes in v1:
time: 236 us; the launch traced here: 231 us
  waiting for transfers between devices  97.6 us (41%)
  starting transfers between devices  37 us (16%)
  local copies, waits for them, and re-layouts  30 us (13%)
  Pallas kernels  22.3 us (9%)
  matrix products  17.6 us (7%)
  between operations  13.7 us (6%)
  other arithmetic  13 us (6%)
    psum x1, waiting for transfers between devices, per_device(): own = lax.psum(gram(gauged, gauged), 'ta')  49.4 us
    psum x1, waiting for transfers between devices, per_device(): cross_left, cross_right = lax.psum((cross_left, cross_right), 'ta')  39.7 us
    pallas_call x1, Pallas kernels, subspace(): pl.pallas_call(subspace_kernel, out_shape=jax.ShapeDtypeStruct((windows,)...  22.3 us
    ppermute x4, starting transfers between devices, shifted(): lax.ppermute(value, axis, [(source, source + steps) for source in range(f...  19.2 us
    ppermute x2, starting transfers between devices, with_halo(): lax.ppermute(lax.slice_in_dim(block, 0, width, axis=dim), axis, backward)  9.2 us
    ppermute x2, starting transfers between devices, with_halo(): lax.ppermute(lax.slice_in_dim(block, block.shape[dim] - width, None, axis...  8.6 us
    dot_general x3, matrix products, gram(): lax.dot_general(a, b, (((1,), (1,)), ((), ())), preferred_element_type=jn...  8.14 us
    dot_general x2, matrix products, per_device(): lax.dot_general(rounded[number, :, 2 * STRIDE:3 * STRIDE], coeffs, (((0,)...  7.94 us
  transfers between devices with their start and end apart: 10, of which 4 were waited for; matrix products, arithmetic and copies ran while one was open for 12% of the time, Pallas kernels for 0%

profile of v1, /device:TPU:97, one launch (start us, length us, event | category | flops | bytes accessed | tf_op | source)
XLA Modules:
  0.0 231.2 jit_solution(16755065323228926721)
XLA Ops:
  6.5 1.1 fusion.24
  7.7 6.7 %collective-permute-start = (bf16[256,64]{1,0:T(8,128)(2,1)S(1)}, bf16[256,64]{1,0:T(8,128)(2,1)S(1)}, u32[]{:S(2)}, u32[]{:S(2)}) collective-permute-start(bf16[256,64]{1,0:T(8,128)(2,1)S(1)} %get-tuple-element.16), channel_id=1, source_target_pairs={{0,1},{1,2},{2,3},{4,5},{5,6},{6,7},{8,9},{9,10},{10,11},{12,13},{... | collective-permute-start | bytes 98312 | tf_op jit(solution)/shard_map/ppermute | solution.py:23
  14.3 1.9 collective-permute-start.1
  16.3 0.7 concatenate.44
  17.0 0.6 tile.10
  17.7 1.0 fusion.17
  18.7 0.1 bitcast_dynamic-update-slice_fusion.17
  18.9 0.1 bitcast_dynamic-update-slice_fusion.16
  19.0 0.1 bitcast_dynamic-update-slice_fusion.15
  20.3 0.1 bitcast_dynamic-update-slice_fusion.6
  20.4 0.1 bitcast_dynamic-update-slice_fusion.5
  20.5 0.1 bitcast_dynamic-update-slice_fusion.4
  20.7 0.1 bitcast_dynamic-update-slice_fusion.3
  21.2 2.6 %collective-permute-done.1 = bf16[256,64]{1,0:T(8,128)(2,1)S(1)} collective-permute-done((bf16[256,64]{1,0:T(8,128)(2,1)S(1)}, bf16[256,64]{1,0:T(8,128)(2,1)S(1)}, u32[]{:S(2)}, u32[]{:S(2)}) %collective-permute-start.1) | collective-permute-done | bytes 32800 | tf_op jit(solution)/shard_map/ppermute | solution.py:26
  23.8 0.2 fusion.15
  24.0 1.6 convolution_bitcast_fusion
  25.6 2.4 %copy-done.1 = f32[256,20,256]{2,0,1:T(8,128)} copy-done((f32[256,20,256]{2,0,1:T(8,128)}, f32[256,20,256]{2,0,1:T(8,128)S(1)}, u32[]{:S(2)}) %copy-start.1) | copy-done | bytes 5242904
  27.9 7.3 %collective-permute-start.2 = (f32[4,5120]{1,0:T(4,128)S(1)}, f32[4,5120]{1,0:T(4,128)S(1)}, u32[]{:S(2)}, u32[]{:S(2)}) collective-permute-start(f32[4,5120]{1,0:T(4,128)S(1)} %bitcast.79), channel_id=1, source_target_pairs={{4,0},{8,4},{12,8},{16,12},{20,16},{24,20},{28,24},{32,28},{36,32}... | collective-permute-start | bytes 245768 | tf_op jit(solution)/shard_map/ppermute | solution.py:26
  35.2 1.9 collective-permute-start.3
  37.2 5.9 %copy.10 = f32[256,20,256]{0,2,1:T(8,128)} copy(f32[256,20,256]{2,0,1:T(8,128)} %copy-done.1) | data formatting | bytes 10485760 | tf_op jit(solution)/shard_map/bct,tu->cbu/transpose | solution.py:101
  43.1 6.0 %copy.11 = f32[256,5120]{1,0:T(8,128)} copy(f32[256,5120]{0,1:T(8,128)} %bitcast.76) | data formatting | bytes 10485760 | tf_op jit(solution)/shard_map/reshape | solution.py:103
  49.0 4.7 %fusion.4 = bf16[256,5120]{1,0:T(8,128)(2,1)S(1)} fusion(f32[256,5120]{1,0:T(8,128)} %copy.11, f32[4,5120]{1,0:T(4,128)S(1)} %collective-permute-done.3, f32[4,5120]{1,0:T(4,128)S(1)} %collective-permute-done.2), kind=kLoop, calls=%fused_computation.11 | loop fusion | flops 5242880 | bytes 8028160 | tf_op jit(solution)/shard_map/convert_element_type | solution.py:105
  53.7 1.9 collective-permute-start.5
  55.7 1.1 slice.176
  56.8 7.6 %collective-permute-start.6 = (bf16[128,5120]{1,0:T(8,128)(2,1)}, bf16[128,5120]{1,0:T(8,128)(2,1)}, u32[]{:S(2)}, u32[]{:S(2)}) collective-permute-start(bf16[128,5120]{1,0:T(8,128)(2,1)} %slice.176), channel_id=1, source_target_pairs={{4,0},{8,4},{12,8},{16,12},{20,16},{24,20},{28,24},{32,28},{36,32}... | collective-permute-start | bytes 3932168 | tf_op jit(solution)/shard_map/ppermute | solution.py:34
  64.4 1.6 fusion.27
  66.1 49.4 %all-reduce.6.cloned.1.call-done = f32[256,256]{1,0:T(8,128)} async-done(((f32[256,256]{1,0:T(8,128)}), f32[256,256]{1,0:T(8,128)}) %all-reduce.6.cloned.1.call-update) | async-done | bytes 262160 | tf_op jit(solution)/shard_map/psum | solution.py:113
  115.5 5.9 %collective-permute-done.5 = bf16[256,5120]{1,0:T(8,128)(2,1)} collective-permute-done((bf16[256,5120]{1,0:T(8,128)(2,1)S(1)}, bf16[256,5120]{1,0:T(8,128)(2,1)}, u32[]{:S(2)}, u32[]{:S(2)}) %collective-permute-start.5) | collective-permute-done | bytes 2621472 | tf_op jit(solution)/shard_map/ppermute | solution.py:34
  121.4 1.4 slice.163
  122.8 3.3 %fusion.28 = f32[256,256]{0,1:T(8,128)} fusion(bf16[256,5120]{1,0:T(8,128)(2,1)} %collective-permute-done.5, bf16[256,5120]{1,0:T(8,128)(2,1)S(1)} %fusion.4), kind=kOutput, calls=%fused_computation.63 | convolution fusion | flops 671088640 | bytes 5505024 | tf_op jit(solution)/shard_map/dot_general | solution.py:45
  126.1 3.2 %fusion.8 = f32[384,128]{1,0:T(8,128)} fusion(bf16[128,5120]{1,0:T(8,128)(2,1)} %collective-permute-done.6, bf16[256,5120]{1,0:T(8,128)(2,1)S(1)} %fusion.4, bf16[128,5120]{1,0:T(8,128)(2,1)S(1)} %slice.163), kind=kOutput, calls=%fused_computation.16 | convolution fusion | flops 511180800 | bytes 5439488 | tf_op jit(solution)/shard_map/dot_general | solution.py:45
  129.5 1.9 collective-permute-start.4
  131.4 0.6 slice.179
  132.1 7.8 %collective-permute-start.7 = (f32[128,128]{1,0:T(8,128)}, f32[128,128]{1,0:T(8,128)}, u32[]{:S(2)}, u32[]{:S(2)}) collective-permute-start(f32[128,128]{1,0:T(8,128)} %slice.179), channel_id=1, source_target_pairs={{4,0},{8,4},{12,8},{16,12},{20,16},{24,20},{28,24},{32,28},{36,32}... | collective-permute-start | bytes 196616 | tf_op jit(solution)/shard_map/ppermute | solution.py:34
  139.8 39.7 %all-reduce.8.cloned.1.call-done = (f32[384,128]{1,0:T(8,128)}, f32[256,256]{0,1:T(8,128)}) async-done(((f32[384,128]{1,0:T(8,128)}, f32[256,256]{0,1:T(8,128)}), (f32[384,128]{1,0:T(8,128)}, f32[256,256]{0,1:T(8,128)})) %all-reduce.8.cloned.1.call-update) | async-done | bytes 458768 | tf_op jit(solution)/shard_map/psum | solution.py:121
  179.5 1.5 fusion.25
  181.0 0.7 copy.20
  181.7 1.6 fusion.26
  183.3 0.7 copy-done.3
  184.0 1.1 select_maximum_fusion
  185.1 1.1 copy.18
  186.2 1.0 copy.17
  187.2 0.9 copy.16
  188.2 2.6 %maximum_multiply_fusion.band_ref = f32[640,640]{1,0:T(8,128)} fusion(f32[128,128]{1,0:T(8,128)} %collective-permute-done.7, f32[128,256]{1,0:T(8,128)S(1)} %copy.17, f32[128,128]{1,0:T(8,128)S(1)} %copy.16, f32[128,128]{1,0:T(8,128)S(1)} %broadcast_in_dim.4, f32[256,128]{1,0:T(8,128)} %get-tuple-element.19, f32[256,256]{1,0:T(8,128)S(1)} %copy-done.2, ...), kind=kLoop, calls=%fused_computation.22 | loop fusion | flops 3276800 | bytes 3276800 | tf_op jit(solution)/shard_map/div | solution.py:132
  190.8 22.3 %shard_map.37 = bf16[2,16,512]{2,1,0:T(8,128)(2,1)} custom-call(f32[640,640]{1,0:T(8,128)} %maximum_multiply_fusion.band_ref, f32[16,512]{1,0:T(8,128)} %bitcast.80), custom_call_target="tpu_custom_call" | custom-call | tf_op jit(solution)/shard_map/pallas_call | solution.py:77
  213.0 4.0 %fusion = bf16[128,5120]{1,0:T(8,128)(2,1)} fusion(bf16[256,5120]{1,0:T(8,128)(2,1)S(1)} %fusion.4, bf16[256,5120]{1,0:T(8,128)(2,1)} %collective-permute-done.5, bf16[2,16,512]{2,1,0:T(8,128)(2,1)} %shard_map.37), kind=kOutput, calls=%fused_computation.2 | convolution fusion | flops 117391360 | bytes 7884800 | tf_op jit(solution)/shard_map/dot_general | solution.py:143
  217.0 4.0 %fusion.1 = bf16[128,5120]{1,0:T(8,128)(2,1)} fusion(bf16[256,5120]{1,0:T(8,128)(2,1)S(1)} %fusion.4, bf16[128,5120]{1,0:T(8,128)(2,1)} %collective-permute-done.6, bf16[256,5120]{1,0:T(8,128)(2,1)} %collective-permute-done.5, bf16[2,16,512]{2,1,0:T(8,128)(2,1)S(1)} %copy-done.4), kind=kOutput, calls=%fused_computation.3 | convolution fusion | flops 122634240 | bytes 9195520 | tf_op jit(solution)/shard_map/dot_general | solution.py:143
  221.0 3.4 %pad_maximum_fusion.6 = bf16[256,5120]{1,0:T(8,128)(2,1)} fusion(bf16[128,5120]{1,0:T(8,128)(2,1)} %fusion.1, bf16[128,5120]{1,0:T(8,128)(2,1)} %fusion), kind=kLoop, calls=%fused_computation.20 | loop fusion | flops 5242880 | bytes 5242880 | tf_op jit(solution)/shard_map/concatenate | solution.py:150
  (35 shorter events, 1.9 us)
Async XLA Ops:
  6.5 12.2 %copy-start = (bf16[256,5120]{1,0:T(8,128)(2,1)S(1)}, bf16[256,5120]{1,0:T(8,128)(2,1)}, u32[]{:S(2)}) copy-start(bf16[256,5120]{1,0:T(8,128)(2,1)} %param.3) | copy-start | bytes 7864324
  6.5 109.0 %all-reduce.6.cloned.1.call-start = ((), (), s32[]{:S(2)}) async-start(), calls=%async_computation | async-start | bytes 524288 | tf_op jit(solution)/shard_map/psum | solution.py:113
  7.7 10.0 %collective-permute-start = (bf16[256,64]{1,0:T(8,128)(2,1)S(1)}, bf16[256,64]{1,0:T(8,128)(2,1)S(1)}, u32[]{:S(2)}, u32[]{:S(2)}) collective-permute-start(bf16[256,64]{1,0:T(8,128)(2,1)S(1)} %get-tuple-element.16), channel_id=1, source_target_pairs={{0,1},{1,2},{2,3},{4,5},{5,6},{6,7},{8,9},{9,10},{10,11},{12,13},{... | collective-permute-start | bytes 98312 | tf_op jit(solution)/shard_map/ppermute | solution.py:23
  14.3 9.5 %collective-permute-start.1 = (bf16[256,64]{1,0:T(8,128)(2,1)S(1)}, bf16[256,64]{1,0:T(8,128)(2,1)S(1)}, u32[]{:S(2)}, u32[]{:S(2)}) collective-permute-start(bf16[256,64]{1,0:T(8,128)(2,1)S(1)} %get-tuple-element.15), channel_id=1, source_target_pairs={{1,0},{2,1},{3,2},{5,4},{6,5},{7,6},{9,8},{10,9},{11,10},{13,12},{... | collective-permute-start | bytes 98312 | tf_op jit(solution)/shard_map/ppermute | solution.py:26
  25.6 2.4 %copy-start.1 = (f32[256,20,256]{2,0,1:T(8,128)}, f32[256,20,256]{2,0,1:T(8,128)S(1)}, u32[]{:S(2)}) copy-start(f32[256,20,256]{2,0,1:T(8,128)S(1)} %convolution_bitcast_fusion) | copy-start | bytes 15728644
  27.9 21.1 %collective-permute-start.2 = (f32[4,5120]{1,0:T(4,128)S(1)}, f32[4,5120]{1,0:T(4,128)S(1)}, u32[]{:S(2)}, u32[]{:S(2)}) collective-permute-start(f32[4,5120]{1,0:T(4,128)S(1)} %bitcast.79), channel_id=1, source_target_pairs={{4,0},{8,4},{12,8},{16,12},{20,16},{24,20},{28,24},{32,28},{36,32}... | collective-permute-start | bytes 245768 | tf_op jit(solution)/shard_map/ppermute | solution.py:26
  35.2 13.8 %collective-permute-start.3 = (f32[4,5120]{1,0:T(4,128)S(1)}, f32[4,5120]{1,0:T(4,128)S(1)}, u32[]{:S(2)}, u32[]{:S(2)}) collective-permute-start(f32[4,5120]{1,0:T(4,128)S(1)} %bitcast.78), channel_id=1, source_target_pairs={{0,4},{4,8},{8,12},{12,16},{16,20},{20,24},{24,28},{28,32},{32,36}... | collective-permute-start | bytes 245768 | tf_op jit(solution)/shard_map/ppermute | solution.py:23
  53.7 67.6 %collective-permute-start.5 = (bf16[256,5120]{1,0:T(8,128)(2,1)S(1)}, bf16[256,5120]{1,0:T(8,128)(2,1)}, u32[]{:S(2)}, u32[]{:S(2)}) collective-permute-start(bf16[256,5120]{1,0:T(8,128)(2,1)S(1)} %fusion.4), channel_id=1, source_target_pairs={{0,4},{4,8},{8,12},{12,16},{16,20},{20,24},{24,28},{28,32},{32,36}... | collective-permute-start | bytes 7864328 | tf_op jit(solution)/shard_map/ppermute | solution.py:34
  56.8 58.7 %collective-permute-start.6 = (bf16[128,5120]{1,0:T(8,128)(2,1)}, bf16[128,5120]{1,0:T(8,128)(2,1)}, u32[]{:S(2)}, u32[]{:S(2)}) collective-permute-start(bf16[128,5120]{1,0:T(8,128)(2,1)} %slice.176), channel_id=1, source_target_pairs={{4,0},{8,4},{12,8},{16,12},{20,16},{24,20},{28,24},{32,28},{36,32}... | collective-permute-start | bytes 3932168 | tf_op jit(solution)/shard_map/ppermute | solution.py:34
  66.0 113.5 %all-reduce.8.cloned.1.call-start = ((), (), s32[]{:S(2)}) async-start(), calls=%async_computation.1 | async-start | bytes 917504 | tf_op jit(solution)/shard_map/psum | solution.py:121
  126.1 3.3 %copy-start.2 = (f32[256,256]{1,0:T(8,128)S(1)}, f32[256,256]{1,0:T(8,128)}, u32[]{:S(2)}) copy-start(f32[256,256]{1,0:T(8,128)} %all-reduce.6.cloned.1.call-done) | copy-start | bytes 786436
  129.5 53.8 %collective-permute-start.4 = (f32[256,256]{0,1:T(8,128)S(1)}, f32[256,256]{0,1:T(8,128)S(1)}, u32[]{:S(2)}, u32[]{:S(2)}) collective-permute-start(f32[256,256]{0,1:T(8,128)S(1)} %copy.13), channel_id=1, source_target_pairs={{0,4},{4,8},{8,12},{12,16},{16,20},{20,24},{24,28},{28,32},{32,36}... | collective-permute-start | bytes 786440 | tf_op jit(solution)/shard_map/ppermute | solution.py:34
  132.1 56.1 %collective-permute-start.7 = (f32[128,128]{1,0:T(8,128)}, f32[128,128]{1,0:T(8,128)}, u32[]{:S(2)}, u32[]{:S(2)}) collective-permute-start(f32[128,128]{1,0:T(8,128)} %slice.179), channel_id=1, source_target_pairs={{4,0},{8,4},{12,8},{16,12},{20,16},{24,20},{28,24},{32,28},{36,32}... | collective-permute-start | bytes 196616 | tf_op jit(solution)/shard_map/ppermute | solution.py:34
  183.3 0.7 copy-start.3
  213.0 4.0 %copy-start.4 = (bf16[2,16,512]{2,1,0:T(8,128)(2,1)S(1)}, bf16[2,16,512]{2,1,0:T(8,128)(2,1)}, u32[]{:S(2)}) copy-start(bf16[2,16,512]{2,1,0:T(8,128)(2,1)} %shard_map.37) | copy-start | bytes 98308
Sparse Core Ops, SparseCore 0:
  66.1 49.3 all-reduce.5
  129.5 49.9 all-reduce.7

commit v2 on v1

--- a/solution.py
+++ b/solution.py
@@ -85,22 +85,55 @@
     )(band, start_t)
 
 
+def fir_kernel(head_ref, tail_ref, top_ref, rest_ref, out_ref):
+    out_ref[...] = jnp.dot(
+        head_ref[...], top_ref[...], preferred_element_type=jnp.float32
+    ) + jnp.dot(tail_ref[...], rest_ref[...], preferred_element_type=jnp.float32)
+
+
+def fir(padded, fir_taps, chans, samples):
+    width = math.gcd(samples, 512)
+    edge = TAPS - 1
+    band = toeplitz_band(fir_taps, width)
+    top, rest = band[:width], band[width:]
+    step = width // edge
+    return pl.pallas_call(
+        fir_kernel,
+        grid=(samples // width,),
+        out_shape=jax.ShapeDtypeStruct((chans, samples), jnp.float32),
+        in_specs=[
+            pl.BlockSpec((chans, width), lambda b: (0, b)),
+            pl.BlockSpec((chans, edge), lambda b: (0, (b + 1) * step)),
+            pl.BlockSpec((width, width), lambda b: (0, 0)),
+            pl.BlockSpec((edge, width), lambda b: (0, 0)),
+        ],
+        out_specs=pl.BlockSpec((chans, width), lambda b: (0, b)),
+    )(padded, padded, top, rest)
+
+
+def ta_sum(value):
+    count = lax.axis_size("ta")
+    if count != 4:
+        return lax.psum(value, "ta")
+    core = lax.axis_index("ta") % 2
+    rows = value.shape[0] // 2
+    low, high = value[:rows], value[rows:]
+    mine = jnp.where(core == 0, low, high)
+    theirs = jnp.where(core == 0, high, low)
+    partner = [(i, i ^ 1) for i in range(count)]
+    across = [(i, i ^ 2) for i in range(count)]
+    part = mine + lax.ppermute(theirs, "ta", partner)
+    part = part + lax.ppermute(part, "ta", across)
+    other = lax.ppermute(part, "ta", partner)
+    return jnp.where(core == 0, jnp.concatenate([part, other]), jnp.concatenate([other, part]))
+
+
 def per_device(raw, fir_taps, start_basis):
     chans = raw.shape[0]
     samples = raw.shape[1]
     half = (TAPS - 1) // 2
-    width = math.gcd(samples, 256)
     padded = with_halo(raw, (("ta", 1),), half)
-    band_matrix = toeplitz_band(fir_taps, width)
-    pieces = jnp.stack(
-        [
-            padded[:, number * width : number * width + width + TAPS - 1]
-            for number in range(samples // width)
-        ]
-    )
-    filtered = jnp.einsum(
-        "bct,tu->cbu", pieces, band_matrix, preferred_element_type=jnp.float32
-    ).reshape(chans, samples)
+    filtered = fir(padded, fir_taps, chans, samples)
     extended = with_halo(filtered, (("ch", 0),), GAUGE)
     gauged = (extended[2 * GAUGE :] - extended[: -2 * GAUGE]).astype(jnp.bfloat16)
 
@@ -110,7 +143,7 @@
     lower_part = shifted(gauged[chans - 2 * STRIDE :], "ch", 1)
     upper_part = shifted(gauged[:STRIDE], "ch", -1)
 
-    own = lax.psum(gram(gauged, gauged), "ta")
+    own = ta_sum(gram(gauged, gauged))
     own_left = shifted(own[chans - 2 * STRIDE :, chans - 2 * STRIDE :], "ch", 1)
     own_right = shifted(own[:STRIDE, :STRIDE], "ch", -1)
 
@@ -118,7 +151,12 @@
     cross_left = gram(lower_part, gauged)
     tail = jnp.concatenate([lower_part[STRIDE:], gauged], axis=0)
     cross_right = gram(tail, upper_part)
-    cross_left, cross_right = lax.psum((cross_left, cross_right), "ta")
+    packed = ta_sum(jnp.concatenate([cross_left[:, :STRIDE], cross_left[:, STRIDE:], cross_right], axis=0))
+    tiles_left = lower_part.shape[0]
+    cross_left = jnp.concatenate(
+        [packed[:tiles_left], packed[tiles_left : 2 * tiles_left]], axis=1
+    )
+    cross_right = packed[2 * tiles_left :]
 
     zeros = jnp.zeros((STRIDE, STRIDE), jnp.float32)
     top = jnp.concatenate(

time: 236 us -> 196 us (0.83); the launches traced: 231 us -> 195 us
  waiting for transfers between devices: 97.6 us -> 73.6 us
  between operations: 13.7 us -> 0.32 us
  local copies, waits for them, and re-layouts: 30 us -> 20.1 us
  Pallas kernels: 22.3 us -> 31.4 us
  starting transfers between devices: 37 us -> 44.8 us
  matrix products: 17.6 us -> 12.6 us
    psum x2 -> x0, waiting for transfers between devices: 89.1 us -> none  [the longest x1 49.4 us: per_device(): own = lax.psum(gram(gauged, gauged), 'ta')]
    ppermute x0 -> x6, waiting for transfers between devices: none -> 45.3 us  [the longest x2 41.5 us: ta_sum(): part = part + lax.ppermute(part, 'ta', across)]
    ppermute x4, waiting for transfers between devices: 5.91 us -> 20.9 us  [shifted(): lax.ppermute(value, axis, [(source, source + steps) for source in range(f...]
    pallas_call x0 -> x1, Pallas kernels: none -> 9.11 us  [fir(): pl.pallas_call(fir_kernel, grid=(samples // width,), out_shape=jax.ShapeD...]
    ppermute x2, waiting for transfers between devices: 0.01 us -> 7.47 us  [with_halo(): lax.ppermute(lax.slice_in_dim(block, block.shape[dim] - width, None, axis...]
    ppermute x0 -> x6, starting transfers between devices: none -> 7.18 us  [the longest x2 3.57 us: ta_sum(): other = lax.ppermute(part, 'ta', partner)]
    unnamed x29 -> x6, local copies, waits for them, and re-layouts: 6.19 us -> 0.01 us
    reshape x1 -> x0, local copies, waits for them, and re-layouts: 5.96 us -> none  [per_device(): filtered = jnp.einsum('bct,tu->cbu', pieces, band_matrix, preferred_eleme...]
  transfers between devices with their start and end apart: 10 -> 14, of which waited for: 4 -> 7; matrix products, arithmetic and copies ran while one was open for 12% -> 8% of each run, Pallas kernels for 0% -> 0%
where the time goes in v2:
time: 196 us; the launch traced here: 195 us
  waiting for transfers between devices  73.6 us (38%)
  starting transfers between devices  44.8 us (23%)
  Pallas kernels  31.4 us (16%)
  local copies, waits for them, and re-layouts  20.1 us (10%)
  matrix products  12.6 us (6%)
  other arithmetic  12.4 us (6%)
    ppermute x2, waiting for transfers between devices, ta_sum(): part = part + lax.ppermute(part, 'ta', across)  41.5 us
    pallas_call x1, Pallas kernels, subspace(): pl.pallas_call(subspace_kernel, out_shape=jax.ShapeDtypeStruct((windows,)...  22.3 us
    ppermute x4, waiting for transfers between devices, shifted(): lax.ppermute(value, axis, [(source, source + steps) for source in range(f...  20.9 us
    ppermute x4, starting transfers between devices, shifted(): lax.ppermute(value, axis, [(source, source + steps) for source in range(f...  19.8 us
    pallas_call x1, Pallas kernels, fir(): pl.pallas_call(fir_kernel, grid=(samples // width,), out_shape=jax.ShapeD...  9.11 us
    ppermute x2, starting transfers between devices, with_halo(): lax.ppermute(lax.slice_in_dim(block, 0, width, axis=dim), axis, backward)  9 us
    ppermute x2, starting transfers between devices, with_halo(): lax.ppermute(lax.slice_in_dim(block, block.shape[dim] - width, None, axis...  8.81 us
    dot_general x2, matrix products, per_device(): lax.dot_general(rounded[number, :, 2 * STRIDE:3 * STRIDE], coeffs, (((0,)...  7.89 us
  transfers between devices with their start and end apart: 14, of which 7 were waited for; matrix products, arithmetic and copies ran while one was open for 8% of the time, Pallas kernels for 0%

profile of v2, /device:TPU:97, one launch (start us, length us, event | category | flops | bytes accessed | tf_op | source)
XLA Modules:
  0.0 195.1 jit_solution(4638562921137885406)
XLA Ops:
  0.0 1.0 fusion.25
  1.0 2.6 %collective-permute-start.1 = (bf16[256,64]{1,0:T(8,128)(2,1)S(1)}, bf16[256,64]{1,0:T(8,128)(2,1)S(1)}, u32[]{:S(2)}, u32[]{:S(2)}) collective-permute-start(bf16[256,64]{1,0:T(8,128)(2,1)S(1)} %get-tuple-element.13), channel_id=1, source_target_pairs={{1,0},{2,1},{3,2},{5,4},{6,5},{7,6},{9,8},{10,9},{11,10},{13,12},{... | collective-permute-start | bytes 98312 | tf_op jit(solution)/shard_map/ppermute | solution.py:26
  3.6 6.9 %collective-permute-start = (bf16[256,64]{1,0:T(8,128)(2,1)S(1)}, bf16[256,64]{1,0:T(8,128)(2,1)S(1)}, u32[]{:S(2)}, u32[]{:S(2)}) collective-permute-start(bf16[256,64]{1,0:T(8,128)(2,1)S(1)} %get-tuple-element.14), channel_id=1, source_target_pairs={{0,1},{1,2},{2,3},{4,5},{5,6},{6,7},{8,9},{9,10},{10,11},{12,13},{... | collective-permute-start | bytes 98312 | tf_op jit(solution)/shard_map/ppermute | solution.py:23
  10.4 0.7 concatenate.64
  11.2 1.3 tile.10
  12.5 0.9 slice.128
  13.3 2.4 %reshape.4 = bf16[512,640]{1,0:T(8,128)(2,1)} reshape(bf16[327680]{0:T(1024)(128)(2,1)} %slice.128) | data formatting | bytes 1310720 | tf_op jit(solution)/shard_map/reshape | solution.py:41
  15.8 1.3 copy.7
  17.1 0.7 slice.130.rest_ref
  17.8 0.8 slice.129.top_ref
  18.6 4.3 %concatenate.63.head_ref.tail_ref = bf16[256,5248]{1,0:T(8,128)(2,1)} concatenate(bf16[256,64]{1,0:T(8,128)(2,1)S(1)} %collective-permute-done, bf16[256,5120]{1,0:T(8,128)(2,1)S(1)} %copy-done, bf16[256,64]{1,0:T(8,128)(2,1)S(1)} %collective-permute-done.1), dimensions={1} | concatenate | bytes 5373952 | tf_op jit(solution)/shard_map/concatenate | solution.py:27
  22.9 9.1 %shard_map.37 = f32[256,5120]{1,0:T(8,128)} custom-call(bf16[256,5248]{1,0:T(8,128)(2,1)} %concatenate.63.head_ref.tail_ref, bf16[256,5248]{1,0:T(8,128)(2,1)} %concatenate.63.head_ref.tail_ref, bf16[512,512]{1,0:T(8,128)(2,1)} %slice.129.top_ref, bf16[128,512]{1,0:T(8,128)(2,1)} %slice.130.rest_ref), custom_call_target="tpu_custom_call" | custom-call | tf_op jit(solution)/shard_map/pallas_call | solution.py:100
  32.0 1.0 fusion.24
  33.1 6.4 %collective-permute-start.2 = (f32[4,5120]{1,0:T(4,128)S(1)}, f32[4,5120]{1,0:T(4,128)S(1)}, u32[]{:S(2)}, u32[]{:S(2)}) collective-permute-start(f32[4,5120]{1,0:T(4,128)S(1)} %get-tuple-element.11), channel_id=1, source_target_pairs={{4,0},{8,4},{12,8},{16,12},{20,16},{24,20},{28,24},{32,28},{36,32}... | collective-permute-start | bytes 245768 | tf_op jit(solution)/shard_map/ppermute | solution.py:26
  39.5 1.9 collective-permute-start.3
  41.4 7.5 %collective-permute-done.3 = f32[4,5120]{1,0:T(4,128)S(1)} collective-permute-done((f32[4,5120]{1,0:T(4,128)S(1)}, f32[4,5120]{1,0:T(4,128)S(1)}, u32[]{:S(2)}, u32[]{:S(2)}) %collective-permute-start.3) | collective-permute-done | bytes 81952 | tf_op jit(solution)/shard_map/ppermute | solution.py:23
  48.9 4.7 %fusion.4 = bf16[256,5120]{1,0:T(8,128)(2,1)S(1)} fusion(f32[256,5120]{1,0:T(8,128)} %shard_map.37, f32[4,5120]{1,0:T(4,128)S(1)} %collective-permute-done.3, f32[4,5120]{1,0:T(4,128)S(1)} %collective-permute-done.2), kind=kLoop, calls=%fused_computation.11 | loop fusion | flops 5242880 | bytes 8028160 | tf_op jit(solution)/shard_map/convert_element_type | solution.py:138
  53.6 1.9 collective-permute-start.8
  55.6 7.6 %collective-permute-start.9 = (bf16[128,5120]{1,0:T(8,128)(2,1)S(1)}, bf16[128,5120]{1,0:T(8,128)(2,1)S(1)}, u32[]{:S(2)}, u32[]{:S(2)}) collective-permute-start(bf16[128,5120]{1,0:T(8,128)(2,1)S(1)} %slice.133), channel_id=1, source_target_pairs={{4,0},{8,4},{12,8},{16,12},{20,16},{24,20},{28,24},{32,28},{36,32}... | collective-permute-start | bytes 3932168 | tf_op jit(solution)/shard_map/ppermute | solution.py:34
  63.2 0.9 fusion.28
  64.1 0.1 collective-permute-start.4
  64.2 1.3 collective-permute-done.4
  65.6 2.3 %collective-permute-start.5 = (f32[128,256]{1,0:T(8,128)S(1)}, f32[128,256]{1,0:T(8,128)S(1)}, u32[]{:S(2)}, u32[]{:S(2)}) collective-permute-start(f32[128,256]{1,0:T(8,128)S(1)} %select_add_fusion.1), channel_id=1, source_target_pairs={{0,2},{1,3},{2,0},{3,1},{4,6},{5,7},{6,4},{7,5},{8,10},{9,11},{10,... | collective-permute-start | bytes 393224 | tf_op jit(solution)/shard_map/ppermute | solution.py:126
  67.9 27.2 %collective-permute-done.5 = f32[128,256]{1,0:T(8,128)S(1)} collective-permute-done((f32[128,256]{1,0:T(8,128)S(1)}, f32[128,256]{1,0:T(8,128)S(1)}, u32[]{:S(2)}, u32[]{:S(2)}) %collective-permute-start.5) | collective-permute-done | bytes 131104 | tf_op jit(solution)/shard_map/ppermute | solution.py:126
  95.1 3.0 %collective-permute-start.6 = (f32[128,256]{1,0:T(8,128)S(1)}, f32[128,256]{1,0:T(8,128)S(1)}, u32[]{:S(2)}, u32[]{:S(2)}) collective-permute-start(f32[128,256]{1,0:T(8,128)S(1)} %add.23), channel_id=1, source_target_pairs={{0,1},{1,0},{2,3},{3,2},{4,5},{5,4},{6,7},{7,6},{8,9},{9,8},{10,11... | collective-permute-start | bytes 393224 | tf_op jit(solution)/shard_map/ppermute | solution.py:127
  98.1 1.0 collective-permute-done.6
  99.2 20.8 %collective-permute-done.8 = bf16[256,5120]{1,0:T(8,128)(2,1)} collective-permute-done((bf16[256,5120]{1,0:T(8,128)(2,1)S(1)}, bf16[256,5120]{1,0:T(8,128)(2,1)}, u32[]{:S(2)}, u32[]{:S(2)}) %collective-permute-start.8) | collective-permute-done | bytes 2621472 | tf_op jit(solution)/shard_map/ppermute | solution.py:34
  120.0 2.6 %fusion.29 = f32[256,256]{1,0:T(8,128)S(1)} fusion(bf16[256,5120]{1,0:T(8,128)(2,1)} %collective-permute-done.8, bf16[256,5120]{1,0:T(8,128)(2,1)S(1)} %fusion.4), kind=kOutput, calls=%fused_computation.51 | convolution fusion | flops 671088640 | bytes 5505024 | tf_op jit(solution)/shard_map/dot_general | solution.py:45
  122.6 1.4 slice.115
  124.1 1.2 fusion.8
  125.3 0.1 collective-permute-start.10
  125.4 1.5 collective-permute-done.10
  126.9 1.1 collective-permute-start.11
  128.0 14.3 %collective-permute-done.11 = f32[448,128]{1,0:T(8,128)S(1)} collective-permute-done((f32[448,128]{1,0:T(8,128)S(1)}, f32[448,128]{1,0:T(8,128)S(1)}, u32[]{:S(2)}, u32[]{:S(2)}) %collective-permute-start.11) | collective-permute-done | bytes 229408 | tf_op jit(solution)/shard_map/ppermute | solution.py:126
  142.4 0.5 collective-permute-start.12
  142.9 0.6 slice.142
  143.5 1.9 collective-permute-start.7
  145.4 8.4 %collective-permute-start.13 = (f32[128,128]{1,0:T(8,128)}, f32[128,128]{1,0:T(8,128)}, u32[]{:S(2)}, u32[]{:S(2)}) collective-permute-start(f32[128,128]{1,0:T(8,128)} %slice.142), channel_id=1, source_target_pairs={{4,0},{8,4},{12,8},{16,12},{20,16},{24,20},{28,24},{32,28},{36,32}... | collective-permute-start | bytes 196616 | tf_op jit(solution)/shard_map/ppermute | solution.py:34
  153.9 0.7 copy.9
  154.6 0.8 fusion.26
  155.4 1.0 copy.10
  156.4 1.6 maximum_bitcast_fusion
  158.0 1.1 copy.8
  159.2 2.5 %fusion.14.band_ref = f32[640,640]{1,0:T(8,128)} fusion(f32[128,128]{1,0:T(8,128)S(1)} %get-tuple-element.20, f32[128,128]{1,0:T(8,128)} %collective-permute-done.13, f32[128,256]{1,0:T(8,128)S(1)} %copy.10, f32[128,128]{1,0:T(8,128)} %copy.9, f32[128,128]{1,0:T(8,128)S(1)} %broadcast_in_dim.4, f32[256,128]{1,0:T(8,128)} %get-tuple-element.17, ...), kind=kLoop, calls=%fused_computation.24 | loop fusion | flops 6553600 | bytes 3211264 | tf_op jit(solution)/shard_map/div | solution.py:170
  161.6 22.3 %shard_map.38 = bf16[2,16,512]{2,1,0:T(8,128)(2,1)} custom-call(f32[640,640]{1,0:T(8,128)} %fusion.14.band_ref, f32[16,512]{1,0:T(8,128)} %bitcast.29), custom_call_target="tpu_custom_call" | custom-call | tf_op jit(solution)/shard_map/pallas_call | solution.py:77
  183.9 3.9 %fusion.1 = bf16[128,5120]{1,0:T(8,128)(2,1)} fusion(bf16[256,5120]{1,0:T(8,128)(2,1)S(1)} %fusion.4, bf16[128,5120]{1,0:T(8,128)(2,1)} %copy-done.2, bf16[256,5120]{1,0:T(8,128)(2,1)} %collective-permute-done.8, bf16[2,16,512]{2,1,0:T(8,128)(2,1)} %shard_map.38), kind=kOutput, calls=%fused_computation.3 | convolution fusion | flops 122634240 | bytes 9195520 | tf_op jit(solution)/shard_map/dot_general | solution.py:181
  187.8 3.9 %fusion = bf16[128,5120]{1,0:T(8,128)(2,1)} fusion(bf16[256,5120]{1,0:T(8,128)(2,1)S(1)} %fusion.4, bf16[256,5120]{1,0:T(8,128)(2,1)} %collective-permute-done.8, bf16[2,16,512]{2,1,0:T(8,128)(2,1)S(1)} %copy-done.1), kind=kOutput, calls=%fused_computation.2 | convolution fusion | flops 117391360 | bytes 7884800 | tf_op jit(solution)/shard_map/dot_general | solution.py:181
  191.8 3.4 %pad_maximum_fusion.6 = bf16[256,5120]{1,0:T(8,128)(2,1)} fusion(bf16[128,5120]{1,0:T(8,128)(2,1)} %fusion.1, bf16[128,5120]{1,0:T(8,128)(2,1)} %fusion), kind=kLoop, calls=%fused_computation.20 | loop fusion | flops 5242880 | bytes 5242880 | tf_op jit(solution)/shard_map/concatenate | solution.py:188
  (26 shorter events, 0.4 us)
Async XLA Ops:
  1.0 17.6 %collective-permute-start.1 = (bf16[256,64]{1,0:T(8,128)(2,1)S(1)}, bf16[256,64]{1,0:T(8,128)(2,1)S(1)}, u32[]{:S(2)}, u32[]{:S(2)}) collective-permute-start(bf16[256,64]{1,0:T(8,128)(2,1)S(1)} %get-tuple-element.13), channel_id=1, source_target_pairs={{1,0},{2,1},{3,2},{5,4},{6,5},{7,6},{9,8},{10,9},{11,10},{13,12},{... | collective-permute-start | bytes 98312 | tf_op jit(solution)/shard_map/ppermute | solution.py:26
  3.6 15.1 %collective-permute-start = (bf16[256,64]{1,0:T(8,128)(2,1)S(1)}, bf16[256,64]{1,0:T(8,128)(2,1)S(1)}, u32[]{:S(2)}, u32[]{:S(2)}) collective-permute-start(bf16[256,64]{1,0:T(8,128)(2,1)S(1)} %get-tuple-element.14), channel_id=1, source_target_pairs={{0,1},{1,2},{2,3},{4,5},{5,6},{6,7},{8,9},{9,10},{10,11},{12,13},{... | collective-permute-start | bytes 98312 | tf_op jit(solution)/shard_map/ppermute | solution.py:23
  12.4 6.2 %copy-start = (bf16[256,5120]{1,0:T(8,128)(2,1)S(1)}, bf16[256,5120]{1,0:T(8,128)(2,1)}, u32[]{:S(2)}) copy-start(bf16[256,5120]{1,0:T(8,128)(2,1)} %param.3) | copy-start | bytes 7864324
  33.1 8.4 %collective-permute-start.2 = (f32[4,5120]{1,0:T(4,128)S(1)}, f32[4,5120]{1,0:T(4,128)S(1)}, u32[]{:S(2)}, u32[]{:S(2)}) collective-permute-start(f32[4,5120]{1,0:T(4,128)S(1)} %get-tuple-element.11), channel_id=1, source_target_pairs={{4,0},{8,4},{12,8},{16,12},{20,16},{24,20},{28,24},{32,28},{36,32}... | collective-permute-start | bytes 245768 | tf_op jit(solution)/shard_map/ppermute | solution.py:26
  39.5 9.4 %collective-permute-start.3 = (f32[4,5120]{1,0:T(4,128)S(1)}, f32[4,5120]{1,0:T(4,128)S(1)}, u32[]{:S(2)}, u32[]{:S(2)}) collective-permute-start(f32[4,5120]{1,0:T(4,128)S(1)} %get-tuple-element.12), channel_id=1, source_target_pairs={{0,4},{4,8},{8,12},{12,16},{16,20},{20,24},{24,28},{28,32},{32,36}... | collective-permute-start | bytes 245768 | tf_op jit(solution)/shard_map/ppermute | solution.py:23
  53.6 66.4 %collective-permute-start.8 = (bf16[256,5120]{1,0:T(8,128)(2,1)S(1)}, bf16[256,5120]{1,0:T(8,128)(2,1)}, u32[]{:S(2)}, u32[]{:S(2)}) collective-permute-start(bf16[256,5120]{1,0:T(8,128)(2,1)S(1)} %fusion.4), channel_id=1, source_target_pairs={{0,4},{4,8},{8,12},{12,16},{16,20},{20,24},{24,28},{28,32},{32,36}... | collective-permute-start | bytes 7864328 | tf_op jit(solution)/shard_map/ppermute | solution.py:34
  55.6 43.5 %collective-permute-start.9 = (bf16[128,5120]{1,0:T(8,128)(2,1)S(1)}, bf16[128,5120]{1,0:T(8,128)(2,1)S(1)}, u32[]{:S(2)}, u32[]{:S(2)}) collective-permute-start(bf16[128,5120]{1,0:T(8,128)(2,1)S(1)} %slice.133), channel_id=1, source_target_pairs={{4,0},{8,4},{12,8},{16,12},{20,16},{24,20},{28,24},{32,28},{36,32}... | collective-permute-start | bytes 3932168 | tf_op jit(solution)/shard_map/ppermute | solution.py:34
  64.1 1.4 collective-permute-start.4
  65.6 29.5 %collective-permute-start.5 = (f32[128,256]{1,0:T(8,128)S(1)}, f32[128,256]{1,0:T(8,128)S(1)}, u32[]{:S(2)}, u32[]{:S(2)}) collective-permute-start(f32[128,256]{1,0:T(8,128)S(1)} %select_add_fusion.1), channel_id=1, source_target_pairs={{0,2},{1,3},{2,0},{3,1},{4,6},{5,7},{6,4},{7,5},{8,10},{9,11},{10,... | collective-permute-start | bytes 393224 | tf_op jit(solution)/shard_map/ppermute | solution.py:126
  95.1 4.0 %collective-permute-start.6 = (f32[128,256]{1,0:T(8,128)S(1)}, f32[128,256]{1,0:T(8,128)S(1)}, u32[]{:S(2)}, u32[]{:S(2)}) collective-permute-start(f32[128,256]{1,0:T(8,128)S(1)} %add.23), channel_id=1, source_target_pairs={{0,1},{1,0},{2,3},{3,2},{4,5},{5,4},{6,7},{7,6},{8,9},{9,8},{10,11... | collective-permute-start | bytes 393224 | tf_op jit(solution)/shard_map/ppermute | solution.py:127
  99.2 24.9 %copy-start.2 = (bf16[128,5120]{1,0:T(8,128)(2,1)}, bf16[128,5120]{1,0:T(8,128)(2,1)S(1)}, u32[]{:S(2)}) copy-start(bf16[128,5120]{1,0:T(8,128)(2,1)S(1)} %collective-permute-done.9) | copy-start | bytes 3932164
  125.3 1.6 collective-permute-start.10
  126.9 15.4 %collective-permute-start.11 = (f32[448,128]{1,0:T(8,128)S(1)}, f32[448,128]{1,0:T(8,128)S(1)}, u32[]{:S(2)}, u32[]{:S(2)}) collective-permute-start(f32[448,128]{1,0:T(8,128)S(1)} %select_add_fusion), channel_id=1, source_target_pairs={{0,2},{1,3},{2,0},{3,1},{4,6},{5,7},{6,4},{7,5},{8,10},{9,11},{10,... | collective-permute-start | bytes 688136 | tf_op jit(solution)/shard_map/ppermute | solution.py:126
  142.4 11.5 %collective-permute-start.12 = (f32[448,128]{1,0:T(8,128)S(1)}, f32[448,128]{1,0:T(8,128)S(1)}, u32[]{:S(2)}, u32[]{:S(2)}) collective-permute-start(f32[448,128]{1,0:T(8,128)S(1)} %add.25), channel_id=1, source_target_pairs={{0,1},{1,0},{2,3},{3,2},{4,5},{5,4},{6,7},{7,6},{8,9},{9,8},{10,11... | collective-permute-start | bytes 688136 | tf_op jit(solution)/shard_map/ppermute | solution.py:127
  143.5 15.6 %collective-permute-start.7 = (f32[256,256]{1,0:T(8,128)S(1)}, f32[256,256]{1,0:T(8,128)}, u32[]{:S(2)}, u32[]{:S(2)}) collective-permute-start(f32[256,256]{1,0:T(8,128)S(1)} %maximum_select_fusion.1), channel_id=1, source_target_pairs={{0,4},{4,8},{8,12},{12,16},{16,20},{20,24},{24,28},{28,32},{32,36}... | collective-permute-start | bytes 786440 | tf_op jit(solution)/shard_map/ppermute | solution.py:34
  145.4 13.7 %collective-permute-start.13 = (f32[128,128]{1,0:T(8,128)}, f32[128,128]{1,0:T(8,128)}, u32[]{:S(2)}, u32[]{:S(2)}) collective-permute-start(f32[128,128]{1,0:T(8,128)} %slice.142), channel_id=1, source_target_pairs={{4,0},{8,4},{12,8},{16,12},{20,16},{24,20},{28,24},{32,28},{36,32}... | collective-permute-start | bytes 196616 | tf_op jit(solution)/shard_map/ppermute | solution.py:34
  183.9 3.9 %copy-start.1 = (bf16[2,16,512]{2,1,0:T(8,128)(2,1)S(1)}, bf16[2,16,512]{2,1,0:T(8,128)(2,1)}, u32[]{:S(2)}) copy-start(bf16[2,16,512]{2,1,0:T(8,128)(2,1)} %shard_map.38) | copy-start | bytes 98308

commit v3 on v2

--- a/solution.py
+++ b/solution.py
@@ -91,8 +91,9 @@
     ) + jnp.dot(tail_ref[...], rest_ref[...], preferred_element_type=jnp.float32)
 
 
-def fir(padded, fir_taps, chans, samples):
-    width = math.gcd(samples, 512)
+def fir(padded, fir_taps, chans, samples, start):
+    width = math.gcd(math.gcd(samples, start) if start else samples, 512)
+    first = start // width
     edge = TAPS - 1
     band = toeplitz_band(fir_taps, width)
     top, rest = band[:width], band[width:]
@@ -102,13 +103,52 @@
         grid=(samples // width,),
         out_shape=jax.ShapeDtypeStruct((chans, samples), jnp.float32),
         in_specs=[
-            pl.BlockSpec((chans, width), lambda b: (0, b)),
-            pl.BlockSpec((chans, edge), lambda b: (0, (b + 1) * step)),
+            pl.BlockSpec((chans, width), lambda b: (0, b + first)),
+            pl.BlockSpec((chans, edge), lambda b: (0, (b + first + 1) * step)),
             pl.BlockSpec((width, width), lambda b: (0, 0)),
             pl.BlockSpec((edge, width), lambda b: (0, 0)),
         ],
         out_specs=pl.BlockSpec((chans, width), lambda b: (0, b)),
     )(padded, padded, top, rest)
+
+
+def clean_kernel(lower_ref, own_ref, upper_ref, basis_ref, middle_ref, out_ref):
+    tiles = own_ref.shape[0] // STRIDE
+    parts = [lower_ref[k * STRIDE : (k + 1) * STRIDE] for k in range(2)]
+    parts += [own_ref[k * STRIDE : (k + 1) * STRIDE] for k in range(tiles)]
+    parts.append(upper_ref[...])
+    for number in range(tiles):
+        coeffs = jnp.dot(basis_ref[number, :, 0:STRIDE], parts[number], preferred_element_type=jnp.float32)
+        for k in range(1, WIN // STRIDE):
+            coeffs = coeffs + jnp.dot(
+                basis_ref[number, :, k * STRIDE : (k + 1) * STRIDE], parts[number + k],
+                preferred_element_type=jnp.float32,
+            )
+        fitted = jnp.dot(
+            middle_ref[number], coeffs.astype(jnp.bfloat16), preferred_element_type=jnp.float32
+        )
+        out_ref[number * STRIDE : (number + 1) * STRIDE] = (
+            parts[number + 2].astype(jnp.float32) - fitted
+        ).astype(out_ref.dtype)
+
+
+def clean(lower, own, upper, rounded):
+    chans, samples = own.shape
+    width = math.gcd(samples, 512)
+    middle = jnp.swapaxes(rounded[:, :, 2 * STRIDE : 3 * STRIDE], 1, 2)
+    return pl.pallas_call(
+        clean_kernel,
+        grid=(samples // width,),
+        out_shape=jax.ShapeDtypeStruct((chans, samples), own.dtype),
+        in_specs=[
+            pl.BlockSpec((lower.shape[0], width), lambda b: (0, b)),
+            pl.BlockSpec((chans, width), lambda b: (0, b)),
+            pl.BlockSpec((STRIDE, width), lambda b: (0, b)),
+            pl.BlockSpec(rounded.shape, lambda b: (0, 0, 0)),
+            pl.BlockSpec(middle.shape, lambda b: (0, 0, 0)),
+        ],
+        out_specs=pl.BlockSpec((chans, width), lambda b: (0, b)),
+    )(lower, own, upper, rounded, middle)
 
 
 def ta_sum(value):
@@ -133,26 +173,40 @@
     samples = raw.shape[1]
     half = (TAPS - 1) // 2
     padded = with_halo(raw, (("ta", 1),), half)
-    filtered = fir(padded, fir_taps, chans, samples)
-    extended = with_halo(filtered, (("ch", 0),), GAUGE)
-    gauged = (extended[2 * GAUGE :] - extended[: -2 * GAUGE]).astype(jnp.bfloat16)
-
+    chunks = 2 if samples % 1024 == 0 else 1
+    piece = samples // chunks
     tiles = chans // STRIDE
     windows = tiles
     total_time = samples * lax.axis_size("ta")
-    lower_part = shifted(gauged[chans - 2 * STRIDE :], "ch", 1)
-    upper_part = shifted(gauged[:STRIDE], "ch", -1)
-
-    own = ta_sum(gram(gauged, gauged))
+    gaugeds, lowers, uppers = [], [], []
+    own = cross_left = cross_right = None
+    for number in range(chunks):
+        filtered = fir(padded, fir_taps, chans, piece, number * piece)
+        extended = with_halo(filtered, (("ch", 0),), GAUGE)
+        gauged = (extended[2 * GAUGE :] - extended[: -2 * GAUGE]).astype(jnp.bfloat16)
+        lower_part = shifted(gauged[chans - 2 * STRIDE :], "ch", 1)
+        upper_part = shifted(gauged[:STRIDE], "ch", -1)
+        local = gram(gauged, gauged)
+        own = local if own is None else own + local
+        gaugeds.append(gauged)
+        lowers.append(lower_part)
+        uppers.append(upper_part)
+
+    own = ta_sum(own)
     own_left = shifted(own[chans - 2 * STRIDE :, chans - 2 * STRIDE :], "ch", 1)
     own_right = shifted(own[:STRIDE, :STRIDE], "ch", -1)
-
-    own, lower_part, upper_part = lax.optimization_barrier((own, lower_part, upper_part))
-    cross_left = gram(lower_part, gauged)
-    tail = jnp.concatenate([lower_part[STRIDE:], gauged], axis=0)
-    cross_right = gram(tail, upper_part)
+    own, lowers, uppers = lax.optimization_barrier((own, lowers, uppers))
+
+    for number in range(chunks):
+        lower_part, gauged, upper_part = lowers[number], gaugeds[number], uppers[number]
+        left = gram(lower_part, gauged)
+        tail = jnp.concatenate([lower_part[STRIDE:], gauged], axis=0)
+        right = gram(tail, upper_part)
+        cross_left = left if cross_left is None else cross_left + left
+        cross_right = right if cross_right is None else cross_right + right
+
     packed = ta_sum(jnp.concatenate([cross_left[:, :STRIDE], cross_left[:, STRIDE:], cross_right], axis=0))
-    tiles_left = lower_part.shape[0]
+    tiles_left = 2 * STRIDE
     cross_left = jnp.concatenate(
         [packed[:tiles_left], packed[tiles_left : 2 * tiles_left]], axis=1
     )
@@ -170,22 +224,10 @@
     band = jnp.concatenate([top, middle, bottom], axis=0) / total_time
 
     rounded = subspace(band, start_basis.T, windows)
-
-    stacked = jnp.concatenate([lower_part, gauged, upper_part], axis=0)
-    outputs = []
-    for number in range(windows):
-        frame = stacked[number * STRIDE : number * STRIDE + WIN]
-        coeffs = jnp.dot(rounded[number], frame, preferred_element_type=jnp.float32).astype(
-            jnp.bfloat16
-        )
-        fitted = lax.dot_general(
-            rounded[number, :, 2 * STRIDE : 3 * STRIDE], coeffs, (((0,), (0,)), ((), ())),
-            preferred_element_type=jnp.float32,
-        )
-        outputs.append(
-            (frame[2 * STRIDE : 3 * STRIDE].astype(jnp.float32) - fitted).astype(jnp.bfloat16)
-        )
-    return jnp.concatenate(outputs, axis=0)
+    outputs = [
+        clean(lowers[number], gaugeds[number], uppers[number], rounded) for number in range(chunks)
+    ]
+    return jnp.concatenate(outputs, axis=1)
 
 
 def solution(mesh):

time: 196 us -> 196 us (level)
  Pallas kernels: 31.4 us -> 45.1 us
  starting transfers between devices: 44.8 us -> 58.3 us
  matrix products: 12.6 us -> 3.46 us
  waiting for transfers between devices: 73.6 us -> 66.3 us
  other arithmetic: 12.4 us -> 5.34 us
  local copies, waits for them, and re-layouts: 20.1 us -> 15.9 us
    pallas_call x0 -> x2, Pallas kernels: none -> 11.9 us  [clean(): pl.pallas_call(clean_kernel, grid=(samples // width,), out_shape=jax.Shap...]
    dot_general x2 -> x0, matrix products: 7.89 us -> none  [per_device(): lax.dot_general(rounded[number, :, 2 * STRIDE:3 * STRIDE], coeffs, (((0,)...]
    ppermute x2 -> x3, starting transfers between devices: 9 us -> 16.6 us  [with_halo(): lax.ppermute(lax.slice_in_dim(block, 0, width, axis=dim), axis, backward)]
    ppermute x4 -> x6, waiting for transfers between devices: 20.9 us -> 13.5 us  [shifted(): lax.ppermute(value, axis, [(source, source + steps) for source in range(f...]
    convert_element_type x1 -> x2, other arithmetic: 4.69 us -> 0.66 us  [per_device(): gauged = (extended[2 * GAUGE:] - extended[:-2 * GAUGE]).astype(jnp.bfloat16)]
    ppermute x4 -> x6, starting transfers between devices: 19.8 us -> 23.6 us  [shifted(): lax.ppermute(value, axis, [(source, source + steps) for source in range(f...]
    ppermute x2, waiting for transfers between devices: 41.5 us -> 44.9 us  [ta_sum(): part = part + lax.ppermute(part, 'ta', across)]
    ppermute x2 -> x3, starting transfers between devices: 8.81 us -> 11 us  [with_halo(): lax.ppermute(lax.slice_in_dim(block, block.shape[dim] - width, None, axis...]
  transfers between devices with their start and end apart: 14 -> 18, of which waited for: 7 -> 8; matrix products, arithmetic and copies ran while one was open for 8% -> 5% of each run, Pallas kernels for 0% -> 0%
where the time goes in v3:
time: 196 us; the launch traced here: 195 us
  waiting for transfers between devices  66.3 us (34%)
  starting transfers between devices  58.3 us (30%)
  Pallas kernels  45.1 us (23%)
  local copies, waits for them, and re-layouts  15.9 us (8%)
  other arithmetic  5.34 us (3%)
  matrix products  3.46 us (2%)
    ppermute x2, waiting for transfers between devices, ta_sum(): part = part + lax.ppermute(part, 'ta', across)  44.9 us
    ppermute x6, starting transfers between devices, shifted(): lax.ppermute(value, axis, [(source, source + steps) for source in range(f...  23.6 us
    pallas_call x1, Pallas kernels, subspace(): pl.pallas_call(subspace_kernel, out_shape=jax.ShapeDtypeStruct((windows,)...  22.3 us
    ppermute x3, starting transfers between devices, with_halo(): lax.ppermute(lax.slice_in_dim(block, 0, width, axis=dim), axis, backward)  16.6 us
    ppermute x6, waiting for transfers between devices, shifted(): lax.ppermute(value, axis, [(source, source + steps) for source in range(f...  13.5 us
    pallas_call x2, Pallas kernels, clean(): pl.pallas_call(clean_kernel, grid=(samples // width,), out_shape=jax.Shap...  11.9 us
    ppermute x3, starting transfers between devices, with_halo(): lax.ppermute(lax.slice_in_dim(block, block.shape[dim] - width, None, axis...  11 us
    pallas_call x2, Pallas kernels, fir(): pl.pallas_call(fir_kernel, grid=(samples // width,), out_shape=jax.ShapeD...  11 us
  transfers between devices with their start and end apart: 18, of which 8 were waited for; matrix products, arithmetic and copies ran while one was open for 5% of the time, Pallas kernels for 0%

profile of v3, /device:TPU:97, one launch (start us, length us, event | category | flops | bytes accessed | tf_op | source)
XLA Modules:
  0.0 195.0 jit_solution(11668270858752859732)
XLA Ops:
  0.0 1.0 fusion.24
  1.0 2.6 %collective-permute-start.1 = (bf16[256,64]{1,0:T(8,128)(2,1)S(1)}, bf16[256,64]{1,0:T(8,128)(2,1)S(1)}, u32[]{:S(2)}, u32[]{:S(2)}) collective-permute-start(bf16[256,64]{1,0:T(8,128)(2,1)S(1)} %get-tuple-element.19), channel_id=1, source_target_pairs={{1,0},{2,1},{3,2},{5,4},{6,5},{7,6},{9,8},{10,9},{11,10},{13,12},{... | collective-permute-start | bytes 98312 | tf_op jit(solution)/shard_map/ppermute | solution.py:26
  3.6 6.9 %collective-permute-start = (bf16[256,64]{1,0:T(8,128)(2,1)S(1)}, bf16[256,64]{1,0:T(8,128)(2,1)S(1)}, u32[]{:S(2)}, u32[]{:S(2)}) collective-permute-start(bf16[256,64]{1,0:T(8,128)(2,1)S(1)} %get-tuple-element.20), channel_id=1, source_target_pairs={{0,1},{1,2},{2,3},{4,5},{5,6},{6,7},{8,9},{9,10},{10,11},{12,13},{... | collective-permute-start | bytes 98312 | tf_op jit(solution)/shard_map/ppermute | solution.py:23
  10.5 0.7 concatenate.69
  11.2 1.3 tile.5
  12.5 1.3 reshape.5
  13.8 1.5 copy.8
  15.3 0.7 slice.133.rest_ref
  16.0 0.8 slice.132.top_ref
  16.8 4.3 %concatenate.68.head_ref.tail_ref = bf16[256,5248]{1,0:T(8,128)(2,1)} concatenate(bf16[256,64]{1,0:T(8,128)(2,1)S(1)} %collective-permute-done, bf16[256,5120]{1,0:T(8,128)(2,1)S(1)} %copy-done.7, bf16[256,64]{1,0:T(8,128)(2,1)S(1)} %collective-permute-done.1), dimensions={1} | concatenate | bytes 5373952 | tf_op jit(solution)/shard_map/concatenate | solution.py:27
  21.1 5.4 %shard_map.38 = f32[256,2560]{1,0:T(8,128)} custom-call(bf16[256,5248]{1,0:T(8,128)(2,1)} %concatenate.68.head_ref.tail_ref, bf16[256,5248]{1,0:T(8,128)(2,1)} %concatenate.68.head_ref.tail_ref, bf16[512,512]{1,0:T(8,128)(2,1)} %slice.132.top_ref, bf16[128,512]{1,0:T(8,128)(2,1)} %slice.133.rest_ref), custom_call_target="tpu_custom_call" | custom-call | tf_op jit(solution)/shard_map/pallas_call | solution.py:101
  26.5 5.6 %shard_map.37 = f32[256,2560]{1,0:T(8,128)} custom-call(bf16[256,5248]{1,0:T(8,128)(2,1)} %concatenate.68.head_ref.tail_ref, bf16[256,5248]{1,0:T(8,128)(2,1)} %concatenate.68.head_ref.tail_ref, bf16[512,512]{1,0:T(8,128)(2,1)} %slice.132.top_ref, bf16[128,512]{1,0:T(8,128)(2,1)} %slice.133.rest_ref), custom_call_target="tpu_custom_call" | custom-call | tf_op jit(solution)/shard_map/pallas_call | solution.py:101
  32.1 6.4 %collective-permute-start.4 = (f32[4,2560]{1,0:T(4,128)S(1)}, f32[4,2560]{1,0:T(4,128)S(1)}, u32[]{:S(2)}, u32[]{:S(2)}) collective-permute-start(f32[4,2560]{1,0:T(4,128)S(1)} %get-tuple-element.17), channel_id=1, source_target_pairs={{4,0},{8,4},{12,8},{16,12},{20,16},{24,20},{28,24},{32,28},{36,32}... | collective-permute-start | bytes 122888 | tf_op jit(solution)/shard_map/ppermute | solution.py:26
  38.5 1.9 collective-permute-start.5
  40.5 0.9 fusion.22
  41.4 7.6 %collective-permute-start.2 = (f32[4,2560]{1,0:T(4,128)S(1)}, f32[4,2560]{1,0:T(4,128)S(1)}, u32[]{:S(2)}, u32[]{:S(2)}) collective-permute-start(f32[4,2560]{1,0:T(4,128)S(1)} %get-tuple-element.15), channel_id=1, source_target_pairs={{4,0},{8,4},{12,8},{16,12},{20,16},{24,20},{28,24},{32,28},{36,32}... | collective-permute-start | bytes 122888 | tf_op jit(solution)/shard_map/ppermute | solution.py:26
  49.0 2.2 %collective-permute-start.3 = (f32[4,2560]{1,0:T(4,128)S(1)}, f32[4,2560]{1,0:T(4,128)S(1)}, u32[]{:S(2)}, u32[]{:S(2)}) collective-permute-start(f32[4,2560]{1,0:T(4,128)S(1)} %get-tuple-element.16), channel_id=1, source_target_pairs={{0,4},{4,8},{8,12},{12,16},{16,20},{20,24},{24,28},{28,32},{32,36}... | collective-permute-start | bytes 122888 | tf_op jit(solution)/shard_map/ppermute | solution.py:23
  51.6 1.9 collective-permute-start.10
  53.5 5.5 %collective-permute-done.3 = f32[4,2560]{1,0:T(4,128)S(1)} collective-permute-done((f32[4,2560]{1,0:T(4,128)S(1)}, f32[4,2560]{1,0:T(4,128)S(1)}, u32[]{:S(2)}, u32[]{:S(2)}) %collective-permute-start.3) | collective-permute-done | bytes 40992 | tf_op jit(solution)/shard_map/ppermute | solution.py:23
  59.3 1.9 collective-permute-start.9
  61.2 0.5 fusion.27
  61.8 0.5 convolution_add_fusion.1
  62.5 7.6 %collective-permute-start.11 = (bf16[128,2560]{1,0:T(8,128)(2,1)S(1)}, bf16[128,2560]{1,0:T(8,128)(2,1)S(1)}, u32[]{:S(2)}, u32[]{:S(2)}) collective-permute-start(bf16[128,2560]{1,0:T(8,128)(2,1)S(1)} %slice.140), channel_id=1, source_target_pairs={{4,0},{8,4},{12,8},{16,12},{20,16},{24,20},{28,24},{32,28},{36,32}... | collective-permute-start | bytes 1966088 | tf_op jit(solution)/shard_map/ppermute | solution.py:34
  70.1 1.9 collective-permute-start.12
  72.1 3.4 %collective-permute-start.7 = (f32[128,256]{1,0:T(8,128)S(1)}, f32[128,256]{1,0:T(8,128)S(1)}, u32[]{:S(2)}, u32[]{:S(2)}) collective-permute-start(f32[128,256]{1,0:T(8,128)S(1)} %select_add_fusion.1), channel_id=1, source_target_pairs={{0,2},{1,3},{2,0},{3,1},{4,6},{5,7},{6,4},{7,5},{8,10},{9,11},{10,... | collective-permute-start | bytes 393224 | tf_op jit(solution)/shard_map/ppermute | solution.py:166
  75.5 30.6 %collective-permute-done.7 = f32[128,256]{1,0:T(8,128)S(1)} collective-permute-done((f32[128,256]{1,0:T(8,128)S(1)}, f32[128,256]{1,0:T(8,128)S(1)}, u32[]{:S(2)}, u32[]{:S(2)}) %collective-permute-start.7) | collective-permute-done | bytes 131104 | tf_op jit(solution)/shard_map/ppermute | solution.py:166
  106.1 1.2 collective-permute-start.8
  107.2 1.0 collective-permute-done.8
  108.3 9.4 %collective-permute-done.9.lower_ref = bf16[256,2560]{1,0:T(8,128)(2,1)S(1)} collective-permute-done((bf16[256,2560]{1,0:T(8,128)(2,1)S(1)}, bf16[256,2560]{1,0:T(8,128)(2,1)S(1)}, u32[]{:S(2)}, u32[]{:S(2)}) %collective-permute-start.9) | collective-permute-done | bytes 1310752 | tf_op jit(solution)/shard_map/ppermute | solution.py:34
  117.7 0.5 fusion.28
  118.8 0.5 convolution_add_fusion
  119.9 0.7 fusion.8
  121.0 0.7 fusion.16
  121.8 1.5 collective-permute-done.14
  123.3 1.7 collective-permute-start.15
  125.0 14.3 %collective-permute-done.15 = f32[448,128]{1,0:T(8,128)S(1)} collective-permute-done((f32[448,128]{1,0:T(8,128)S(1)}, f32[448,128]{1,0:T(8,128)S(1)}, u32[]{:S(2)}, u32[]{:S(2)}) %collective-permute-start.15) | collective-permute-done | bytes 229408 | tf_op jit(solution)/shard_map/ppermute | solution.py:166
  139.3 0.8 collective-permute-start.16
  140.2 1.9 collective-permute-start.13
  142.1 8.3 %collective-permute-start.17 = (f32[128,128]{1,0:T(8,128)S(1)}, f32[128,128]{1,0:T(8,128)S(1)}, u32[]{:S(2)}, u32[]{:S(2)}) collective-permute-start(f32[128,128]{1,0:T(8,128)S(1)} %slice.148), channel_id=1, source_target_pairs={{4,0},{8,4},{12,8},{16,12},{20,16},{24,20},{28,24},{32,28},{36,32}... | collective-permute-start | bytes 196616 | tf_op jit(solution)/shard_map/ppermute | solution.py:34
  150.9 0.7 collective-permute-done.17
  151.5 3.4 %collective-permute-done.13 = f32[256,256]{1,0:T(8,128)S(1)} collective-permute-done((f32[256,256]{1,0:T(8,128)S(1)}, f32[256,256]{1,0:T(8,128)S(1)}, u32[]{:S(2)}, u32[]{:S(2)}) %collective-permute-start.13) | collective-permute-done | bytes 262176 | tf_op jit(solution)/shard_map/ppermute | solution.py:34
  154.9 1.3 fusion.14.band_ref
  156.2 22.3 %shard_map.39.basis_ref = bf16[2,16,512]{2,1,0:T(8,128)(2,1)} custom-call(f32[640,640]{1,0:T(8,128)} %fusion.14.band_ref, f32[16,512]{1,0:T(8,128)} %bitcast.23), custom_call_target="tpu_custom_call" | custom-call | tf_op jit(solution)/shard_map/pallas_call | solution.py:77
  178.5 0.7 slice.149
  179.2 0.7 copy.12
  179.9 5.9 %shard_map.41 = bf16[256,2560]{1,0:T(8,128)(2,1)} custom-call(bf16[256,2560]{1,0:T(8,128)(2,1)} %copy-done.4, bf16[256,2560]{1,0:T(8,128)(2,1)} %copy-done, bf16[128,2560]{1,0:T(8,128)(2,1)} %copy-done.9, bf16[2,16,512]{2,1,0:T(8,128)(2,1)} %shard_map.39.basis_ref, bf16[2,128,16]{2,1,0:T(8,128)(2,1)} %bitcast.21), custom_call_target="tpu_custom_call" | custom-call | tf_op jit(solution)/shard_map/pallas_call | solution.py:139
  185.8 6.0 %shard_map.40 = bf16[256,2560]{1,0:T(8,128)(2,1)} custom-call(bf16[256,2560]{1,0:T(8,128)(2,1)} %copy-done.5, bf16[256,2560]{1,0:T(8,128)(2,1)} %copy-done.1, bf16[128,2560]{1,0:T(8,128)(2,1)} %copy-done.8, bf16[2,16,512]{2,1,0:T(8,128)(2,1)} %shard_map.39.basis_ref, bf16[2,128,16]{2,1,0:T(8,128)(2,1)} %bitcast.22), custom_call_target="tpu_custom_call" | custom-call | tf_op jit(solution)/shard_map/pallas_call | solution.py:139
  191.8 3.2 %pad_maximum_fusion.4 = bf16[256,5120]{1,0:T(8,128)(2,1)} fusion(bf16[256,2560]{1,0:T(8,128)(2,1)S(1)} %copy-done.6, bf16[256,2560]{1,0:T(8,128)(2,1)} %shard_map.40), kind=kLoop, calls=%fused_computation.8 | loop fusion | flops 5242880 | bytes 5242880 | tf_op jit(solution)/shard_map/concatenate | solution.py:230
  (60 shorter events, 3.1 us)
Async XLA Ops:
  1.0 15.8 %collective-permute-start.1 = (bf16[256,64]{1,0:T(8,128)(2,1)S(1)}, bf16[256,64]{1,0:T(8,128)(2,1)S(1)}, u32[]{:S(2)}, u32[]{:S(2)}) collective-permute-start(bf16[256,64]{1,0:T(8,128)(2,1)S(1)} %get-tuple-element.19), channel_id=1, source_target_pairs={{1,0},{2,1},{3,2},{5,4},{6,5},{7,6},{9,8},{10,9},{11,10},{13,12},{... | collective-permute-start | bytes 98312 | tf_op jit(solution)/shard_map/ppermute | solution.py:26
  3.6 13.2 %collective-permute-start = (bf16[256,64]{1,0:T(8,128)(2,1)S(1)}, bf16[256,64]{1,0:T(8,128)(2,1)S(1)}, u32[]{:S(2)}, u32[]{:S(2)}) collective-permute-start(bf16[256,64]{1,0:T(8,128)(2,1)S(1)} %get-tuple-element.20), channel_id=1, source_target_pairs={{0,1},{1,2},{2,3},{4,5},{5,6},{6,7},{8,9},{9,10},{10,11},{12,13},{... | collective-permute-start | bytes 98312 | tf_op jit(solution)/shard_map/ppermute | solution.py:23
  13.8 3.0 %copy-start.7 = (bf16[256,5120]{1,0:T(8,128)(2,1)S(1)}, bf16[256,5120]{1,0:T(8,128)(2,1)}, u32[]{:S(2)}) copy-start(bf16[256,5120]{1,0:T(8,128)(2,1)} %param.3) | copy-start | bytes 7864324
  26.5 5.6 %copy-start.3 = (f32[256,2560]{1,0:T(8,128)S(1)}, f32[256,2560]{1,0:T(8,128)}, u32[]{:S(2)}) copy-start(f32[256,2560]{1,0:T(8,128)} %shard_map.38) | copy-start | bytes 7864324
  32.1 19.1 %collective-permute-start.4 = (f32[4,2560]{1,0:T(4,128)S(1)}, f32[4,2560]{1,0:T(4,128)S(1)}, u32[]{:S(2)}, u32[]{:S(2)}) collective-permute-start(f32[4,2560]{1,0:T(4,128)S(1)} %get-tuple-element.17), channel_id=1, source_target_pairs={{4,0},{8,4},{12,8},{16,12},{20,16},{24,20},{28,24},{32,28},{36,32}... | collective-permute-start | bytes 122888 | tf_op jit(solution)/shard_map/ppermute | solution.py:26
  38.5 12.7 %collective-permute-start.5 = (f32[4,2560]{1,0:T(4,128)S(1)}, f32[4,2560]{1,0:T(4,128)S(1)}, u32[]{:S(2)}, u32[]{:S(2)}) collective-permute-start(f32[4,2560]{1,0:T(4,128)S(1)} %get-tuple-element.18), channel_id=1, source_target_pairs={{0,4},{4,8},{8,12},{12,16},{16,20},{20,24},{24,28},{28,32},{32,36}... | collective-permute-start | bytes 122888 | tf_op jit(solution)/shard_map/ppermute | solution.py:23
  41.4 12.1 %collective-permute-start.2 = (f32[4,2560]{1,0:T(4,128)S(1)}, f32[4,2560]{1,0:T(4,128)S(1)}, u32[]{:S(2)}, u32[]{:S(2)}) collective-permute-start(f32[4,2560]{1,0:T(4,128)S(1)} %get-tuple-element.15), channel_id=1, source_target_pairs={{4,0},{8,4},{12,8},{16,12},{20,16},{24,20},{28,24},{32,28},{36,32}... | collective-permute-start | bytes 122888 | tf_op jit(solution)/shard_map/ppermute | solution.py:26
  49.0 10.0 %copy-start.2 = (f32[256,2560]{1,0:T(8,128)S(1)}, f32[256,2560]{1,0:T(8,128)}, u32[]{:S(2)}) copy-start(f32[256,2560]{1,0:T(8,128)} %shard_map.37) | copy-start | bytes 7864324
  49.0 10.0 %collective-permute-start.3 = (f32[4,2560]{1,0:T(4,128)S(1)}, f32[4,2560]{1,0:T(4,128)S(1)}, u32[]{:S(2)}, u32[]{:S(2)}) collective-permute-start(f32[4,2560]{1,0:T(4,128)S(1)} %get-tuple-element.16), channel_id=1, source_target_pairs={{0,4},{4,8},{8,12},{12,16},{16,20},{20,24},{24,28},{28,32},{32,36}... | collective-permute-start | bytes 122888 | tf_op jit(solution)/shard_map/ppermute | solution.py:23
  51.5 67.8 %copy-start = (bf16[256,2560]{1,0:T(8,128)(2,1)}, bf16[256,2560]{1,0:T(8,128)(2,1)S(1)}, u32[]{:S(2)}) copy-start(bf16[256,2560]{1,0:T(8,128)(2,1)S(1)} %fusion.1.own_ref) | copy-start | bytes 3932164
  51.6 56.7 %collective-permute-start.10 = (bf16[256,2560]{1,0:T(8,128)(2,1)S(1)}, bf16[256,2560]{1,0:T(8,128)(2,1)S(1)}, u32[]{:S(2)}, u32[]{:S(2)}) collective-permute-start(bf16[256,2560]{1,0:T(8,128)(2,1)S(1)} %fusion.1.own_ref), channel_id=1, source_target_pairs={{0,4},{4,8},{8,12},{12,16},{16,20},{20,24},{24,28},{28,32},{32,36}... | collective-permute-start | bytes 3932168 | tf_op jit(solution)/shard_map/ppermute | solution.py:34
  59.3 61.2 %copy-start.1 = (bf16[256,2560]{1,0:T(8,128)(2,1)}, bf16[256,2560]{1,0:T(8,128)(2,1)S(1)}, u32[]{:S(2)}) copy-start(bf16[256,2560]{1,0:T(8,128)(2,1)S(1)} %fusion.3.own_ref) | copy-start | bytes 3932164
  59.3 58.4 %collective-permute-start.9 = (bf16[256,2560]{1,0:T(8,128)(2,1)S(1)}, bf16[256,2560]{1,0:T(8,128)(2,1)S(1)}, u32[]{:S(2)}, u32[]{:S(2)}) collective-permute-start(bf16[256,2560]{1,0:T(8,128)(2,1)S(1)} %fusion.3.own_ref), channel_id=1, source_target_pairs={{0,4},{4,8},{8,12},{12,16},{16,20},{20,24},{24,28},{28,32},{32,36}... | collective-permute-start | bytes 3932168 | tf_op jit(solution)/shard_map/ppermute | solution.py:34
  62.3 9.7 %collective-permute-start.6 = (f32[128,256]{1,0:T(8,128)S(1)}, f32[128,256]{1,0:T(8,128)S(1)}, u32[]{:S(2)}, u32[]{:S(2)}) collective-permute-start(f32[128,256]{1,0:T(8,128)S(1)} %slice_select_fusion), channel_id=1, source_target_pairs={{0,1},{1,0},{2,3},{3,2},{4,5},{5,4},{6,7},{7,6},{8,9},{9,8},{10,11... | collective-permute-start | bytes 393224 | tf_op jit(solution)/shard_map/ppermute | solution.py:165
  62.5 45.7 %collective-permute-start.11 = (bf16[128,2560]{1,0:T(8,128)(2,1)S(1)}, bf16[128,2560]{1,0:T(8,128)(2,1)S(1)}, u32[]{:S(2)}, u32[]{:S(2)}) collective-permute-start(bf16[128,2560]{1,0:T(8,128)(2,1)S(1)} %slice.140), channel_id=1, source_target_pairs={{4,0},{8,4},{12,8},{16,12},{20,16},{24,20},{28,24},{32,28},{36,32}... | collective-permute-start | bytes 1966088 | tf_op jit(solution)/shard_map/ppermute | solution.py:34
  70.1 38.1 %collective-permute-start.12 = (bf16[128,2560]{1,0:T(8,128)(2,1)S(1)}, bf16[128,2560]{1,0:T(8,128)(2,1)S(1)}, u32[]{:S(2)}, u32[]{:S(2)}) collective-permute-start(bf16[128,2560]{1,0:T(8,128)(2,1)S(1)} %slice.141), channel_id=1, source_target_pairs={{4,0},{8,4},{12,8},{16,12},{20,16},{24,20},{28,24},{32,28},{36,32}... | collective-permute-start | bytes 1966088 | tf_op jit(solution)/shard_map/ppermute | solution.py:34
  72.1 34.0 %collective-permute-start.7 = (f32[128,256]{1,0:T(8,128)S(1)}, f32[128,256]{1,0:T(8,128)S(1)}, u32[]{:S(2)}, u32[]{:S(2)}) collective-permute-start(f32[128,256]{1,0:T(8,128)S(1)} %select_add_fusion.1), channel_id=1, source_target_pairs={{0,2},{1,3},{2,0},{3,1},{4,6},{5,7},{6,4},{7,5},{8,10},{9,11},{10,... | collective-permute-start | bytes 393224 | tf_op jit(solution)/shard_map/ppermute | solution.py:166
  106.1 2.2 %collective-permute-start.8 = (f32[128,256]{1,0:T(8,128)S(1)}, f32[128,256]{1,0:T(8,128)S(1)}, u32[]{:S(2)}, u32[]{:S(2)}) collective-permute-start(f32[128,256]{1,0:T(8,128)S(1)} %add.33), channel_id=1, source_target_pairs={{0,1},{1,0},{2,3},{3,2},{4,5},{5,4},{6,7},{7,6},{8,9},{9,8},{10,11... | collective-permute-start | bytes 393224 | tf_op jit(solution)/shard_map/ppermute | solution.py:167
  108.3 12.3 %copy-start.8 = (bf16[128,2560]{1,0:T(8,128)(2,1)}, bf16[128,2560]{1,0:T(8,128)(2,1)S(1)}, u32[]{:S(2)}) copy-start(bf16[128,2560]{1,0:T(8,128)(2,1)S(1)} %collective-permute-done.11.upper_ref) | copy-start | bytes 1966084
  108.3 11.1 %copy-start.9 = (bf16[128,2560]{1,0:T(8,128)(2,1)}, bf16[128,2560]{1,0:T(8,128)(2,1)S(1)}, u32[]{:S(2)}) copy-start(bf16[128,2560]{1,0:T(8,128)(2,1)S(1)} %collective-permute-done.12.upper_ref) | copy-start | bytes 1966084
  108.3 9.9 %copy-start.4 = (bf16[256,2560]{1,0:T(8,128)(2,1)}, bf16[256,2560]{1,0:T(8,128)(2,1)S(1)}, u32[]{:S(2)}) copy-start(bf16[256,2560]{1,0:T(8,128)(2,1)S(1)} %collective-permute-done.10.lower_ref) | copy-start | bytes 3932164
  117.7 1.1 copy-start.5
  118.8 1.1 slice-start
  119.9 1.1 slice-start.1
  121.7 1.6 collective-permute-start.14
  123.3 16.0 %collective-permute-start.15 = (f32[448,128]{1,0:T(8,128)S(1)}, f32[448,128]{1,0:T(8,128)S(1)}, u32[]{:S(2)}, u32[]{:S(2)}) collective-permute-start(f32[448,128]{1,0:T(8,128)S(1)} %select_add_fusion), channel_id=1, source_target_pairs={{0,2},{1,3},{2,0},{3,1},{4,6},{5,7},{6,4},{7,5},{8,10},{9,11},{10,... | collective-permute-start | bytes 688136 | tf_op jit(solution)/shard_map/ppermute | solution.py:166
  139.3 11.1 %collective-permute-start.16 = (f32[448,128]{1,0:T(8,128)S(1)}, f32[448,128]{1,0:T(8,128)S(1)}, u32[]{:S(2)}, u32[]{:S(2)}) collective-permute-start(f32[448,128]{1,0:T(8,128)S(1)} %add.37), channel_id=1, source_target_pairs={{0,1},{1,0},{2,3},{3,2},{4,5},{5,4},{6,7},{7,6},{8,9},{9,8},{10,11... | collective-permute-start | bytes 688136 | tf_op jit(solution)/shard_map/ppermute | solution.py:167
  140.2 14.8 %collective-permute-start.13 = (f32[256,256]{1,0:T(8,128)S(1)}, f32[256,256]{1,0:T(8,128)S(1)}, u32[]{:S(2)}, u32[]{:S(2)}) collective-permute-start(f32[256,256]{1,0:T(8,128)S(1)} %maximum_select_fusion.1), channel_id=1, source_target_pairs={{0,4},{4,8},{8,12},{12,16},{16,20},{20,24},{24,28},{28,32},{32,36}... | collective-permute-start | bytes 786440 | tf_op jit(solution)/shard_map/ppermute | solution.py:34
  142.1 9.4 %collective-permute-start.17 = (f32[128,128]{1,0:T(8,128)S(1)}, f32[128,128]{1,0:T(8,128)S(1)}, u32[]{:S(2)}, u32[]{:S(2)}) collective-permute-start(f32[128,128]{1,0:T(8,128)S(1)} %slice.148), channel_id=1, source_target_pairs={{4,0},{8,4},{12,8},{16,12},{20,16},{24,20},{28,24},{32,28},{36,32}... | collective-permute-start | bytes 196616 | tf_op jit(solution)/shard_map/ppermute | solution.py:34
  185.8 6.0 %copy-start.6 = (bf16[256,2560]{1,0:T(8,128)(2,1)S(1)}, bf16[256,2560]{1,0:T(8,128)(2,1)}, u32[]{:S(2)}) copy-start(bf16[256,2560]{1,0:T(8,128)(2,1)} %shard_map.41) | copy-start | bytes 3932164

commit v4 on v3

--- a/solution.py
+++ b/solution.py
@@ -85,34 +85,48 @@
     )(band, start_t)
 
 
-def fir_kernel(head_ref, tail_ref, top_ref, rest_ref, out_ref):
-    out_ref[...] = jnp.dot(
-        head_ref[...], top_ref[...], preferred_element_type=jnp.float32
-    ) + jnp.dot(tail_ref[...], rest_ref[...], preferred_element_type=jnp.float32)
-
-
-def fir(padded, fir_taps, chans, samples, start):
-    width = math.gcd(math.gcd(samples, start) if start else samples, 512)
+def fir_kernel(left_ref, right_ref, prev_ref, cur_ref, next_ref, lo_ref, mid_ref, hi_ref, out_ref, *, first, last):
+    block = pl.program_id(0) + first
+    before = jnp.where(block == 0, left_ref[...], prev_ref[...])
+    after = jnp.where(block == last, right_ref[...], next_ref[...])
+    out_ref[...] = (
+        jnp.dot(before, lo_ref[...], preferred_element_type=jnp.float32)
+        + jnp.dot(cur_ref[...], mid_ref[...], preferred_element_type=jnp.float32)
+        + jnp.dot(after, hi_ref[...], preferred_element_type=jnp.float32)
+    )
+
+
+def fir(raw, left, right, band, start, length):
+    chans, samples = raw.shape
+    width = band.shape[1]
+    edge = 128
+    step = width // edge
     first = start // width
-    edge = TAPS - 1
-    band = toeplitz_band(fir_taps, width)
-    top, rest = band[:width], band[width:]
-    step = width // edge
+    lo, mid, hi = band[:edge], band[edge : edge + width], band[edge + width :]
+    kernel = lambda *refs: fir_kernel(*refs, first=first, last=samples // width - 1)
+    full = lambda b: (0, 0)
     return pl.pallas_call(
-        fir_kernel,
-        grid=(samples // width,),
-        out_shape=jax.ShapeDtypeStruct((chans, samples), jnp.float32),
+        kernel,
+        grid=(length // width,),
+        out_shape=jax.ShapeDtypeStruct((chans, length), jnp.float32),
         in_specs=[
+            pl.BlockSpec((chans, edge), full),
+            pl.BlockSpec((chans, edge), full),
+            pl.BlockSpec((chans, edge), lambda b: (0, jnp.maximum((b + first) * step - 1, 0))),
             pl.BlockSpec((chans, width), lambda b: (0, b + first)),
-            pl.BlockSpec((chans, edge), lambda b: (0, (b + first + 1) * step)),
-            pl.BlockSpec((width, width), lambda b: (0, 0)),
-            pl.BlockSpec((edge, width), lambda b: (0, 0)),
+            pl.BlockSpec(
+                (chans, edge), lambda b: (0, jnp.minimum((b + first + 1) * step, samples // edge - 1))
+            ),
+            pl.BlockSpec((edge, width), full),
+            pl.BlockSpec((width, width), full),
+            pl.BlockSpec((edge, width), full),
         ],
         out_specs=pl.BlockSpec((chans, width), lambda b: (0, b)),
-    )(padded, padded, top, rest)
-
-
-def clean_kernel(lower_ref, own_ref, upper_ref, basis_ref, middle_ref, out_ref):
+    )(left, right, raw, raw, raw, lo, mid, hi)
+
+
+def clean_kernel(lower_ref, own_ref, upper_ref, basis_ref, middle_ref, *rest):
+    out_ref = rest[-1]
     tiles = own_ref.shape[0] // STRIDE
     parts = [lower_ref[k * STRIDE : (k + 1) * STRIDE] for k in range(2)]
     parts += [own_ref[k * STRIDE : (k + 1) * STRIDE] for k in range(tiles)]
@@ -132,23 +146,25 @@
         ).astype(out_ref.dtype)
 
 
-def clean(lower, own, upper, rounded):
+def clean(lower, own, upper, rounded, total, start, into):
     chans, samples = own.shape
-    width = math.gcd(samples, 512)
+    width = math.gcd(math.gcd(samples, start) if start else samples, 512)
+    first = start // width
     middle = jnp.swapaxes(rounded[:, :, 2 * STRIDE : 3 * STRIDE], 1, 2)
     return pl.pallas_call(
         clean_kernel,
         grid=(samples // width,),
-        out_shape=jax.ShapeDtypeStruct((chans, samples), own.dtype),
+        out_shape=jax.ShapeDtypeStruct((chans, total), own.dtype),
         in_specs=[
             pl.BlockSpec((lower.shape[0], width), lambda b: (0, b)),
             pl.BlockSpec((chans, width), lambda b: (0, b)),
             pl.BlockSpec((STRIDE, width), lambda b: (0, b)),
             pl.BlockSpec(rounded.shape, lambda b: (0, 0, 0)),
             pl.BlockSpec(middle.shape, lambda b: (0, 0, 0)),
-        ],
-        out_specs=pl.BlockSpec((chans, width), lambda b: (0, b)),
-    )(lower, own, upper, rounded, middle)
+        ] + ([] if into is None else [pl.BlockSpec(memory_space=pl.ANY)]),
+        out_specs=pl.BlockSpec((chans, width), lambda b: (0, b + first)),
+        input_output_aliases={} if into is None else {5: 0},
+    )(lower, own, upper, rounded, middle, *([] if into is None else [into]))
 
 
 def ta_sum(value):
@@ -172,7 +188,15 @@
     chans = raw.shape[0]
     samples = raw.shape[1]
     half = (TAPS - 1) // 2
-    padded = with_halo(raw, (("ta", 1),), half)
+    count = lax.axis_size("ta")
+    forward = [(i, i + 1) for i in range(count - 1)]
+    backward = [(target, source) for source, target in forward]
+    blank = jnp.zeros((chans, STRIDE - half), raw.dtype)
+    left = jnp.concatenate([blank, lax.ppermute(raw[:, samples - half :], "ta", forward)], axis=1)
+    right = jnp.concatenate([lax.ppermute(raw[:, :half], "ta", backward), blank], axis=1)
+    width = math.gcd(samples, 512)
+    band = jnp.pad(toeplitz_band(fir_taps, width), ((half, half), (0, 0)))
+    source = raw
     chunks = 2 if samples % 1024 == 0 else 1
     piece = samples // chunks
     tiles = chans // STRIDE
@@ -181,7 +205,7 @@
     gaugeds, lowers, uppers = [], [], []
     own = cross_left = cross_right = None
     for number in range(chunks):
-        filtered = fir(padded, fir_taps, chans, piece, number * piece)
+        filtered = fir(source, left, right, band, number * piece, piece)
         extended = with_halo(filtered, (("ch", 0),), GAUGE)
         gauged = (extended[2 * GAUGE :] - extended[: -2 * GAUGE]).astype(jnp.bfloat16)
         lower_part = shifted(gauged[chans - 2 * STRIDE :], "ch", 1)
@@ -189,6 +213,7 @@
         local = gram(gauged, gauged)
         own = local if own is None else own + local
         gaugeds.append(gauged)
+        source, gauged = lax.optimization_barrier((source, gauged))
         lowers.append(lower_part)
         uppers.append(upper_part)
 
@@ -224,10 +249,12 @@
     band = jnp.concatenate([top, middle, bottom], axis=0) / total_time
 
     rounded = subspace(band, start_basis.T, windows)
-    outputs = [
-        clean(lowers[number], gaugeds[number], uppers[number], rounded) for number in range(chunks)
-    ]
-    return jnp.concatenate(outputs, axis=1)
+    cleaned = None
+    for number in range(chunks):
+        cleaned = clean(
+            lowers[number], gaugeds[number], uppers[number], rounded, samples, number * piece, cleaned
+        )
+    return cleaned
 
 
 def solution(mesh):

time: 196 us -> 195 us (level)
  local copies, waits for them, and re-layouts: 15.9 us -> 11.9 us
  other arithmetic: 5.34 us -> 7.76 us
    ppermute x0 -> x2, starting transfers between devices: none -> 9.47 us  [the longest x1 6.89 us: per_device(): lax.ppermute(raw[:, samples - half:], 'ta', forward)]
    ppermute x3 -> x2, starting transfers between devices: 16.6 us -> 8.33 us  [with_halo(): lax.ppermute(lax.slice_in_dim(block, 0, width, axis=dim), axis, backward)]
    ppermute x3 -> x2, starting transfers between devices: 11 us -> 5.28 us  [with_halo(): lax.ppermute(lax.slice_in_dim(block, block.shape[dim] - width, None, axis...]
    convert_element_type x2, other arithmetic: 0.66 us -> 6.23 us  [per_device(): gauged = (extended[2 * GAUGE:] - extended[:-2 * GAUGE]).astype(jnp.bfloat16)]
    ppermute x3 -> x2, waiting for transfers between devices: 5.47 us -> 10.7 us  [with_halo(): lax.ppermute(lax.slice_in_dim(block, block.shape[dim] - width, None, axis...]
    ppermute x6, waiting for transfers between devices: 13.5 us -> 8.95 us  [shifted(): lax.ppermute(value, axis, [(source, source + steps) for source in range(f...]
    concatenate x1 -> x0, other arithmetic: 3.15 us -> none  [per_device(): return jnp.concatenate(outputs, axis=1)]
    concatenate x1 -> x2, local copies, waits for them, and re-layouts: 4.33 us -> 1.36 us  [the longest x1 0.72 us: per_device(): jnp.concatenate([blank, lax.ppermute(raw[:, samples - half:], 'ta', forwa...]
  transfers between devices with their start and end apart: 18 -> 18, of which waited for: 8 -> 9; matrix products, arithmetic and copies ran while one was open for 5% -> 5% of each run, Pallas kernels for 0% -> 0%
where the time goes in v4:
time: 195 us; the launch traced here: 194 us
  waiting for transfers between devices  67.6 us (35%)
  starting transfers between devices  56.6 us (29%)
  Pallas kernels  46.2 us (24%)
  local copies, waits for them, and re-layouts  11.9 us (6%)
  other arithmetic  7.76 us (4%)
  matrix products  3.47 us (2%)
    ppermute x2, waiting for transfers between devices, ta_sum(): part = part + lax.ppermute(part, 'ta', across)  45.5 us
    ppermute x6, starting transfers between devices, shifted(): lax.ppermute(value, axis, [(source, source + steps) for source in range(f...  24.1 us
    pallas_call x1, Pallas kernels, subspace(): pl.pallas_call(subspace_kernel, out_shape=jax.ShapeDtypeStruct((windows,)...  22.3 us
    pallas_call x2, Pallas kernels, fir(): pl.pallas_call(kernel, grid=(length // width,), out_shape=jax.ShapeDtypeS...  12.2 us
    pallas_call x2, Pallas kernels, clean(): pl.pallas_call(clean_kernel, grid=(samples // width,), out_shape=jax.Shap...  11.8 us
    ppermute x2, waiting for transfers between devices, with_halo(): lax.ppermute(lax.slice_in_dim(block, block.shape[dim] - width, None, axis...  10.7 us
    ppermute x6, waiting for transfers between devices, shifted(): lax.ppermute(value, axis, [(source, source + steps) for source in range(f...  8.95 us
    ppermute x2, starting transfers between devices, with_halo(): lax.ppermute(lax.slice_in_dim(block, 0, width, axis=dim), axis, backward)  8.33 us
  transfers between devices with their start and end apart: 18, of which 9 were waited for; matrix products, arithmetic and copies ran while one was open for 5% of the time, Pallas kernels for 0%

profile of v4, /device:TPU:97, one launch (start us, length us, event | category | flops | bytes accessed | tf_op | source)
XLA Modules:
  0.0 194.0 jit_solution(1607966664276309491)
XLA Ops:
  0.0 1.0 fusion.24
  1.0 2.6 %collective-permute-start.1 = (bf16[256,64]{1,0:T(8,128)(2,1)S(1)}, bf16[256,64]{1,0:T(8,128)(2,1)S(1)}, u32[]{:S(2)}, u32[]{:S(2)}) collective-permute-start(bf16[256,64]{1,0:T(8,128)(2,1)S(1)} %get-tuple-element.21), channel_id=1, source_target_pairs={{1,0},{2,1},{3,2},{5,4},{6,5},{7,6},{9,8},{10,9},{11,10},{13,12},{... | collective-permute-start | bytes 98312 | tf_op jit(solution)/shard_map/ppermute | solution.py:196
  3.6 6.9 %collective-permute-start = (bf16[256,64]{1,0:T(8,128)(2,1)S(1)}, bf16[256,64]{1,0:T(8,128)(2,1)S(1)}, u32[]{:S(2)}, u32[]{:S(2)}) collective-permute-start(bf16[256,64]{1,0:T(8,128)(2,1)S(1)} %get-tuple-element.22), channel_id=1, source_target_pairs={{0,1},{1,2},{2,3},{4,5},{5,6},{6,7},{8,9},{9,10},{10,11},{12,13},{... | collective-permute-start | bytes 98312 | tf_op jit(solution)/shard_map/ppermute | solution.py:195
  10.4 0.7 concatenate.69
  11.2 1.3 tile.10
  13.2 0.7 pad_slice_fusion
  14.0 0.8 slice.137.refs_6_
  14.8 0.6 concatenate.68.refs_1_
  15.5 0.7 concatenate.67.refs_0_
  16.2 5.8 %shard_map.37 = f32[256,2560]{1,0:T(8,128)} custom-call(bf16[256,128]{1,0:T(8,128)(2,1)} %concatenate.67.refs_0_, bf16[256,128]{1,0:T(8,128)(2,1)} %concatenate.68.refs_1_, bf16[256,5120]{1,0:T(8,128)(2,1)} %refs_4_.2, bf16[256,5120]{1,0:T(8,128)(2,1)} %refs_4_.2, bf16[256,5120]{1,0:T(8,128)(2,1)} %refs_4_.2, bf16[128,512]{1,0:T(8,128)(2,1)} %get-tuple-element.24.refs_5_, ...), custom_call_target="tpu_custom_call" | custom-call | tf_op jit(solution)/shard_map/pallas_call | solution.py:108
  22.0 0.9 fusion.23
  23.0 6.4 %collective-permute-start.2 = (f32[4,2560]{1,0:T(4,128)S(1)}, f32[4,2560]{1,0:T(4,128)S(1)}, u32[]{:S(2)}, u32[]{:S(2)}) collective-permute-start(f32[4,2560]{1,0:T(4,128)S(1)} %get-tuple-element.19), channel_id=1, source_target_pairs={{4,0},{8,4},{12,8},{16,12},{20,16},{24,20},{28,24},{32,28},{36,32}... | collective-permute-start | bytes 122888 | tf_op jit(solution)/shard_map/ppermute | solution.py:26
  29.4 1.9 collective-permute-start.3
  31.3 7.0 %collective-permute-done.3 = f32[4,2560]{1,0:T(4,128)S(1)} collective-permute-done((f32[4,2560]{1,0:T(4,128)S(1)}, f32[4,2560]{1,0:T(4,128)S(1)}, u32[]{:S(2)}, u32[]{:S(2)}) %collective-permute-start.3) | collective-permute-done | bytes 40992 | tf_op jit(solution)/shard_map/ppermute | solution.py:23
  38.3 3.1 %fusion.3.own_ref = bf16[256,2560]{1,0:T(8,128)(2,1)S(1)} fusion(f32[256,2560]{1,0:T(8,128)} %shard_map.37, f32[4,2560]{1,0:T(4,128)S(1)} %collective-permute-done.3, f32[4,2560]{1,0:T(4,128)S(1)} %collective-permute-done.2), kind=kLoop, calls=%fused_computation.6 | loop fusion | flops 2621440 | bytes 4014080 | tf_op jit(solution)/shard_map/convert_element_type | solution.py:210
  41.5 6.3 %shard_map.38 = f32[256,2560]{1,0:T(8,128)} custom-call(bf16[256,128]{1,0:T(8,128)(2,1)} %concatenate.67.refs_0_, bf16[256,128]{1,0:T(8,128)(2,1)} %concatenate.68.refs_1_, bf16[256,5120]{1,0:T(8,128)(2,1)} %refs_4_.2, bf16[256,5120]{1,0:T(8,128)(2,1)} %refs_4_.2, bf16[256,5120]{1,0:T(8,128)(2,1)} %refs_4_.2, bf16[128,512]{1,0:T(8,128)(2,1)} %get-tuple-element.24.refs_5_, ...), custom_call_target="tpu_custom_call" | custom-call | tf_op jit(solution)/shard_map/pallas_call | solution.py:108
  47.8 0.9 fusion.22
  48.7 1.9 collective-permute-start.4
  50.7 3.4 %collective-permute-start.5 = (f32[4,2560]{1,0:T(4,128)S(1)}, f32[4,2560]{1,0:T(4,128)S(1)}, u32[]{:S(2)}, u32[]{:S(2)}) collective-permute-start(f32[4,2560]{1,0:T(4,128)S(1)} %get-tuple-element.18), channel_id=1, source_target_pairs={{0,4},{4,8},{8,12},{12,16},{16,20},{20,24},{24,28},{28,32},{32,36}... | collective-permute-start | bytes 122888 | tf_op jit(solution)/shard_map/ppermute | solution.py:23
  54.0 1.9 collective-permute-start.9
  56.0 3.6 %collective-permute-done.5 = f32[4,2560]{1,0:T(4,128)S(1)} collective-permute-done((f32[4,2560]{1,0:T(4,128)S(1)}, f32[4,2560]{1,0:T(4,128)S(1)}, u32[]{:S(2)}, u32[]{:S(2)}) %collective-permute-start.5) | collective-permute-done | bytes 40992 | tf_op jit(solution)/shard_map/ppermute | solution.py:23
  59.6 3.1 %fusion.1.own_ref = bf16[256,2560]{1,0:T(8,128)(2,1)S(1)} fusion(f32[256,2560]{1,0:T(8,128)} %shard_map.38, f32[4,2560]{1,0:T(4,128)S(1)} %collective-permute-done.5, f32[4,2560]{1,0:T(4,128)S(1)} %collective-permute-done.4), kind=kLoop, calls=%fused_computation.2 | loop fusion | flops 2621440 | bytes 4014080 | tf_op jit(solution)/shard_map/convert_element_type | solution.py:210
  62.7 1.9 collective-permute-start.10
  64.7 0.5 fusion.27
  65.9 7.6 %collective-permute-start.11 = (bf16[128,2560]{1,0:T(8,128)(2,1)S(1)}, bf16[128,2560]{1,0:T(8,128)(2,1)S(1)}, u32[]{:S(2)}, u32[]{:S(2)}) collective-permute-start(bf16[128,2560]{1,0:T(8,128)(2,1)S(1)} %slice.144), channel_id=1, source_target_pairs={{4,0},{8,4},{12,8},{16,12},{20,16},{24,20},{28,24},{32,28},{36,32}... | collective-permute-start | bytes 1966088 | tf_op jit(solution)/shard_map/ppermute | solution.py:34
  73.6 1.9 collective-permute-start.12
  75.6 6.0 %collective-permute-start.7 = (f32[128,256]{1,0:T(8,128)S(1)}, f32[128,256]{1,0:T(8,128)S(1)}, u32[]{:S(2)}, u32[]{:S(2)}) collective-permute-start(f32[128,256]{1,0:T(8,128)S(1)} %select_add_fusion.1), channel_id=1, source_target_pairs={{0,2},{1,3},{2,0},{3,1},{4,6},{5,7},{6,4},{7,5},{8,10},{9,11},{10,... | collective-permute-start | bytes 393224 | tf_op jit(solution)/shard_map/ppermute | solution.py:182
  81.6 32.3 %collective-permute-done.7 = f32[128,256]{1,0:T(8,128)S(1)} collective-permute-done((f32[128,256]{1,0:T(8,128)S(1)}, f32[128,256]{1,0:T(8,128)S(1)}, u32[]{:S(2)}, u32[]{:S(2)}) %collective-permute-start.7) | collective-permute-done | bytes 131104 | tf_op jit(solution)/shard_map/ppermute | solution.py:182
  114.0 1.0 collective-permute-start.8
  114.9 1.0 collective-permute-done.8
  116.0 4.9 %collective-permute-done.10.lower_ref = bf16[256,2560]{1,0:T(8,128)(2,1)S(1)} collective-permute-done((bf16[256,2560]{1,0:T(8,128)(2,1)S(1)}, bf16[256,2560]{1,0:T(8,128)(2,1)S(1)}, u32[]{:S(2)}, u32[]{:S(2)}) %collective-permute-start.10) | collective-permute-done | bytes 1310752 | tf_op jit(solution)/shard_map/ppermute | solution.py:34
  121.4 0.5 copy-done.3
  123.1 0.7 fusion.8
  124.2 0.7 fusion.16
  125.0 1.5 collective-permute-done.14
  126.5 1.7 collective-permute-start.15
  128.2 13.2 %collective-permute-done.15 = f32[448,128]{1,0:T(8,128)S(1)} collective-permute-done((f32[448,128]{1,0:T(8,128)S(1)}, f32[448,128]{1,0:T(8,128)S(1)}, u32[]{:S(2)}, u32[]{:S(2)}) %collective-permute-start.15) | collective-permute-done | bytes 229408 | tf_op jit(solution)/shard_map/ppermute | solution.py:182
  141.4 0.5 collective-permute-start.16
  141.9 1.9 collective-permute-start.13
  143.9 8.8 %collective-permute-start.17 = (f32[128,128]{1,0:T(8,128)S(1)}, f32[128,128]{1,0:T(8,128)S(1)}, u32[]{:S(2)}, u32[]{:S(2)}) collective-permute-start(f32[128,128]{1,0:T(8,128)S(1)} %slice.152), channel_id=1, source_target_pairs={{4,0},{8,4},{12,8},{16,12},{20,16},{24,20},{28,24},{32,28},{36,32}... | collective-permute-start | bytes 196616 | tf_op jit(solution)/shard_map/ppermute | solution.py:34
  153.2 0.7 collective-permute-done.17
  153.8 3.4 %collective-permute-done.13 = f32[256,256]{1,0:T(8,128)S(1)} collective-permute-done((f32[256,256]{1,0:T(8,128)S(1)}, f32[256,256]{1,0:T(8,128)S(1)}, u32[]{:S(2)}, u32[]{:S(2)}) %collective-permute-start.13) | collective-permute-done | bytes 262176 | tf_op jit(solution)/shard_map/ppermute | solution.py:34
  157.2 1.3 fusion.14.band_ref
  158.5 22.3 %shard_map.39.basis_ref = bf16[2,16,512]{2,1,0:T(8,128)(2,1)} custom-call(f32[640,640]{1,0:T(8,128)} %fusion.14.band_ref, f32[16,512]{1,0:T(8,128)} %bitcast.23), custom_call_target="tpu_custom_call" | custom-call | tf_op jit(solution)/shard_map/pallas_call | solution.py:77
  180.8 0.7 slice.153
  181.5 0.7 copy.13
  182.2 5.9 %shard_map.40.rest_0_ = bf16[256,5120]{1,0:T(8,128)(2,1)} custom-call(bf16[256,2560]{1,0:T(8,128)(2,1)} %copy-done.2, bf16[256,2560]{1,0:T(8,128)(2,1)} %copy-done, bf16[128,2560]{1,0:T(8,128)(2,1)} %copy-done.5, bf16[2,16,512]{2,1,0:T(8,128)(2,1)} %shard_map.39.basis_ref, bf16[2,128,16]{2,1,0:T(8,128)(2,1)} %bitcast.21), custom_call_target="tpu_custom_call" | custom-call | tf_op jit(solution)/shard_map/pallas_call | solution.py:154
  188.1 5.9 %shard_map.41 = bf16[256,5120]{1,0:T(8,128)(2,1)} custom-call(bf16[256,2560]{1,0:T(8,128)(2,1)} %copy-done.3, bf16[256,2560]{1,0:T(8,128)(2,1)} %copy-done.1, bf16[128,2560]{1,0:T(8,128)(2,1)} %copy-done.4, bf16[2,16,512]{2,1,0:T(8,128)(2,1)} %shard_map.39.basis_ref, bf16[2,128,16]{2,1,0:T(8,128)(2,1)} %bitcast.22, ...), custom_call_target="tpu_custom_call", output_to_operand_aliasing={{}: (5, {})} | custom-call | tf_op jit(solution)/shard_map/pallas_call | solution.py:154
  (52 shorter events, 4.3 us)
Async XLA Ops:
  1.0 13.8 %collective-permute-start.1 = (bf16[256,64]{1,0:T(8,128)(2,1)S(1)}, bf16[256,64]{1,0:T(8,128)(2,1)S(1)}, u32[]{:S(2)}, u32[]{:S(2)}) collective-permute-start(bf16[256,64]{1,0:T(8,128)(2,1)S(1)} %get-tuple-element.21), channel_id=1, source_target_pairs={{1,0},{2,1},{3,2},{5,4},{6,5},{7,6},{9,8},{10,9},{11,10},{13,12},{... | collective-permute-start | bytes 98312 | tf_op jit(solution)/shard_map/ppermute | solution.py:196
  3.6 11.9 %collective-permute-start = (bf16[256,64]{1,0:T(8,128)(2,1)S(1)}, bf16[256,64]{1,0:T(8,128)(2,1)S(1)}, u32[]{:S(2)}, u32[]{:S(2)}) collective-permute-start(bf16[256,64]{1,0:T(8,128)(2,1)S(1)} %get-tuple-element.22), channel_id=1, source_target_pairs={{0,1},{1,2},{2,3},{4,5},{5,6},{6,7},{8,9},{9,10},{10,11},{12,13},{... | collective-permute-start | bytes 98312 | tf_op jit(solution)/shard_map/ppermute | solution.py:195
  23.0 8.4 %collective-permute-start.2 = (f32[4,2560]{1,0:T(4,128)S(1)}, f32[4,2560]{1,0:T(4,128)S(1)}, u32[]{:S(2)}, u32[]{:S(2)}) collective-permute-start(f32[4,2560]{1,0:T(4,128)S(1)} %get-tuple-element.19), channel_id=1, source_target_pairs={{4,0},{8,4},{12,8},{16,12},{20,16},{24,20},{28,24},{32,28},{36,32}... | collective-permute-start | bytes 122888 | tf_op jit(solution)/shard_map/ppermute | solution.py:26
  29.4 9.0 %collective-permute-start.3 = (f32[4,2560]{1,0:T(4,128)S(1)}, f32[4,2560]{1,0:T(4,128)S(1)}, u32[]{:S(2)}, u32[]{:S(2)}) collective-permute-start(f32[4,2560]{1,0:T(4,128)S(1)} %get-tuple-element.20), channel_id=1, source_target_pairs={{0,4},{4,8},{8,12},{12,16},{16,20},{20,24},{24,28},{28,32},{32,36}... | collective-permute-start | bytes 122888 | tf_op jit(solution)/shard_map/ppermute | solution.py:23
  41.5 82.3 %copy-start = (bf16[256,2560]{1,0:T(8,128)(2,1)}, bf16[256,2560]{1,0:T(8,128)(2,1)S(1)}, u32[]{:S(2)}) copy-start(bf16[256,2560]{1,0:T(8,128)(2,1)S(1)} %fusion.3.own_ref) | copy-start | bytes 3932164
  48.7 7.2 %collective-permute-start.4 = (f32[4,2560]{1,0:T(4,128)S(1)}, f32[4,2560]{1,0:T(4,128)S(1)}, u32[]{:S(2)}, u32[]{:S(2)}) collective-permute-start(f32[4,2560]{1,0:T(4,128)S(1)} %get-tuple-element.17), channel_id=1, source_target_pairs={{4,0},{8,4},{12,8},{16,12},{20,16},{24,20},{28,24},{32,28},{36,32}... | collective-permute-start | bytes 122888 | tf_op jit(solution)/shard_map/ppermute | solution.py:26
  50.7 9.0 %collective-permute-start.5 = (f32[4,2560]{1,0:T(4,128)S(1)}, f32[4,2560]{1,0:T(4,128)S(1)}, u32[]{:S(2)}, u32[]{:S(2)}) collective-permute-start(f32[4,2560]{1,0:T(4,128)S(1)} %get-tuple-element.18), channel_id=1, source_target_pairs={{0,4},{4,8},{8,12},{12,16},{16,20},{20,24},{24,28},{28,32},{32,36}... | collective-permute-start | bytes 122888 | tf_op jit(solution)/shard_map/ppermute | solution.py:23
  54.0 62.0 %collective-permute-start.9 = (bf16[256,2560]{1,0:T(8,128)(2,1)S(1)}, bf16[256,2560]{1,0:T(8,128)(2,1)S(1)}, u32[]{:S(2)}, u32[]{:S(2)}) collective-permute-start(bf16[256,2560]{1,0:T(8,128)(2,1)S(1)} %fusion.3.own_ref), channel_id=1, source_target_pairs={{0,4},{4,8},{8,12},{12,16},{16,20},{20,24},{24,28},{28,32},{32,36}... | collective-permute-start | bytes 3932168 | tf_op jit(solution)/shard_map/ppermute | solution.py:34
  62.7 59.8 %copy-start.1 = (bf16[256,2560]{1,0:T(8,128)(2,1)}, bf16[256,2560]{1,0:T(8,128)(2,1)S(1)}, u32[]{:S(2)}) copy-start(bf16[256,2560]{1,0:T(8,128)(2,1)S(1)} %fusion.1.own_ref) | copy-start | bytes 3932164
  62.7 58.2 %collective-permute-start.10 = (bf16[256,2560]{1,0:T(8,128)(2,1)S(1)}, bf16[256,2560]{1,0:T(8,128)(2,1)S(1)}, u32[]{:S(2)}, u32[]{:S(2)}) collective-permute-start(bf16[256,2560]{1,0:T(8,128)(2,1)S(1)} %fusion.1.own_ref), channel_id=1, source_target_pairs={{0,4},{4,8},{8,12},{12,16},{16,20},{20,24},{24,28},{28,32},{32,36}... | collective-permute-start | bytes 3932168 | tf_op jit(solution)/shard_map/ppermute | solution.py:34
  65.8 9.7 %collective-permute-start.6 = (f32[128,256]{1,0:T(8,128)S(1)}, f32[128,256]{1,0:T(8,128)S(1)}, u32[]{:S(2)}, u32[]{:S(2)}) collective-permute-start(f32[128,256]{1,0:T(8,128)S(1)} %slice_select_fusion), channel_id=1, source_target_pairs={{0,1},{1,0},{2,3},{3,2},{4,5},{5,4},{6,7},{7,6},{8,9},{9,8},{10,11... | collective-permute-start | bytes 393224 | tf_op jit(solution)/shard_map/ppermute | solution.py:181
  65.9 50.0 %collective-permute-start.11 = (bf16[128,2560]{1,0:T(8,128)(2,1)S(1)}, bf16[128,2560]{1,0:T(8,128)(2,1)S(1)}, u32[]{:S(2)}, u32[]{:S(2)}) collective-permute-start(bf16[128,2560]{1,0:T(8,128)(2,1)S(1)} %slice.144), channel_id=1, source_target_pairs={{4,0},{8,4},{12,8},{16,12},{20,16},{24,20},{28,24},{32,28},{36,32}... | collective-permute-start | bytes 1966088 | tf_op jit(solution)/shard_map/ppermute | solution.py:34
  73.6 42.4 %collective-permute-start.12 = (bf16[128,2560]{1,0:T(8,128)(2,1)S(1)}, bf16[128,2560]{1,0:T(8,128)(2,1)S(1)}, u32[]{:S(2)}, u32[]{:S(2)}) collective-permute-start(bf16[128,2560]{1,0:T(8,128)(2,1)S(1)} %slice.145), channel_id=1, source_target_pairs={{4,0},{8,4},{12,8},{16,12},{20,16},{24,20},{28,24},{32,28},{36,32}... | collective-permute-start | bytes 1966088 | tf_op jit(solution)/shard_map/ppermute | solution.py:34
  75.6 38.4 %collective-permute-start.7 = (f32[128,256]{1,0:T(8,128)S(1)}, f32[128,256]{1,0:T(8,128)S(1)}, u32[]{:S(2)}, u32[]{:S(2)}) collective-permute-start(f32[128,256]{1,0:T(8,128)S(1)} %select_add_fusion.1), channel_id=1, source_target_pairs={{0,2},{1,3},{2,0},{3,1},{4,6},{5,7},{6,4},{7,5},{8,10},{9,11},{10,... | collective-permute-start | bytes 393224 | tf_op jit(solution)/shard_map/ppermute | solution.py:182
  114.0 2.0 %collective-permute-start.8 = (f32[128,256]{1,0:T(8,128)S(1)}, f32[128,256]{1,0:T(8,128)S(1)}, u32[]{:S(2)}, u32[]{:S(2)}) collective-permute-start(f32[128,256]{1,0:T(8,128)S(1)} %add.39), channel_id=1, source_target_pairs={{0,1},{1,0},{2,3},{3,2},{4,5},{5,4},{6,7},{7,6},{8,9},{9,8},{10,11... | collective-permute-start | bytes 393224 | tf_op jit(solution)/shard_map/ppermute | solution.py:183
  116.0 7.8 %copy-start.5 = (bf16[128,2560]{1,0:T(8,128)(2,1)}, bf16[128,2560]{1,0:T(8,128)(2,1)S(1)}, u32[]{:S(2)}) copy-start(bf16[128,2560]{1,0:T(8,128)(2,1)S(1)} %collective-permute-done.11.upper_ref) | copy-start | bytes 1966084
  116.0 6.6 %copy-start.4 = (bf16[128,2560]{1,0:T(8,128)(2,1)}, bf16[128,2560]{1,0:T(8,128)(2,1)S(1)}, u32[]{:S(2)}) copy-start(bf16[128,2560]{1,0:T(8,128)(2,1)S(1)} %collective-permute-done.12.upper_ref) | copy-start | bytes 1966084
  116.0 6.0 %copy-start.2 = (bf16[256,2560]{1,0:T(8,128)(2,1)}, bf16[256,2560]{1,0:T(8,128)(2,1)S(1)}, u32[]{:S(2)}) copy-start(bf16[256,2560]{1,0:T(8,128)(2,1)S(1)} %collective-permute-done.9.lower_ref) | copy-start | bytes 3932164
  120.9 1.1 copy-start.3
  122.0 1.1 slice-start.1
  123.1 1.1 slice-start
  124.9 1.6 collective-permute-start.14
  126.5 14.9 %collective-permute-start.15 = (f32[448,128]{1,0:T(8,128)S(1)}, f32[448,128]{1,0:T(8,128)S(1)}, u32[]{:S(2)}, u32[]{:S(2)}) collective-permute-start(f32[448,128]{1,0:T(8,128)S(1)} %select_add_fusion), channel_id=1, source_target_pairs={{0,2},{1,3},{2,0},{3,1},{4,6},{5,7},{6,4},{7,5},{8,10},{9,11},{10,... | collective-permute-start | bytes 688136 | tf_op jit(solution)/shard_map/ppermute | solution.py:182
  141.4 11.3 %collective-permute-start.16 = (f32[448,128]{1,0:T(8,128)S(1)}, f32[448,128]{1,0:T(8,128)S(1)}, u32[]{:S(2)}, u32[]{:S(2)}) collective-permute-start(f32[448,128]{1,0:T(8,128)S(1)} %add.43), channel_id=1, source_target_pairs={{0,1},{1,0},{2,3},{3,2},{4,5},{5,4},{6,7},{7,6},{8,9},{9,8},{10,11... | collective-permute-start | bytes 688136 | tf_op jit(solution)/shard_map/ppermute | solution.py:183
  141.9 15.3 %collective-permute-start.13 = (f32[256,256]{1,0:T(8,128)S(1)}, f32[256,256]{1,0:T(8,128)S(1)}, u32[]{:S(2)}, u32[]{:S(2)}) collective-permute-start(f32[256,256]{1,0:T(8,128)S(1)} %maximum_select_fusion.1), channel_id=1, source_target_pairs={{0,4},{4,8},{8,12},{12,16},{16,20},{20,24},{24,28},{28,32},{32,36}... | collective-permute-start | bytes 786440 | tf_op jit(solution)/shard_map/ppermute | solution.py:34
  143.9 10.0 %collective-permute-start.17 = (f32[128,128]{1,0:T(8,128)S(1)}, f32[128,128]{1,0:T(8,128)S(1)}, u32[]{:S(2)}, u32[]{:S(2)}) collective-permute-start(f32[128,128]{1,0:T(8,128)S(1)} %slice.152), channel_id=1, source_target_pairs={{4,0},{8,4},{12,8},{16,12},{20,16},{24,20},{28,24},{32,28},{36,32}... | collective-permute-start | bytes 196616 | tf_op jit(solution)/shard_map/ppermute | solution.py:34

commit v5 on v4

--- a/solution.py
+++ b/solution.py
@@ -45,13 +45,22 @@
     return lax.dot_general(a, b, (((1,), (1,)), ((), ())), preferred_element_type=jnp.float32)
 
 
-def orthonormal_rows(image, rows):
+def orthonormal_rows(image, rows, lanes):
+    rank = image.shape[0]
+    gram_mat = lax.dot_general(
+        image, image, (((1,), (1,)), ((), ())), precision=lax.Precision.HIGHEST,
+        preferred_element_type=jnp.float32,
+    )
     result = image
-    for i in range(image.shape[0]):
-        row = result[i : i + 1, :]
-        unit = row / jnp.sqrt(jnp.sum(row * row, axis=1, keepdims=True))
-        proj = jnp.sum(result * unit, axis=1, keepdims=True)
-        result = jnp.where(rows > i, result - proj * unit, jnp.where(rows == i, unit, result))
+    for j in range(rank):
+        column = jnp.sum(jnp.where(lanes == j, gram_mat, 0.0), axis=1, keepdims=True)
+        scale = 1.0 / jnp.sqrt(column[j : j + 1, :])
+        factor = column * scale
+        pivot_row = gram_mat[j : j + 1, :] * scale
+        image_row = result[j : j + 1, :] * scale
+        below = rows > j
+        gram_mat = jnp.where(below, gram_mat - factor * pivot_row, gram_mat)
+        result = jnp.where(below, result - factor * image_row, jnp.where(rows == j, image_row, result))
     return result
 
 
@@ -59,6 +68,7 @@
     windows = out_ref.shape[0]
     rank, win = start_ref.shape
     rows = lax.broadcasted_iota(jnp.int32, (rank, 1), 0)
+    lanes = lax.broadcasted_iota(jnp.int32, (rank, rank), 1)
     bases = [start_ref[...] for _ in range(windows)]
     for sweep in range(ITERS):
         for number in range(windows):
@@ -68,7 +78,7 @@
                 bases[number], scatter_mat, precision=lax.Precision.HIGHEST,
                 preferred_element_type=jnp.float32,
             )
-            bases[number] = orthonormal_rows(image, rows)
+            bases[number] = orthonormal_rows(image, rows, lanes)
     for number in range(windows):
         out_ref[number] = bases[number].astype(out_ref.dtype)
 

time: 195 us -> 190 us (0.974)
  Pallas kernels: 46.2 us -> 41 us
    pallas_call x1, Pallas kernels: 22.3 us -> 17.1 us  [subspace(): pl.pallas_call(subspace_kernel, out_shape=jax.ShapeDtypeStruct((windows,)...]
where the time goes in v5:
time: 190 us; the launch traced here: 189 us
  waiting for transfers between devices  67.6 us (36%)
  starting transfers between devices  56.6 us (30%)
  Pallas kernels  41 us (22%)
  local copies, waits for them, and re-layouts  11.9 us (6%)
  other arithmetic  7.76 us (4%)
  matrix products  3.47 us (2%)
    ppermute x2, waiting for transfers between devices, ta_sum(): part = part + lax.ppermute(part, 'ta', across)  45.5 us
    ppermute x6, starting transfers between devices, shifted(): lax.ppermute(value, axis, [(source, source + steps) for source in range(f...  24.1 us
    pallas_call x1, Pallas kernels, subspace(): pl.pallas_call(subspace_kernel, out_shape=jax.ShapeDtypeStruct((windows,)...  17.1 us
    pallas_call x2, Pallas kernels, fir(): pl.pallas_call(kernel, grid=(length // width,), out_shape=jax.ShapeDtypeS...  12.2 us
    pallas_call x2, Pallas kernels, clean(): pl.pallas_call(clean_kernel, grid=(samples // width,), out_shape=jax.Shap...  11.8 us
    ppermute x2, waiting for transfers between devices, with_halo(): lax.ppermute(lax.slice_in_dim(block, block.shape[dim] - width, None, axis...  10.7 us
    ppermute x6, waiting for transfers between devices, shifted(): lax.ppermute(value, axis, [(source, source + steps) for source in range(f...  8.95 us
    ppermute x2, starting transfers between devices, with_halo(): lax.ppermute(lax.slice_in_dim(block, 0, width, axis=dim), axis, backward)  8.33 us
  transfers between devices with their start and end apart: 18, of which 9 were waited for; matrix products, arithmetic and copies ran while one was open for 5% of the time, Pallas kernels for 0%

profile of v5, /device:TPU:97, one launch (start us, length us, event | category | flops | bytes accessed | tf_op | source)
XLA Modules:
  0.0 188.9 jit_solution(9080098175483027190)
XLA Ops:
  0.0 1.0 fusion.24
  1.0 2.6 %collective-permute-start.1 = (bf16[256,64]{1,0:T(8,128)(2,1)S(1)}, bf16[256,64]{1,0:T(8,128)(2,1)S(1)}, u32[]{:S(2)}, u32[]{:S(2)}) collective-permute-start(bf16[256,64]{1,0:T(8,128)(2,1)S(1)} %get-tuple-element.21), channel_id=1, source_target_pairs={{1,0},{2,1},{3,2},{5,4},{6,5},{7,6},{9,8},{10,9},{11,10},{13,12},{... | collective-permute-start | bytes 98312 | tf_op jit(solution)/shard_map/ppermute | solution.py:206
  3.6 6.9 %collective-permute-start = (bf16[256,64]{1,0:T(8,128)(2,1)S(1)}, bf16[256,64]{1,0:T(8,128)(2,1)S(1)}, u32[]{:S(2)}, u32[]{:S(2)}) collective-permute-start(bf16[256,64]{1,0:T(8,128)(2,1)S(1)} %get-tuple-element.22), channel_id=1, source_target_pairs={{0,1},{1,2},{2,3},{4,5},{5,6},{6,7},{8,9},{9,10},{10,11},{12,13},{... | collective-permute-start | bytes 98312 | tf_op jit(solution)/shard_map/ppermute | solution.py:205
  10.4 0.7 concatenate.69
  11.2 1.3 tile.10
  13.2 0.7 pad_slice_fusion
  14.0 0.8 slice.137.refs_6_
  14.8 0.6 concatenate.68.refs_1_
  15.5 0.7 concatenate.67.refs_0_
  16.2 5.8 %shard_map.37 = f32[256,2560]{1,0:T(8,128)} custom-call(bf16[256,128]{1,0:T(8,128)(2,1)} %concatenate.67.refs_0_, bf16[256,128]{1,0:T(8,128)(2,1)} %concatenate.68.refs_1_, bf16[256,5120]{1,0:T(8,128)(2,1)} %refs_4_.2, bf16[256,5120]{1,0:T(8,128)(2,1)} %refs_4_.2, bf16[256,5120]{1,0:T(8,128)(2,1)} %refs_4_.2, bf16[128,512]{1,0:T(8,128)(2,1)} %get-tuple-element.24.refs_5_, ...), custom_call_target="tpu_custom_call" | custom-call | tf_op jit(solution)/shard_map/pallas_call | solution.py:118
  22.0 0.9 fusion.23
  23.0 6.4 %collective-permute-start.2 = (f32[4,2560]{1,0:T(4,128)S(1)}, f32[4,2560]{1,0:T(4,128)S(1)}, u32[]{:S(2)}, u32[]{:S(2)}) collective-permute-start(f32[4,2560]{1,0:T(4,128)S(1)} %get-tuple-element.19), channel_id=1, source_target_pairs={{4,0},{8,4},{12,8},{16,12},{20,16},{24,20},{28,24},{32,28},{36,32}... | collective-permute-start | bytes 122888 | tf_op jit(solution)/shard_map/ppermute | solution.py:26
  29.4 1.9 %collective-permute-start.3 = (f32[4,2560]{1,0:T(4,128)S(1)}, f32[4,2560]{1,0:T(4,128)S(1)}, u32[]{:S(2)}, u32[]{:S(2)}) collective-permute-start(f32[4,2560]{1,0:T(4,128)S(1)} %get-tuple-element.20), channel_id=1, source_target_pairs={{0,4},{4,8},{8,12},{12,16},{16,20},{20,24},{24,28},{28,32},{32,36}... | collective-permute-start | bytes 122888 | tf_op jit(solution)/shard_map/ppermute | solution.py:23
  31.3 7.0 %collective-permute-done.3 = f32[4,2560]{1,0:T(4,128)S(1)} collective-permute-done((f32[4,2560]{1,0:T(4,128)S(1)}, f32[4,2560]{1,0:T(4,128)S(1)}, u32[]{:S(2)}, u32[]{:S(2)}) %collective-permute-start.3) | collective-permute-done | bytes 40992 | tf_op jit(solution)/shard_map/ppermute | solution.py:23
  38.3 3.1 %fusion.3.own_ref = bf16[256,2560]{1,0:T(8,128)(2,1)S(1)} fusion(f32[256,2560]{1,0:T(8,128)} %shard_map.37, f32[4,2560]{1,0:T(4,128)S(1)} %collective-permute-done.3, f32[4,2560]{1,0:T(4,128)S(1)} %collective-permute-done.2), kind=kLoop, calls=%fused_computation.6 | loop fusion | flops 2621440 | bytes 4014080 | tf_op jit(solution)/shard_map/convert_element_type | solution.py:220
  41.5 6.3 %shard_map.38 = f32[256,2560]{1,0:T(8,128)} custom-call(bf16[256,128]{1,0:T(8,128)(2,1)} %concatenate.67.refs_0_, bf16[256,128]{1,0:T(8,128)(2,1)} %concatenate.68.refs_1_, bf16[256,5120]{1,0:T(8,128)(2,1)} %refs_4_.2, bf16[256,5120]{1,0:T(8,128)(2,1)} %refs_4_.2, bf16[256,5120]{1,0:T(8,128)(2,1)} %refs_4_.2, bf16[128,512]{1,0:T(8,128)(2,1)} %get-tuple-element.24.refs_5_, ...), custom_call_target="tpu_custom_call" | custom-call | tf_op jit(solution)/shard_map/pallas_call | solution.py:118
  47.8 0.9 fusion.22
  48.7 1.9 %collective-permute-start.4 = (f32[4,2560]{1,0:T(4,128)S(1)}, f32[4,2560]{1,0:T(4,128)S(1)}, u32[]{:S(2)}, u32[]{:S(2)}) collective-permute-start(f32[4,2560]{1,0:T(4,128)S(1)} %get-tuple-element.17), channel_id=1, source_target_pairs={{4,0},{8,4},{12,8},{16,12},{20,16},{24,20},{28,24},{32,28},{36,32}... | collective-permute-start | bytes 122888 | tf_op jit(solution)/shard_map/ppermute | solution.py:26
  50.7 3.4 %collective-permute-start.5 = (f32[4,2560]{1,0:T(4,128)S(1)}, f32[4,2560]{1,0:T(4,128)S(1)}, u32[]{:S(2)}, u32[]{:S(2)}) collective-permute-start(f32[4,2560]{1,0:T(4,128)S(1)} %get-tuple-element.18), channel_id=1, source_target_pairs={{0,4},{4,8},{8,12},{12,16},{16,20},{20,24},{24,28},{28,32},{32,36}... | collective-permute-start | bytes 122888 | tf_op jit(solution)/shard_map/ppermute | solution.py:23
  54.0 1.9 %collective-permute-start.9 = (bf16[256,2560]{1,0:T(8,128)(2,1)S(1)}, bf16[256,2560]{1,0:T(8,128)(2,1)S(1)}, u32[]{:S(2)}, u32[]{:S(2)}) collective-permute-start(bf16[256,2560]{1,0:T(8,128)(2,1)S(1)} %fusion.3.own_ref), channel_id=1, source_target_pairs={{0,4},{4,8},{8,12},{12,16},{16,20},{20,24},{24,28},{28,32},{32,36}... | collective-permute-start | bytes 3932168 | tf_op jit(solution)/shard_map/ppermute | solution.py:34
  56.0 3.6 %collective-permute-done.5 = f32[4,2560]{1,0:T(4,128)S(1)} collective-permute-done((f32[4,2560]{1,0:T(4,128)S(1)}, f32[4,2560]{1,0:T(4,128)S(1)}, u32[]{:S(2)}, u32[]{:S(2)}) %collective-permute-start.5) | collective-permute-done | bytes 40992 | tf_op jit(solution)/shard_map/ppermute | solution.py:23
  59.6 3.1 %fusion.1.own_ref = bf16[256,2560]{1,0:T(8,128)(2,1)S(1)} fusion(f32[256,2560]{1,0:T(8,128)} %shard_map.38, f32[4,2560]{1,0:T(4,128)S(1)} %collective-permute-done.5, f32[4,2560]{1,0:T(4,128)S(1)} %collective-permute-done.4), kind=kLoop, calls=%fused_computation.2 | loop fusion | flops 2621440 | bytes 4014080 | tf_op jit(solution)/shard_map/convert_element_type | solution.py:220
  62.7 1.9 %collective-permute-start.10 = (bf16[256,2560]{1,0:T(8,128)(2,1)S(1)}, bf16[256,2560]{1,0:T(8,128)(2,1)S(1)}, u32[]{:S(2)}, u32[]{:S(2)}) collective-permute-start(bf16[256,2560]{1,0:T(8,128)(2,1)S(1)} %fusion.1.own_ref), channel_id=1, source_target_pairs={{0,4},{4,8},{8,12},{12,16},{16,20},{20,24},{24,28},{28,32},{32,36}... | collective-permute-start | bytes 3932168 | tf_op jit(solution)/shard_map/ppermute | solution.py:34
  64.7 0.5 fusion.27
  65.9 7.6 %collective-permute-start.11 = (bf16[128,2560]{1,0:T(8,128)(2,1)S(1)}, bf16[128,2560]{1,0:T(8,128)(2,1)S(1)}, u32[]{:S(2)}, u32[]{:S(2)}) collective-permute-start(bf16[128,2560]{1,0:T(8,128)(2,1)S(1)} %slice.144), channel_id=1, source_target_pairs={{4,0},{8,4},{12,8},{16,12},{20,16},{24,20},{28,24},{32,28},{36,32}... | collective-permute-start | bytes 1966088 | tf_op jit(solution)/shard_map/ppermute | solution.py:34
  73.6 1.9 %collective-permute-start.12 = (bf16[128,2560]{1,0:T(8,128)(2,1)S(1)}, bf16[128,2560]{1,0:T(8,128)(2,1)S(1)}, u32[]{:S(2)}, u32[]{:S(2)}) collective-permute-start(bf16[128,2560]{1,0:T(8,128)(2,1)S(1)} %slice.145), channel_id=1, source_target_pairs={{4,0},{8,4},{12,8},{16,12},{20,16},{24,20},{28,24},{32,28},{36,32}... | collective-permute-start | bytes 1966088 | tf_op jit(solution)/shard_map/ppermute | solution.py:34
  75.6 6.0 %collective-permute-start.7 = (f32[128,256]{1,0:T(8,128)S(1)}, f32[128,256]{1,0:T(8,128)S(1)}, u32[]{:S(2)}, u32[]{:S(2)}) collective-permute-start(f32[128,256]{1,0:T(8,128)S(1)} %select_add_fusion.1), channel_id=1, source_target_pairs={{0,2},{1,3},{2,0},{3,1},{4,6},{5,7},{6,4},{7,5},{8,10},{9,11},{10,... | collective-permute-start | bytes 393224 | tf_op jit(solution)/shard_map/ppermute | solution.py:192
  81.6 32.3 %collective-permute-done.7 = f32[128,256]{1,0:T(8,128)S(1)} collective-permute-done((f32[128,256]{1,0:T(8,128)S(1)}, f32[128,256]{1,0:T(8,128)S(1)}, u32[]{:S(2)}, u32[]{:S(2)}) %collective-permute-start.7) | collective-permute-done | bytes 131104 | tf_op jit(solution)/shard_map/ppermute | solution.py:192
  114.0 1.0 collective-permute-start.8
  114.9 1.0 collective-permute-done.8
  116.0 4.9 %collective-permute-done.10.lower_ref = bf16[256,2560]{1,0:T(8,128)(2,1)S(1)} collective-permute-done((bf16[256,2560]{1,0:T(8,128)(2,1)S(1)}, bf16[256,2560]{1,0:T(8,128)(2,1)S(1)}, u32[]{:S(2)}, u32[]{:S(2)}) %collective-permute-start.10) | collective-permute-done | bytes 1310752 | tf_op jit(solution)/shard_map/ppermute | solution.py:34
  121.4 0.5 copy-done.3
  123.1 0.7 fusion.8
  124.2 0.7 fusion.16
  125.0 1.5 collective-permute-done.14
  126.5 1.7 collective-permute-start.15
  128.2 13.2 %collective-permute-done.15 = f32[448,128]{1,0:T(8,128)S(1)} collective-permute-done((f32[448,128]{1,0:T(8,128)S(1)}, f32[448,128]{1,0:T(8,128)S(1)}, u32[]{:S(2)}, u32[]{:S(2)}) %collective-permute-start.15) | collective-permute-done | bytes 229408 | tf_op jit(solution)/shard_map/ppermute | solution.py:192
  141.4 0.5 collective-permute-start.16
  141.9 1.9 %collective-permute-start.13 = (f32[256,256]{1,0:T(8,128)S(1)}, f32[256,256]{1,0:T(8,128)S(1)}, u32[]{:S(2)}, u32[]{:S(2)}) collective-permute-start(f32[256,256]{1,0:T(8,128)S(1)} %maximum_select_fusion.1), channel_id=1, source_target_pairs={{0,4},{4,8},{8,12},{12,16},{16,20},{20,24},{24,28},{28,32},{32,36}... | collective-permute-start | bytes 786440 | tf_op jit(solution)/shard_map/ppermute | solution.py:34
  143.9 8.8 %collective-permute-start.17 = (f32[128,128]{1,0:T(8,128)S(1)}, f32[128,128]{1,0:T(8,128)S(1)}, u32[]{:S(2)}, u32[]{:S(2)}) collective-permute-start(f32[128,128]{1,0:T(8,128)S(1)} %slice.152), channel_id=1, source_target_pairs={{4,0},{8,4},{12,8},{16,12},{20,16},{24,20},{28,24},{32,28},{36,32}... | collective-permute-start | bytes 196616 | tf_op jit(solution)/shard_map/ppermute | solution.py:34
  153.2 0.7 collective-permute-done.17
  153.8 3.4 %collective-permute-done.13 = f32[256,256]{1,0:T(8,128)S(1)} collective-permute-done((f32[256,256]{1,0:T(8,128)S(1)}, f32[256,256]{1,0:T(8,128)S(1)}, u32[]{:S(2)}, u32[]{:S(2)}) %collective-permute-start.13) | collective-permute-done | bytes 262176 | tf_op jit(solution)/shard_map/ppermute | solution.py:34
  157.2 1.3 fusion.14.band_ref
  158.5 17.1 %shard_map.39.basis_ref = bf16[2,16,512]{2,1,0:T(8,128)(2,1)} custom-call(f32[640,640]{1,0:T(8,128)} %fusion.14.band_ref, f32[16,512]{1,0:T(8,128)} %bitcast.23), custom_call_target="tpu_custom_call" | custom-call | tf_op jit(solution)/shard_map/pallas_call | solution.py:87
  175.6 0.7 slice.153
  176.3 0.7 copy.13
  177.1 5.9 %shard_map.40.rest_0_ = bf16[256,5120]{1,0:T(8,128)(2,1)} custom-call(bf16[256,2560]{1,0:T(8,128)(2,1)} %copy-done.2, bf16[256,2560]{1,0:T(8,128)(2,1)} %copy-done, bf16[128,2560]{1,0:T(8,128)(2,1)} %copy-done.5, bf16[2,16,512]{2,1,0:T(8,128)(2,1)} %shard_map.39.basis_ref, bf16[2,128,16]{2,1,0:T(8,128)(2,1)} %bitcast.21), custom_call_target="tpu_custom_call" | custom-call | tf_op jit(solution)/shard_map/pallas_call | solution.py:164
  183.0 5.9 %shard_map.41 = bf16[256,5120]{1,0:T(8,128)(2,1)} custom-call(bf16[256,2560]{1,0:T(8,128)(2,1)} %copy-done.3, bf16[256,2560]{1,0:T(8,128)(2,1)} %copy-done.1, bf16[128,2560]{1,0:T(8,128)(2,1)} %copy-done.4, bf16[2,16,512]{2,1,0:T(8,128)(2,1)} %shard_map.39.basis_ref, bf16[2,128,16]{2,1,0:T(8,128)(2,1)} %bitcast.22, ...), custom_call_target="tpu_custom_call", output_to_operand_aliasing={{}: (5, {})} | custom-call | tf_op jit(solution)/shard_map/pallas_call | solution.py:164
  (52 shorter events, 4.3 us)
Async XLA Ops:
  1.0 13.8 %collective-permute-start.1 = (bf16[256,64]{1,0:T(8,128)(2,1)S(1)}, bf16[256,64]{1,0:T(8,128)(2,1)S(1)}, u32[]{:S(2)}, u32[]{:S(2)}) collective-permute-start(bf16[256,64]{1,0:T(8,128)(2,1)S(1)} %get-tuple-element.21), channel_id=1, source_target_pairs={{1,0},{2,1},{3,2},{5,4},{6,5},{7,6},{9,8},{10,9},{11,10},{13,12},{... | collective-permute-start | bytes 98312 | tf_op jit(solution)/shard_map/ppermute | solution.py:206
  3.6 11.9 %collective-permute-start = (bf16[256,64]{1,0:T(8,128)(2,1)S(1)}, bf16[256,64]{1,0:T(8,128)(2,1)S(1)}, u32[]{:S(2)}, u32[]{:S(2)}) collective-permute-start(bf16[256,64]{1,0:T(8,128)(2,1)S(1)} %get-tuple-element.22), channel_id=1, source_target_pairs={{0,1},{1,2},{2,3},{4,5},{5,6},{6,7},{8,9},{9,10},{10,11},{12,13},{... | collective-permute-start | bytes 98312 | tf_op jit(solution)/shard_map/ppermute | solution.py:205
  23.0 8.4 %collective-permute-start.2 = (f32[4,2560]{1,0:T(4,128)S(1)}, f32[4,2560]{1,0:T(4,128)S(1)}, u32[]{:S(2)}, u32[]{:S(2)}) collective-permute-start(f32[4,2560]{1,0:T(4,128)S(1)} %get-tuple-element.19), channel_id=1, source_target_pairs={{4,0},{8,4},{12,8},{16,12},{20,16},{24,20},{28,24},{32,28},{36,32}... | collective-permute-start | bytes 122888 | tf_op jit(solution)/shard_map/ppermute | solution.py:26
  29.4 9.0 %collective-permute-start.3 = (f32[4,2560]{1,0:T(4,128)S(1)}, f32[4,2560]{1,0:T(4,128)S(1)}, u32[]{:S(2)}, u32[]{:S(2)}) collective-permute-start(f32[4,2560]{1,0:T(4,128)S(1)} %get-tuple-element.20), channel_id=1, source_target_pairs={{0,4},{4,8},{8,12},{12,16},{16,20},{20,24},{24,28},{28,32},{32,36}... | collective-permute-start | bytes 122888 | tf_op jit(solution)/shard_map/ppermute | solution.py:23
  41.5 82.3 %copy-start = (bf16[256,2560]{1,0:T(8,128)(2,1)}, bf16[256,2560]{1,0:T(8,128)(2,1)S(1)}, u32[]{:S(2)}) copy-start(bf16[256,2560]{1,0:T(8,128)(2,1)S(1)} %fusion.3.own_ref) | copy-start | bytes 3932164
  48.7 7.2 %collective-permute-start.4 = (f32[4,2560]{1,0:T(4,128)S(1)}, f32[4,2560]{1,0:T(4,128)S(1)}, u32[]{:S(2)}, u32[]{:S(2)}) collective-permute-start(f32[4,2560]{1,0:T(4,128)S(1)} %get-tuple-element.17), channel_id=1, source_target_pairs={{4,0},{8,4},{12,8},{16,12},{20,16},{24,20},{28,24},{32,28},{36,32}... | collective-permute-start | bytes 122888 | tf_op jit(solution)/shard_map/ppermute | solution.py:26
  50.7 9.0 %collective-permute-start.5 = (f32[4,2560]{1,0:T(4,128)S(1)}, f32[4,2560]{1,0:T(4,128)S(1)}, u32[]{:S(2)}, u32[]{:S(2)}) collective-permute-start(f32[4,2560]{1,0:T(4,128)S(1)} %get-tuple-element.18), channel_id=1, source_target_pairs={{0,4},{4,8},{8,12},{12,16},{16,20},{20,24},{24,28},{28,32},{32,36}... | collective-permute-start | bytes 122888 | tf_op jit(solution)/shard_map/ppermute | solution.py:23
  54.0 62.0 %collective-permute-start.9 = (bf16[256,2560]{1,0:T(8,128)(2,1)S(1)}, bf16[256,2560]{1,0:T(8,128)(2,1)S(1)}, u32[]{:S(2)}, u32[]{:S(2)}) collective-permute-start(bf16[256,2560]{1,0:T(8,128)(2,1)S(1)} %fusion.3.own_ref), channel_id=1, source_target_pairs={{0,4},{4,8},{8,12},{12,16},{16,20},{20,24},{24,28},{28,32},{32,36}... | collective-permute-start | bytes 3932168 | tf_op jit(solution)/shard_map/ppermute | solution.py:34
  62.7 59.8 %copy-start.1 = (bf16[256,2560]{1,0:T(8,128)(2,1)}, bf16[256,2560]{1,0:T(8,128)(2,1)S(1)}, u32[]{:S(2)}) copy-start(bf16[256,2560]{1,0:T(8,128)(2,1)S(1)} %fusion.1.own_ref) | copy-start | bytes 3932164
  62.7 58.2 %collective-permute-start.10 = (bf16[256,2560]{1,0:T(8,128)(2,1)S(1)}, bf16[256,2560]{1,0:T(8,128)(2,1)S(1)}, u32[]{:S(2)}, u32[]{:S(2)}) collective-permute-start(bf16[256,2560]{1,0:T(8,128)(2,1)S(1)} %fusion.1.own_ref), channel_id=1, source_target_pairs={{0,4},{4,8},{8,12},{12,16},{16,20},{20,24},{24,28},{28,32},{32,36}... | collective-permute-start | bytes 3932168 | tf_op jit(solution)/shard_map/ppermute | solution.py:34
  65.8 9.7 %collective-permute-start.6 = (f32[128,256]{1,0:T(8,128)S(1)}, f32[128,256]{1,0:T(8,128)S(1)}, u32[]{:S(2)}, u32[]{:S(2)}) collective-permute-start(f32[128,256]{1,0:T(8,128)S(1)} %slice_select_fusion), channel_id=1, source_target_pairs={{0,1},{1,0},{2,3},{3,2},{4,5},{5,4},{6,7},{7,6},{8,9},{9,8},{10,11... | collective-permute-start | bytes 393224 | tf_op jit(solution)/shard_map/ppermute | solution.py:191
  65.9 50.0 %collective-permute-start.11 = (bf16[128,2560]{1,0:T(8,128)(2,1)S(1)}, bf16[128,2560]{1,0:T(8,128)(2,1)S(1)}, u32[]{:S(2)}, u32[]{:S(2)}) collective-permute-start(bf16[128,2560]{1,0:T(8,128)(2,1)S(1)} %slice.144), channel_id=1, source_target_pairs={{4,0},{8,4},{12,8},{16,12},{20,16},{24,20},{28,24},{32,28},{36,32}... | collective-permute-start | bytes 1966088 | tf_op jit(solution)/shard_map/ppermute | solution.py:34
  73.6 42.4 %collective-permute-start.12 = (bf16[128,2560]{1,0:T(8,128)(2,1)S(1)}, bf16[128,2560]{1,0:T(8,128)(2,1)S(1)}, u32[]{:S(2)}, u32[]{:S(2)}) collective-permute-start(bf16[128,2560]{1,0:T(8,128)(2,1)S(1)} %slice.145), channel_id=1, source_target_pairs={{4,0},{8,4},{12,8},{16,12},{20,16},{24,20},{28,24},{32,28},{36,32}... | collective-permute-start | bytes 1966088 | tf_op jit(solution)/shard_map/ppermute | solution.py:34
  75.6 38.4 %collective-permute-start.7 = (f32[128,256]{1,0:T(8,128)S(1)}, f32[128,256]{1,0:T(8,128)S(1)}, u32[]{:S(2)}, u32[]{:S(2)}) collective-permute-start(f32[128,256]{1,0:T(8,128)S(1)} %select_add_fusion.1), channel_id=1, source_target_pairs={{0,2},{1,3},{2,0},{3,1},{4,6},{5,7},{6,4},{7,5},{8,10},{9,11},{10,... | collective-permute-start | bytes 393224 | tf_op jit(solution)/shard_map/ppermute | solution.py:192
  114.0 2.0 %collective-permute-start.8 = (f32[128,256]{1,0:T(8,128)S(1)}, f32[128,256]{1,0:T(8,128)S(1)}, u32[]{:S(2)}, u32[]{:S(2)}) collective-permute-start(f32[128,256]{1,0:T(8,128)S(1)} %add.39), channel_id=1, source_target_pairs={{0,1},{1,0},{2,3},{3,2},{4,5},{5,4},{6,7},{7,6},{8,9},{9,8},{10,11... | collective-permute-start | bytes 393224 | tf_op jit(solution)/shard_map/ppermute | solution.py:193
  116.0 7.8 %copy-start.5 = (bf16[128,2560]{1,0:T(8,128)(2,1)}, bf16[128,2560]{1,0:T(8,128)(2,1)S(1)}, u32[]{:S(2)}) copy-start(bf16[128,2560]{1,0:T(8,128)(2,1)S(1)} %collective-permute-done.11.upper_ref) | copy-start | bytes 1966084
  116.0 6.6 %copy-start.4 = (bf16[128,2560]{1,0:T(8,128)(2,1)}, bf16[128,2560]{1,0:T(8,128)(2,1)S(1)}, u32[]{:S(2)}) copy-start(bf16[128,2560]{1,0:T(8,128)(2,1)S(1)} %collective-permute-done.12.upper_ref) | copy-start | bytes 1966084
  116.0 6.0 %copy-start.2 = (bf16[256,2560]{1,0:T(8,128)(2,1)}, bf16[256,2560]{1,0:T(8,128)(2,1)S(1)}, u32[]{:S(2)}) copy-start(bf16[256,2560]{1,0:T(8,128)(2,1)S(1)} %collective-permute-done.9.lower_ref) | copy-start | bytes 3932164
  120.9 1.1 copy-start.3
  122.0 1.1 slice-start.1
  123.1 1.1 slice-start
  124.9 1.6 collective-permute-start.14
  126.5 14.9 %collective-permute-start.15 = (f32[448,128]{1,0:T(8,128)S(1)}, f32[448,128]{1,0:T(8,128)S(1)}, u32[]{:S(2)}, u32[]{:S(2)}) collective-permute-start(f32[448,128]{1,0:T(8,128)S(1)} %select_add_fusion), channel_id=1, source_target_pairs={{0,2},{1,3},{2,0},{3,1},{4,6},{5,7},{6,4},{7,5},{8,10},{9,11},{10,... | collective-permute-start | bytes 688136 | tf_op jit(solution)/shard_map/ppermute | solution.py:192
  141.4 11.3 %collective-permute-start.16 = (f32[448,128]{1,0:T(8,128)S(1)}, f32[448,128]{1,0:T(8,128)S(1)}, u32[]{:S(2)}, u32[]{:S(2)}) collective-permute-start(f32[448,128]{1,0:T(8,128)S(1)} %add.43), channel_id=1, source_target_pairs={{0,1},{1,0},{2,3},{3,2},{4,5},{5,4},{6,7},{7,6},{8,9},{9,8},{10,11... | collective-permute-start | bytes 688136 | tf_op jit(solution)/shard_map/ppermute | solution.py:193
  141.9 15.3 %collective-permute-start.13 = (f32[256,256]{1,0:T(8,128)S(1)}, f32[256,256]{1,0:T(8,128)S(1)}, u32[]{:S(2)}, u32[]{:S(2)}) collective-permute-start(f32[256,256]{1,0:T(8,128)S(1)} %maximum_select_fusion.1), channel_id=1, source_target_pairs={{0,4},{4,8},{8,12},{12,16},{16,20},{20,24},{24,28},{28,32},{32,36}... | collective-permute-start | bytes 786440 | tf_op jit(solution)/shard_map/ppermute | solution.py:34
  143.9 10.0 %collective-permute-start.17 = (f32[128,128]{1,0:T(8,128)S(1)}, f32[128,128]{1,0:T(8,128)S(1)}, u32[]{:S(2)}, u32[]{:S(2)}) collective-permute-start(f32[128,128]{1,0:T(8,128)S(1)} %slice.152), channel_id=1, source_target_pairs={{4,0},{8,4},{12,8},{16,12},{20,16},{24,20},{28,24},{32,28},{36,32}... | collective-permute-start | bytes 196616 | tf_op jit(solution)/shard_map/ppermute | solution.py:34

commit v6 on v5

--- a/solution.py
+++ b/solution.py
@@ -96,7 +96,7 @@
 
 
 def fir_kernel(left_ref, right_ref, prev_ref, cur_ref, next_ref, lo_ref, mid_ref, hi_ref, out_ref, *, first, last):
-    block = pl.program_id(0) + first
+    block = (pl.program_id(0) + first) % (last + 1)
     before = jnp.where(block == 0, left_ref[...], prev_ref[...])
     after = jnp.where(block == last, right_ref[...], next_ref[...])
     out_ref[...] = (
@@ -112,9 +112,11 @@
     edge = 128
     step = width // edge
     first = start // width
+    blocks = samples // width
     lo, mid, hi = band[:edge], band[edge : edge + width], band[edge + width :]
-    kernel = lambda *refs: fir_kernel(*refs, first=first, last=samples // width - 1)
+    kernel = lambda *refs: fir_kernel(*refs, first=first, last=blocks - 1)
     full = lambda b: (0, 0)
+    at = lambda b: (b + first) % blocks
     return pl.pallas_call(
         kernel,
         grid=(length // width,),
@@ -122,11 +124,9 @@
         in_specs=[
             pl.BlockSpec((chans, edge), full),
             pl.BlockSpec((chans, edge), full),
-            pl.BlockSpec((chans, edge), lambda b: (0, jnp.maximum((b + first) * step - 1, 0))),
-            pl.BlockSpec((chans, width), lambda b: (0, b + first)),
-            pl.BlockSpec(
-                (chans, edge), lambda b: (0, jnp.minimum((b + first + 1) * step, samples // edge - 1))
-            ),
+            pl.BlockSpec((chans, edge), lambda b: (0, jnp.maximum(at(b) * step - 1, 0))),
+            pl.BlockSpec((chans, width), lambda b: (0, at(b))),
+            pl.BlockSpec((chans, edge), lambda b: (0, jnp.minimum((at(b) + 1) * step, samples // edge - 1))),
             pl.BlockSpec((edge, width), full),
             pl.BlockSpec((width, width), full),
             pl.BlockSpec((edge, width), full),
@@ -172,7 +172,7 @@
             pl.BlockSpec(rounded.shape, lambda b: (0, 0, 0)),
             pl.BlockSpec(middle.shape, lambda b: (0, 0, 0)),
         ] + ([] if into is None else [pl.BlockSpec(memory_space=pl.ANY)]),
-        out_specs=pl.BlockSpec((chans, width), lambda b: (0, b + first)),
+        out_specs=pl.BlockSpec((chans, width), lambda b: (0, (b + first) % (total // width))),
         input_output_aliases={} if into is None else {5: 0},
     )(lower, own, upper, rounded, middle, *([] if into is None else [into]))
 
@@ -215,7 +215,9 @@
     gaugeds, lowers, uppers = [], [], []
     own = cross_left = cross_right = None
     for number in range(chunks):
-        filtered = fir(source, left, right, band, number * piece, piece)
+        start = number * piece + width
+        edges = (left, right) if number == chunks - 1 else (source[:, :STRIDE], source[:, :STRIDE])
+        filtered = fir(source, *edges, band, start, piece)
         extended = with_halo(filtered, (("ch", 0),), GAUGE)
         gauged = (extended[2 * GAUGE :] - extended[: -2 * GAUGE]).astype(jnp.bfloat16)
         lower_part = shifted(gauged[chans - 2 * STRIDE :], "ch", 1)
@@ -262,7 +264,7 @@
     cleaned = None
     for number in range(chunks):
         cleaned = clean(
-            lowers[number], gaugeds[number], uppers[number], rounded, samples, number * piece, cleaned
+            lowers[number], gaugeds[number], uppers[number], rounded, samples, number * piece + width, cleaned
         )
     return cleaned
 

time: 190 us -> 192 us (1.011)
  waiting for transfers between devices: 67.6 us -> 58.8 us
  starting transfers between devices: 56.6 us -> 64 us
    ppermute x2, starting transfers between devices: 8.33 us -> 14.2 us  [with_halo(): lax.ppermute(lax.slice_in_dim(block, 0, width, axis=dim), axis, backward)]
    ppermute x6, waiting for transfers between devices: 8.95 us -> 4.06 us  [shifted(): lax.ppermute(value, axis, [(source, source + steps) for source in range(f...]
    ppermute x2, waiting for transfers between devices: 10.7 us -> 5.82 us  [with_halo(): lax.ppermute(lax.slice_in_dim(block, block.shape[dim] - width, None, axis...]
    ppermute x2, starting transfers between devices: 7.71 us -> 9.83 us  [ta_sum(): part = part + lax.ppermute(part, 'ta', across)]
  transfers between devices with their start and end apart: 18 -> 18, of which waited for: 9 -> 8; matrix products, arithmetic and copies ran while one was open for 5% -> 4% of each run, Pallas kernels for 0% -> 0%
where the time goes in v6:
time: 192 us; the launch traced here: 189 us
  starting transfers between devices  64 us (33%)
  waiting for transfers between devices  58.8 us (31%)
  Pallas kernels  41 us (21%)
  local copies, waits for them, and re-layouts  13.8 us (7%)
  other arithmetic  7.76 us (4%)
  matrix products  3.49 us (2%)
    ppermute x2, waiting for transfers between devices, ta_sum(): part = part + lax.ppermute(part, 'ta', across)  46.1 us
    ppermute x6, starting transfers between devices, shifted(): lax.ppermute(value, axis, [(source, source + steps) for source in range(f...  23.6 us
    pallas_call x1, Pallas kernels, subspace(): pl.pallas_call(subspace_kernel, out_shape=jax.ShapeDtypeStruct((windows,)...  17.1 us
    ppermute x2, starting transfers between devices, with_halo(): lax.ppermute(lax.slice_in_dim(block, 0, width, axis=dim), axis, backward)  14.2 us
    pallas_call x2, Pallas kernels, fir(): pl.pallas_call(kernel, grid=(length // width,), out_shape=jax.ShapeDtypeS...  12.2 us
    pallas_call x2, Pallas kernels, clean(): pl.pallas_call(clean_kernel, grid=(samples // width,), out_shape=jax.Shap...  11.8 us
    ppermute x2, starting transfers between devices, ta_sum(): part = part + lax.ppermute(part, 'ta', across)  9.83 us
    ppermute x1, starting transfers between devices, per_device(): lax.ppermute(raw[:, samples - half:], 'ta', forward)  6.92 us
  transfers between devices with their start and end apart: 18, of which 8 were waited for; matrix products, arithmetic and copies ran while one was open for 4% of the time, Pallas kernels for 0%

profile of v6, /device:TPU:97, one launch (start us, length us, event | category | flops | bytes accessed | tf_op | source)
XLA Modules:
  0.0 189.4 jit_solution(4305623826726879144)
XLA Ops:
  0.0 0.7 concatenate.67
  0.7 1.3 tile.10
  2.8 0.7 pad_slice_fusion
  3.5 0.8 slice.142.refs_6_
  4.4 1.5 slice.110.refs_0_.refs_1_
  5.8 5.8 %shard_map.37 = f32[256,2560]{1,0:T(8,128)} custom-call(bf16[256,128]{1,0:T(8,128)(2,1)} %slice.110.refs_0_.refs_1_, bf16[256,128]{1,0:T(8,128)(2,1)} %slice.110.refs_0_.refs_1_, bf16[256,5120]{1,0:T(8,128)(2,1)} %refs_4_.2, bf16[256,5120]{1,0:T(8,128)(2,1)} %refs_4_.2, bf16[256,5120]{1,0:T(8,128)(2,1)} %refs_4_.2, ...), custom_call_target="tpu_custom_call" | custom-call | tf_op jit(solution)/shard_map/pallas_call | solution.py:120
  11.7 0.9 fusion.23
  12.6 6.4 %collective-permute-start = (f32[4,2560]{1,0:T(4,128)S(1)}, f32[4,2560]{1,0:T(4,128)S(1)}, u32[]{:S(2)}, u32[]{:S(2)}) collective-permute-start(f32[4,2560]{1,0:T(4,128)S(1)} %get-tuple-element.19), channel_id=1, source_target_pairs={{4,0},{8,4},{12,8},{16,12},{20,16},{24,20},{28,24},{32,28},{36,32}... | collective-permute-start | bytes 122888 | tf_op jit(solution)/shard_map/ppermute | solution.py:26
  19.0 1.9 %collective-permute-start.1 = (f32[4,2560]{1,0:T(4,128)S(1)}, f32[4,2560]{1,0:T(4,128)S(1)}, u32[]{:S(2)}, u32[]{:S(2)}) collective-permute-start(f32[4,2560]{1,0:T(4,128)S(1)} %get-tuple-element.20), channel_id=1, source_target_pairs={{0,4},{4,8},{8,12},{12,16},{16,20},{20,24},{24,28},{28,32},{32,36}... | collective-permute-start | bytes 122888 | tf_op jit(solution)/shard_map/ppermute | solution.py:23
  20.9 1.0 fusion.24
  21.9 2.9 %collective-permute-start.3 = (bf16[256,64]{1,0:T(8,128)(2,1)S(1)}, bf16[256,64]{1,0:T(8,128)(2,1)S(1)}, u32[]{:S(2)}, u32[]{:S(2)}) collective-permute-start(bf16[256,64]{1,0:T(8,128)(2,1)S(1)} %get-tuple-element.21), channel_id=1, source_target_pairs={{1,0},{2,1},{3,2},{5,4},{6,5},{7,6},{9,8},{10,9},{11,10},{13,12},{... | collective-permute-start | bytes 98312 | tf_op jit(solution)/shard_map/ppermute | solution.py:206
  24.8 6.9 %collective-permute-start.2 = (bf16[256,64]{1,0:T(8,128)(2,1)S(1)}, bf16[256,64]{1,0:T(8,128)(2,1)S(1)}, u32[]{:S(2)}, u32[]{:S(2)}) collective-permute-start(bf16[256,64]{1,0:T(8,128)(2,1)S(1)} %get-tuple-element.22), channel_id=1, source_target_pairs={{0,1},{1,2},{2,3},{4,5},{5,6},{6,7},{8,9},{9,10},{10,11},{12,13},{... | collective-permute-start | bytes 98312 | tf_op jit(solution)/shard_map/ppermute | solution.py:205
  31.7 0.6 concatenate.71.refs_1_
  32.3 0.7 collective-permute-done.2
  33.0 0.7 concatenate.70.refs_0_
  33.7 3.1 %fusion.3.own_ref = bf16[256,2560]{1,0:T(8,128)(2,1)S(1)} fusion(f32[256,2560]{1,0:T(8,128)} %shard_map.37, f32[4,2560]{1,0:T(4,128)S(1)} %collective-permute-done.1, f32[4,2560]{1,0:T(4,128)S(1)} %collective-permute-done), kind=kLoop, calls=%fused_computation.6 | loop fusion | flops 2621440 | bytes 4014080 | tf_op jit(solution)/shard_map/convert_element_type | solution.py:222
  36.8 6.3 %shard_map.38 = f32[256,2560]{1,0:T(8,128)} custom-call(bf16[256,128]{1,0:T(8,128)(2,1)} %concatenate.70.refs_0_, bf16[256,128]{1,0:T(8,128)(2,1)} %concatenate.71.refs_1_, bf16[256,5120]{1,0:T(8,128)(2,1)} %refs_4_.2, bf16[256,5120]{1,0:T(8,128)(2,1)} %refs_4_.2, bf16[256,5120]{1,0:T(8,128)(2,1)} %refs_4_.2, bf16[128,512]{1,0:T(8,128)(2,1)} %get-tuple-element.24.refs_5_, ...), custom_call_target="tpu_custom_call" | custom-call | tf_op jit(solution)/shard_map/pallas_call | solution.py:120
  43.2 0.9 fusion.22
  44.1 7.9 %collective-permute-start.4 = (f32[4,2560]{1,0:T(4,128)S(1)}, f32[4,2560]{1,0:T(4,128)S(1)}, u32[]{:S(2)}, u32[]{:S(2)}) collective-permute-start(f32[4,2560]{1,0:T(4,128)S(1)} %get-tuple-element.17), channel_id=1, source_target_pairs={{4,0},{8,4},{12,8},{16,12},{20,16},{24,20},{28,24},{32,28},{36,32}... | collective-permute-start | bytes 122888 | tf_op jit(solution)/shard_map/ppermute | solution.py:26
  52.0 1.9 %collective-permute-start.5 = (f32[4,2560]{1,0:T(4,128)S(1)}, f32[4,2560]{1,0:T(4,128)S(1)}, u32[]{:S(2)}, u32[]{:S(2)}) collective-permute-start(f32[4,2560]{1,0:T(4,128)S(1)} %get-tuple-element.18), channel_id=1, source_target_pairs={{0,4},{4,8},{8,12},{12,16},{16,20},{20,24},{24,28},{28,32},{32,36}... | collective-permute-start | bytes 122888 | tf_op jit(solution)/shard_map/ppermute | solution.py:23
  53.9 1.9 %collective-permute-start.9 = (bf16[256,2560]{1,0:T(8,128)(2,1)S(1)}, bf16[256,2560]{1,0:T(8,128)(2,1)S(1)}, u32[]{:S(2)}, u32[]{:S(2)}) collective-permute-start(bf16[256,2560]{1,0:T(8,128)(2,1)S(1)} %fusion.3.own_ref), channel_id=1, source_target_pairs={{0,4},{4,8},{8,12},{12,16},{16,20},{20,24},{24,28},{28,32},{32,36}... | collective-permute-start | bytes 3932168 | tf_op jit(solution)/shard_map/ppermute | solution.py:34
  55.9 5.8 %collective-permute-done.5 = f32[4,2560]{1,0:T(4,128)S(1)} collective-permute-done((f32[4,2560]{1,0:T(4,128)S(1)}, f32[4,2560]{1,0:T(4,128)S(1)}, u32[]{:S(2)}, u32[]{:S(2)}) %collective-permute-start.5) | collective-permute-done | bytes 40992 | tf_op jit(solution)/shard_map/ppermute | solution.py:23
  61.7 3.1 %fusion.1.own_ref = bf16[256,2560]{1,0:T(8,128)(2,1)S(1)} fusion(f32[256,2560]{1,0:T(8,128)} %shard_map.38, f32[4,2560]{1,0:T(4,128)S(1)} %collective-permute-done.5, f32[4,2560]{1,0:T(4,128)S(1)} %collective-permute-done.4), kind=kLoop, calls=%fused_computation.2 | loop fusion | flops 2621440 | bytes 4014080 | tf_op jit(solution)/shard_map/convert_element_type | solution.py:222
  64.8 1.9 %collective-permute-start.10 = (bf16[256,2560]{1,0:T(8,128)(2,1)S(1)}, bf16[256,2560]{1,0:T(8,128)(2,1)S(1)}, u32[]{:S(2)}, u32[]{:S(2)}) collective-permute-start(bf16[256,2560]{1,0:T(8,128)(2,1)S(1)} %fusion.1.own_ref), channel_id=1, source_target_pairs={{0,4},{4,8},{8,12},{12,16},{16,20},{20,24},{24,28},{28,32},{32,36}... | collective-permute-start | bytes 3932168 | tf_op jit(solution)/shard_map/ppermute | solution.py:34
  66.7 0.5 fusion.27
  68.0 7.6 %collective-permute-start.11 = (bf16[128,2560]{1,0:T(8,128)(2,1)S(1)}, bf16[128,2560]{1,0:T(8,128)(2,1)S(1)}, u32[]{:S(2)}, u32[]{:S(2)}) collective-permute-start(bf16[128,2560]{1,0:T(8,128)(2,1)S(1)} %slice.149), channel_id=1, source_target_pairs={{4,0},{8,4},{12,8},{16,12},{20,16},{24,20},{28,24},{32,28},{36,32}... | collective-permute-start | bytes 1966088 | tf_op jit(solution)/shard_map/ppermute | solution.py:34
  75.6 1.9 %collective-permute-start.12 = (bf16[128,2560]{1,0:T(8,128)(2,1)S(1)}, bf16[128,2560]{1,0:T(8,128)(2,1)S(1)}, u32[]{:S(2)}, u32[]{:S(2)}) collective-permute-start(bf16[128,2560]{1,0:T(8,128)(2,1)S(1)} %slice.150), channel_id=1, source_target_pairs={{4,0},{8,4},{12,8},{16,12},{20,16},{24,20},{28,24},{32,28},{36,32}... | collective-permute-start | bytes 1966088 | tf_op jit(solution)/shard_map/ppermute | solution.py:34
  77.6 7.9 %collective-permute-start.7 = (f32[128,256]{1,0:T(8,128)S(1)}, f32[128,256]{1,0:T(8,128)S(1)}, u32[]{:S(2)}, u32[]{:S(2)}) collective-permute-start(f32[128,256]{1,0:T(8,128)S(1)} %select_add_fusion.1), channel_id=1, source_target_pairs={{0,2},{1,3},{2,0},{3,1},{4,6},{5,7},{6,4},{7,5},{8,10},{9,11},{10,... | collective-permute-start | bytes 393224 | tf_op jit(solution)/shard_map/ppermute | solution.py:192
  85.5 32.3 %collective-permute-done.7 = f32[128,256]{1,0:T(8,128)S(1)} collective-permute-done((f32[128,256]{1,0:T(8,128)S(1)}, f32[128,256]{1,0:T(8,128)S(1)}, u32[]{:S(2)}, u32[]{:S(2)}) %collective-permute-start.7) | collective-permute-done | bytes 131104 | tf_op jit(solution)/shard_map/ppermute | solution.py:192
  117.8 1.0 collective-permute-start.8
  118.8 1.0 collective-permute-done.8
  120.4 1.0 copy-done.3
  122.5 0.7 fusion.8
  123.6 0.7 fusion.16
  124.8 1.1 collective-permute-done.14
  125.9 2.0 %collective-permute-start.15 = (f32[448,128]{1,0:T(8,128)S(1)}, f32[448,128]{1,0:T(8,128)S(1)}, u32[]{:S(2)}, u32[]{:S(2)}) collective-permute-start(f32[448,128]{1,0:T(8,128)S(1)} %select_add_fusion), channel_id=1, source_target_pairs={{0,2},{1,3},{2,0},{3,1},{4,6},{5,7},{6,4},{7,5},{8,10},{9,11},{10,... | collective-permute-start | bytes 688136 | tf_op jit(solution)/shard_map/ppermute | solution.py:192
  127.9 13.8 %collective-permute-done.15 = f32[448,128]{1,0:T(8,128)S(1)} collective-permute-done((f32[448,128]{1,0:T(8,128)S(1)}, f32[448,128]{1,0:T(8,128)S(1)}, u32[]{:S(2)}, u32[]{:S(2)}) %collective-permute-start.15) | collective-permute-done | bytes 229408 | tf_op jit(solution)/shard_map/ppermute | solution.py:192
  141.7 1.3 collective-permute-start.16
  143.0 1.9 %collective-permute-start.13 = (f32[256,256]{1,0:T(8,128)S(1)}, f32[256,256]{1,0:T(8,128)S(1)}, u32[]{:S(2)}, u32[]{:S(2)}) collective-permute-start(f32[256,256]{1,0:T(8,128)S(1)} %maximum_select_fusion.1), channel_id=1, source_target_pairs={{0,4},{4,8},{8,12},{12,16},{16,20},{20,24},{24,28},{28,32},{32,36}... | collective-permute-start | bytes 786440 | tf_op jit(solution)/shard_map/ppermute | solution.py:34
  144.9 8.3 %collective-permute-start.17 = (f32[128,128]{1,0:T(8,128)S(1)}, f32[128,128]{1,0:T(8,128)S(1)}, u32[]{:S(2)}, u32[]{:S(2)}) collective-permute-start(f32[128,128]{1,0:T(8,128)S(1)} %slice.157), channel_id=1, source_target_pairs={{4,0},{8,4},{12,8},{16,12},{20,16},{24,20},{28,24},{32,28},{36,32}... | collective-permute-start | bytes 196616 | tf_op jit(solution)/shard_map/ppermute | solution.py:34
  153.7 0.7 collective-permute-done.17
  154.4 3.4 %collective-permute-done.13 = f32[256,256]{1,0:T(8,128)S(1)} collective-permute-done((f32[256,256]{1,0:T(8,128)S(1)}, f32[256,256]{1,0:T(8,128)S(1)}, u32[]{:S(2)}, u32[]{:S(2)}) %collective-permute-start.13) | collective-permute-done | bytes 262176 | tf_op jit(solution)/shard_map/ppermute | solution.py:34
  157.8 1.3 fusion.14.band_ref
  159.1 17.1 %shard_map.39.basis_ref = bf16[2,16,512]{2,1,0:T(8,128)(2,1)} custom-call(f32[640,640]{1,0:T(8,128)} %fusion.14.band_ref, f32[16,512]{1,0:T(8,128)} %bitcast.23), custom_call_target="tpu_custom_call" | custom-call | tf_op jit(solution)/shard_map/pallas_call | solution.py:87
  176.2 0.7 slice.158
  176.9 0.7 copy.13
  177.6 5.9 %shard_map.40.rest_0_ = bf16[256,5120]{1,0:T(8,128)(2,1)} custom-call(bf16[256,2560]{1,0:T(8,128)(2,1)} %copy-done.2, bf16[256,2560]{1,0:T(8,128)(2,1)} %copy-done, bf16[128,2560]{1,0:T(8,128)(2,1)} %copy-done.5, bf16[2,16,512]{2,1,0:T(8,128)(2,1)} %shard_map.39.basis_ref, bf16[2,128,16]{2,1,0:T(8,128)(2,1)} %bitcast.21), custom_call_target="tpu_custom_call" | custom-call | tf_op jit(solution)/shard_map/pallas_call | solution.py:164
  183.5 5.9 %shard_map.41 = bf16[256,5120]{1,0:T(8,128)(2,1)} custom-call(bf16[256,2560]{1,0:T(8,128)(2,1)} %copy-done.3, bf16[256,2560]{1,0:T(8,128)(2,1)} %copy-done.1, bf16[128,2560]{1,0:T(8,128)(2,1)} %copy-done.4, bf16[2,16,512]{2,1,0:T(8,128)(2,1)} %shard_map.39.basis_ref, bf16[2,128,16]{2,1,0:T(8,128)(2,1)} %bitcast.22, ...), custom_call_target="tpu_custom_call", output_to_operand_aliasing={{}: (5, {})} | custom-call | tf_op jit(solution)/shard_map/pallas_call | solution.py:164
  (53 shorter events, 4.6 us)
Async XLA Ops:
  12.6 21.1 %collective-permute-start = (f32[4,2560]{1,0:T(4,128)S(1)}, f32[4,2560]{1,0:T(4,128)S(1)}, u32[]{:S(2)}, u32[]{:S(2)}) collective-permute-start(f32[4,2560]{1,0:T(4,128)S(1)} %get-tuple-element.19), channel_id=1, source_target_pairs={{4,0},{8,4},{12,8},{16,12},{20,16},{24,20},{28,24},{32,28},{36,32}... | collective-permute-start | bytes 122888 | tf_op jit(solution)/shard_map/ppermute | solution.py:26
  19.0 14.7 %collective-permute-start.1 = (f32[4,2560]{1,0:T(4,128)S(1)}, f32[4,2560]{1,0:T(4,128)S(1)}, u32[]{:S(2)}, u32[]{:S(2)}) collective-permute-start(f32[4,2560]{1,0:T(4,128)S(1)} %get-tuple-element.20), channel_id=1, source_target_pairs={{0,4},{4,8},{8,12},{12,16},{16,20},{20,24},{24,28},{28,32},{32,36}... | collective-permute-start | bytes 122888 | tf_op jit(solution)/shard_map/ppermute | solution.py:23
  21.9 9.8 %collective-permute-start.3 = (bf16[256,64]{1,0:T(8,128)(2,1)S(1)}, bf16[256,64]{1,0:T(8,128)(2,1)S(1)}, u32[]{:S(2)}, u32[]{:S(2)}) collective-permute-start(bf16[256,64]{1,0:T(8,128)(2,1)S(1)} %get-tuple-element.21), channel_id=1, source_target_pairs={{1,0},{2,1},{3,2},{5,4},{6,5},{7,6},{9,8},{10,9},{11,10},{13,12},{... | collective-permute-start | bytes 98312 | tf_op jit(solution)/shard_map/ppermute | solution.py:206
  24.8 8.2 %collective-permute-start.2 = (bf16[256,64]{1,0:T(8,128)(2,1)S(1)}, bf16[256,64]{1,0:T(8,128)(2,1)S(1)}, u32[]{:S(2)}, u32[]{:S(2)}) collective-permute-start(bf16[256,64]{1,0:T(8,128)(2,1)S(1)} %get-tuple-element.22), channel_id=1, source_target_pairs={{0,1},{1,2},{2,3},{4,5},{5,6},{6,7},{8,9},{9,10},{10,11},{12,13},{... | collective-permute-start | bytes 98312 | tf_op jit(solution)/shard_map/ppermute | solution.py:205
  36.8 86.3 %copy-start = (bf16[256,2560]{1,0:T(8,128)(2,1)}, bf16[256,2560]{1,0:T(8,128)(2,1)S(1)}, u32[]{:S(2)}) copy-start(bf16[256,2560]{1,0:T(8,128)(2,1)S(1)} %fusion.3.own_ref) | copy-start | bytes 3932164
  44.1 11.7 %collective-permute-start.4 = (f32[4,2560]{1,0:T(4,128)S(1)}, f32[4,2560]{1,0:T(4,128)S(1)}, u32[]{:S(2)}, u32[]{:S(2)}) collective-permute-start(f32[4,2560]{1,0:T(4,128)S(1)} %get-tuple-element.17), channel_id=1, source_target_pairs={{4,0},{8,4},{12,8},{16,12},{20,16},{24,20},{28,24},{32,28},{36,32}... | collective-permute-start | bytes 122888 | tf_op jit(solution)/shard_map/ppermute | solution.py:26
  52.0 9.7 %collective-permute-start.5 = (f32[4,2560]{1,0:T(4,128)S(1)}, f32[4,2560]{1,0:T(4,128)S(1)}, u32[]{:S(2)}, u32[]{:S(2)}) collective-permute-start(f32[4,2560]{1,0:T(4,128)S(1)} %get-tuple-element.18), channel_id=1, source_target_pairs={{0,4},{4,8},{8,12},{12,16},{16,20},{20,24},{24,28},{28,32},{32,36}... | collective-permute-start | bytes 122888 | tf_op jit(solution)/shard_map/ppermute | solution.py:23
  53.9 65.9 %collective-permute-start.9 = (bf16[256,2560]{1,0:T(8,128)(2,1)S(1)}, bf16[256,2560]{1,0:T(8,128)(2,1)S(1)}, u32[]{:S(2)}, u32[]{:S(2)}) collective-permute-start(bf16[256,2560]{1,0:T(8,128)(2,1)S(1)} %fusion.3.own_ref), channel_id=1, source_target_pairs={{0,4},{4,8},{8,12},{12,16},{16,20},{20,24},{24,28},{28,32},{32,36}... | collective-permute-start | bytes 3932168 | tf_op jit(solution)/shard_map/ppermute | solution.py:34
  64.8 57.2 %copy-start.1 = (bf16[256,2560]{1,0:T(8,128)(2,1)}, bf16[256,2560]{1,0:T(8,128)(2,1)S(1)}, u32[]{:S(2)}) copy-start(bf16[256,2560]{1,0:T(8,128)(2,1)S(1)} %fusion.1.own_ref) | copy-start | bytes 3932164
  64.8 55.1 %collective-permute-start.10 = (bf16[256,2560]{1,0:T(8,128)(2,1)S(1)}, bf16[256,2560]{1,0:T(8,128)(2,1)S(1)}, u32[]{:S(2)}, u32[]{:S(2)}) collective-permute-start(bf16[256,2560]{1,0:T(8,128)(2,1)S(1)} %fusion.1.own_ref), channel_id=1, source_target_pairs={{0,4},{4,8},{8,12},{12,16},{16,20},{20,24},{24,28},{28,32},{32,36}... | collective-permute-start | bytes 3932168 | tf_op jit(solution)/shard_map/ppermute | solution.py:34
  67.8 9.7 %collective-permute-start.6 = (f32[128,256]{1,0:T(8,128)S(1)}, f32[128,256]{1,0:T(8,128)S(1)}, u32[]{:S(2)}, u32[]{:S(2)}) collective-permute-start(f32[128,256]{1,0:T(8,128)S(1)} %slice_select_fusion), channel_id=1, source_target_pairs={{0,1},{1,0},{2,3},{3,2},{4,5},{5,4},{6,7},{7,6},{8,9},{9,8},{10,11... | collective-permute-start | bytes 393224 | tf_op jit(solution)/shard_map/ppermute | solution.py:191
  68.0 51.8 %collective-permute-start.11 = (bf16[128,2560]{1,0:T(8,128)(2,1)S(1)}, bf16[128,2560]{1,0:T(8,128)(2,1)S(1)}, u32[]{:S(2)}, u32[]{:S(2)}) collective-permute-start(bf16[128,2560]{1,0:T(8,128)(2,1)S(1)} %slice.149), channel_id=1, source_target_pairs={{4,0},{8,4},{12,8},{16,12},{20,16},{24,20},{28,24},{32,28},{36,32}... | collective-permute-start | bytes 1966088 | tf_op jit(solution)/shard_map/ppermute | solution.py:34
  75.6 44.2 %collective-permute-start.12 = (bf16[128,2560]{1,0:T(8,128)(2,1)S(1)}, bf16[128,2560]{1,0:T(8,128)(2,1)S(1)}, u32[]{:S(2)}, u32[]{:S(2)}) collective-permute-start(bf16[128,2560]{1,0:T(8,128)(2,1)S(1)} %slice.150), channel_id=1, source_target_pairs={{4,0},{8,4},{12,8},{16,12},{20,16},{24,20},{28,24},{32,28},{36,32}... | collective-permute-start | bytes 1966088 | tf_op jit(solution)/shard_map/ppermute | solution.py:34
  77.6 40.2 %collective-permute-start.7 = (f32[128,256]{1,0:T(8,128)S(1)}, f32[128,256]{1,0:T(8,128)S(1)}, u32[]{:S(2)}, u32[]{:S(2)}) collective-permute-start(f32[128,256]{1,0:T(8,128)S(1)} %select_add_fusion.1), channel_id=1, source_target_pairs={{0,2},{1,3},{2,0},{3,1},{4,6},{5,7},{6,4},{7,5},{8,10},{9,11},{10,... | collective-permute-start | bytes 393224 | tf_op jit(solution)/shard_map/ppermute | solution.py:192
  117.8 2.0 %collective-permute-start.8 = (f32[128,256]{1,0:T(8,128)S(1)}, f32[128,256]{1,0:T(8,128)S(1)}, u32[]{:S(2)}, u32[]{:S(2)}) collective-permute-start(f32[128,256]{1,0:T(8,128)S(1)} %add.39), channel_id=1, source_target_pairs={{0,1},{1,0},{2,3},{3,2},{4,5},{5,4},{6,7},{7,6},{8,9},{9,8},{10,11... | collective-permute-start | bytes 393224 | tf_op jit(solution)/shard_map/ppermute | solution.py:193
  119.8 3.4 %copy-start.5 = (bf16[128,2560]{1,0:T(8,128)(2,1)}, bf16[128,2560]{1,0:T(8,128)(2,1)S(1)}, u32[]{:S(2)}) copy-start(bf16[128,2560]{1,0:T(8,128)(2,1)S(1)} %collective-permute-done.11.upper_ref) | copy-start | bytes 1966084
  119.8 2.2 %copy-start.4 = (bf16[128,2560]{1,0:T(8,128)(2,1)}, bf16[128,2560]{1,0:T(8,128)(2,1)S(1)}, u32[]{:S(2)}) copy-start(bf16[128,2560]{1,0:T(8,128)(2,1)S(1)} %collective-permute-done.12.upper_ref) | copy-start | bytes 1966084
  119.8 1.6 copy-start.2
  119.9 1.5 copy-start.3
  121.4 1.1 slice-start.1
  122.5 1.1 slice-start
  124.3 1.6 collective-permute-start.14
  125.9 15.7 %collective-permute-start.15 = (f32[448,128]{1,0:T(8,128)S(1)}, f32[448,128]{1,0:T(8,128)S(1)}, u32[]{:S(2)}, u32[]{:S(2)}) collective-permute-start(f32[448,128]{1,0:T(8,128)S(1)} %select_add_fusion), channel_id=1, source_target_pairs={{0,2},{1,3},{2,0},{3,1},{4,6},{5,7},{6,4},{7,5},{8,10},{9,11},{10,... | collective-permute-start | bytes 688136 | tf_op jit(solution)/shard_map/ppermute | solution.py:192
  141.7 11.5 %collective-permute-start.16 = (f32[448,128]{1,0:T(8,128)S(1)}, f32[448,128]{1,0:T(8,128)S(1)}, u32[]{:S(2)}, u32[]{:S(2)}) collective-permute-start(f32[448,128]{1,0:T(8,128)S(1)} %add.43), channel_id=1, source_target_pairs={{0,1},{1,0},{2,3},{3,2},{4,5},{5,4},{6,7},{7,6},{8,9},{9,8},{10,11... | collective-permute-start | bytes 688136 | tf_op jit(solution)/shard_map/ppermute | solution.py:193
  143.0 14.8 %collective-permute-start.13 = (f32[256,256]{1,0:T(8,128)S(1)}, f32[256,256]{1,0:T(8,128)S(1)}, u32[]{:S(2)}, u32[]{:S(2)}) collective-permute-start(f32[256,256]{1,0:T(8,128)S(1)} %maximum_select_fusion.1), channel_id=1, source_target_pairs={{0,4},{4,8},{8,12},{12,16},{16,20},{20,24},{24,28},{28,32},{32,36}... | collective-permute-start | bytes 786440 | tf_op jit(solution)/shard_map/ppermute | solution.py:34
  144.9 9.5 %collective-permute-start.17 = (f32[128,128]{1,0:T(8,128)S(1)}, f32[128,128]{1,0:T(8,128)S(1)}, u32[]{:S(2)}, u32[]{:S(2)}) collective-permute-start(f32[128,128]{1,0:T(8,128)S(1)} %slice.157), channel_id=1, source_target_pairs={{4,0},{8,4},{12,8},{16,12},{20,16},{24,20},{28,24},{32,28},{36,32}... | collective-permute-start | bytes 196616 | tf_op jit(solution)/shard_map/ppermute | solution.py:34

commit v7 on v6

--- a/solution.py
+++ b/solution.py
@@ -206,7 +206,6 @@
     right = jnp.concatenate([lax.ppermute(raw[:, :half], "ta", backward), blank], axis=1)
     width = math.gcd(samples, 512)
     band = jnp.pad(toeplitz_band(fir_taps, width), ((half, half), (0, 0)))
-    source = raw
     chunks = 2 if samples % 1024 == 0 else 1
     piece = samples // chunks
     tiles = chans // STRIDE
@@ -214,18 +213,20 @@
     total_time = samples * lax.axis_size("ta")
     gaugeds, lowers, uppers = [], [], []
     own = cross_left = cross_right = None
+    filters = []
     for number in range(chunks):
         start = number * piece + width
-        edges = (left, right) if number == chunks - 1 else (source[:, :STRIDE], source[:, :STRIDE])
-        filtered = fir(source, *edges, band, start, piece)
-        extended = with_halo(filtered, (("ch", 0),), GAUGE)
+        edges = (left, right) if number == chunks - 1 else (raw[:, :STRIDE], raw[:, :STRIDE])
+        filters.append(fir(raw, *edges, band, start, piece))
+    filters = lax.optimization_barrier(filters)
+    for number in range(chunks):
+        extended = with_halo(filters[number], (("ch", 0),), GAUGE)
         gauged = (extended[2 * GAUGE :] - extended[: -2 * GAUGE]).astype(jnp.bfloat16)
         lower_part = shifted(gauged[chans - 2 * STRIDE :], "ch", 1)
         upper_part = shifted(gauged[:STRIDE], "ch", -1)
         local = gram(gauged, gauged)
         own = local if own is None else own + local
         gaugeds.append(gauged)
-        source, gauged = lax.optimization_barrier((source, gauged))
         lowers.append(lower_part)
         uppers.append(upper_part)
 

time: 192 us -> 188 us (0.979)
  waiting for transfers between devices: 58.8 us -> 66.2 us
  starting transfers between devices: 64 us -> 58 us
  other arithmetic: 7.76 us -> 4.98 us
    ppermute x6, waiting for transfers between devices: 4.06 us -> 17.6 us  [shifted(): lax.ppermute(value, axis, [(source, source + steps) for source in range(f...]
    ppermute x2, starting transfers between devices: 9.83 us -> 4.63 us  [ta_sum(): part = part + lax.ppermute(part, 'ta', across)]
    ppermute x2, waiting for transfers between devices: 5.82 us -> 1.95 us  [with_halo(): lax.ppermute(lax.slice_in_dim(block, block.shape[dim] - width, None, axis...]
    convert_element_type x2, other arithmetic: 6.23 us -> 3.45 us  [per_device(): gauged = (extended[2 * GAUGE:] - extended[:-2 * GAUGE]).astype(jnp.bfloat16)]
  transfers between devices with their start and end apart: 18 -> 18, of which waited for: 8 -> 8; matrix products, arithmetic and copies ran while one was open for 4% -> 7% of each run, Pallas kernels for 0% -> 3%
where the time goes in v7:
time: 188 us; the launch traced here: 187 us
  waiting for transfers between devices  66.2 us (35%)
  starting transfers between devices  58 us (31%)
  Pallas kernels  40.6 us (22%)
  local copies, waits for them, and re-layouts  13.3 us (7%)
  other arithmetic  4.98 us (3%)
  matrix products  3.46 us (2%)
    ppermute x2, waiting for transfers between devices, ta_sum(): part = part + lax.ppermute(part, 'ta', across)  44.3 us
    ppermute x6, starting transfers between devices, shifted(): lax.ppermute(value, axis, [(source, source + steps) for source in range(f...  23.6 us
    ppermute x6, waiting for transfers between devices, shifted(): lax.ppermute(value, axis, [(source, source + steps) for source in range(f...  17.6 us
    pallas_call x1, Pallas kernels, subspace(): pl.pallas_call(subspace_kernel, out_shape=jax.ShapeDtypeStruct((windows,)...  17.1 us
    ppermute x2, starting transfers between devices, with_halo(): lax.ppermute(lax.slice_in_dim(block, 0, width, axis=dim), axis, backward)  14 us
    pallas_call x2, Pallas kernels, clean(): pl.pallas_call(clean_kernel, grid=(samples // width,), out_shape=jax.Shap...  11.8 us
    pallas_call x2, Pallas kernels, fir(): pl.pallas_call(kernel, grid=(length // width,), out_shape=jax.ShapeDtypeS...  11.7 us
    ppermute x1, starting transfers between devices, per_device(): lax.ppermute(raw[:, samples - half:], 'ta', forward)  6.89 us
  transfers between devices with their start and end apart: 18, of which 8 were waited for; matrix products, arithmetic and copies ran while one was open for 7% of the time, Pallas kernels for 3%

profile of v7, /device:TPU:97, one launch (start us, length us, event | category | flops | bytes accessed | tf_op | source)
XLA Modules:
  0.0 187.2 jit_solution(12120364063318047130)
XLA Ops:
  0.0 1.0 fusion.24
  1.0 2.6 %collective-permute-start.1 = (bf16[256,64]{1,0:T(8,128)(2,1)S(1)}, bf16[256,64]{1,0:T(8,128)(2,1)S(1)}, u32[]{:S(2)}, u32[]{:S(2)}) collective-permute-start(bf16[256,64]{1,0:T(8,128)(2,1)S(1)} %get-tuple-element.23), channel_id=1, source_target_pairs={{1,0},{2,1},{3,2},{5,4},{6,5},{7,6},{9,8},{10,9},{11,10},{13,12},{... | collective-permute-start | bytes 98312 | tf_op jit(solution)/shard_map/ppermute | solution.py:206
  3.6 6.9 %collective-permute-start = (bf16[256,64]{1,0:T(8,128)(2,1)S(1)}, bf16[256,64]{1,0:T(8,128)(2,1)S(1)}, u32[]{:S(2)}, u32[]{:S(2)}) collective-permute-start(bf16[256,64]{1,0:T(8,128)(2,1)S(1)} %get-tuple-element.24), channel_id=1, source_target_pairs={{0,1},{1,2},{2,3},{4,5},{5,6},{6,7},{8,9},{9,10},{10,11},{12,13},{... | collective-permute-start | bytes 98312 | tf_op jit(solution)/shard_map/ppermute | solution.py:205
  10.4 0.7 concatenate.67
  11.2 1.3 tile.10
  13.2 0.7 pad_slice_fusion
  13.9 1.5 slice.110.refs_0_.refs_1_
  15.4 0.8 slice.142.refs_6_
  16.2 5.9 %shard_map.37 = f32[256,2560]{1,0:T(8,128)} custom-call(bf16[256,128]{1,0:T(8,128)(2,1)} %slice.110.refs_0_.refs_1_, bf16[256,128]{1,0:T(8,128)(2,1)} %slice.110.refs_0_.refs_1_, bf16[256,5120]{1,0:T(8,128)(2,1)} %refs_4_.3, bf16[256,5120]{1,0:T(8,128)(2,1)} %refs_4_.3, bf16[256,5120]{1,0:T(8,128)(2,1)} %refs_4_.3, ...), custom_call_target="tpu_custom_call" | custom-call | tf_op jit(solution)/shard_map/pallas_call | solution.py:120
  22.1 0.6 concatenate.69.refs_1_
  22.8 0.7 concatenate.68.refs_0_
  23.5 5.8 %shard_map.38 = f32[256,2560]{1,0:T(8,128)} custom-call(bf16[256,128]{1,0:T(8,128)(2,1)} %concatenate.68.refs_0_, bf16[256,128]{1,0:T(8,128)(2,1)} %concatenate.69.refs_1_, bf16[256,5120]{1,0:T(8,128)(2,1)} %refs_4_.3, bf16[256,5120]{1,0:T(8,128)(2,1)} %refs_4_.3, bf16[256,5120]{1,0:T(8,128)(2,1)} %refs_4_.3, bf16[128,512]{1,0:T(8,128)(2,1)} %get-tuple-element.26.refs_5_, ...), custom_call_target="tpu_custom_call" | custom-call | tf_op jit(solution)/shard_map/pallas_call | solution.py:120
  29.3 0.9 fusion.23
  30.3 6.4 %collective-permute-start.4 = (f32[4,2560]{1,0:T(4,128)S(1)}, f32[4,2560]{1,0:T(4,128)S(1)}, u32[]{:S(2)}, u32[]{:S(2)}) collective-permute-start(f32[4,2560]{1,0:T(4,128)S(1)} %get-tuple-element.21), channel_id=1, source_target_pairs={{4,0},{8,4},{12,8},{16,12},{20,16},{24,20},{28,24},{32,28},{36,32}... | collective-permute-start | bytes 122888 | tf_op jit(solution)/shard_map/ppermute | solution.py:26
  36.7 1.9 %collective-permute-start.5 = (f32[4,2560]{1,0:T(4,128)S(1)}, f32[4,2560]{1,0:T(4,128)S(1)}, u32[]{:S(2)}, u32[]{:S(2)}) collective-permute-start(f32[4,2560]{1,0:T(4,128)S(1)} %get-tuple-element.22), channel_id=1, source_target_pairs={{0,4},{4,8},{8,12},{12,16},{16,20},{20,24},{24,28},{28,32},{32,36}... | collective-permute-start | bytes 122888 | tf_op jit(solution)/shard_map/ppermute | solution.py:23
  38.6 0.9 fusion.22
  39.6 7.6 %collective-permute-start.2 = (f32[4,2560]{1,0:T(4,128)S(1)}, f32[4,2560]{1,0:T(4,128)S(1)}, u32[]{:S(2)}, u32[]{:S(2)}) collective-permute-start(f32[4,2560]{1,0:T(4,128)S(1)} %get-tuple-element.19), channel_id=1, source_target_pairs={{4,0},{8,4},{12,8},{16,12},{20,16},{24,20},{28,24},{32,28},{36,32}... | collective-permute-start | bytes 122888 | tf_op jit(solution)/shard_map/ppermute | solution.py:26
  47.1 2.2 %collective-permute-start.3 = (f32[4,2560]{1,0:T(4,128)S(1)}, f32[4,2560]{1,0:T(4,128)S(1)}, u32[]{:S(2)}, u32[]{:S(2)}) collective-permute-start(f32[4,2560]{1,0:T(4,128)S(1)} %get-tuple-element.20), channel_id=1, source_target_pairs={{0,4},{4,8},{8,12},{12,16},{16,20},{20,24},{24,28},{28,32},{32,36}... | collective-permute-start | bytes 122888 | tf_op jit(solution)/shard_map/ppermute | solution.py:23
  49.4 3.1 %fusion.1.own_ref = bf16[256,2560]{1,0:T(8,128)(2,1)S(1)} fusion(f32[256,2560]{1,0:T(8,128)} %shard_map.38, f32[4,2560]{1,0:T(4,128)S(1)} %collective-permute-done.5, f32[4,2560]{1,0:T(4,128)S(1)} %collective-permute-done.4), kind=kLoop, calls=%fused_computation.2 | loop fusion | flops 2621440 | bytes 4014080 | tf_op jit(solution)/shard_map/convert_element_type | solution.py:224
  52.5 1.9 %collective-permute-start.10 = (bf16[256,2560]{1,0:T(8,128)(2,1)S(1)}, bf16[256,2560]{1,0:T(8,128)(2,1)S(1)}, u32[]{:S(2)}, u32[]{:S(2)}) collective-permute-start(bf16[256,2560]{1,0:T(8,128)(2,1)S(1)} %fusion.1.own_ref), channel_id=1, source_target_pairs={{0,4},{4,8},{8,12},{12,16},{16,20},{20,24},{24,28},{28,32},{32,36}... | collective-permute-start | bytes 3932168 | tf_op jit(solution)/shard_map/ppermute | solution.py:34
  54.4 1.9 %collective-permute-done.3 = f32[4,2560]{1,0:T(4,128)S(1)} collective-permute-done((f32[4,2560]{1,0:T(4,128)S(1)}, f32[4,2560]{1,0:T(4,128)S(1)}, u32[]{:S(2)}, u32[]{:S(2)}) %collective-permute-start.3) | collective-permute-done | bytes 40992 | tf_op jit(solution)/shard_map/ppermute | solution.py:23
  56.7 1.9 %collective-permute-start.9 = (bf16[256,2560]{1,0:T(8,128)(2,1)S(1)}, bf16[256,2560]{1,0:T(8,128)(2,1)S(1)}, u32[]{:S(2)}, u32[]{:S(2)}) collective-permute-start(bf16[256,2560]{1,0:T(8,128)(2,1)S(1)} %fusion.3.own_ref), channel_id=1, source_target_pairs={{0,4},{4,8},{8,12},{12,16},{16,20},{20,24},{24,28},{28,32},{32,36}... | collective-permute-start | bytes 3932168 | tf_op jit(solution)/shard_map/ppermute | solution.py:34
  58.7 0.5 fusion.27
  59.2 0.5 convolution_add_fusion.1
  60.0 7.6 %collective-permute-start.11 = (bf16[128,2560]{1,0:T(8,128)(2,1)S(1)}, bf16[128,2560]{1,0:T(8,128)(2,1)S(1)}, u32[]{:S(2)}, u32[]{:S(2)}) collective-permute-start(bf16[128,2560]{1,0:T(8,128)(2,1)S(1)} %slice.145), channel_id=1, source_target_pairs={{4,0},{8,4},{12,8},{16,12},{20,16},{24,20},{28,24},{32,28},{36,32}... | collective-permute-start | bytes 1966088 | tf_op jit(solution)/shard_map/ppermute | solution.py:34
  67.6 1.9 %collective-permute-start.12 = (bf16[128,2560]{1,0:T(8,128)(2,1)S(1)}, bf16[128,2560]{1,0:T(8,128)(2,1)S(1)}, u32[]{:S(2)}, u32[]{:S(2)}) collective-permute-start(bf16[128,2560]{1,0:T(8,128)(2,1)S(1)} %slice.146), channel_id=1, source_target_pairs={{4,0},{8,4},{12,8},{16,12},{20,16},{24,20},{28,24},{32,28},{36,32}... | collective-permute-start | bytes 1966088 | tf_op jit(solution)/shard_map/ppermute | solution.py:34
  69.5 2.9 %collective-permute-start.7 = (f32[128,256]{1,0:T(8,128)S(1)}, f32[128,256]{1,0:T(8,128)S(1)}, u32[]{:S(2)}, u32[]{:S(2)}) collective-permute-start(f32[128,256]{1,0:T(8,128)S(1)} %select_add_fusion.1), channel_id=1, source_target_pairs={{0,2},{1,3},{2,0},{3,1},{4,6},{5,7},{6,4},{7,5},{8,10},{9,11},{10,... | collective-permute-start | bytes 393224 | tf_op jit(solution)/shard_map/ppermute | solution.py:192
  72.5 30.1 %collective-permute-done.7 = f32[128,256]{1,0:T(8,128)S(1)} collective-permute-done((f32[128,256]{1,0:T(8,128)S(1)}, f32[128,256]{1,0:T(8,128)S(1)}, u32[]{:S(2)}, u32[]{:S(2)}) %collective-permute-start.7) | collective-permute-done | bytes 131104 | tf_op jit(solution)/shard_map/ppermute | solution.py:192
  102.6 1.1 collective-permute-start.8
  103.6 1.0 collective-permute-done.8
  104.7 13.5 %collective-permute-done.9.lower_ref = bf16[256,2560]{1,0:T(8,128)(2,1)S(1)} collective-permute-done((bf16[256,2560]{1,0:T(8,128)(2,1)S(1)}, bf16[256,2560]{1,0:T(8,128)(2,1)S(1)}, u32[]{:S(2)}, u32[]{:S(2)}) %collective-permute-start.9) | collective-permute-done | bytes 1310752 | tf_op jit(solution)/shard_map/ppermute | solution.py:34
  118.8 0.6 copy-done.3
  120.4 0.7 fusion.8
  121.5 0.7 fusion.16
  122.3 1.5 collective-permute-done.14
  123.8 1.7 collective-permute-start.15
  125.5 14.2 %collective-permute-done.15 = f32[448,128]{1,0:T(8,128)S(1)} collective-permute-done((f32[448,128]{1,0:T(8,128)S(1)}, f32[448,128]{1,0:T(8,128)S(1)}, u32[]{:S(2)}, u32[]{:S(2)}) %collective-permute-start.15) | collective-permute-done | bytes 229408 | tf_op jit(solution)/shard_map/ppermute | solution.py:192
  139.7 1.0 collective-permute-start.16
  140.7 1.9 %collective-permute-start.13 = (f32[256,256]{1,0:T(8,128)S(1)}, f32[256,256]{1,0:T(8,128)S(1)}, u32[]{:S(2)}, u32[]{:S(2)}) collective-permute-start(f32[256,256]{1,0:T(8,128)S(1)} %maximum_select_fusion.1), channel_id=1, source_target_pairs={{0,4},{4,8},{8,12},{12,16},{16,20},{20,24},{24,28},{28,32},{32,36}... | collective-permute-start | bytes 786440 | tf_op jit(solution)/shard_map/ppermute | solution.py:34
  142.6 8.4 %collective-permute-start.17 = (f32[128,128]{1,0:T(8,128)S(1)}, f32[128,128]{1,0:T(8,128)S(1)}, u32[]{:S(2)}, u32[]{:S(2)}) collective-permute-start(f32[128,128]{1,0:T(8,128)S(1)} %slice.153), channel_id=1, source_target_pairs={{4,0},{8,4},{12,8},{16,12},{20,16},{24,20},{28,24},{32,28},{36,32}... | collective-permute-start | bytes 196616 | tf_op jit(solution)/shard_map/ppermute | solution.py:34
  151.5 0.7 collective-permute-done.17
  152.1 3.4 %collective-permute-done.13 = f32[256,256]{1,0:T(8,128)S(1)} collective-permute-done((f32[256,256]{1,0:T(8,128)S(1)}, f32[256,256]{1,0:T(8,128)S(1)}, u32[]{:S(2)}, u32[]{:S(2)}) %collective-permute-start.13) | collective-permute-done | bytes 262176 | tf_op jit(solution)/shard_map/ppermute | solution.py:34
  155.5 1.3 fusion.14.band_ref
  156.8 17.1 %shard_map.39.basis_ref = bf16[2,16,512]{2,1,0:T(8,128)(2,1)} custom-call(f32[640,640]{1,0:T(8,128)} %fusion.14.band_ref, f32[16,512]{1,0:T(8,128)} %bitcast.23), custom_call_target="tpu_custom_call" | custom-call | tf_op jit(solution)/shard_map/pallas_call | solution.py:87
  173.9 0.7 slice.154
  174.6 0.7 copy.13
  175.4 5.9 %shard_map.40.rest_0_ = bf16[256,5120]{1,0:T(8,128)(2,1)} custom-call(bf16[256,2560]{1,0:T(8,128)(2,1)} %copy-done.3, bf16[256,2560]{1,0:T(8,128)(2,1)} %copy-done, bf16[128,2560]{1,0:T(8,128)(2,1)} %copy-done.6, bf16[2,16,512]{2,1,0:T(8,128)(2,1)} %shard_map.39.basis_ref, bf16[2,128,16]{2,1,0:T(8,128)(2,1)} %bitcast.21), custom_call_target="tpu_custom_call" | custom-call | tf_op jit(solution)/shard_map/pallas_call | solution.py:164
  181.3 5.9 %shard_map.41 = bf16[256,5120]{1,0:T(8,128)(2,1)} custom-call(bf16[256,2560]{1,0:T(8,128)(2,1)} %copy-done.4, bf16[256,2560]{1,0:T(8,128)(2,1)} %copy-done.1, bf16[128,2560]{1,0:T(8,128)(2,1)} %copy-done.5, bf16[2,16,512]{2,1,0:T(8,128)(2,1)} %shard_map.39.basis_ref, bf16[2,128,16]{2,1,0:T(8,128)(2,1)} %bitcast.22, ...), custom_call_target="tpu_custom_call", output_to_operand_aliasing={{}: (5, {})} | custom-call | tf_op jit(solution)/shard_map/pallas_call | solution.py:164
  (55 shorter events, 4.1 us)
Async XLA Ops:
  1.0 21.2 %collective-permute-start.1 = (bf16[256,64]{1,0:T(8,128)(2,1)S(1)}, bf16[256,64]{1,0:T(8,128)(2,1)S(1)}, u32[]{:S(2)}, u32[]{:S(2)}) collective-permute-start(bf16[256,64]{1,0:T(8,128)(2,1)S(1)} %get-tuple-element.23), channel_id=1, source_target_pairs={{1,0},{2,1},{3,2},{5,4},{6,5},{7,6},{9,8},{10,9},{11,10},{13,12},{... | collective-permute-start | bytes 98312 | tf_op jit(solution)/shard_map/ppermute | solution.py:206
  3.6 19.2 %collective-permute-start = (bf16[256,64]{1,0:T(8,128)(2,1)S(1)}, bf16[256,64]{1,0:T(8,128)(2,1)S(1)}, u32[]{:S(2)}, u32[]{:S(2)}) collective-permute-start(bf16[256,64]{1,0:T(8,128)(2,1)S(1)} %get-tuple-element.24), channel_id=1, source_target_pairs={{0,1},{1,2},{2,3},{4,5},{5,6},{6,7},{8,9},{9,10},{10,11},{12,13},{... | collective-permute-start | bytes 98312 | tf_op jit(solution)/shard_map/ppermute | solution.py:205
  30.3 19.1 %collective-permute-start.4 = (f32[4,2560]{1,0:T(4,128)S(1)}, f32[4,2560]{1,0:T(4,128)S(1)}, u32[]{:S(2)}, u32[]{:S(2)}) collective-permute-start(f32[4,2560]{1,0:T(4,128)S(1)} %get-tuple-element.21), channel_id=1, source_target_pairs={{4,0},{8,4},{12,8},{16,12},{20,16},{24,20},{28,24},{32,28},{36,32}... | collective-permute-start | bytes 122888 | tf_op jit(solution)/shard_map/ppermute | solution.py:26
  36.7 12.7 %collective-permute-start.5 = (f32[4,2560]{1,0:T(4,128)S(1)}, f32[4,2560]{1,0:T(4,128)S(1)}, u32[]{:S(2)}, u32[]{:S(2)}) collective-permute-start(f32[4,2560]{1,0:T(4,128)S(1)} %get-tuple-element.22), channel_id=1, source_target_pairs={{0,4},{4,8},{8,12},{12,16},{16,20},{20,24},{24,28},{28,32},{32,36}... | collective-permute-start | bytes 122888 | tf_op jit(solution)/shard_map/ppermute | solution.py:23
  39.6 14.9 %collective-permute-start.2 = (f32[4,2560]{1,0:T(4,128)S(1)}, f32[4,2560]{1,0:T(4,128)S(1)}, u32[]{:S(2)}, u32[]{:S(2)}) collective-permute-start(f32[4,2560]{1,0:T(4,128)S(1)} %get-tuple-element.19), channel_id=1, source_target_pairs={{4,0},{8,4},{12,8},{16,12},{20,16},{24,20},{28,24},{32,28},{36,32}... | collective-permute-start | bytes 122888 | tf_op jit(solution)/shard_map/ppermute | solution.py:26
  47.1 9.2 %copy-start.2 = (f32[256,2560]{1,0:T(8,128)S(1)}, f32[256,2560]{1,0:T(8,128)}, u32[]{:S(2)}) copy-start(f32[256,2560]{1,0:T(8,128)} %shard_map.37) | copy-start | bytes 7864324
  47.1 9.2 %collective-permute-start.3 = (f32[4,2560]{1,0:T(4,128)S(1)}, f32[4,2560]{1,0:T(4,128)S(1)}, u32[]{:S(2)}, u32[]{:S(2)}) collective-permute-start(f32[4,2560]{1,0:T(4,128)S(1)} %get-tuple-element.20), channel_id=1, source_target_pairs={{0,4},{4,8},{8,12},{12,16},{16,20},{20,24},{24,28},{28,32},{32,36}... | collective-permute-start | bytes 122888 | tf_op jit(solution)/shard_map/ppermute | solution.py:23
  52.5 67.4 %copy-start.1 = (bf16[256,2560]{1,0:T(8,128)(2,1)}, bf16[256,2560]{1,0:T(8,128)(2,1)S(1)}, u32[]{:S(2)}) copy-start(bf16[256,2560]{1,0:T(8,128)(2,1)S(1)} %fusion.1.own_ref) | copy-start | bytes 3932164
  52.5 52.2 %collective-permute-start.10 = (bf16[256,2560]{1,0:T(8,128)(2,1)S(1)}, bf16[256,2560]{1,0:T(8,128)(2,1)S(1)}, u32[]{:S(2)}, u32[]{:S(2)}) collective-permute-start(bf16[256,2560]{1,0:T(8,128)(2,1)S(1)} %fusion.1.own_ref), channel_id=1, source_target_pairs={{0,4},{4,8},{8,12},{12,16},{16,20},{20,24},{24,28},{28,32},{32,36}... | collective-permute-start | bytes 3932168 | tf_op jit(solution)/shard_map/ppermute | solution.py:34
  56.7 64.4 %copy-start = (bf16[256,2560]{1,0:T(8,128)(2,1)}, bf16[256,2560]{1,0:T(8,128)(2,1)S(1)}, u32[]{:S(2)}) copy-start(bf16[256,2560]{1,0:T(8,128)(2,1)S(1)} %fusion.3.own_ref) | copy-start | bytes 3932164
  56.7 61.5 %collective-permute-start.9 = (bf16[256,2560]{1,0:T(8,128)(2,1)S(1)}, bf16[256,2560]{1,0:T(8,128)(2,1)S(1)}, u32[]{:S(2)}, u32[]{:S(2)}) collective-permute-start(bf16[256,2560]{1,0:T(8,128)(2,1)S(1)} %fusion.3.own_ref), channel_id=1, source_target_pairs={{0,4},{4,8},{8,12},{12,16},{16,20},{20,24},{24,28},{28,32},{32,36}... | collective-permute-start | bytes 3932168 | tf_op jit(solution)/shard_map/ppermute | solution.py:34
  59.8 9.7 %collective-permute-start.6 = (f32[128,256]{1,0:T(8,128)S(1)}, f32[128,256]{1,0:T(8,128)S(1)}, u32[]{:S(2)}, u32[]{:S(2)}) collective-permute-start(f32[128,256]{1,0:T(8,128)S(1)} %slice_select_fusion), channel_id=1, source_target_pairs={{0,1},{1,0},{2,3},{3,2},{4,5},{5,4},{6,7},{7,6},{8,9},{9,8},{10,11... | collective-permute-start | bytes 393224 | tf_op jit(solution)/shard_map/ppermute | solution.py:191
  60.0 44.7 %collective-permute-start.11 = (bf16[128,2560]{1,0:T(8,128)(2,1)S(1)}, bf16[128,2560]{1,0:T(8,128)(2,1)S(1)}, u32[]{:S(2)}, u32[]{:S(2)}) collective-permute-start(bf16[128,2560]{1,0:T(8,128)(2,1)S(1)} %slice.145), channel_id=1, source_target_pairs={{4,0},{8,4},{12,8},{16,12},{20,16},{24,20},{28,24},{32,28},{36,32}... | collective-permute-start | bytes 1966088 | tf_op jit(solution)/shard_map/ppermute | solution.py:34
  67.6 37.1 %collective-permute-start.12 = (bf16[128,2560]{1,0:T(8,128)(2,1)S(1)}, bf16[128,2560]{1,0:T(8,128)(2,1)S(1)}, u32[]{:S(2)}, u32[]{:S(2)}) collective-permute-start(bf16[128,2560]{1,0:T(8,128)(2,1)S(1)} %slice.146), channel_id=1, source_target_pairs={{4,0},{8,4},{12,8},{16,12},{20,16},{24,20},{28,24},{32,28},{36,32}... | collective-permute-start | bytes 1966088 | tf_op jit(solution)/shard_map/ppermute | solution.py:34
  69.5 33.0 %collective-permute-start.7 = (f32[128,256]{1,0:T(8,128)S(1)}, f32[128,256]{1,0:T(8,128)S(1)}, u32[]{:S(2)}, u32[]{:S(2)}) collective-permute-start(f32[128,256]{1,0:T(8,128)S(1)} %select_add_fusion.1), channel_id=1, source_target_pairs={{0,2},{1,3},{2,0},{3,1},{4,6},{5,7},{6,4},{7,5},{8,10},{9,11},{10,... | collective-permute-start | bytes 393224 | tf_op jit(solution)/shard_map/ppermute | solution.py:192
  102.6 2.0 %collective-permute-start.8 = (f32[128,256]{1,0:T(8,128)S(1)}, f32[128,256]{1,0:T(8,128)S(1)}, u32[]{:S(2)}, u32[]{:S(2)}) collective-permute-start(f32[128,256]{1,0:T(8,128)S(1)} %add.39), channel_id=1, source_target_pairs={{0,1},{1,0},{2,3},{3,2},{4,5},{5,4},{6,7},{7,6},{8,9},{9,8},{10,11... | collective-permute-start | bytes 393224 | tf_op jit(solution)/shard_map/ppermute | solution.py:193
  104.7 16.4 %copy-start.6 = (bf16[128,2560]{1,0:T(8,128)(2,1)}, bf16[128,2560]{1,0:T(8,128)(2,1)S(1)}, u32[]{:S(2)}) copy-start(bf16[128,2560]{1,0:T(8,128)(2,1)S(1)} %collective-permute-done.11.upper_ref) | copy-start | bytes 1966084
  104.7 15.2 %copy-start.5 = (bf16[128,2560]{1,0:T(8,128)(2,1)}, bf16[128,2560]{1,0:T(8,128)(2,1)S(1)}, u32[]{:S(2)}) copy-start(bf16[128,2560]{1,0:T(8,128)(2,1)S(1)} %collective-permute-done.12.upper_ref) | copy-start | bytes 1966084
  104.7 14.0 %copy-start.4 = (bf16[256,2560]{1,0:T(8,128)(2,1)}, bf16[256,2560]{1,0:T(8,128)(2,1)S(1)}, u32[]{:S(2)}) copy-start(bf16[256,2560]{1,0:T(8,128)(2,1)S(1)} %collective-permute-done.10.lower_ref) | copy-start | bytes 3932164
  118.2 1.1 copy-start.3
  119.3 1.1 slice-start.1
  120.4 1.1 slice-start
  122.2 1.6 collective-permute-start.14
  123.8 15.9 %collective-permute-start.15 = (f32[448,128]{1,0:T(8,128)S(1)}, f32[448,128]{1,0:T(8,128)S(1)}, u32[]{:S(2)}, u32[]{:S(2)}) collective-permute-start(f32[448,128]{1,0:T(8,128)S(1)} %select_add_fusion), channel_id=1, source_target_pairs={{0,2},{1,3},{2,0},{3,1},{4,6},{5,7},{6,4},{7,5},{8,10},{9,11},{10,... | collective-permute-start | bytes 688136 | tf_op jit(solution)/shard_map/ppermute | solution.py:192
  139.7 11.3 %collective-permute-start.16 = (f32[448,128]{1,0:T(8,128)S(1)}, f32[448,128]{1,0:T(8,128)S(1)}, u32[]{:S(2)}, u32[]{:S(2)}) collective-permute-start(f32[448,128]{1,0:T(8,128)S(1)} %add.43), channel_id=1, source_target_pairs={{0,1},{1,0},{2,3},{3,2},{4,5},{5,4},{6,7},{7,6},{8,9},{9,8},{10,11... | collective-permute-start | bytes 688136 | tf_op jit(solution)/shard_map/ppermute | solution.py:193
  140.7 14.8 %collective-permute-start.13 = (f32[256,256]{1,0:T(8,128)S(1)}, f32[256,256]{1,0:T(8,128)S(1)}, u32[]{:S(2)}, u32[]{:S(2)}) collective-permute-start(f32[256,256]{1,0:T(8,128)S(1)} %maximum_select_fusion.1), channel_id=1, source_target_pairs={{0,4},{4,8},{8,12},{12,16},{16,20},{20,24},{24,28},{28,32},{32,36}... | collective-permute-start | bytes 786440 | tf_op jit(solution)/shard_map/ppermute | solution.py:34
  142.6 9.5 %collective-permute-start.17 = (f32[128,128]{1,0:T(8,128)S(1)}, f32[128,128]{1,0:T(8,128)S(1)}, u32[]{:S(2)}, u32[]{:S(2)}) collective-permute-start(f32[128,128]{1,0:T(8,128)S(1)} %slice.153), channel_id=1, source_target_pairs={{4,0},{8,4},{12,8},{16,12},{20,16},{24,20},{28,24},{32,28},{36,32}... | collective-permute-start | bytes 196616 | tf_op jit(solution)/shard_map/ppermute | solution.py:34

commit v8 on v7

--- a/solution.py
+++ b/solution.py
@@ -194,6 +194,14 @@
     return jnp.where(core == 0, jnp.concatenate([part, other]), jnp.concatenate([other, part]))
 
 
+def ta_sum_full(value):
+    count = lax.axis_size("ta")
+    if count != 4:
+        return lax.psum(value, "ta")
+    value = value + lax.ppermute(value, "ta", [(i, i ^ 1) for i in range(count)])
+    return value + lax.ppermute(value, "ta", [(i, i ^ 2) for i in range(count)])
+
+
 def per_device(raw, fir_taps, start_basis):
     chans = raw.shape[0]
     samples = raw.shape[1]
@@ -243,7 +251,7 @@
         cross_left = left if cross_left is None else cross_left + left
         cross_right = right if cross_right is None else cross_right + right
 
-    packed = ta_sum(jnp.concatenate([cross_left[:, :STRIDE], cross_left[:, STRIDE:], cross_right], axis=0))
+    packed = ta_sum_full(jnp.concatenate([cross_left[:, :STRIDE], cross_left[:, STRIDE:], cross_right], axis=0))
     tiles_left = 2 * STRIDE
     cross_left = jnp.concatenate(
         [packed[:tiles_left], packed[tiles_left : 2 * tiles_left]], axis=1

time: 188 us -> 191 us (1.016)
  waiting for transfers between devices: 66.2 us -> 68.2 us
    ppermute x0 -> x2, waiting for transfers between devices: none -> 14.5 us  [the longest x1 12.7 us: ta_sum_full(): return value + lax.ppermute(value, 'ta', [(i, i ^ 2) for i in range(count)])]
    ppermute x2 -> x1, waiting for transfers between devices: 44.3 us -> 30.1 us  [ta_sum(): part = part + lax.ppermute(part, 'ta', across)]
    ppermute x6, waiting for transfers between devices: 17.6 us -> 20.7 us  [shifted(): lax.ppermute(value, axis, [(source, source + steps) for source in range(f...]
    ppermute x2 -> x1, starting transfers between devices: 4.63 us -> 2.95 us  [ta_sum(): part = part + lax.ppermute(part, 'ta', across)]
  transfers between devices with their start and end apart: 18 -> 17, of which waited for: 8 -> 7; matrix products, arithmetic and copies ran while one was open for 7% -> 7% of each run, Pallas kernels for 3% -> 3%
where the time goes in v8:
time: 191 us; the launch traced here: 189 us
  waiting for transfers between devices  68.2 us (36%)
  starting transfers between devices  57.9 us (30%)
  Pallas kernels  40.6 us (21%)
  local copies, waits for them, and re-layouts  13.4 us (7%)
  other arithmetic  5 us (3%)
  matrix products  3.47 us (2%)
    ppermute x1, waiting for transfers between devices, ta_sum(): part = part + lax.ppermute(part, 'ta', across)  30.1 us
    ppermute x6, starting transfers between devices, shifted(): lax.ppermute(value, axis, [(source, source + steps) for source in range(f...  24.5 us
    ppermute x6, waiting for transfers between devices, shifted(): lax.ppermute(value, axis, [(source, source + steps) for source in range(f...  20.7 us
    pallas_call x1, Pallas kernels, subspace(): pl.pallas_call(subspace_kernel, out_shape=jax.ShapeDtypeStruct((windows,)...  17.1 us
    ppermute x2, starting transfers between devices, with_halo(): lax.ppermute(lax.slice_in_dim(block, 0, width, axis=dim), axis, backward)  14 us
    ppermute x1, waiting for transfers between devices, ta_sum_full(): return value + lax.ppermute(value, 'ta', [(i, i ^ 2) for i in range(count)])  12.7 us
    pallas_call x2, Pallas kernels, clean(): pl.pallas_call(clean_kernel, grid=(samples // width,), out_shape=jax.Shap...  11.8 us
    pallas_call x2, Pallas kernels, fir(): pl.pallas_call(kernel, grid=(length // width,), out_shape=jax.ShapeDtypeS...  11.7 us
  transfers between devices with their start and end apart: 17, of which 7 were waited for; matrix products, arithmetic and copies ran while one was open for 7% of the time, Pallas kernels for 3%

profile of v8, /device:TPU:97, one launch (start us, length us, event | category | flops | bytes accessed | tf_op | source)
XLA Modules:
  0.0 189.0 jit_solution(9661211253505844591)
XLA Ops:
  0.0 1.0 fusion.24
  1.0 2.6 %collective-permute-start.1 = (bf16[256,64]{1,0:T(8,128)(2,1)S(1)}, bf16[256,64]{1,0:T(8,128)(2,1)S(1)}, u32[]{:S(2)}, u32[]{:S(2)}) collective-permute-start(bf16[256,64]{1,0:T(8,128)(2,1)S(1)} %get-tuple-element.23), channel_id=1, source_target_pairs={{1,0},{2,1},{3,2},{5,4},{6,5},{7,6},{9,8},{10,9},{11,10},{13,12},{... | collective-permute-start | bytes 98312 | tf_op jit(solution)/shard_map/ppermute | solution.py:214
  3.6 6.9 %collective-permute-start = (bf16[256,64]{1,0:T(8,128)(2,1)S(1)}, bf16[256,64]{1,0:T(8,128)(2,1)S(1)}, u32[]{:S(2)}, u32[]{:S(2)}) collective-permute-start(bf16[256,64]{1,0:T(8,128)(2,1)S(1)} %get-tuple-element.24), channel_id=1, source_target_pairs={{0,1},{1,2},{2,3},{4,5},{5,6},{6,7},{8,9},{9,10},{10,11},{12,13},{... | collective-permute-start | bytes 98312 | tf_op jit(solution)/shard_map/ppermute | solution.py:213
  10.4 0.7 concatenate.57
  11.2 1.3 tile.10
  13.2 0.7 pad_slice_fusion
  13.9 1.5 slice.102.refs_0_.refs_1_
  15.4 0.8 slice.132.refs_6_
  16.2 5.9 %shard_map.37 = f32[256,2560]{1,0:T(8,128)} custom-call(bf16[256,128]{1,0:T(8,128)(2,1)} %slice.102.refs_0_.refs_1_, bf16[256,128]{1,0:T(8,128)(2,1)} %slice.102.refs_0_.refs_1_, bf16[256,5120]{1,0:T(8,128)(2,1)} %refs_4_.3, bf16[256,5120]{1,0:T(8,128)(2,1)} %refs_4_.3, bf16[256,5120]{1,0:T(8,128)(2,1)} %refs_4_.3, ...), custom_call_target="tpu_custom_call" | custom-call | tf_op jit(solution)/shard_map/pallas_call | solution.py:120
  22.2 0.6 concatenate.59.refs_1_
  22.8 0.7 concatenate.58.refs_0_
  23.5 5.8 %shard_map.38 = f32[256,2560]{1,0:T(8,128)} custom-call(bf16[256,128]{1,0:T(8,128)(2,1)} %concatenate.58.refs_0_, bf16[256,128]{1,0:T(8,128)(2,1)} %concatenate.59.refs_1_, bf16[256,5120]{1,0:T(8,128)(2,1)} %refs_4_.3, bf16[256,5120]{1,0:T(8,128)(2,1)} %refs_4_.3, bf16[256,5120]{1,0:T(8,128)(2,1)} %refs_4_.3, bf16[128,512]{1,0:T(8,128)(2,1)} %get-tuple-element.26.refs_5_, ...), custom_call_target="tpu_custom_call" | custom-call | tf_op jit(solution)/shard_map/pallas_call | solution.py:120
  29.4 0.9 fusion.23
  30.3 6.4 %collective-permute-start.4 = (f32[4,2560]{1,0:T(4,128)S(1)}, f32[4,2560]{1,0:T(4,128)S(1)}, u32[]{:S(2)}, u32[]{:S(2)}) collective-permute-start(f32[4,2560]{1,0:T(4,128)S(1)} %get-tuple-element.21), channel_id=1, source_target_pairs={{4,0},{8,4},{12,8},{16,12},{20,16},{24,20},{28,24},{32,28},{36,32}... | collective-permute-start | bytes 122888 | tf_op jit(solution)/shard_map/ppermute | solution.py:26
  36.7 1.9 %collective-permute-start.5 = (f32[4,2560]{1,0:T(4,128)S(1)}, f32[4,2560]{1,0:T(4,128)S(1)}, u32[]{:S(2)}, u32[]{:S(2)}) collective-permute-start(f32[4,2560]{1,0:T(4,128)S(1)} %get-tuple-element.22), channel_id=1, source_target_pairs={{0,4},{4,8},{8,12},{12,16},{16,20},{20,24},{24,28},{28,32},{32,36}... | collective-permute-start | bytes 122888 | tf_op jit(solution)/shard_map/ppermute | solution.py:23
  38.7 0.9 fusion.22
  39.6 7.6 %collective-permute-start.2 = (f32[4,2560]{1,0:T(4,128)S(1)}, f32[4,2560]{1,0:T(4,128)S(1)}, u32[]{:S(2)}, u32[]{:S(2)}) collective-permute-start(f32[4,2560]{1,0:T(4,128)S(1)} %get-tuple-element.19), channel_id=1, source_target_pairs={{4,0},{8,4},{12,8},{16,12},{20,16},{24,20},{28,24},{32,28},{36,32}... | collective-permute-start | bytes 122888 | tf_op jit(solution)/shard_map/ppermute | solution.py:26
  47.2 2.2 %collective-permute-start.3 = (f32[4,2560]{1,0:T(4,128)S(1)}, f32[4,2560]{1,0:T(4,128)S(1)}, u32[]{:S(2)}, u32[]{:S(2)}) collective-permute-start(f32[4,2560]{1,0:T(4,128)S(1)} %get-tuple-element.20), channel_id=1, source_target_pairs={{0,4},{4,8},{8,12},{12,16},{16,20},{20,24},{24,28},{28,32},{32,36}... | collective-permute-start | bytes 122888 | tf_op jit(solution)/shard_map/ppermute | solution.py:23
  49.4 3.1 %fusion.1.own_ref = bf16[256,2560]{1,0:T(8,128)(2,1)S(1)} fusion(f32[256,2560]{1,0:T(8,128)} %shard_map.38, f32[4,2560]{1,0:T(4,128)S(1)} %collective-permute-done.5, f32[4,2560]{1,0:T(4,128)S(1)} %collective-permute-done.4), kind=kLoop, calls=%fused_computation.2 | loop fusion | flops 2621440 | bytes 4014080 | tf_op jit(solution)/shard_map/convert_element_type | solution.py:232
  52.5 1.9 %collective-permute-start.10 = (bf16[256,2560]{1,0:T(8,128)(2,1)S(1)}, bf16[256,2560]{1,0:T(8,128)(2,1)S(1)}, u32[]{:S(2)}, u32[]{:S(2)}) collective-permute-start(bf16[256,2560]{1,0:T(8,128)(2,1)S(1)} %fusion.1.own_ref), channel_id=1, source_target_pairs={{0,4},{4,8},{8,12},{12,16},{16,20},{20,24},{24,28},{28,32},{32,36}... | collective-permute-start | bytes 3932168 | tf_op jit(solution)/shard_map/ppermute | solution.py:34
  54.5 1.9 %collective-permute-done.3 = f32[4,2560]{1,0:T(4,128)S(1)} collective-permute-done((f32[4,2560]{1,0:T(4,128)S(1)}, f32[4,2560]{1,0:T(4,128)S(1)}, u32[]{:S(2)}, u32[]{:S(2)}) %collective-permute-start.3) | collective-permute-done | bytes 40992 | tf_op jit(solution)/shard_map/ppermute | solution.py:23
  56.8 1.9 %collective-permute-start.9 = (bf16[256,2560]{1,0:T(8,128)(2,1)S(1)}, bf16[256,2560]{1,0:T(8,128)(2,1)S(1)}, u32[]{:S(2)}, u32[]{:S(2)}) collective-permute-start(bf16[256,2560]{1,0:T(8,128)(2,1)S(1)} %fusion.3.own_ref), channel_id=1, source_target_pairs={{0,4},{4,8},{8,12},{12,16},{16,20},{20,24},{24,28},{28,32},{32,36}... | collective-permute-start | bytes 3932168 | tf_op jit(solution)/shard_map/ppermute | solution.py:34
  58.7 0.5 fusion.27
  59.2 0.5 convolution_add_fusion.1
  60.0 7.6 %collective-permute-start.11 = (bf16[128,2560]{1,0:T(8,128)(2,1)S(1)}, bf16[128,2560]{1,0:T(8,128)(2,1)S(1)}, u32[]{:S(2)}, u32[]{:S(2)}) collective-permute-start(bf16[128,2560]{1,0:T(8,128)(2,1)S(1)} %slice.135), channel_id=1, source_target_pairs={{4,0},{8,4},{12,8},{16,12},{20,16},{24,20},{28,24},{32,28},{36,32}... | collective-permute-start | bytes 1966088 | tf_op jit(solution)/shard_map/ppermute | solution.py:34
  67.6 1.9 %collective-permute-start.12 = (bf16[128,2560]{1,0:T(8,128)(2,1)S(1)}, bf16[128,2560]{1,0:T(8,128)(2,1)S(1)}, u32[]{:S(2)}, u32[]{:S(2)}) collective-permute-start(bf16[128,2560]{1,0:T(8,128)(2,1)S(1)} %slice.136), channel_id=1, source_target_pairs={{4,0},{8,4},{12,8},{16,12},{20,16},{24,20},{28,24},{32,28},{36,32}... | collective-permute-start | bytes 1966088 | tf_op jit(solution)/shard_map/ppermute | solution.py:34
  69.6 2.9 %collective-permute-start.7 = (f32[128,256]{1,0:T(8,128)S(1)}, f32[128,256]{1,0:T(8,128)S(1)}, u32[]{:S(2)}, u32[]{:S(2)}) collective-permute-start(f32[128,256]{1,0:T(8,128)S(1)} %select_add_fusion), channel_id=1, source_target_pairs={{0,2},{1,3},{2,0},{3,1},{4,6},{5,7},{6,4},{7,5},{8,10},{9,11},{10,... | collective-permute-start | bytes 393224 | tf_op jit(solution)/shard_map/ppermute | solution.py:192
  72.5 30.1 %collective-permute-done.7 = f32[128,256]{1,0:T(8,128)S(1)} collective-permute-done((f32[128,256]{1,0:T(8,128)S(1)}, f32[128,256]{1,0:T(8,128)S(1)}, u32[]{:S(2)}, u32[]{:S(2)}) %collective-permute-start.7) | collective-permute-done | bytes 131104 | tf_op jit(solution)/shard_map/ppermute | solution.py:192
  102.6 1.1 collective-permute-start.8
  103.7 1.0 collective-permute-done.8
  104.8 13.5 %collective-permute-done.9.lower_ref = bf16[256,2560]{1,0:T(8,128)(2,1)S(1)} collective-permute-done((bf16[256,2560]{1,0:T(8,128)(2,1)S(1)}, bf16[256,2560]{1,0:T(8,128)(2,1)S(1)}, u32[]{:S(2)}, u32[]{:S(2)}) %collective-permute-start.9) | collective-permute-done | bytes 1310752 | tf_op jit(solution)/shard_map/ppermute | solution.py:34
  118.3 0.5 fusion.28
  118.8 0.6 copy-done.3
  119.4 0.5 convolution_add_fusion
  120.5 0.7 fusion.8
  121.6 0.7 fusion.16
  122.4 1.8 collective-permute-done.14
  124.2 1.7 collective-permute-start.15
  125.9 1.9 %collective-permute-start.13 = (f32[256,256]{1,0:T(8,128)S(1)}, f32[256,256]{1,0:T(8,128)S(1)}, u32[]{:S(2)}, u32[]{:S(2)}) collective-permute-start(f32[256,256]{1,0:T(8,128)S(1)} %maximum_select_fusion), channel_id=1, source_target_pairs={{0,4},{4,8},{8,12},{12,16},{16,20},{20,24},{24,28},{28,32},{32,36}... | collective-permute-start | bytes 786440 | tf_op jit(solution)/shard_map/ppermute | solution.py:34
  127.8 9.2 %collective-permute-start.16 = (f32[128,128]{1,0:T(8,128)S(1)}, f32[128,128]{1,0:T(8,128)S(1)}, u32[]{:S(2)}, u32[]{:S(2)}) collective-permute-start(f32[128,128]{1,0:T(8,128)S(1)} %slice.143), channel_id=1, source_target_pairs={{4,0},{8,4},{12,8},{16,12},{20,16},{24,20},{28,24},{32,28},{36,32}... | collective-permute-start | bytes 196616 | tf_op jit(solution)/shard_map/ppermute | solution.py:34
  137.1 12.7 %collective-permute-done.15 = f32[896,128]{1,0:T(8,128)S(1)} collective-permute-done((f32[896,128]{1,0:T(8,128)S(1)}, f32[896,128]{1,0:T(8,128)S(1)}, u32[]{:S(2)}, u32[]{:S(2)}) %collective-permute-start.15) | collective-permute-done | bytes 458784 | tf_op jit(solution)/shard_map/ppermute | solution.py:202
  150.2 7.2 %collective-permute-done.13 = f32[256,256]{1,0:T(8,128)S(1)} collective-permute-done((f32[256,256]{1,0:T(8,128)S(1)}, f32[256,256]{1,0:T(8,128)S(1)}, u32[]{:S(2)}, u32[]{:S(2)}) %collective-permute-start.13) | collective-permute-done | bytes 262176 | tf_op jit(solution)/shard_map/ppermute | solution.py:34
  157.4 1.3 fusion.14.band_ref
  158.7 17.1 %shard_map.39.basis_ref = bf16[2,16,512]{2,1,0:T(8,128)(2,1)} custom-call(f32[640,640]{1,0:T(8,128)} %fusion.14.band_ref, f32[16,512]{1,0:T(8,128)} %bitcast.23), custom_call_target="tpu_custom_call" | custom-call | tf_op jit(solution)/shard_map/pallas_call | solution.py:87
  175.8 0.7 slice.144
  176.5 0.7 copy.13
  177.3 5.9 %shard_map.40.rest_0_ = bf16[256,5120]{1,0:T(8,128)(2,1)} custom-call(bf16[256,2560]{1,0:T(8,128)(2,1)} %copy-done.3, bf16[256,2560]{1,0:T(8,128)(2,1)} %copy-done, bf16[128,2560]{1,0:T(8,128)(2,1)} %copy-done.6, bf16[2,16,512]{2,1,0:T(8,128)(2,1)} %shard_map.39.basis_ref, bf16[2,128,16]{2,1,0:T(8,128)(2,1)} %bitcast.21), custom_call_target="tpu_custom_call" | custom-call | tf_op jit(solution)/shard_map/pallas_call | solution.py:164
  183.2 5.9 %shard_map.41 = bf16[256,5120]{1,0:T(8,128)(2,1)} custom-call(bf16[256,2560]{1,0:T(8,128)(2,1)} %copy-done.4, bf16[256,2560]{1,0:T(8,128)(2,1)} %copy-done.1, bf16[128,2560]{1,0:T(8,128)(2,1)} %copy-done.5, bf16[2,16,512]{2,1,0:T(8,128)(2,1)} %shard_map.39.basis_ref, bf16[2,128,16]{2,1,0:T(8,128)(2,1)} %bitcast.22, ...), custom_call_target="tpu_custom_call", output_to_operand_aliasing={{}: (5, {})} | custom-call | tf_op jit(solution)/shard_map/pallas_call | solution.py:164
  (52 shorter events, 3.0 us)
Async XLA Ops:
  1.0 21.2 %collective-permute-start.1 = (bf16[256,64]{1,0:T(8,128)(2,1)S(1)}, bf16[256,64]{1,0:T(8,128)(2,1)S(1)}, u32[]{:S(2)}, u32[]{:S(2)}) collective-permute-start(bf16[256,64]{1,0:T(8,128)(2,1)S(1)} %get-tuple-element.23), channel_id=1, source_target_pairs={{1,0},{2,1},{3,2},{5,4},{6,5},{7,6},{9,8},{10,9},{11,10},{13,12},{... | collective-permute-start | bytes 98312 | tf_op jit(solution)/shard_map/ppermute | solution.py:214
  3.6 19.3 %collective-permute-start = (bf16[256,64]{1,0:T(8,128)(2,1)S(1)}, bf16[256,64]{1,0:T(8,128)(2,1)S(1)}, u32[]{:S(2)}, u32[]{:S(2)}) collective-permute-start(bf16[256,64]{1,0:T(8,128)(2,1)S(1)} %get-tuple-element.24), channel_id=1, source_target_pairs={{0,1},{1,2},{2,3},{4,5},{5,6},{6,7},{8,9},{9,10},{10,11},{12,13},{... | collective-permute-start | bytes 98312 | tf_op jit(solution)/shard_map/ppermute | solution.py:213
  30.3 19.1 %collective-permute-start.4 = (f32[4,2560]{1,0:T(4,128)S(1)}, f32[4,2560]{1,0:T(4,128)S(1)}, u32[]{:S(2)}, u32[]{:S(2)}) collective-permute-start(f32[4,2560]{1,0:T(4,128)S(1)} %get-tuple-element.21), channel_id=1, source_target_pairs={{4,0},{8,4},{12,8},{16,12},{20,16},{24,20},{28,24},{32,28},{36,32}... | collective-permute-start | bytes 122888 | tf_op jit(solution)/shard_map/ppermute | solution.py:26
  36.7 12.7 %collective-permute-start.5 = (f32[4,2560]{1,0:T(4,128)S(1)}, f32[4,2560]{1,0:T(4,128)S(1)}, u32[]{:S(2)}, u32[]{:S(2)}) collective-permute-start(f32[4,2560]{1,0:T(4,128)S(1)} %get-tuple-element.22), channel_id=1, source_target_pairs={{0,4},{4,8},{8,12},{12,16},{16,20},{20,24},{24,28},{28,32},{32,36}... | collective-permute-start | bytes 122888 | tf_op jit(solution)/shard_map/ppermute | solution.py:23
  39.6 14.9 %collective-permute-start.2 = (f32[4,2560]{1,0:T(4,128)S(1)}, f32[4,2560]{1,0:T(4,128)S(1)}, u32[]{:S(2)}, u32[]{:S(2)}) collective-permute-start(f32[4,2560]{1,0:T(4,128)S(1)} %get-tuple-element.19), channel_id=1, source_target_pairs={{4,0},{8,4},{12,8},{16,12},{20,16},{24,20},{28,24},{32,28},{36,32}... | collective-permute-start | bytes 122888 | tf_op jit(solution)/shard_map/ppermute | solution.py:26
  47.2 9.2 %copy-start.2 = (f32[256,2560]{1,0:T(8,128)S(1)}, f32[256,2560]{1,0:T(8,128)}, u32[]{:S(2)}) copy-start(f32[256,2560]{1,0:T(8,128)} %shard_map.37) | copy-start | bytes 7864324
  47.2 9.2 %collective-permute-start.3 = (f32[4,2560]{1,0:T(4,128)S(1)}, f32[4,2560]{1,0:T(4,128)S(1)}, u32[]{:S(2)}, u32[]{:S(2)}) collective-permute-start(f32[4,2560]{1,0:T(4,128)S(1)} %get-tuple-element.20), channel_id=1, source_target_pairs={{0,4},{4,8},{8,12},{12,16},{16,20},{20,24},{24,28},{28,32},{32,36}... | collective-permute-start | bytes 122888 | tf_op jit(solution)/shard_map/ppermute | solution.py:23
  52.5 67.4 %copy-start.1 = (bf16[256,2560]{1,0:T(8,128)(2,1)}, bf16[256,2560]{1,0:T(8,128)(2,1)S(1)}, u32[]{:S(2)}) copy-start(bf16[256,2560]{1,0:T(8,128)(2,1)S(1)} %fusion.1.own_ref) | copy-start | bytes 3932164
  52.5 52.2 %collective-permute-start.10 = (bf16[256,2560]{1,0:T(8,128)(2,1)S(1)}, bf16[256,2560]{1,0:T(8,128)(2,1)S(1)}, u32[]{:S(2)}, u32[]{:S(2)}) collective-permute-start(bf16[256,2560]{1,0:T(8,128)(2,1)S(1)} %fusion.1.own_ref), channel_id=1, source_target_pairs={{0,4},{4,8},{8,12},{12,16},{16,20},{20,24},{24,28},{28,32},{32,36}... | collective-permute-start | bytes 3932168 | tf_op jit(solution)/shard_map/ppermute | solution.py:34
  56.8 64.4 %copy-start = (bf16[256,2560]{1,0:T(8,128)(2,1)}, bf16[256,2560]{1,0:T(8,128)(2,1)S(1)}, u32[]{:S(2)}) copy-start(bf16[256,2560]{1,0:T(8,128)(2,1)S(1)} %fusion.3.own_ref) | copy-start | bytes 3932164
  56.8 61.5 %collective-permute-start.9 = (bf16[256,2560]{1,0:T(8,128)(2,1)S(1)}, bf16[256,2560]{1,0:T(8,128)(2,1)S(1)}, u32[]{:S(2)}, u32[]{:S(2)}) collective-permute-start(bf16[256,2560]{1,0:T(8,128)(2,1)S(1)} %fusion.3.own_ref), channel_id=1, source_target_pairs={{0,4},{4,8},{8,12},{12,16},{16,20},{20,24},{24,28},{28,32},{32,36}... | collective-permute-start | bytes 3932168 | tf_op jit(solution)/shard_map/ppermute | solution.py:34
  59.8 9.7 %collective-permute-start.6 = (f32[128,256]{1,0:T(8,128)S(1)}, f32[128,256]{1,0:T(8,128)S(1)}, u32[]{:S(2)}, u32[]{:S(2)}) collective-permute-start(f32[128,256]{1,0:T(8,128)S(1)} %slice_select_fusion), channel_id=1, source_target_pairs={{0,1},{1,0},{2,3},{3,2},{4,5},{5,4},{6,7},{7,6},{8,9},{9,8},{10,11... | collective-permute-start | bytes 393224 | tf_op jit(solution)/shard_map/ppermute | solution.py:191
  60.0 44.7 %collective-permute-start.11 = (bf16[128,2560]{1,0:T(8,128)(2,1)S(1)}, bf16[128,2560]{1,0:T(8,128)(2,1)S(1)}, u32[]{:S(2)}, u32[]{:S(2)}) collective-permute-start(bf16[128,2560]{1,0:T(8,128)(2,1)S(1)} %slice.135), channel_id=1, source_target_pairs={{4,0},{8,4},{12,8},{16,12},{20,16},{24,20},{28,24},{32,28},{36,32}... | collective-permute-start | bytes 1966088 | tf_op jit(solution)/shard_map/ppermute | solution.py:34
  67.6 37.1 %collective-permute-start.12 = (bf16[128,2560]{1,0:T(8,128)(2,1)S(1)}, bf16[128,2560]{1,0:T(8,128)(2,1)S(1)}, u32[]{:S(2)}, u32[]{:S(2)}) collective-permute-start(bf16[128,2560]{1,0:T(8,128)(2,1)S(1)} %slice.136), channel_id=1, source_target_pairs={{4,0},{8,4},{12,8},{16,12},{20,16},{24,20},{28,24},{32,28},{36,32}... | collective-permute-start | bytes 1966088 | tf_op jit(solution)/shard_map/ppermute | solution.py:34
  69.6 33.0 %collective-permute-start.7 = (f32[128,256]{1,0:T(8,128)S(1)}, f32[128,256]{1,0:T(8,128)S(1)}, u32[]{:S(2)}, u32[]{:S(2)}) collective-permute-start(f32[128,256]{1,0:T(8,128)S(1)} %select_add_fusion), channel_id=1, source_target_pairs={{0,2},{1,3},{2,0},{3,1},{4,6},{5,7},{6,4},{7,5},{8,10},{9,11},{10,... | collective-permute-start | bytes 393224 | tf_op jit(solution)/shard_map/ppermute | solution.py:192
  102.6 2.0 %collective-permute-start.8 = (f32[128,256]{1,0:T(8,128)S(1)}, f32[128,256]{1,0:T(8,128)S(1)}, u32[]{:S(2)}, u32[]{:S(2)}) collective-permute-start(f32[128,256]{1,0:T(8,128)S(1)} %add.38), channel_id=1, source_target_pairs={{0,1},{1,0},{2,3},{3,2},{4,5},{5,4},{6,7},{7,6},{8,9},{9,8},{10,11... | collective-permute-start | bytes 393224 | tf_op jit(solution)/shard_map/ppermute | solution.py:193
  104.7 16.4 %copy-start.6 = (bf16[128,2560]{1,0:T(8,128)(2,1)}, bf16[128,2560]{1,0:T(8,128)(2,1)S(1)}, u32[]{:S(2)}) copy-start(bf16[128,2560]{1,0:T(8,128)(2,1)S(1)} %collective-permute-done.11.upper_ref) | copy-start | bytes 1966084
  104.7 15.2 %copy-start.5 = (bf16[128,2560]{1,0:T(8,128)(2,1)}, bf16[128,2560]{1,0:T(8,128)(2,1)S(1)}, u32[]{:S(2)}) copy-start(bf16[128,2560]{1,0:T(8,128)(2,1)S(1)} %collective-permute-done.12.upper_ref) | copy-start | bytes 1966084
  104.8 14.1 %copy-start.4 = (bf16[256,2560]{1,0:T(8,128)(2,1)}, bf16[256,2560]{1,0:T(8,128)(2,1)S(1)}, u32[]{:S(2)}) copy-start(bf16[256,2560]{1,0:T(8,128)(2,1)S(1)} %collective-permute-done.10.lower_ref) | copy-start | bytes 3932164
  118.3 1.1 copy-start.3
  119.4 1.1 slice-start.1
  120.5 1.1 slice-start
  122.3 1.9 %collective-permute-start.14 = (f32[896,128]{1,0:T(8,128)S(1)}, f32[896,128]{1,0:T(8,128)S(1)}, u32[]{:S(2)}, u32[]{:S(2)}) collective-permute-start(f32[896,128]{1,0:T(8,128)S(1)} %pad_maximum_fusion.4), channel_id=1, source_target_pairs={{0,1},{1,0},{2,3},{3,2},{4,5},{5,4},{6,7},{7,6},{8,9},{9,8},{10,11... | collective-permute-start | bytes 1376264 | tf_op jit(solution)/shard_map/ppermute | solution.py:201
  124.2 25.5 %collective-permute-start.15 = (f32[896,128]{1,0:T(8,128)S(1)}, f32[896,128]{1,0:T(8,128)S(1)}, u32[]{:S(2)}, u32[]{:S(2)}) collective-permute-start(f32[896,128]{1,0:T(8,128)S(1)} %fusion.21), channel_id=1, source_target_pairs={{0,2},{1,3},{2,0},{3,1},{4,6},{5,7},{6,4},{7,5},{8,10},{9,11},{10,... | collective-permute-start | bytes 1376264 | tf_op jit(solution)/shard_map/ppermute | solution.py:202
  125.9 31.5 %collective-permute-start.13 = (f32[256,256]{1,0:T(8,128)S(1)}, f32[256,256]{1,0:T(8,128)S(1)}, u32[]{:S(2)}, u32[]{:S(2)}) collective-permute-start(f32[256,256]{1,0:T(8,128)S(1)} %maximum_select_fusion), channel_id=1, source_target_pairs={{0,4},{4,8},{8,12},{12,16},{16,20},{20,24},{24,28},{28,32},{32,36}... | collective-permute-start | bytes 786440 | tf_op jit(solution)/shard_map/ppermute | solution.py:34
  127.8 22.4 %collective-permute-start.16 = (f32[128,128]{1,0:T(8,128)S(1)}, f32[128,128]{1,0:T(8,128)S(1)}, u32[]{:S(2)}, u32[]{:S(2)}) collective-permute-start(f32[128,128]{1,0:T(8,128)S(1)} %slice.143), channel_id=1, source_target_pairs={{4,0},{8,4},{12,8},{16,12},{20,16},{24,20},{28,24},{32,28},{36,32}... | collective-permute-start | bytes 196616 | tf_op jit(solution)/shard_map/ppermute | solution.py:34

commit v9 on v7

--- a/solution.py
+++ b/solution.py
@@ -32,6 +32,16 @@
     count = lax.axis_size(axis)
     first, last = (max(0, -steps), min(count, count - steps))
     return lax.ppermute(value, axis, [(source, source + steps) for source in range(first, last)])
+
+
+def diagonal(value, dc, dt):
+    chs, count = lax.axis_size("ch"), lax.axis_size("ta")
+    pairs = [
+        (c * count + t, (c + dc) * count + t + dt)
+        for c in range(chs) for t in range(count)
+        if 0 <= c + dc < chs and 0 <= t + dt < count
+    ]
+    return lax.ppermute(value, ("ch", "ta"), pairs)
 
 
 def toeplitz_band(taps, width):
@@ -204,6 +214,22 @@
     blank = jnp.zeros((chans, STRIDE - half), raw.dtype)
     left = jnp.concatenate([blank, lax.ppermute(raw[:, samples - half :], "ta", forward)], axis=1)
     right = jnp.concatenate([lax.ppermute(raw[:, :half], "ta", backward), blank], axis=1)
+    edge_rows = jnp.concatenate(
+        [shifted(raw[chans - GAUGE :], "ch", 1), shifted(raw[:GAUGE], "ch", -1)], axis=0
+    )
+    corner = lambda rows, cols, dc, dt: diagonal(raw[rows, cols], dc, dt)
+    tail_cols, head_cols = slice(samples - half, None), slice(0, half)
+    last_rows, first_rows = slice(chans - GAUGE, None), slice(0, GAUGE)
+    edge_blank = jnp.zeros((2 * GAUGE, STRIDE - half), raw.dtype)
+    edge_left = jnp.concatenate(
+        [edge_blank, jnp.concatenate(
+            [corner(last_rows, tail_cols, 1, 1), corner(first_rows, tail_cols, -1, 1)], axis=0)], axis=1
+    )
+    edge_right = jnp.concatenate(
+        [jnp.concatenate(
+            [corner(last_rows, head_cols, 1, -1), corner(first_rows, head_cols, -1, -1)], axis=0),
+         edge_blank], axis=1
+    )
     width = math.gcd(samples, 512)
     band = jnp.pad(toeplitz_band(fir_taps, width), ((half, half), (0, 0)))
     chunks = 2 if samples % 1024 == 0 else 1
@@ -216,11 +242,14 @@
     filters = []
     for number in range(chunks):
         start = number * piece + width
-        edges = (left, right) if number == chunks - 1 else (raw[:, :STRIDE], raw[:, :STRIDE])
-        filters.append(fir(raw, *edges, band, start, piece))
+        wraps = number == chunks - 1
+        edges = (left, right) if wraps else (raw[:, :STRIDE], raw[:, :STRIDE])
+        outer = (edge_left, edge_right) if wraps else (edge_rows[:, :STRIDE], edge_rows[:, :STRIDE])
+        filters.append((fir(raw, *edges, band, start, piece), fir(edge_rows, *outer, band, start, piece)))
     filters = lax.optimization_barrier(filters)
     for number in range(chunks):
-        extended = with_halo(filters[number], (("ch", 0),), GAUGE)
+        inner, outer = filters[number]
+        extended = jnp.concatenate([outer[:GAUGE], inner, outer[GAUGE:]], axis=0)
         gauged = (extended[2 * GAUGE :] - extended[: -2 * GAUGE]).astype(jnp.bfloat16)
         lower_part = shifted(gauged[chans - 2 * STRIDE :], "ch", 1)
         upper_part = shifted(gauged[:STRIDE], "ch", -1)

time: 188 us -> 210 us (1.12)
  the two profiles are of different devices: /device:TPU:97 before, /device:TPU:33 now
where the time goes in v9:
time: 210 us; the launch traced here: 209 us
  starting transfers between devices  82.2 us (39%)
  waiting for transfers between devices  54.3 us (26%)
  Pallas kernels  48.3 us (23%)
  local copies, waits for them, and re-layouts  15.2 us (7%)
  other arithmetic  4.7 us (2%)
  matrix products  3.47 us (2%)
    ppermute x2, waiting for transfers between devices, ta_sum(): part = part + lax.ppermute(part, 'ta', across)  39 us
    ppermute x8, starting transfers between devices, shifted(): lax.ppermute(value, axis, [(source, source + steps) for source in range(f...  33.3 us
    ppermute x4, starting transfers between devices, diagonal(): return lax.ppermute(value, ('ch', 'ta'), pairs)  24.4 us
    pallas_call x4, Pallas kernels, fir(): pl.pallas_call(kernel, grid=(length // width,), out_shape=jax.ShapeDtypeS...  19.4 us
    pallas_call x1, Pallas kernels, subspace(): pl.pallas_call(subspace_kernel, out_shape=jax.ShapeDtypeStruct((windows,)...  17.1 us
    ppermute x2, starting transfers between devices, ta_sum(): part = part + lax.ppermute(part, 'ta', across)  12.9 us
    ppermute x8, waiting for transfers between devices, shifted(): lax.ppermute(value, axis, [(source, source + steps) for source in range(f...  12.8 us
    pallas_call x2, Pallas kernels, clean(): pl.pallas_call(clean_kernel, grid=(samples // width,), out_shape=jax.Shap...  11.8 us
  transfers between devices with their start and end apart: 20, of which 8 were waited for; matrix products, arithmetic and copies ran while one was open for 6% of the time, Pallas kernels for 6%

profile of v9, /device:TPU:33, one launch (start us, length us, event | category | flops | bytes accessed | tf_op | source)
XLA Modules:
  0.0 208.7 jit_solution(17952918040142447968)
XLA Ops:
  0.0 0.8 fusion.29
  0.8 3.7 %collective-permute-start.6 = (bf16[4,64]{1,0:T(4,128)(2,1)S(1)}, bf16[4,64]{1,0:T(4,128)(2,1)S(1)}, u32[]{:S(2)}, u32[]{:S(2)}) collective-permute-start(bf16[4,64]{1,0:T(4,128)(2,1)S(1)} %get-tuple-element.23), channel_id=1, source_target_pairs={{1,4},{2,5},{3,6},{5,8},{6,9},{7,10},{9,12},{10,13},{11,14},{13,16... | collective-permute-start | bytes 1544 | tf_op jit(solution)/shard_map/ppermute | solution.py:44
  4.5 10.9 %collective-permute-start.5 = (bf16[4,64]{1,0:T(4,128)(2,1)S(1)}, bf16[4,64]{1,0:T(4,128)(2,1)S(1)}, u32[]{:S(2)}, u32[]{:S(2)}) collective-permute-start(bf16[4,64]{1,0:T(4,128)(2,1)S(1)} %get-tuple-element.24), channel_id=1, source_target_pairs={{4,1},{5,2},{6,3},{8,5},{9,6},{10,7},{12,9},{13,10},{14,11},{16,13... | collective-permute-start | bytes 1544 | tf_op jit(solution)/shard_map/ppermute | solution.py:44
  15.4 1.9 collective-permute-start.4
  17.3 7.9 %collective-permute-start.7 = (bf16[4,64]{1,0:T(4,128)(2,1)S(1)}, bf16[4,64]{1,0:T(4,128)(2,1)S(1)}, u32[]{:S(2)}, u32[]{:S(2)}) collective-permute-start(bf16[4,64]{1,0:T(4,128)(2,1)S(1)} %get-tuple-element.26), channel_id=1, source_target_pairs={{5,0},{6,1},{7,2},{9,4},{10,5},{11,6},{13,8},{14,9},{15,10},{17,12... | collective-permute-start | bytes 1544 | tf_op jit(solution)/shard_map/ppermute | solution.py:44
  25.2 1.0 fusion.31
  26.2 2.2 %collective-permute-start.1 = (bf16[4,5120]{1,0:T(4,128)(2,1)S(1)}, bf16[4,5120]{1,0:T(4,128)(2,1)S(1)}, u32[]{:S(2)}, u32[]{:S(2)}) collective-permute-start(bf16[4,5120]{1,0:T(4,128)(2,1)S(1)} %get-tuple-element.29), channel_id=1, source_target_pairs={{4,0},{8,4},{12,8},{16,12},{20,16},{24,20},{28,24},{32,28},{36,32}... | collective-permute-start | bytes 122888 | tf_op jit(solution)/shard_map/ppermute | solution.py:34
  28.4 1.0 fusion.30
  29.4 0.7 concatenate.82
  30.1 1.3 tile.10
  32.1 0.7 pad_slice_fusion
  32.9 1.5 slice.138.refs_0_.refs_1_
  34.3 0.8 slice.177.refs_6_
  35.2 5.9 %shard_map.37 = f32[256,2560]{1,0:T(8,128)} custom-call(bf16[256,128]{1,0:T(8,128)(2,1)} %slice.138.refs_0_.refs_1_, bf16[256,128]{1,0:T(8,128)(2,1)} %slice.138.refs_0_.refs_1_, bf16[256,5120]{1,0:T(8,128)(2,1)} %refs_4_.3, bf16[256,5120]{1,0:T(8,128)(2,1)} %refs_4_.3, bf16[256,5120]{1,0:T(8,128)(2,1)} %refs_4_.3, ...), custom_call_target="tpu_custom_call" | custom-call | tf_op jit(solution)/shard_map/pallas_call | solution.py:130
  41.0 3.0 %collective-permute-start = (bf16[4,5120]{1,0:T(4,128)(2,1)S(1)}, bf16[4,5120]{1,0:T(4,128)(2,1)S(1)}, u32[]{:S(2)}, u32[]{:S(2)}) collective-permute-start(bf16[4,5120]{1,0:T(4,128)(2,1)S(1)} %get-tuple-element.30), channel_id=1, source_target_pairs={{0,4},{4,8},{8,12},{12,16},{16,20},{20,24},{24,28},{28,32},{32,36}... | collective-permute-start | bytes 122888 | tf_op jit(solution)/shard_map/ppermute | solution.py:34
  44.1 1.9 collective-permute-start.3
  46.7 7.5 %collective-permute-start.2 = (bf16[256,64]{1,0:T(8,128)(2,1)S(1)}, bf16[256,64]{1,0:T(8,128)(2,1)S(1)}, u32[]{:S(2)}, u32[]{:S(2)}) collective-permute-start(bf16[256,64]{1,0:T(8,128)(2,1)S(1)} %get-tuple-element.28), channel_id=1, source_target_pairs={{0,1},{1,2},{2,3},{4,5},{5,6},{6,7},{8,9},{9,10},{10,11},{12,13},{... | collective-permute-start | bytes 98312 | tf_op jit(solution)/shard_map/ppermute | solution.py:215
  55.6 0.7 concatenate.84.refs_0_
  56.3 5.8 %shard_map.39 = f32[256,2560]{1,0:T(8,128)} custom-call(bf16[256,128]{1,0:T(8,128)(2,1)} %concatenate.84.refs_0_, bf16[256,128]{1,0:T(8,128)(2,1)} %concatenate.85.refs_1_, bf16[256,5120]{1,0:T(8,128)(2,1)} %refs_4_.3, bf16[256,5120]{1,0:T(8,128)(2,1)} %refs_4_.3, bf16[256,5120]{1,0:T(8,128)(2,1)} %refs_4_.3, bf16[128,512]{1,0:T(8,128)(2,1)} %get-tuple-element.32.refs_5_, ...), custom_call_target="tpu_custom_call" | custom-call | tf_op jit(solution)/shard_map/pallas_call | solution.py:130
  62.7 0.7 pad_maximum_fusion.6.refs_2_.refs_3_.refs_4_
  63.4 3.8 %shard_map.38 = f32[8,2560]{1,0:T(8,128)} custom-call(bf16[8,128]{1,0:T(8,128)(2,1)} %fusion.24.refs_0_.refs_1_, bf16[8,128]{1,0:T(8,128)(2,1)} %fusion.24.refs_0_.refs_1_, bf16[8,5120]{1,0:T(8,128)(2,1)} %pad_maximum_fusion.6.refs_2_.refs_3_.refs_4_, bf16[8,5120]{1,0:T(8,128)(2,1)} %pad_maximum_fusion.6.refs_2_.refs_3_.refs_4_, ...), custom_call_target="tpu_custom_call" | custom-call | tf_op jit(solution)/shard_map/pallas_call | solution.py:130
  67.2 3.9 %shard_map.40 = f32[8,2560]{1,0:T(8,128)} custom-call(bf16[8,128]{1,0:T(8,128)(2,1)} %fusion.25.refs_0_, bf16[8,128]{1,0:T(8,128)(2,1)} %fusion.26.refs_1_, bf16[8,5120]{1,0:T(8,128)(2,1)} %pad_maximum_fusion.6.refs_2_.refs_3_.refs_4_, bf16[8,5120]{1,0:T(8,128)(2,1)} %pad_maximum_fusion.6.refs_2_.refs_3_.refs_4_, ...), custom_call_target="tpu_custom_call" | custom-call | tf_op jit(solution)/shard_map/pallas_call | solution.py:130
  71.1 1.0 fusion.35
  72.1 1.0 fusion.34
  73.5 2.2 %collective-permute-start.12 = (bf16[256,2560]{1,0:T(8,128)(2,1)S(1)}, bf16[256,2560]{1,0:T(8,128)(2,1)S(1)}, u32[]{:S(2)}, u32[]{:S(2)}) collective-permute-start(bf16[256,2560]{1,0:T(8,128)(2,1)S(1)} %fusion.1.own_ref), channel_id=1, source_target_pairs={{0,4},{4,8},{8,12},{12,16},{16,20},{20,24},{24,28},{28,32},{32,36}... | collective-permute-start | bytes 3932168 | tf_op jit(solution)/shard_map/ppermute | solution.py:34
  76.0 1.9 collective-permute-start.11
  79.2 7.6 %collective-permute-start.13 = (bf16[128,2560]{1,0:T(8,128)(2,1)S(1)}, bf16[128,2560]{1,0:T(8,128)(2,1)S(1)}, u32[]{:S(2)}, u32[]{:S(2)}) collective-permute-start(bf16[128,2560]{1,0:T(8,128)(2,1)S(1)} %slice.182), channel_id=1, source_target_pairs={{4,0},{8,4},{12,8},{16,12},{20,16},{24,20},{28,24},{32,28},{36,32}... | collective-permute-start | bytes 1966088 | tf_op jit(solution)/shard_map/ppermute | solution.py:34
  86.8 3.4 %collective-permute-start.14 = (bf16[128,2560]{1,0:T(8,128)(2,1)S(1)}, bf16[128,2560]{1,0:T(8,128)(2,1)S(1)}, u32[]{:S(2)}, u32[]{:S(2)}) collective-permute-start(bf16[128,2560]{1,0:T(8,128)(2,1)S(1)} %slice.183), channel_id=1, source_target_pairs={{4,0},{8,4},{12,8},{16,12},{20,16},{24,20},{28,24},{32,28},{36,32}... | collective-permute-start | bytes 1966088 | tf_op jit(solution)/shard_map/ppermute | solution.py:34
  90.2 7.0 %collective-permute-start.9 = (f32[128,256]{1,0:T(8,128)S(1)}, f32[128,256]{1,0:T(8,128)S(1)}, u32[]{:S(2)}, u32[]{:S(2)}) collective-permute-start(f32[128,256]{1,0:T(8,128)S(1)} %select_add_fusion.1), channel_id=1, source_target_pairs={{0,2},{1,3},{2,0},{3,1},{4,6},{5,7},{6,4},{7,5},{8,10},{9,11},{10,... | collective-permute-start | bytes 393224 | tf_op jit(solution)/shard_map/ppermute | solution.py:202
  97.3 28.5 %collective-permute-done.9 = f32[128,256]{1,0:T(8,128)S(1)} collective-permute-done((f32[128,256]{1,0:T(8,128)S(1)}, f32[128,256]{1,0:T(8,128)S(1)}, u32[]{:S(2)}, u32[]{:S(2)}) %collective-permute-start.9) | collective-permute-done | bytes 131104 | tf_op jit(solution)/shard_map/ppermute | solution.py:202
  125.7 1.0 collective-permute-start.10
  126.7 1.0 collective-permute-done.10
  127.8 8.7 %collective-permute-done.11.lower_ref = bf16[256,2560]{1,0:T(8,128)(2,1)S(1)} collective-permute-done((bf16[256,2560]{1,0:T(8,128)(2,1)S(1)}, bf16[256,2560]{1,0:T(8,128)(2,1)S(1)}, u32[]{:S(2)}, u32[]{:S(2)}) %collective-permute-start.11) | collective-permute-done | bytes 1310752 | tf_op jit(solution)/shard_map/ppermute | solution.py:34
  138.7 0.7 fusion.8
  139.7 0.7 fusion.16
  140.6 1.5 collective-permute-done.16
  142.1 5.9 %collective-permute-start.17 = (f32[448,128]{1,0:T(8,128)S(1)}, f32[448,128]{1,0:T(8,128)S(1)}, u32[]{:S(2)}, u32[]{:S(2)}) collective-permute-start(f32[448,128]{1,0:T(8,128)S(1)} %select_add_fusion), channel_id=1, source_target_pairs={{0,2},{1,3},{2,0},{3,1},{4,6},{5,7},{6,4},{7,5},{8,10},{9,11},{10,... | collective-permute-start | bytes 688136 | tf_op jit(solution)/shard_map/ppermute | solution.py:202
  147.9 10.5 %collective-permute-done.17 = f32[448,128]{1,0:T(8,128)S(1)} collective-permute-done((f32[448,128]{1,0:T(8,128)S(1)}, f32[448,128]{1,0:T(8,128)S(1)}, u32[]{:S(2)}, u32[]{:S(2)}) %collective-permute-start.17) | collective-permute-done | bytes 229408 | tf_op jit(solution)/shard_map/ppermute | solution.py:202
  158.5 1.1 collective-permute-start.18
  159.6 1.9 collective-permute-start.15
  161.5 11.0 %collective-permute-start.19 = (f32[128,128]{1,0:T(8,128)S(1)}, f32[128,128]{1,0:T(8,128)S(1)}, u32[]{:S(2)}, u32[]{:S(2)}) collective-permute-start(f32[128,128]{1,0:T(8,128)S(1)} %slice.190), channel_id=1, source_target_pairs={{4,0},{8,4},{12,8},{16,12},{20,16},{24,20},{28,24},{32,28},{36,32}... | collective-permute-start | bytes 196616 | tf_op jit(solution)/shard_map/ppermute | solution.py:34
  173.7 3.4 %collective-permute-done.15 = f32[256,256]{1,0:T(8,128)S(1)} collective-permute-done((f32[256,256]{1,0:T(8,128)S(1)}, f32[256,256]{1,0:T(8,128)S(1)}, u32[]{:S(2)}, u32[]{:S(2)}) %collective-permute-start.15) | collective-permute-done | bytes 262176 | tf_op jit(solution)/shard_map/ppermute | solution.py:34
  177.1 1.3 fusion.14.band_ref
  178.4 17.1 %shard_map.41.basis_ref = bf16[2,16,512]{2,1,0:T(8,128)(2,1)} custom-call(f32[640,640]{1,0:T(8,128)} %fusion.14.band_ref, f32[16,512]{1,0:T(8,128)} %bitcast.23), custom_call_target="tpu_custom_call" | custom-call | tf_op jit(solution)/shard_map/pallas_call | solution.py:97
  195.5 0.7 slice.191
  196.2 0.7 copy.13
  196.9 5.9 %shard_map.42.rest_0_ = bf16[256,5120]{1,0:T(8,128)(2,1)} custom-call(bf16[256,2560]{1,0:T(8,128)(2,1)} %copy-done.4, bf16[256,2560]{1,0:T(8,128)(2,1)} %copy-done, bf16[128,2560]{1,0:T(8,128)(2,1)} %copy-done.7, bf16[2,16,512]{2,1,0:T(8,128)(2,1)} %shard_map.41.basis_ref, bf16[2,128,16]{2,1,0:T(8,128)(2,1)} %bitcast.21), custom_call_target="tpu_custom_call" | custom-call | tf_op jit(solution)/shard_map/pallas_call | solution.py:174
  202.8 5.9 %shard_map.43 = bf16[256,5120]{1,0:T(8,128)(2,1)} custom-call(bf16[256,2560]{1,0:T(8,128)(2,1)} %copy-done.5, bf16[256,2560]{1,0:T(8,128)(2,1)} %copy-done.1, bf16[128,2560]{1,0:T(8,128)(2,1)} %copy-done.6, bf16[2,16,512]{2,1,0:T(8,128)(2,1)} %shard_map.41.basis_ref, bf16[2,128,16]{2,1,0:T(8,128)(2,1)} %bitcast.22, ...), custom_call_target="tpu_custom_call", output_to_operand_aliasing={{}: (5, {})} | custom-call | tf_op jit(solution)/shard_map/pallas_call | solution.py:174
  (69 shorter events, 9.2 us)
Async XLA Ops:
  0.8 45.9 %collective-permute-start.6 = (bf16[4,64]{1,0:T(4,128)(2,1)S(1)}, bf16[4,64]{1,0:T(4,128)(2,1)S(1)}, u32[]{:S(2)}, u32[]{:S(2)}) collective-permute-start(bf16[4,64]{1,0:T(4,128)(2,1)S(1)} %get-tuple-element.23), channel_id=1, source_target_pairs={{1,4},{2,5},{3,6},{5,8},{6,9},{7,10},{9,12},{10,13},{11,14},{13,16... | collective-permute-start | bytes 1544 | tf_op jit(solution)/shard_map/ppermute | solution.py:44
  4.5 36.6 %collective-permute-start.5 = (bf16[4,64]{1,0:T(4,128)(2,1)S(1)}, bf16[4,64]{1,0:T(4,128)(2,1)S(1)}, u32[]{:S(2)}, u32[]{:S(2)}) collective-permute-start(bf16[4,64]{1,0:T(4,128)(2,1)S(1)} %get-tuple-element.24), channel_id=1, source_target_pairs={{4,1},{5,2},{6,3},{8,5},{9,6},{10,7},{12,9},{13,10},{14,11},{16,13... | collective-permute-start | bytes 1544 | tf_op jit(solution)/shard_map/ppermute | solution.py:44
  15.4 28.7 %collective-permute-start.4 = (bf16[4,64]{1,0:T(4,128)(2,1)S(1)}, bf16[4,64]{1,0:T(4,128)(2,1)S(1)}, u32[]{:S(2)}, u32[]{:S(2)}) collective-permute-start(bf16[4,64]{1,0:T(4,128)(2,1)S(1)} %get-tuple-element.25), channel_id=1, source_target_pairs={{0,5},{1,6},{2,7},{4,9},{5,10},{6,11},{8,13},{9,14},{10,15},{12,17... | collective-permute-start | bytes 1544 | tf_op jit(solution)/shard_map/ppermute | solution.py:44
  17.3 36.9 %collective-permute-start.7 = (bf16[4,64]{1,0:T(4,128)(2,1)S(1)}, bf16[4,64]{1,0:T(4,128)(2,1)S(1)}, u32[]{:S(2)}, u32[]{:S(2)}) collective-permute-start(bf16[4,64]{1,0:T(4,128)(2,1)S(1)} %get-tuple-element.26), channel_id=1, source_target_pairs={{5,0},{6,1},{7,2},{9,4},{10,5},{11,6},{13,8},{14,9},{15,10},{17,12... | collective-permute-start | bytes 1544 | tf_op jit(solution)/shard_map/ppermute | solution.py:44
  26.2 36.0 %collective-permute-start.1 = (bf16[4,5120]{1,0:T(4,128)(2,1)S(1)}, bf16[4,5120]{1,0:T(4,128)(2,1)S(1)}, u32[]{:S(2)}, u32[]{:S(2)}) collective-permute-start(bf16[4,5120]{1,0:T(4,128)(2,1)S(1)} %get-tuple-element.29), channel_id=1, source_target_pairs={{4,0},{8,4},{12,8},{16,12},{20,16},{24,20},{28,24},{32,28},{36,32}... | collective-permute-start | bytes 122888 | tf_op jit(solution)/shard_map/ppermute | solution.py:34
  41.0 21.1 %collective-permute-start = (bf16[4,5120]{1,0:T(4,128)(2,1)S(1)}, bf16[4,5120]{1,0:T(4,128)(2,1)S(1)}, u32[]{:S(2)}, u32[]{:S(2)}) collective-permute-start(bf16[4,5120]{1,0:T(4,128)(2,1)S(1)} %get-tuple-element.30), channel_id=1, source_target_pairs={{0,4},{4,8},{8,12},{12,16},{16,20},{20,24},{24,28},{28,32},{32,36}... | collective-permute-start | bytes 122888 | tf_op jit(solution)/shard_map/ppermute | solution.py:34
  44.1 10.7 %collective-permute-start.3 = (bf16[256,64]{1,0:T(8,128)(2,1)S(1)}, bf16[256,64]{1,0:T(8,128)(2,1)S(1)}, u32[]{:S(2)}, u32[]{:S(2)}) collective-permute-start(bf16[256,64]{1,0:T(8,128)(2,1)S(1)} %get-tuple-element.27), channel_id=1, source_target_pairs={{1,0},{2,1},{3,2},{5,4},{6,5},{7,6},{9,8},{10,9},{11,10},{13,12},{... | collective-permute-start | bytes 98312 | tf_op jit(solution)/shard_map/ppermute | solution.py:216
  46.7 8.9 %collective-permute-start.2 = (bf16[256,64]{1,0:T(8,128)(2,1)S(1)}, bf16[256,64]{1,0:T(8,128)(2,1)S(1)}, u32[]{:S(2)}, u32[]{:S(2)}) collective-permute-start(bf16[256,64]{1,0:T(8,128)(2,1)S(1)} %get-tuple-element.28), channel_id=1, source_target_pairs={{0,1},{1,2},{2,3},{4,5},{5,6},{6,7},{8,9},{9,10},{10,11},{12,13},{... | collective-permute-start | bytes 98312 | tf_op jit(solution)/shard_map/ppermute | solution.py:215
  62.1 11.0 %copy-start.3 = (f32[256,2560]{1,0:T(8,128)S(1)}, f32[256,2560]{1,0:T(8,128)}, u32[]{:S(2)}) copy-start(f32[256,2560]{1,0:T(8,128)} %shard_map.39) | copy-start | bytes 7864324
  73.1 2.5 %copy-start.2 = (f32[256,2560]{1,0:T(8,128)S(1)}, f32[256,2560]{1,0:T(8,128)}, u32[]{:S(2)}) copy-start(f32[256,2560]{1,0:T(8,128)} %shard_map.37) | copy-start | bytes 7864324
  73.4 64.7 %copy-start.1 = (bf16[256,2560]{1,0:T(8,128)(2,1)}, bf16[256,2560]{1,0:T(8,128)(2,1)S(1)}, u32[]{:S(2)}) copy-start(bf16[256,2560]{1,0:T(8,128)(2,1)S(1)} %fusion.1.own_ref) | copy-start | bytes 3932164
  73.5 54.3 %collective-permute-start.12 = (bf16[256,2560]{1,0:T(8,128)(2,1)S(1)}, bf16[256,2560]{1,0:T(8,128)(2,1)S(1)}, u32[]{:S(2)}, u32[]{:S(2)}) collective-permute-start(bf16[256,2560]{1,0:T(8,128)(2,1)S(1)} %fusion.1.own_ref), channel_id=1, source_target_pairs={{0,4},{4,8},{8,12},{12,16},{16,20},{20,24},{24,28},{28,32},{32,36}... | collective-permute-start | bytes 3932168 | tf_op jit(solution)/shard_map/ppermute | solution.py:34
  76.0 63.3 %copy-start = (bf16[256,2560]{1,0:T(8,128)(2,1)}, bf16[256,2560]{1,0:T(8,128)(2,1)S(1)}, u32[]{:S(2)}) copy-start(bf16[256,2560]{1,0:T(8,128)(2,1)S(1)} %fusion.3.own_ref) | copy-start | bytes 3932164
  76.0 60.5 %collective-permute-start.11 = (bf16[256,2560]{1,0:T(8,128)(2,1)S(1)}, bf16[256,2560]{1,0:T(8,128)(2,1)S(1)}, u32[]{:S(2)}, u32[]{:S(2)}) collective-permute-start(bf16[256,2560]{1,0:T(8,128)(2,1)S(1)} %fusion.3.own_ref), channel_id=1, source_target_pairs={{0,4},{4,8},{8,12},{12,16},{16,20},{20,24},{24,28},{28,32},{32,36}... | collective-permute-start | bytes 3932168 | tf_op jit(solution)/shard_map/ppermute | solution.py:34
  79.0 11.2 %collective-permute-start.8 = (f32[128,256]{1,0:T(8,128)S(1)}, f32[128,256]{1,0:T(8,128)S(1)}, u32[]{:S(2)}, u32[]{:S(2)}) collective-permute-start(f32[128,256]{1,0:T(8,128)S(1)} %slice_select_fusion), channel_id=1, source_target_pairs={{0,1},{1,0},{2,3},{3,2},{4,5},{5,4},{6,7},{7,6},{8,9},{9,8},{10,11... | collective-permute-start | bytes 393224 | tf_op jit(solution)/shard_map/ppermute | solution.py:201
  79.2 48.5 %collective-permute-start.13 = (bf16[128,2560]{1,0:T(8,128)(2,1)S(1)}, bf16[128,2560]{1,0:T(8,128)(2,1)S(1)}, u32[]{:S(2)}, u32[]{:S(2)}) collective-permute-start(bf16[128,2560]{1,0:T(8,128)(2,1)S(1)} %slice.182), channel_id=1, source_target_pairs={{4,0},{8,4},{12,8},{16,12},{20,16},{24,20},{28,24},{32,28},{36,32}... | collective-permute-start | bytes 1966088 | tf_op jit(solution)/shard_map/ppermute | solution.py:34
  86.8 40.9 %collective-permute-start.14 = (bf16[128,2560]{1,0:T(8,128)(2,1)S(1)}, bf16[128,2560]{1,0:T(8,128)(2,1)S(1)}, u32[]{:S(2)}, u32[]{:S(2)}) collective-permute-start(bf16[128,2560]{1,0:T(8,128)(2,1)S(1)} %slice.183), channel_id=1, source_target_pairs={{4,0},{8,4},{12,8},{16,12},{20,16},{24,20},{28,24},{32,28},{36,32}... | collective-permute-start | bytes 1966088 | tf_op jit(solution)/shard_map/ppermute | solution.py:34
  90.2 35.5 %collective-permute-start.9 = (f32[128,256]{1,0:T(8,128)S(1)}, f32[128,256]{1,0:T(8,128)S(1)}, u32[]{:S(2)}, u32[]{:S(2)}) collective-permute-start(f32[128,256]{1,0:T(8,128)S(1)} %select_add_fusion.1), channel_id=1, source_target_pairs={{0,2},{1,3},{2,0},{3,1},{4,6},{5,7},{6,4},{7,5},{8,10},{9,11},{10,... | collective-permute-start | bytes 393224 | tf_op jit(solution)/shard_map/ppermute | solution.py:202
  125.7 2.0 collective-permute-start.10
  127.7 11.6 %copy-start.7 = (bf16[128,2560]{1,0:T(8,128)(2,1)}, bf16[128,2560]{1,0:T(8,128)(2,1)S(1)}, u32[]{:S(2)}) copy-start(bf16[128,2560]{1,0:T(8,128)(2,1)S(1)} %collective-permute-done.13.upper_ref) | copy-start | bytes 1966084
  127.7 10.4 %copy-start.6 = (bf16[128,2560]{1,0:T(8,128)(2,1)}, bf16[128,2560]{1,0:T(8,128)(2,1)S(1)}, u32[]{:S(2)}) copy-start(bf16[128,2560]{1,0:T(8,128)(2,1)S(1)} %collective-permute-done.14.upper_ref) | copy-start | bytes 1966084
  127.8 9.3 %copy-start.5 = (bf16[256,2560]{1,0:T(8,128)(2,1)}, bf16[256,2560]{1,0:T(8,128)(2,1)S(1)}, u32[]{:S(2)}) copy-start(bf16[256,2560]{1,0:T(8,128)(2,1)S(1)} %collective-permute-done.12.lower_ref) | copy-start | bytes 3932164
  136.5 1.1 copy-start.4
  137.6 1.1 slice-start.1
  138.7 1.1 slice-start
  140.5 1.6 collective-permute-start.16
  142.1 16.4 %collective-permute-start.17 = (f32[448,128]{1,0:T(8,128)S(1)}, f32[448,128]{1,0:T(8,128)S(1)}, u32[]{:S(2)}, u32[]{:S(2)}) collective-permute-start(f32[448,128]{1,0:T(8,128)S(1)} %select_add_fusion), channel_id=1, source_target_pairs={{0,2},{1,3},{2,0},{3,1},{4,6},{5,7},{6,4},{7,5},{8,10},{9,11},{10,... | collective-permute-start | bytes 688136 | tf_op jit(solution)/shard_map/ppermute | solution.py:202
  158.5 14.1 %collective-permute-start.18 = (f32[448,128]{1,0:T(8,128)S(1)}, f32[448,128]{1,0:T(8,128)S(1)}, u32[]{:S(2)}, u32[]{:S(2)}) collective-permute-start(f32[448,128]{1,0:T(8,128)S(1)} %add.47), channel_id=1, source_target_pairs={{0,1},{1,0},{2,3},{3,2},{4,5},{5,4},{6,7},{7,6},{8,9},{9,8},{10,11... | collective-permute-start | bytes 688136 | tf_op jit(solution)/shard_map/ppermute | solution.py:203
  159.6 17.5 %collective-permute-start.15 = (f32[256,256]{1,0:T(8,128)S(1)}, f32[256,256]{1,0:T(8,128)S(1)}, u32[]{:S(2)}, u32[]{:S(2)}) collective-permute-start(f32[256,256]{1,0:T(8,128)S(1)} %maximum_select_fusion.1), channel_id=1, source_target_pairs={{0,4},{4,8},{8,12},{12,16},{16,20},{20,24},{24,28},{28,32},{32,36}... | collective-permute-start | bytes 786440 | tf_op jit(solution)/shard_map/ppermute | solution.py:34
  161.5 12.2 %collective-permute-start.19 = (f32[128,128]{1,0:T(8,128)S(1)}, f32[128,128]{1,0:T(8,128)S(1)}, u32[]{:S(2)}, u32[]{:S(2)}) collective-permute-start(f32[128,128]{1,0:T(8,128)S(1)} %slice.190), channel_id=1, source_target_pairs={{4,0},{8,4},{12,8},{16,12},{20,16},{24,20},{28,24},{32,28},{36,32}... | collective-permute-start | bytes 196616 | tf_op jit(solution)/shard_map/ppermute | solution.py:34

commit v10 on v7

--- a/solution.py
+++ b/solution.py
@@ -45,40 +45,54 @@
     return lax.dot_general(a, b, (((1,), (1,)), ((), ())), preferred_element_type=jnp.float32)
 
 
-def orthonormal_rows(image, rows, lanes):
-    rank = image.shape[0]
-    gram_mat = lax.dot_general(
-        image, image, (((1,), (1,)), ((), ())), precision=lax.Precision.HIGHEST,
-        preferred_element_type=jnp.float32,
-    )
-    result = image
+def orthonormal_rows(images, rank, rows, lanes):
+    windows = len(images)
+    gram_mat = jnp.concatenate([
+        lax.dot_general(
+            image, image, (((1,), (1,)), ((), ())), precision=lax.Precision.HIGHEST,
+            preferred_element_type=jnp.float32,
+        )
+        for image in images
+    ], axis=0)
+    result = jnp.concatenate(images, axis=0)
+    local = rows % rank
+    owner = rows // rank
+
+    def pick(value, j):
+        picked = value[j : j + 1]
+        for number in range(1, windows):
+            at = number * rank + j
+            picked = jnp.where(owner == number, value[at : at + 1], picked)
+        return picked
+
     for j in range(rank):
         column = jnp.sum(jnp.where(lanes == j, gram_mat, 0.0), axis=1, keepdims=True)
-        scale = 1.0 / jnp.sqrt(column[j : j + 1, :])
+        scale = 1.0 / jnp.sqrt(pick(column, j))
         factor = column * scale
-        pivot_row = gram_mat[j : j + 1, :] * scale
-        image_row = result[j : j + 1, :] * scale
-        below = rows > j
+        pivot_row = pick(gram_mat, j) * scale
+        image_row = pick(result, j) * scale
+        below = local > j
         gram_mat = jnp.where(below, gram_mat - factor * pivot_row, gram_mat)
-        result = jnp.where(below, result - factor * image_row, jnp.where(rows == j, image_row, result))
-    return result
+        result = jnp.where(below, result - factor * image_row, jnp.where(local == j, image_row, result))
+    return [result[number * rank : (number + 1) * rank] for number in range(windows)]
 
 
 def subspace_kernel(band_ref, start_ref, out_ref):
     windows = out_ref.shape[0]
     rank, win = start_ref.shape
-    rows = lax.broadcasted_iota(jnp.int32, (rank, 1), 0)
-    lanes = lax.broadcasted_iota(jnp.int32, (rank, rank), 1)
+    rows = lax.broadcasted_iota(jnp.int32, (windows * rank, 1), 0)
+    lanes = lax.broadcasted_iota(jnp.int32, (windows * rank, rank), 1)
     bases = [start_ref[...] for _ in range(windows)]
     for sweep in range(ITERS):
+        images = []
         for number in range(windows):
             lo = number * STRIDE
             scatter_mat = band_ref[lo : lo + win, lo : lo + win]
-            image = jnp.dot(
+            images.append(jnp.dot(
                 bases[number], scatter_mat, precision=lax.Precision.HIGHEST,
                 preferred_element_type=jnp.float32,
-            )
-            bases[number] = orthonormal_rows(image, rows, lanes)
+            ))
+        bases = orthonormal_rows(images, rank, rows, lanes)
     for number in range(windows):
         out_ref[number] = bases[number].astype(out_ref.dtype)
 

time: 188 us -> 191 us (1.016)
  Pallas kernels: 40.6 us -> 43.2 us
    pallas_call x1, Pallas kernels: 17.1 us -> 19.7 us  [subspace(): pl.pallas_call(subspace_kernel, out_shape=jax.ShapeDtypeStruct((windows,)...]
where the time goes in v10:
time: 191 us; the launch traced here: 190 us
  waiting for transfers between devices  66.2 us (35%)
  starting transfers between devices  58 us (30%)
  Pallas kernels  43.2 us (23%)
  local copies, waits for them, and re-layouts  13.3 us (7%)
  other arithmetic  4.98 us (3%)
  matrix products  3.46 us (2%)
    ppermute x2, waiting for transfers between devices, ta_sum(): part = part + lax.ppermute(part, 'ta', across)  44.3 us
    ppermute x6, starting transfers between devices, shifted(): lax.ppermute(value, axis, [(source, source + steps) for source in range(f...  23.6 us
    pallas_call x1, Pallas kernels, subspace(): pl.pallas_call(subspace_kernel, out_shape=jax.ShapeDtypeStruct((windows,)...  19.7 us
    ppermute x6, waiting for transfers between devices, shifted(): lax.ppermute(value, axis, [(source, source + steps) for source in range(f...  17.6 us
    ppermute x2, starting transfers between devices, with_halo(): lax.ppermute(lax.slice_in_dim(block, 0, width, axis=dim), axis, backward)  14 us
    pallas_call x2, Pallas kernels, clean(): pl.pallas_call(clean_kernel, grid=(samples // width,), out_shape=jax.Shap...  11.8 us
    pallas_call x2, Pallas kernels, fir(): pl.pallas_call(kernel, grid=(length // width,), out_shape=jax.ShapeDtypeS...  11.7 us
    ppermute x1, starting transfers between devices, per_device(): lax.ppermute(raw[:, samples - half:], 'ta', forward)  6.89 us
  transfers between devices with their start and end apart: 18, of which 8 were waited for; matrix products, arithmetic and copies ran while one was open for 7% of the time, Pallas kernels for 3%

profile of v10, /device:TPU:97, one launch (start us, length us, event | category | flops | bytes accessed | tf_op | source)
XLA Modules:
  0.0 189.7 jit_solution(1003375956814316333)
XLA Ops:
  0.0 1.0 fusion.24
  1.0 2.6 %collective-permute-start.1 = (bf16[256,64]{1,0:T(8,128)(2,1)S(1)}, bf16[256,64]{1,0:T(8,128)(2,1)S(1)}, u32[]{:S(2)}, u32[]{:S(2)}) collective-permute-start(bf16[256,64]{1,0:T(8,128)(2,1)S(1)} %get-tuple-element.23), channel_id=1, source_target_pairs={{1,0},{2,1},{3,2},{5,4},{6,5},{7,6},{9,8},{10,9},{11,10},{13,12},{... | collective-permute-start | bytes 98312 | tf_op jit(solution)/shard_map/ppermute | solution.py:220
  3.6 6.9 %collective-permute-start = (bf16[256,64]{1,0:T(8,128)(2,1)S(1)}, bf16[256,64]{1,0:T(8,128)(2,1)S(1)}, u32[]{:S(2)}, u32[]{:S(2)}) collective-permute-start(bf16[256,64]{1,0:T(8,128)(2,1)S(1)} %get-tuple-element.24), channel_id=1, source_target_pairs={{0,1},{1,2},{2,3},{4,5},{5,6},{6,7},{8,9},{9,10},{10,11},{12,13},{... | collective-permute-start | bytes 98312 | tf_op jit(solution)/shard_map/ppermute | solution.py:219
  10.4 0.7 concatenate.67
  11.2 1.3 tile.10
  13.2 0.7 pad_slice_fusion
  13.9 1.5 slice.110.refs_0_.refs_1_
  15.4 0.8 slice.142.refs_6_
  16.2 5.9 %shard_map.37 = f32[256,2560]{1,0:T(8,128)} custom-call(bf16[256,128]{1,0:T(8,128)(2,1)} %slice.110.refs_0_.refs_1_, bf16[256,128]{1,0:T(8,128)(2,1)} %slice.110.refs_0_.refs_1_, bf16[256,5120]{1,0:T(8,128)(2,1)} %refs_4_.3, bf16[256,5120]{1,0:T(8,128)(2,1)} %refs_4_.3, bf16[256,5120]{1,0:T(8,128)(2,1)} %refs_4_.3, ...), custom_call_target="tpu_custom_call" | custom-call | tf_op jit(solution)/shard_map/pallas_call | solution.py:134
  22.1 0.6 concatenate.69.refs_1_
  22.8 0.7 concatenate.68.refs_0_
  23.5 5.8 %shard_map.38 = f32[256,2560]{1,0:T(8,128)} custom-call(bf16[256,128]{1,0:T(8,128)(2,1)} %concatenate.68.refs_0_, bf16[256,128]{1,0:T(8,128)(2,1)} %concatenate.69.refs_1_, bf16[256,5120]{1,0:T(8,128)(2,1)} %refs_4_.3, bf16[256,5120]{1,0:T(8,128)(2,1)} %refs_4_.3, bf16[256,5120]{1,0:T(8,128)(2,1)} %refs_4_.3, bf16[128,512]{1,0:T(8,128)(2,1)} %get-tuple-element.26.refs_5_, ...), custom_call_target="tpu_custom_call" | custom-call | tf_op jit(solution)/shard_map/pallas_call | solution.py:134
  29.3 0.9 fusion.23
  30.3 6.4 %collective-permute-start.4 = (f32[4,2560]{1,0:T(4,128)S(1)}, f32[4,2560]{1,0:T(4,128)S(1)}, u32[]{:S(2)}, u32[]{:S(2)}) collective-permute-start(f32[4,2560]{1,0:T(4,128)S(1)} %get-tuple-element.21), channel_id=1, source_target_pairs={{4,0},{8,4},{12,8},{16,12},{20,16},{24,20},{28,24},{32,28},{36,32}... | collective-permute-start | bytes 122888 | tf_op jit(solution)/shard_map/ppermute | solution.py:26
  36.7 1.9 %collective-permute-start.5 = (f32[4,2560]{1,0:T(4,128)S(1)}, f32[4,2560]{1,0:T(4,128)S(1)}, u32[]{:S(2)}, u32[]{:S(2)}) collective-permute-start(f32[4,2560]{1,0:T(4,128)S(1)} %get-tuple-element.22), channel_id=1, source_target_pairs={{0,4},{4,8},{8,12},{12,16},{16,20},{20,24},{24,28},{28,32},{32,36}... | collective-permute-start | bytes 122888 | tf_op jit(solution)/shard_map/ppermute | solution.py:23
  38.6 0.9 fusion.22
  39.6 7.6 %collective-permute-start.2 = (f32[4,2560]{1,0:T(4,128)S(1)}, f32[4,2560]{1,0:T(4,128)S(1)}, u32[]{:S(2)}, u32[]{:S(2)}) collective-permute-start(f32[4,2560]{1,0:T(4,128)S(1)} %get-tuple-element.19), channel_id=1, source_target_pairs={{4,0},{8,4},{12,8},{16,12},{20,16},{24,20},{28,24},{32,28},{36,32}... | collective-permute-start | bytes 122888 | tf_op jit(solution)/shard_map/ppermute | solution.py:26
  47.1 2.2 %collective-permute-start.3 = (f32[4,2560]{1,0:T(4,128)S(1)}, f32[4,2560]{1,0:T(4,128)S(1)}, u32[]{:S(2)}, u32[]{:S(2)}) collective-permute-start(f32[4,2560]{1,0:T(4,128)S(1)} %get-tuple-element.20), channel_id=1, source_target_pairs={{0,4},{4,8},{8,12},{12,16},{16,20},{20,24},{24,28},{28,32},{32,36}... | collective-permute-start | bytes 122888 | tf_op jit(solution)/shard_map/ppermute | solution.py:23
  49.4 3.1 %fusion.1.own_ref = bf16[256,2560]{1,0:T(8,128)(2,1)S(1)} fusion(f32[256,2560]{1,0:T(8,128)} %shard_map.38, f32[4,2560]{1,0:T(4,128)S(1)} %collective-permute-done.5, f32[4,2560]{1,0:T(4,128)S(1)} %collective-permute-done.4), kind=kLoop, calls=%fused_computation.2 | loop fusion | flops 2621440 | bytes 4014080 | tf_op jit(solution)/shard_map/convert_element_type | solution.py:238
  52.5 1.9 %collective-permute-start.10 = (bf16[256,2560]{1,0:T(8,128)(2,1)S(1)}, bf16[256,2560]{1,0:T(8,128)(2,1)S(1)}, u32[]{:S(2)}, u32[]{:S(2)}) collective-permute-start(bf16[256,2560]{1,0:T(8,128)(2,1)S(1)} %fusion.1.own_ref), channel_id=1, source_target_pairs={{0,4},{4,8},{8,12},{12,16},{16,20},{20,24},{24,28},{28,32},{32,36}... | collective-permute-start | bytes 3932168 | tf_op jit(solution)/shard_map/ppermute | solution.py:34
  54.4 1.9 %collective-permute-done.3 = f32[4,2560]{1,0:T(4,128)S(1)} collective-permute-done((f32[4,2560]{1,0:T(4,128)S(1)}, f32[4,2560]{1,0:T(4,128)S(1)}, u32[]{:S(2)}, u32[]{:S(2)}) %collective-permute-start.3) | collective-permute-done | bytes 40992 | tf_op jit(solution)/shard_map/ppermute | solution.py:23
  56.7 1.9 %collective-permute-start.9 = (bf16[256,2560]{1,0:T(8,128)(2,1)S(1)}, bf16[256,2560]{1,0:T(8,128)(2,1)S(1)}, u32[]{:S(2)}, u32[]{:S(2)}) collective-permute-start(bf16[256,2560]{1,0:T(8,128)(2,1)S(1)} %fusion.3.own_ref), channel_id=1, source_target_pairs={{0,4},{4,8},{8,12},{12,16},{16,20},{20,24},{24,28},{28,32},{32,36}... | collective-permute-start | bytes 3932168 | tf_op jit(solution)/shard_map/ppermute | solution.py:34
  58.7 0.5 fusion.27
  59.2 0.5 convolution_add_fusion.1
  60.0 7.6 %collective-permute-start.11 = (bf16[128,2560]{1,0:T(8,128)(2,1)S(1)}, bf16[128,2560]{1,0:T(8,128)(2,1)S(1)}, u32[]{:S(2)}, u32[]{:S(2)}) collective-permute-start(bf16[128,2560]{1,0:T(8,128)(2,1)S(1)} %slice.145), channel_id=1, source_target_pairs={{4,0},{8,4},{12,8},{16,12},{20,16},{24,20},{28,24},{32,28},{36,32}... | collective-permute-start | bytes 1966088 | tf_op jit(solution)/shard_map/ppermute | solution.py:34
  67.6 1.9 %collective-permute-start.12 = (bf16[128,2560]{1,0:T(8,128)(2,1)S(1)}, bf16[128,2560]{1,0:T(8,128)(2,1)S(1)}, u32[]{:S(2)}, u32[]{:S(2)}) collective-permute-start(bf16[128,2560]{1,0:T(8,128)(2,1)S(1)} %slice.146), channel_id=1, source_target_pairs={{4,0},{8,4},{12,8},{16,12},{20,16},{24,20},{28,24},{32,28},{36,32}... | collective-permute-start | bytes 1966088 | tf_op jit(solution)/shard_map/ppermute | solution.py:34
  69.5 2.9 %collective-permute-start.7 = (f32[128,256]{1,0:T(8,128)S(1)}, f32[128,256]{1,0:T(8,128)S(1)}, u32[]{:S(2)}, u32[]{:S(2)}) collective-permute-start(f32[128,256]{1,0:T(8,128)S(1)} %select_add_fusion.1), channel_id=1, source_target_pairs={{0,2},{1,3},{2,0},{3,1},{4,6},{5,7},{6,4},{7,5},{8,10},{9,11},{10,... | collective-permute-start | bytes 393224 | tf_op jit(solution)/shard_map/ppermute | solution.py:206
  72.5 30.1 %collective-permute-done.7 = f32[128,256]{1,0:T(8,128)S(1)} collective-permute-done((f32[128,256]{1,0:T(8,128)S(1)}, f32[128,256]{1,0:T(8,128)S(1)}, u32[]{:S(2)}, u32[]{:S(2)}) %collective-permute-start.7) | collective-permute-done | bytes 131104 | tf_op jit(solution)/shard_map/ppermute | solution.py:206
  102.6 1.1 collective-permute-start.8
  103.6 1.0 collective-permute-done.8
  104.7 13.5 %collective-permute-done.9.lower_ref = bf16[256,2560]{1,0:T(8,128)(2,1)S(1)} collective-permute-done((bf16[256,2560]{1,0:T(8,128)(2,1)S(1)}, bf16[256,2560]{1,0:T(8,128)(2,1)S(1)}, u32[]{:S(2)}, u32[]{:S(2)}) %collective-permute-start.9) | collective-permute-done | bytes 1310752 | tf_op jit(solution)/shard_map/ppermute | solution.py:34
  118.8 0.6 copy-done.3
  120.4 0.7 fusion.8
  121.5 0.7 fusion.16
  122.3 1.5 collective-permute-done.14
  123.8 1.7 collective-permute-start.15
  125.5 14.2 %collective-permute-done.15 = f32[448,128]{1,0:T(8,128)S(1)} collective-permute-done((f32[448,128]{1,0:T(8,128)S(1)}, f32[448,128]{1,0:T(8,128)S(1)}, u32[]{:S(2)}, u32[]{:S(2)}) %collective-permute-start.15) | collective-permute-done | bytes 229408 | tf_op jit(solution)/shard_map/ppermute | solution.py:206
  139.7 1.0 collective-permute-start.16
  140.7 1.9 %collective-permute-start.13 = (f32[256,256]{1,0:T(8,128)S(1)}, f32[256,256]{1,0:T(8,128)S(1)}, u32[]{:S(2)}, u32[]{:S(2)}) collective-permute-start(f32[256,256]{1,0:T(8,128)S(1)} %maximum_select_fusion.1), channel_id=1, source_target_pairs={{0,4},{4,8},{8,12},{12,16},{16,20},{20,24},{24,28},{28,32},{32,36}... | collective-permute-start | bytes 786440 | tf_op jit(solution)/shard_map/ppermute | solution.py:34
  142.6 8.4 %collective-permute-start.17 = (f32[128,128]{1,0:T(8,128)S(1)}, f32[128,128]{1,0:T(8,128)S(1)}, u32[]{:S(2)}, u32[]{:S(2)}) collective-permute-start(f32[128,128]{1,0:T(8,128)S(1)} %slice.153), channel_id=1, source_target_pairs={{4,0},{8,4},{12,8},{16,12},{20,16},{24,20},{28,24},{32,28},{36,32}... | collective-permute-start | bytes 196616 | tf_op jit(solution)/shard_map/ppermute | solution.py:34
  151.5 0.7 collective-permute-done.17
  152.1 3.4 %collective-permute-done.13 = f32[256,256]{1,0:T(8,128)S(1)} collective-permute-done((f32[256,256]{1,0:T(8,128)S(1)}, f32[256,256]{1,0:T(8,128)S(1)}, u32[]{:S(2)}, u32[]{:S(2)}) %collective-permute-start.13) | collective-permute-done | bytes 262176 | tf_op jit(solution)/shard_map/ppermute | solution.py:34
  155.5 1.3 fusion.14.band_ref
  156.8 19.7 %shard_map.39.basis_ref = bf16[2,16,512]{2,1,0:T(8,128)(2,1)} custom-call(f32[640,640]{1,0:T(8,128)} %fusion.14.band_ref, f32[16,512]{1,0:T(8,128)} %bitcast.23), custom_call_target="tpu_custom_call" | custom-call | tf_op jit(solution)/shard_map/pallas_call | solution.py:101
  176.5 0.7 slice.154
  177.2 0.7 copy.13
  178.0 5.9 %shard_map.40.rest_0_ = bf16[256,5120]{1,0:T(8,128)(2,1)} custom-call(bf16[256,2560]{1,0:T(8,128)(2,1)} %copy-done.3, bf16[256,2560]{1,0:T(8,128)(2,1)} %copy-done, bf16[128,2560]{1,0:T(8,128)(2,1)} %copy-done.6, bf16[2,16,512]{2,1,0:T(8,128)(2,1)} %shard_map.39.basis_ref, bf16[2,128,16]{2,1,0:T(8,128)(2,1)} %bitcast.21), custom_call_target="tpu_custom_call" | custom-call | tf_op jit(solution)/shard_map/pallas_call | solution.py:178
  183.8 5.9 %shard_map.41 = bf16[256,5120]{1,0:T(8,128)(2,1)} custom-call(bf16[256,2560]{1,0:T(8,128)(2,1)} %copy-done.4, bf16[256,2560]{1,0:T(8,128)(2,1)} %copy-done.1, bf16[128,2560]{1,0:T(8,128)(2,1)} %copy-done.5, bf16[2,16,512]{2,1,0:T(8,128)(2,1)} %shard_map.39.basis_ref, bf16[2,128,16]{2,1,0:T(8,128)(2,1)} %bitcast.22, ...), custom_call_target="tpu_custom_call", output_to_operand_aliasing={{}: (5, {})} | custom-call | tf_op jit(solution)/shard_map/pallas_call | solution.py:178
  (55 shorter events, 4.1 us)
Async XLA Ops:
  1.0 21.2 %collective-permute-start.1 = (bf16[256,64]{1,0:T(8,128)(2,1)S(1)}, bf16[256,64]{1,0:T(8,128)(2,1)S(1)}, u32[]{:S(2)}, u32[]{:S(2)}) collective-permute-start(bf16[256,64]{1,0:T(8,128)(2,1)S(1)} %get-tuple-element.23), channel_id=1, source_target_pairs={{1,0},{2,1},{3,2},{5,4},{6,5},{7,6},{9,8},{10,9},{11,10},{13,12},{... | collective-permute-start | bytes 98312 | tf_op jit(solution)/shard_map/ppermute | solution.py:220
  3.6 19.2 %collective-permute-start = (bf16[256,64]{1,0:T(8,128)(2,1)S(1)}, bf16[256,64]{1,0:T(8,128)(2,1)S(1)}, u32[]{:S(2)}, u32[]{:S(2)}) collective-permute-start(bf16[256,64]{1,0:T(8,128)(2,1)S(1)} %get-tuple-element.24), channel_id=1, source_target_pairs={{0,1},{1,2},{2,3},{4,5},{5,6},{6,7},{8,9},{9,10},{10,11},{12,13},{... | collective-permute-start | bytes 98312 | tf_op jit(solution)/shard_map/ppermute | solution.py:219
  30.3 19.1 %collective-permute-start.4 = (f32[4,2560]{1,0:T(4,128)S(1)}, f32[4,2560]{1,0:T(4,128)S(1)}, u32[]{:S(2)}, u32[]{:S(2)}) collective-permute-start(f32[4,2560]{1,0:T(4,128)S(1)} %get-tuple-element.21), channel_id=1, source_target_pairs={{4,0},{8,4},{12,8},{16,12},{20,16},{24,20},{28,24},{32,28},{36,32}... | collective-permute-start | bytes 122888 | tf_op jit(solution)/shard_map/ppermute | solution.py:26
  36.7 12.7 %collective-permute-start.5 = (f32[4,2560]{1,0:T(4,128)S(1)}, f32[4,2560]{1,0:T(4,128)S(1)}, u32[]{:S(2)}, u32[]{:S(2)}) collective-permute-start(f32[4,2560]{1,0:T(4,128)S(1)} %get-tuple-element.22), channel_id=1, source_target_pairs={{0,4},{4,8},{8,12},{12,16},{16,20},{20,24},{24,28},{28,32},{32,36}... | collective-permute-start | bytes 122888 | tf_op jit(solution)/shard_map/ppermute | solution.py:23
  39.6 14.9 %collective-permute-start.2 = (f32[4,2560]{1,0:T(4,128)S(1)}, f32[4,2560]{1,0:T(4,128)S(1)}, u32[]{:S(2)}, u32[]{:S(2)}) collective-permute-start(f32[4,2560]{1,0:T(4,128)S(1)} %get-tuple-element.19), channel_id=1, source_target_pairs={{4,0},{8,4},{12,8},{16,12},{20,16},{24,20},{28,24},{32,28},{36,32}... | collective-permute-start | bytes 122888 | tf_op jit(solution)/shard_map/ppermute | solution.py:26
  47.1 9.2 %copy-start.2 = (f32[256,2560]{1,0:T(8,128)S(1)}, f32[256,2560]{1,0:T(8,128)}, u32[]{:S(2)}) copy-start(f32[256,2560]{1,0:T(8,128)} %shard_map.37) | copy-start | bytes 7864324
  47.1 9.2 %collective-permute-start.3 = (f32[4,2560]{1,0:T(4,128)S(1)}, f32[4,2560]{1,0:T(4,128)S(1)}, u32[]{:S(2)}, u32[]{:S(2)}) collective-permute-start(f32[4,2560]{1,0:T(4,128)S(1)} %get-tuple-element.20), channel_id=1, source_target_pairs={{0,4},{4,8},{8,12},{12,16},{16,20},{20,24},{24,28},{28,32},{32,36}... | collective-permute-start | bytes 122888 | tf_op jit(solution)/shard_map/ppermute | solution.py:23
  52.5 67.4 %copy-start.1 = (bf16[256,2560]{1,0:T(8,128)(2,1)}, bf16[256,2560]{1,0:T(8,128)(2,1)S(1)}, u32[]{:S(2)}) copy-start(bf16[256,2560]{1,0:T(8,128)(2,1)S(1)} %fusion.1.own_ref) | copy-start | bytes 3932164
  52.5 52.2 %collective-permute-start.10 = (bf16[256,2560]{1,0:T(8,128)(2,1)S(1)}, bf16[256,2560]{1,0:T(8,128)(2,1)S(1)}, u32[]{:S(2)}, u32[]{:S(2)}) collective-permute-start(bf16[256,2560]{1,0:T(8,128)(2,1)S(1)} %fusion.1.own_ref), channel_id=1, source_target_pairs={{0,4},{4,8},{8,12},{12,16},{16,20},{20,24},{24,28},{28,32},{32,36}... | collective-permute-start | bytes 3932168 | tf_op jit(solution)/shard_map/ppermute | solution.py:34
  56.7 64.4 %copy-start = (bf16[256,2560]{1,0:T(8,128)(2,1)}, bf16[256,2560]{1,0:T(8,128)(2,1)S(1)}, u32[]{:S(2)}) copy-start(bf16[256,2560]{1,0:T(8,128)(2,1)S(1)} %fusion.3.own_ref) | copy-start | bytes 3932164
  56.7 61.5 %collective-permute-start.9 = (bf16[256,2560]{1,0:T(8,128)(2,1)S(1)}, bf16[256,2560]{1,0:T(8,128)(2,1)S(1)}, u32[]{:S(2)}, u32[]{:S(2)}) collective-permute-start(bf16[256,2560]{1,0:T(8,128)(2,1)S(1)} %fusion.3.own_ref), channel_id=1, source_target_pairs={{0,4},{4,8},{8,12},{12,16},{16,20},{20,24},{24,28},{28,32},{32,36}... | collective-permute-start | bytes 3932168 | tf_op jit(solution)/shard_map/ppermute | solution.py:34
  59.8 9.7 %collective-permute-start.6 = (f32[128,256]{1,0:T(8,128)S(1)}, f32[128,256]{1,0:T(8,128)S(1)}, u32[]{:S(2)}, u32[]{:S(2)}) collective-permute-start(f32[128,256]{1,0:T(8,128)S(1)} %slice_select_fusion), channel_id=1, source_target_pairs={{0,1},{1,0},{2,3},{3,2},{4,5},{5,4},{6,7},{7,6},{8,9},{9,8},{10,11... | collective-permute-start | bytes 393224 | tf_op jit(solution)/shard_map/ppermute | solution.py:205
  60.0 44.7 %collective-permute-start.11 = (bf16[128,2560]{1,0:T(8,128)(2,1)S(1)}, bf16[128,2560]{1,0:T(8,128)(2,1)S(1)}, u32[]{:S(2)}, u32[]{:S(2)}) collective-permute-start(bf16[128,2560]{1,0:T(8,128)(2,1)S(1)} %slice.145), channel_id=1, source_target_pairs={{4,0},{8,4},{12,8},{16,12},{20,16},{24,20},{28,24},{32,28},{36,32}... | collective-permute-start | bytes 1966088 | tf_op jit(solution)/shard_map/ppermute | solution.py:34
  67.6 37.1 %collective-permute-start.12 = (bf16[128,2560]{1,0:T(8,128)(2,1)S(1)}, bf16[128,2560]{1,0:T(8,128)(2,1)S(1)}, u32[]{:S(2)}, u32[]{:S(2)}) collective-permute-start(bf16[128,2560]{1,0:T(8,128)(2,1)S(1)} %slice.146), channel_id=1, source_target_pairs={{4,0},{8,4},{12,8},{16,12},{20,16},{24,20},{28,24},{32,28},{36,32}... | collective-permute-start | bytes 1966088 | tf_op jit(solution)/shard_map/ppermute | solution.py:34
  69.5 33.0 %collective-permute-start.7 = (f32[128,256]{1,0:T(8,128)S(1)}, f32[128,256]{1,0:T(8,128)S(1)}, u32[]{:S(2)}, u32[]{:S(2)}) collective-permute-start(f32[128,256]{1,0:T(8,128)S(1)} %select_add_fusion.1), channel_id=1, source_target_pairs={{0,2},{1,3},{2,0},{3,1},{4,6},{5,7},{6,4},{7,5},{8,10},{9,11},{10,... | collective-permute-start | bytes 393224 | tf_op jit(solution)/shard_map/ppermute | solution.py:206
  102.6 2.0 %collective-permute-start.8 = (f32[128,256]{1,0:T(8,128)S(1)}, f32[128,256]{1,0:T(8,128)S(1)}, u32[]{:S(2)}, u32[]{:S(2)}) collective-permute-start(f32[128,256]{1,0:T(8,128)S(1)} %add.39), channel_id=1, source_target_pairs={{0,1},{1,0},{2,3},{3,2},{4,5},{5,4},{6,7},{7,6},{8,9},{9,8},{10,11... | collective-permute-start | bytes 393224 | tf_op jit(solution)/shard_map/ppermute | solution.py:207
  104.7 16.4 %copy-start.6 = (bf16[128,2560]{1,0:T(8,128)(2,1)}, bf16[128,2560]{1,0:T(8,128)(2,1)S(1)}, u32[]{:S(2)}) copy-start(bf16[128,2560]{1,0:T(8,128)(2,1)S(1)} %collective-permute-done.11.upper_ref) | copy-start | bytes 1966084
  104.7 15.2 %copy-start.5 = (bf16[128,2560]{1,0:T(8,128)(2,1)}, bf16[128,2560]{1,0:T(8,128)(2,1)S(1)}, u32[]{:S(2)}) copy-start(bf16[128,2560]{1,0:T(8,128)(2,1)S(1)} %collective-permute-done.12.upper_ref) | copy-start | bytes 1966084
  104.7 14.0 %copy-start.4 = (bf16[256,2560]{1,0:T(8,128)(2,1)}, bf16[256,2560]{1,0:T(8,128)(2,1)S(1)}, u32[]{:S(2)}) copy-start(bf16[256,2560]{1,0:T(8,128)(2,1)S(1)} %collective-permute-done.10.lower_ref) | copy-start | bytes 3932164
  118.2 1.1 copy-start.3
  119.3 1.1 slice-start.1
  120.4 1.1 slice-start
  122.2 1.6 collective-permute-start.14
  123.8 15.9 %collective-permute-start.15 = (f32[448,128]{1,0:T(8,128)S(1)}, f32[448,128]{1,0:T(8,128)S(1)}, u32[]{:S(2)}, u32[]{:S(2)}) collective-permute-start(f32[448,128]{1,0:T(8,128)S(1)} %select_add_fusion), channel_id=1, source_target_pairs={{0,2},{1,3},{2,0},{3,1},{4,6},{5,7},{6,4},{7,5},{8,10},{9,11},{10,... | collective-permute-start | bytes 688136 | tf_op jit(solution)/shard_map/ppermute | solution.py:206
  139.7 11.3 %collective-permute-start.16 = (f32[448,128]{1,0:T(8,128)S(1)}, f32[448,128]{1,0:T(8,128)S(1)}, u32[]{:S(2)}, u32[]{:S(2)}) collective-permute-start(f32[448,128]{1,0:T(8,128)S(1)} %add.43), channel_id=1, source_target_pairs={{0,1},{1,0},{2,3},{3,2},{4,5},{5,4},{6,7},{7,6},{8,9},{9,8},{10,11... | collective-permute-start | bytes 688136 | tf_op jit(solution)/shard_map/ppermute | solution.py:207
  140.7 14.8 %collective-permute-start.13 = (f32[256,256]{1,0:T(8,128)S(1)}, f32[256,256]{1,0:T(8,128)S(1)}, u32[]{:S(2)}, u32[]{:S(2)}) collective-permute-start(f32[256,256]{1,0:T(8,128)S(1)} %maximum_select_fusion.1), channel_id=1, source_target_pairs={{0,4},{4,8},{8,12},{12,16},{16,20},{20,24},{24,28},{28,32},{32,36}... | collective-permute-start | bytes 786440 | tf_op jit(solution)/shard_map/ppermute | solution.py:34
  142.6 9.5 %collective-permute-start.17 = (f32[128,128]{1,0:T(8,128)S(1)}, f32[128,128]{1,0:T(8,128)S(1)}, u32[]{:S(2)}, u32[]{:S(2)}) collective-permute-start(f32[128,128]{1,0:T(8,128)S(1)} %slice.153), channel_id=1, source_target_pairs={{4,0},{8,4},{12,8},{16,12},{20,16},{24,20},{28,24},{32,28},{36,32}... | collective-permute-start | bytes 196616 | tf_op jit(solution)/shard_map/ppermute | solution.py:34

commit v11 on v7

--- a/solution.py
+++ b/solution.py
@@ -138,22 +138,37 @@
 def clean_kernel(lower_ref, own_ref, upper_ref, basis_ref, middle_ref, *rest):
     out_ref = rest[-1]
     tiles = own_ref.shape[0] // STRIDE
+    rank = middle_ref.shape[2]
+    span = WIN // STRIDE
     parts = [lower_ref[k * STRIDE : (k + 1) * STRIDE] for k in range(2)]
     parts += [own_ref[k * STRIDE : (k + 1) * STRIDE] for k in range(tiles)]
     parts.append(upper_ref[...])
+    coeffs = [None] * tiles
+    for k in range(len(parts)):
+        users = [number for number in range(tiles) if number <= k < number + span]
+        product = jnp.dot(basis_ref[k, : len(users) * rank], parts[k], preferred_element_type=jnp.float32)
+        for slot, number in enumerate(users):
+            piece = product[slot * rank : (slot + 1) * rank]
+            coeffs[number] = piece if coeffs[number] is None else coeffs[number] + piece
     for number in range(tiles):
-        coeffs = jnp.dot(basis_ref[number, :, 0:STRIDE], parts[number], preferred_element_type=jnp.float32)
-        for k in range(1, WIN // STRIDE):
-            coeffs = coeffs + jnp.dot(
-                basis_ref[number, :, k * STRIDE : (k + 1) * STRIDE], parts[number + k],
-                preferred_element_type=jnp.float32,
-            )
         fitted = jnp.dot(
-            middle_ref[number], coeffs.astype(jnp.bfloat16), preferred_element_type=jnp.float32
+            middle_ref[number], coeffs[number].astype(jnp.bfloat16), preferred_element_type=jnp.float32
         )
         out_ref[number * STRIDE : (number + 1) * STRIDE] = (
             parts[number + 2].astype(jnp.float32) - fitted
         ).astype(out_ref.dtype)
+
+
+def stack_basis(rounded):
+    windows, rank, win = rounded.shape
+    span = win // STRIDE
+    stacks = []
+    for k in range(windows + span - 1):
+        users = [number for number in range(windows) if number <= k < number + span]
+        rows = [rounded[number, :, (k - number) * STRIDE : (k - number + 1) * STRIDE] for number in users]
+        rows += [jnp.zeros((rank, STRIDE), rounded.dtype)] * (min(windows, span) - len(users))
+        stacks.append(jnp.concatenate(rows, axis=0))
+    return jnp.stack(stacks)
 
 
 def clean(lower, own, upper, rounded, total, start, into):
@@ -161,6 +176,7 @@
     width = math.gcd(math.gcd(samples, start) if start else samples, 512)
     first = start // width
     middle = jnp.swapaxes(rounded[:, :, 2 * STRIDE : 3 * STRIDE], 1, 2)
+    stacked = stack_basis(rounded)
     return pl.pallas_call(
         clean_kernel,
         grid=(samples // width,),
@@ -169,12 +185,12 @@
             pl.BlockSpec((lower.shape[0], width), lambda b: (0, b)),
             pl.BlockSpec((chans, width), lambda b: (0, b)),
             pl.BlockSpec((STRIDE, width), lambda b: (0, b)),
-            pl.BlockSpec(rounded.shape, lambda b: (0, 0, 0)),
+            pl.BlockSpec(stacked.shape, lambda b: (0, 0, 0)),
             pl.BlockSpec(middle.shape, lambda b: (0, 0, 0)),
         ] + ([] if into is None else [pl.BlockSpec(memory_space=pl.ANY)]),
         out_specs=pl.BlockSpec((chans, width), lambda b: (0, (b + first) % (total // width))),
         input_output_aliases={} if into is None else {5: 0},
-    )(lower, own, upper, rounded, middle, *([] if into is None else [into]))
+    )(lower, own, upper, stacked, middle, *([] if into is None else [into]))
 
 
 def ta_sum(value):

time: 188 us -> 189 us (level)
  no operation moved by 1% of the time
where the time goes in v11:
time: 189 us; the launch traced here: 188 us
  waiting for transfers between devices  66.2 us (35%)
  starting transfers between devices  58 us (31%)
  Pallas kernels  39.7 us (21%)
  local copies, waits for them, and re-layouts  14.7 us (8%)
  other arithmetic  5 us (3%)
  matrix products  3.47 us (2%)
    ppermute x2, waiting for transfers between devices, ta_sum(): part = part + lax.ppermute(part, 'ta', across)  44.3 us
    ppermute x6, starting transfers between devices, shifted(): lax.ppermute(value, axis, [(source, source + steps) for source in range(f...  23.6 us
    ppermute x6, waiting for transfers between devices, shifted(): lax.ppermute(value, axis, [(source, source + steps) for source in range(f...  17.6 us
    pallas_call x1, Pallas kernels, subspace(): pl.pallas_call(subspace_kernel, out_shape=jax.ShapeDtypeStruct((windows,)...  17.1 us
    ppermute x2, starting transfers between devices, with_halo(): lax.ppermute(lax.slice_in_dim(block, 0, width, axis=dim), axis, backward)  14 us
    pallas_call x2, Pallas kernels, fir(): pl.pallas_call(kernel, grid=(length // width,), out_shape=jax.ShapeDtypeS...  11.7 us
    pallas_call x2, Pallas kernels, clean(): pl.pallas_call(clean_kernel, grid=(samples // width,), out_shape=jax.Shap...  10.8 us
    ppermute x1, starting transfers between devices, per_device(): lax.ppermute(raw[:, samples - half:], 'ta', forward)  6.89 us
  transfers between devices with their start and end apart: 18, of which 8 were waited for; matrix products, arithmetic and copies ran while one was open for 7% of the time, Pallas kernels for 3%

profile of v11, /device:TPU:97, one launch (start us, length us, event | category | flops | bytes accessed | tf_op | source)
XLA Modules:
  0.0 187.6 jit_solution(4012412322153071745)
XLA Ops:
  0.0 1.0 fusion.24
  1.0 2.6 %collective-permute-start.1 = (bf16[256,64]{1,0:T(8,128)(2,1)S(1)}, bf16[256,64]{1,0:T(8,128)(2,1)S(1)}, u32[]{:S(2)}, u32[]{:S(2)}) collective-permute-start(bf16[256,64]{1,0:T(8,128)(2,1)S(1)} %get-tuple-element.23), channel_id=1, source_target_pairs={{1,0},{2,1},{3,2},{5,4},{6,5},{7,6},{9,8},{10,9},{11,10},{13,12},{... | collective-permute-start | bytes 98312 | tf_op jit(solution)/shard_map/ppermute | solution.py:222
  3.6 6.9 %collective-permute-start = (bf16[256,64]{1,0:T(8,128)(2,1)S(1)}, bf16[256,64]{1,0:T(8,128)(2,1)S(1)}, u32[]{:S(2)}, u32[]{:S(2)}) collective-permute-start(bf16[256,64]{1,0:T(8,128)(2,1)S(1)} %get-tuple-element.24), channel_id=1, source_target_pairs={{0,1},{1,2},{2,3},{4,5},{5,6},{6,7},{8,9},{9,10},{10,11},{12,13},{... | collective-permute-start | bytes 98312 | tf_op jit(solution)/shard_map/ppermute | solution.py:221
  10.4 0.7 concatenate.87
  11.2 1.3 tile.10
  13.2 0.7 pad_slice_fusion
  13.9 1.5 slice.142.refs_0_.refs_1_
  15.4 0.8 slice.182.refs_6_
  16.2 5.9 %shard_map.37 = f32[256,2560]{1,0:T(8,128)} custom-call(bf16[256,128]{1,0:T(8,128)(2,1)} %slice.142.refs_0_.refs_1_, bf16[256,128]{1,0:T(8,128)(2,1)} %slice.142.refs_0_.refs_1_, bf16[256,5120]{1,0:T(8,128)(2,1)} %refs_4_.3, bf16[256,5120]{1,0:T(8,128)(2,1)} %refs_4_.3, bf16[256,5120]{1,0:T(8,128)(2,1)} %refs_4_.3, ...), custom_call_target="tpu_custom_call" | custom-call | tf_op jit(solution)/shard_map/pallas_call | solution.py:120
  22.1 0.6 concatenate.89.refs_1_
  22.8 0.7 concatenate.88.refs_0_
  23.5 5.8 %shard_map.38 = f32[256,2560]{1,0:T(8,128)} custom-call(bf16[256,128]{1,0:T(8,128)(2,1)} %concatenate.88.refs_0_, bf16[256,128]{1,0:T(8,128)(2,1)} %concatenate.89.refs_1_, bf16[256,5120]{1,0:T(8,128)(2,1)} %refs_4_.3, bf16[256,5120]{1,0:T(8,128)(2,1)} %refs_4_.3, bf16[256,5120]{1,0:T(8,128)(2,1)} %refs_4_.3, bf16[128,512]{1,0:T(8,128)(2,1)} %get-tuple-element.26.refs_5_, ...), custom_call_target="tpu_custom_call" | custom-call | tf_op jit(solution)/shard_map/pallas_call | solution.py:120
  29.3 0.9 fusion.23
  30.3 6.4 %collective-permute-start.4 = (f32[4,2560]{1,0:T(4,128)S(1)}, f32[4,2560]{1,0:T(4,128)S(1)}, u32[]{:S(2)}, u32[]{:S(2)}) collective-permute-start(f32[4,2560]{1,0:T(4,128)S(1)} %get-tuple-element.21), channel_id=1, source_target_pairs={{4,0},{8,4},{12,8},{16,12},{20,16},{24,20},{28,24},{32,28},{36,32}... | collective-permute-start | bytes 122888 | tf_op jit(solution)/shard_map/ppermute | solution.py:26
  36.7 1.9 %collective-permute-start.5 = (f32[4,2560]{1,0:T(4,128)S(1)}, f32[4,2560]{1,0:T(4,128)S(1)}, u32[]{:S(2)}, u32[]{:S(2)}) collective-permute-start(f32[4,2560]{1,0:T(4,128)S(1)} %get-tuple-element.22), channel_id=1, source_target_pairs={{0,4},{4,8},{8,12},{12,16},{16,20},{20,24},{24,28},{28,32},{32,36}... | collective-permute-start | bytes 122888 | tf_op jit(solution)/shard_map/ppermute | solution.py:23
  38.6 0.9 fusion.22
  39.6 7.6 %collective-permute-start.2 = (f32[4,2560]{1,0:T(4,128)S(1)}, f32[4,2560]{1,0:T(4,128)S(1)}, u32[]{:S(2)}, u32[]{:S(2)}) collective-permute-start(f32[4,2560]{1,0:T(4,128)S(1)} %get-tuple-element.19), channel_id=1, source_target_pairs={{4,0},{8,4},{12,8},{16,12},{20,16},{24,20},{28,24},{32,28},{36,32}... | collective-permute-start | bytes 122888 | tf_op jit(solution)/shard_map/ppermute | solution.py:26
  47.2 2.2 %collective-permute-start.3 = (f32[4,2560]{1,0:T(4,128)S(1)}, f32[4,2560]{1,0:T(4,128)S(1)}, u32[]{:S(2)}, u32[]{:S(2)}) collective-permute-start(f32[4,2560]{1,0:T(4,128)S(1)} %get-tuple-element.20), channel_id=1, source_target_pairs={{0,4},{4,8},{8,12},{12,16},{16,20},{20,24},{24,28},{28,32},{32,36}... | collective-permute-start | bytes 122888 | tf_op jit(solution)/shard_map/ppermute | solution.py:23
  49.4 3.1 %fusion.1.own_ref = bf16[256,2560]{1,0:T(8,128)(2,1)S(1)} fusion(f32[256,2560]{1,0:T(8,128)} %shard_map.38, f32[4,2560]{1,0:T(4,128)S(1)} %collective-permute-done.5, f32[4,2560]{1,0:T(4,128)S(1)} %collective-permute-done.4), kind=kLoop, calls=%fused_computation.2 | loop fusion | flops 2621440 | bytes 4014080 | tf_op jit(solution)/shard_map/convert_element_type | solution.py:240
  52.5 1.9 %collective-permute-start.10 = (bf16[256,2560]{1,0:T(8,128)(2,1)S(1)}, bf16[256,2560]{1,0:T(8,128)(2,1)S(1)}, u32[]{:S(2)}, u32[]{:S(2)}) collective-permute-start(bf16[256,2560]{1,0:T(8,128)(2,1)S(1)} %fusion.1.own_ref), channel_id=1, source_target_pairs={{0,4},{4,8},{8,12},{12,16},{16,20},{20,24},{24,28},{28,32},{32,36}... | collective-permute-start | bytes 3932168 | tf_op jit(solution)/shard_map/ppermute | solution.py:34
  54.4 1.9 %collective-permute-done.3 = f32[4,2560]{1,0:T(4,128)S(1)} collective-permute-done((f32[4,2560]{1,0:T(4,128)S(1)}, f32[4,2560]{1,0:T(4,128)S(1)}, u32[]{:S(2)}, u32[]{:S(2)}) %collective-permute-start.3) | collective-permute-done | bytes 40992 | tf_op jit(solution)/shard_map/ppermute | solution.py:23
  56.7 1.9 %collective-permute-start.9 = (bf16[256,2560]{1,0:T(8,128)(2,1)S(1)}, bf16[256,2560]{1,0:T(8,128)(2,1)S(1)}, u32[]{:S(2)}, u32[]{:S(2)}) collective-permute-start(bf16[256,2560]{1,0:T(8,128)(2,1)S(1)} %fusion.3.own_ref), channel_id=1, source_target_pairs={{0,4},{4,8},{8,12},{12,16},{16,20},{20,24},{24,28},{28,32},{32,36}... | collective-permute-start | bytes 3932168 | tf_op jit(solution)/shard_map/ppermute | solution.py:34
  60.0 7.6 %collective-permute-start.11 = (bf16[128,2560]{1,0:T(8,128)(2,1)S(1)}, bf16[128,2560]{1,0:T(8,128)(2,1)S(1)}, u32[]{:S(2)}, u32[]{:S(2)}) collective-permute-start(bf16[128,2560]{1,0:T(8,128)(2,1)S(1)} %slice.185), channel_id=1, source_target_pairs={{4,0},{8,4},{12,8},{16,12},{20,16},{24,20},{28,24},{32,28},{36,32}... | collective-permute-start | bytes 1966088 | tf_op jit(solution)/shard_map/ppermute | solution.py:34
  67.6 1.9 %collective-permute-start.12 = (bf16[128,2560]{1,0:T(8,128)(2,1)S(1)}, bf16[128,2560]{1,0:T(8,128)(2,1)S(1)}, u32[]{:S(2)}, u32[]{:S(2)}) collective-permute-start(bf16[128,2560]{1,0:T(8,128)(2,1)S(1)} %slice.186), channel_id=1, source_target_pairs={{4,0},{8,4},{12,8},{16,12},{20,16},{24,20},{28,24},{32,28},{36,32}... | collective-permute-start | bytes 1966088 | tf_op jit(solution)/shard_map/ppermute | solution.py:34
  69.5 2.9 %collective-permute-start.7 = (f32[128,256]{1,0:T(8,128)S(1)}, f32[128,256]{1,0:T(8,128)S(1)}, u32[]{:S(2)}, u32[]{:S(2)}) collective-permute-start(f32[128,256]{1,0:T(8,128)S(1)} %select_add_fusion.1), channel_id=1, source_target_pairs={{0,2},{1,3},{2,0},{3,1},{4,6},{5,7},{6,4},{7,5},{8,10},{9,11},{10,... | collective-permute-start | bytes 393224 | tf_op jit(solution)/shard_map/ppermute | solution.py:208
  72.5 30.1 %collective-permute-done.7 = f32[128,256]{1,0:T(8,128)S(1)} collective-permute-done((f32[128,256]{1,0:T(8,128)S(1)}, f32[128,256]{1,0:T(8,128)S(1)}, u32[]{:S(2)}, u32[]{:S(2)}) %collective-permute-start.7) | collective-permute-done | bytes 131104 | tf_op jit(solution)/shard_map/ppermute | solution.py:208
  102.6 1.1 collective-permute-start.8
  103.6 1.0 collective-permute-done.8
  104.7 13.5 %collective-permute-done.9.lower_ref = bf16[256,2560]{1,0:T(8,128)(2,1)S(1)} collective-permute-done((bf16[256,2560]{1,0:T(8,128)(2,1)S(1)}, bf16[256,2560]{1,0:T(8,128)(2,1)S(1)}, u32[]{:S(2)}, u32[]{:S(2)}) %collective-permute-start.9) | collective-permute-done | bytes 1310752 | tf_op jit(solution)/shard_map/ppermute | solution.py:34
  118.8 0.6 copy-done.4
  120.4 0.7 fusion.8
  121.5 0.7 fusion.16
  122.3 1.5 collective-permute-done.14
  123.8 1.7 collective-permute-start.15
  125.5 14.2 %collective-permute-done.15 = f32[448,128]{1,0:T(8,128)S(1)} collective-permute-done((f32[448,128]{1,0:T(8,128)S(1)}, f32[448,128]{1,0:T(8,128)S(1)}, u32[]{:S(2)}, u32[]{:S(2)}) %collective-permute-start.15) | collective-permute-done | bytes 229408 | tf_op jit(solution)/shard_map/ppermute | solution.py:208
  139.7 1.0 collective-permute-start.16
  140.7 1.9 %collective-permute-start.13 = (f32[256,256]{1,0:T(8,128)S(1)}, f32[256,256]{1,0:T(8,128)S(1)}, u32[]{:S(2)}, u32[]{:S(2)}) collective-permute-start(f32[256,256]{1,0:T(8,128)S(1)} %maximum_select_fusion.1), channel_id=1, source_target_pairs={{0,4},{4,8},{8,12},{12,16},{16,20},{20,24},{24,28},{28,32},{32,36}... | collective-permute-start | bytes 786440 | tf_op jit(solution)/shard_map/ppermute | solution.py:34
  142.6 8.4 %collective-permute-start.17 = (f32[128,128]{1,0:T(8,128)S(1)}, f32[128,128]{1,0:T(8,128)S(1)}, u32[]{:S(2)}, u32[]{:S(2)}) collective-permute-start(f32[128,128]{1,0:T(8,128)S(1)} %slice.193), channel_id=1, source_target_pairs={{4,0},{8,4},{12,8},{16,12},{20,16},{24,20},{28,24},{32,28},{36,32}... | collective-permute-start | bytes 196616 | tf_op jit(solution)/shard_map/ppermute | solution.py:34
  151.5 0.7 collective-permute-done.17
  152.1 3.4 %collective-permute-done.13 = f32[256,256]{1,0:T(8,128)S(1)} collective-permute-done((f32[256,256]{1,0:T(8,128)S(1)}, f32[256,256]{1,0:T(8,128)S(1)}, u32[]{:S(2)}, u32[]{:S(2)}) %collective-permute-start.13) | collective-permute-done | bytes 262176 | tf_op jit(solution)/shard_map/ppermute | solution.py:34
  155.5 1.3 fusion.14.band_ref
  156.8 17.1 %shard_map.39 = bf16[2,16,512]{2,1,0:T(8,128)(2,1)} custom-call(f32[640,640]{1,0:T(8,128)} %fusion.14.band_ref, f32[16,512]{1,0:T(8,128)} %bitcast.55), custom_call_target="tpu_custom_call" | custom-call | tf_op jit(solution)/shard_map/pallas_call | solution.py:87
  173.9 0.7 slice.202
  174.6 0.7 slice_bitcast_fusion
  175.4 0.7 copy.13
  176.1 0.6 copy-done.7
  176.7 5.4 %shard_map.40.rest_0_ = bf16[256,5120]{1,0:T(8,128)(2,1)} custom-call(bf16[256,2560]{1,0:T(8,128)(2,1)} %copy-done.4, bf16[256,2560]{1,0:T(8,128)(2,1)} %copy-done.1, bf16[128,2560]{1,0:T(8,128)(2,1)} %copy-done.6, bf16[5,32,128]{2,1,0:T(8,128)(2,1)} %copy-done.7, bf16[2,128,16]{2,1,0:T(8,128)(2,1)} %bitcast.53), custom_call_target="tpu_custom_call" | custom-call | tf_op jit(solution)/shard_map/pallas_call | solution.py:180
  182.1 5.4 %shard_map.41 = bf16[256,5120]{1,0:T(8,128)(2,1)} custom-call(bf16[256,2560]{1,0:T(8,128)(2,1)} %copy-done.3, bf16[256,2560]{1,0:T(8,128)(2,1)} %copy-done, bf16[128,2560]{1,0:T(8,128)(2,1)} %copy-done.5, bf16[5,32,128]{2,1,0:T(8,128)(2,1)} %copy-done.7, bf16[2,128,16]{2,1,0:T(8,128)(2,1)} %bitcast.54, ...), custom_call_target="tpu_custom_call", output_to_operand_aliasing={{}: (5, {})} | custom-call | tf_op jit(solution)/shard_map/pallas_call | solution.py:180
  (63 shorter events, 5.2 us)
Async XLA Ops:
  1.0 21.2 %collective-permute-start.1 = (bf16[256,64]{1,0:T(8,128)(2,1)S(1)}, bf16[256,64]{1,0:T(8,128)(2,1)S(1)}, u32[]{:S(2)}, u32[]{:S(2)}) collective-permute-start(bf16[256,64]{1,0:T(8,128)(2,1)S(1)} %get-tuple-element.23), channel_id=1, source_target_pairs={{1,0},{2,1},{3,2},{5,4},{6,5},{7,6},{9,8},{10,9},{11,10},{13,12},{... | collective-permute-start | bytes 98312 | tf_op jit(solution)/shard_map/ppermute | solution.py:222
  3.6 19.2 %collective-permute-start = (bf16[256,64]{1,0:T(8,128)(2,1)S(1)}, bf16[256,64]{1,0:T(8,128)(2,1)S(1)}, u32[]{:S(2)}, u32[]{:S(2)}) collective-permute-start(bf16[256,64]{1,0:T(8,128)(2,1)S(1)} %get-tuple-element.24), channel_id=1, source_target_pairs={{0,1},{1,2},{2,3},{4,5},{5,6},{6,7},{8,9},{9,10},{10,11},{12,13},{... | collective-permute-start | bytes 98312 | tf_op jit(solution)/shard_map/ppermute | solution.py:221
  30.3 19.1 %collective-permute-start.4 = (f32[4,2560]{1,0:T(4,128)S(1)}, f32[4,2560]{1,0:T(4,128)S(1)}, u32[]{:S(2)}, u32[]{:S(2)}) collective-permute-start(f32[4,2560]{1,0:T(4,128)S(1)} %get-tuple-element.21), channel_id=1, source_target_pairs={{4,0},{8,4},{12,8},{16,12},{20,16},{24,20},{28,24},{32,28},{36,32}... | collective-permute-start | bytes 122888 | tf_op jit(solution)/shard_map/ppermute | solution.py:26
  36.7 12.7 %collective-permute-start.5 = (f32[4,2560]{1,0:T(4,128)S(1)}, f32[4,2560]{1,0:T(4,128)S(1)}, u32[]{:S(2)}, u32[]{:S(2)}) collective-permute-start(f32[4,2560]{1,0:T(4,128)S(1)} %get-tuple-element.22), channel_id=1, source_target_pairs={{0,4},{4,8},{8,12},{12,16},{16,20},{20,24},{24,28},{28,32},{32,36}... | collective-permute-start | bytes 122888 | tf_op jit(solution)/shard_map/ppermute | solution.py:23
  39.6 14.9 %collective-permute-start.2 = (f32[4,2560]{1,0:T(4,128)S(1)}, f32[4,2560]{1,0:T(4,128)S(1)}, u32[]{:S(2)}, u32[]{:S(2)}) collective-permute-start(f32[4,2560]{1,0:T(4,128)S(1)} %get-tuple-element.19), channel_id=1, source_target_pairs={{4,0},{8,4},{12,8},{16,12},{20,16},{24,20},{28,24},{32,28},{36,32}... | collective-permute-start | bytes 122888 | tf_op jit(solution)/shard_map/ppermute | solution.py:26
  47.1 9.2 %copy-start.2 = (f32[256,2560]{1,0:T(8,128)S(1)}, f32[256,2560]{1,0:T(8,128)}, u32[]{:S(2)}) copy-start(f32[256,2560]{1,0:T(8,128)} %shard_map.37) | copy-start | bytes 7864324
  47.2 9.2 %collective-permute-start.3 = (f32[4,2560]{1,0:T(4,128)S(1)}, f32[4,2560]{1,0:T(4,128)S(1)}, u32[]{:S(2)}, u32[]{:S(2)}) collective-permute-start(f32[4,2560]{1,0:T(4,128)S(1)} %get-tuple-element.20), channel_id=1, source_target_pairs={{0,4},{4,8},{8,12},{12,16},{16,20},{20,24},{24,28},{28,32},{32,36}... | collective-permute-start | bytes 122888 | tf_op jit(solution)/shard_map/ppermute | solution.py:23
  52.5 67.4 %copy-start = (bf16[256,2560]{1,0:T(8,128)(2,1)}, bf16[256,2560]{1,0:T(8,128)(2,1)S(1)}, u32[]{:S(2)}) copy-start(bf16[256,2560]{1,0:T(8,128)(2,1)S(1)} %fusion.1.own_ref) | copy-start | bytes 3932164
  52.5 52.2 %collective-permute-start.10 = (bf16[256,2560]{1,0:T(8,128)(2,1)S(1)}, bf16[256,2560]{1,0:T(8,128)(2,1)S(1)}, u32[]{:S(2)}, u32[]{:S(2)}) collective-permute-start(bf16[256,2560]{1,0:T(8,128)(2,1)S(1)} %fusion.1.own_ref), channel_id=1, source_target_pairs={{0,4},{4,8},{8,12},{12,16},{16,20},{20,24},{24,28},{28,32},{32,36}... | collective-permute-start | bytes 3932168 | tf_op jit(solution)/shard_map/ppermute | solution.py:34
  56.7 64.4 %copy-start.1 = (bf16[256,2560]{1,0:T(8,128)(2,1)}, bf16[256,2560]{1,0:T(8,128)(2,1)S(1)}, u32[]{:S(2)}) copy-start(bf16[256,2560]{1,0:T(8,128)(2,1)S(1)} %fusion.3.own_ref) | copy-start | bytes 3932164
  56.7 61.5 %collective-permute-start.9 = (bf16[256,2560]{1,0:T(8,128)(2,1)S(1)}, bf16[256,2560]{1,0:T(8,128)(2,1)S(1)}, u32[]{:S(2)}, u32[]{:S(2)}) collective-permute-start(bf16[256,2560]{1,0:T(8,128)(2,1)S(1)} %fusion.3.own_ref), channel_id=1, source_target_pairs={{0,4},{4,8},{8,12},{12,16},{16,20},{20,24},{24,28},{28,32},{32,36}... | collective-permute-start | bytes 3932168 | tf_op jit(solution)/shard_map/ppermute | solution.py:34
  59.8 9.7 %collective-permute-start.6 = (f32[128,256]{1,0:T(8,128)S(1)}, f32[128,256]{1,0:T(8,128)S(1)}, u32[]{:S(2)}, u32[]{:S(2)}) collective-permute-start(f32[128,256]{1,0:T(8,128)S(1)} %slice_select_fusion), channel_id=1, source_target_pairs={{0,1},{1,0},{2,3},{3,2},{4,5},{5,4},{6,7},{7,6},{8,9},{9,8},{10,11... | collective-permute-start | bytes 393224 | tf_op jit(solution)/shard_map/ppermute | solution.py:207
  60.0 44.7 %collective-permute-start.11 = (bf16[128,2560]{1,0:T(8,128)(2,1)S(1)}, bf16[128,2560]{1,0:T(8,128)(2,1)S(1)}, u32[]{:S(2)}, u32[]{:S(2)}) collective-permute-start(bf16[128,2560]{1,0:T(8,128)(2,1)S(1)} %slice.185), channel_id=1, source_target_pairs={{4,0},{8,4},{12,8},{16,12},{20,16},{24,20},{28,24},{32,28},{36,32}... | collective-permute-start | bytes 1966088 | tf_op jit(solution)/shard_map/ppermute | solution.py:34
  67.6 37.1 %collective-permute-start.12 = (bf16[128,2560]{1,0:T(8,128)(2,1)S(1)}, bf16[128,2560]{1,0:T(8,128)(2,1)S(1)}, u32[]{:S(2)}, u32[]{:S(2)}) collective-permute-start(bf16[128,2560]{1,0:T(8,128)(2,1)S(1)} %slice.186), channel_id=1, source_target_pairs={{4,0},{8,4},{12,8},{16,12},{20,16},{24,20},{28,24},{32,28},{36,32}... | collective-permute-start | bytes 1966088 | tf_op jit(solution)/shard_map/ppermute | solution.py:34
  69.5 33.0 %collective-permute-start.7 = (f32[128,256]{1,0:T(8,128)S(1)}, f32[128,256]{1,0:T(8,128)S(1)}, u32[]{:S(2)}, u32[]{:S(2)}) collective-permute-start(f32[128,256]{1,0:T(8,128)S(1)} %select_add_fusion.1), channel_id=1, source_target_pairs={{0,2},{1,3},{2,0},{3,1},{4,6},{5,7},{6,4},{7,5},{8,10},{9,11},{10,... | collective-permute-start | bytes 393224 | tf_op jit(solution)/shard_map/ppermute | solution.py:208
  102.6 2.0 %collective-permute-start.8 = (f32[128,256]{1,0:T(8,128)S(1)}, f32[128,256]{1,0:T(8,128)S(1)}, u32[]{:S(2)}, u32[]{:S(2)}) collective-permute-start(f32[128,256]{1,0:T(8,128)S(1)} %add.43), channel_id=1, source_target_pairs={{0,1},{1,0},{2,3},{3,2},{4,5},{5,4},{6,7},{7,6},{8,9},{9,8},{10,11... | collective-permute-start | bytes 393224 | tf_op jit(solution)/shard_map/ppermute | solution.py:209
  104.7 16.4 %copy-start.6 = (bf16[128,2560]{1,0:T(8,128)(2,1)}, bf16[128,2560]{1,0:T(8,128)(2,1)S(1)}, u32[]{:S(2)}) copy-start(bf16[128,2560]{1,0:T(8,128)(2,1)S(1)} %collective-permute-done.11.upper_ref) | copy-start | bytes 1966084
  104.7 15.2 %copy-start.5 = (bf16[128,2560]{1,0:T(8,128)(2,1)}, bf16[128,2560]{1,0:T(8,128)(2,1)S(1)}, u32[]{:S(2)}) copy-start(bf16[128,2560]{1,0:T(8,128)(2,1)S(1)} %collective-permute-done.12.upper_ref) | copy-start | bytes 1966084
  104.7 14.1 %copy-start.3 = (bf16[256,2560]{1,0:T(8,128)(2,1)}, bf16[256,2560]{1,0:T(8,128)(2,1)S(1)}, u32[]{:S(2)}) copy-start(bf16[256,2560]{1,0:T(8,128)(2,1)S(1)} %collective-permute-done.10.lower_ref) | copy-start | bytes 3932164
  118.2 1.1 copy-start.4
  119.3 1.1 slice-start
  120.4 1.1 slice-start.1
  122.2 1.6 collective-permute-start.14
  123.8 15.8 %collective-permute-start.15 = (f32[448,128]{1,0:T(8,128)S(1)}, f32[448,128]{1,0:T(8,128)S(1)}, u32[]{:S(2)}, u32[]{:S(2)}) collective-permute-start(f32[448,128]{1,0:T(8,128)S(1)} %select_add_fusion), channel_id=1, source_target_pairs={{0,2},{1,3},{2,0},{3,1},{4,6},{5,7},{6,4},{7,5},{8,10},{9,11},{10,... | collective-permute-start | bytes 688136 | tf_op jit(solution)/shard_map/ppermute | solution.py:208
  139.7 11.3 %collective-permute-start.16 = (f32[448,128]{1,0:T(8,128)S(1)}, f32[448,128]{1,0:T(8,128)S(1)}, u32[]{:S(2)}, u32[]{:S(2)}) collective-permute-start(f32[448,128]{1,0:T(8,128)S(1)} %add.47), channel_id=1, source_target_pairs={{0,1},{1,0},{2,3},{3,2},{4,5},{5,4},{6,7},{7,6},{8,9},{9,8},{10,11... | collective-permute-start | bytes 688136 | tf_op jit(solution)/shard_map/ppermute | solution.py:209
  140.7 14.8 %collective-permute-start.13 = (f32[256,256]{1,0:T(8,128)S(1)}, f32[256,256]{1,0:T(8,128)S(1)}, u32[]{:S(2)}, u32[]{:S(2)}) collective-permute-start(f32[256,256]{1,0:T(8,128)S(1)} %maximum_select_fusion.1), channel_id=1, source_target_pairs={{0,4},{4,8},{8,12},{12,16},{16,20},{20,24},{24,28},{28,32},{32,36}... | collective-permute-start | bytes 786440 | tf_op jit(solution)/shard_map/ppermute | solution.py:34
  142.6 9.5 %collective-permute-start.17 = (f32[128,128]{1,0:T(8,128)S(1)}, f32[128,128]{1,0:T(8,128)S(1)}, u32[]{:S(2)}, u32[]{:S(2)}) collective-permute-start(f32[128,128]{1,0:T(8,128)S(1)} %slice.193), channel_id=1, source_target_pairs={{4,0},{8,4},{12,8},{16,12},{20,16},{24,20},{28,24},{32,28},{36,32}... | collective-permute-start | bytes 196616 | tf_op jit(solution)/shard_map/ppermute | solution.py:34
  176.1 0.6 copy-start.7

commit v12 on v7

--- a/solution.py
+++ b/solution.py
@@ -213,14 +213,22 @@
     total_time = samples * lax.axis_size("ta")
     gaugeds, lowers, uppers = [], [], []
     own = cross_left = cross_right = None
+    rimmed = jnp.concatenate(
+        [shifted(raw[chans - GAUGE :], "ch", 1), raw, shifted(raw[:GAUGE], "ch", -1)], axis=0
+    )
     filters = []
     for number in range(chunks):
         start = number * piece + width
-        edges = (left, right) if number == chunks - 1 else (raw[:, :STRIDE], raw[:, :STRIDE])
-        filters.append(fir(raw, *edges, band, start, piece))
+        if number == chunks - 1:
+            filters.append(fir(raw, left, right, band, start, piece))
+        else:
+            filters.append(fir(rimmed, rimmed[:, :STRIDE], rimmed[:, :STRIDE], band, start, piece))
     filters = lax.optimization_barrier(filters)
     for number in range(chunks):
-        extended = with_halo(filters[number], (("ch", 0),), GAUGE)
+        if number == chunks - 1:
+            extended = with_halo(filters[number], (("ch", 0),), GAUGE)
+        else:
+            extended = filters[number]
         gauged = (extended[2 * GAUGE :] - extended[: -2 * GAUGE]).astype(jnp.bfloat16)
         lower_part = shifted(gauged[chans - 2 * STRIDE :], "ch", 1)
         upper_part = shifted(gauged[:STRIDE], "ch", -1)

time: 188 us -> 187 us (level)
  waiting for transfers between devices: 66.2 us -> 63.6 us
  other arithmetic: 4.98 us -> 7.26 us
    ppermute x2 -> x1, starting transfers between devices: 14 us -> 2.75 us  [with_halo(): lax.ppermute(lax.slice_in_dim(block, 0, width, axis=dim), axis, backward)]
    ppermute x6 -> x8, starting transfers between devices: 23.6 us -> 33.3 us  [shifted(): lax.ppermute(value, axis, [(source, source + steps) for source in range(f...]
    ppermute x6 -> x8, waiting for transfers between devices: 17.6 us -> 14.6 us  [shifted(): lax.ppermute(value, axis, [(source, source + steps) for source in range(f...]
    concatenate x0 -> x1, other arithmetic: none -> 2.42 us  [per_device(): jnp.concatenate([shifted(raw[chans - GAUGE:], 'ch', 1), raw, shifted(raw[...]
    ppermute x2 -> x1, starting transfers between devices: 4.1 us -> 2.53 us  [with_halo(): lax.ppermute(lax.slice_in_dim(block, block.shape[dim] - width, None, axis...]
  transfers between devices with their start and end apart: 18 -> 18, of which waited for: 8 -> 8; matrix products, arithmetic and copies ran while one was open for 7% -> 6% of each run, Pallas kernels for 3% -> 3%
where the time goes in v12:
time: 187 us; the launch traced here: 186 us
  waiting for transfers between devices  63.6 us (34%)
  starting transfers between devices  57.2 us (31%)
  Pallas kernels  40.8 us (22%)
  local copies, waits for them, and re-layouts  13.4 us (7%)
  other arithmetic  7.26 us (4%)
  matrix products  3.47 us (2%)
    ppermute x2, waiting for transfers between devices, ta_sum(): part = part + lax.ppermute(part, 'ta', across)  45 us
    ppermute x8, starting transfers between devices, shifted(): lax.ppermute(value, axis, [(source, source + steps) for source in range(f...  33.3 us
    pallas_call x1, Pallas kernels, subspace(): pl.pallas_call(subspace_kernel, out_shape=jax.ShapeDtypeStruct((windows,)...  17.1 us
    ppermute x8, waiting for transfers between devices, shifted(): lax.ppermute(value, axis, [(source, source + steps) for source in range(f...  14.6 us
    pallas_call x2, Pallas kernels, fir(): pl.pallas_call(kernel, grid=(length // width,), out_shape=jax.ShapeDtypeS...  11.9 us
    pallas_call x2, Pallas kernels, clean(): pl.pallas_call(clean_kernel, grid=(samples // width,), out_shape=jax.Shap...  11.8 us
    ppermute x1, starting transfers between devices, per_device(): lax.ppermute(raw[:, samples - half:], 'ta', forward)  6.33 us
    ppermute x2, starting transfers between devices, ta_sum(): part = part + lax.ppermute(part, 'ta', across)  5.56 us
  transfers between devices with their start and end apart: 18, of which 8 were waited for; matrix products, arithmetic and copies ran while one was open for 6% of the time, Pallas kernels for 3%

profile of v12, /device:TPU:97, one launch (start us, length us, event | category | flops | bytes accessed | tf_op | source)
XLA Modules:
  0.0 186.1 jit_solution(13817002760688293973)
XLA Ops:
  0.0 1.0 fusion.22
  1.0 3.1 %collective-permute-start = (bf16[4,5120]{1,0:T(4,128)(2,1)S(1)}, bf16[4,5120]{1,0:T(4,128)(2,1)S(1)}, u32[]{:S(2)}, u32[]{:S(2)}) collective-permute-start(bf16[4,5120]{1,0:T(4,128)(2,1)S(1)} %get-tuple-element.23), channel_id=1, source_target_pairs={{0,4},{4,8},{8,12},{12,16},{16,20},{20,24},{24,28},{28,32},{32,36}... | collective-permute-start | bytes 122888 | tf_op jit(solution)/shard_map/ppermute | solution.py:34
  4.1 6.4 %collective-permute-start.1 = (bf16[4,5120]{1,0:T(4,128)(2,1)S(1)}, bf16[4,5120]{1,0:T(4,128)(2,1)S(1)}, u32[]{:S(2)}, u32[]{:S(2)}) collective-permute-start(bf16[4,5120]{1,0:T(4,128)(2,1)S(1)} %get-tuple-element.24), channel_id=1, source_target_pairs={{4,0},{8,4},{12,8},{16,12},{20,16},{24,20},{28,24},{32,28},{36,32}... | collective-permute-start | bytes 122888 | tf_op jit(solution)/shard_map/ppermute | solution.py:34
  10.5 1.0 fusion.21
  11.4 3.1 %collective-permute-start.3 = (bf16[256,64]{1,0:T(8,128)(2,1)S(1)}, bf16[256,64]{1,0:T(8,128)(2,1)S(1)}, u32[]{:S(2)}, u32[]{:S(2)}) collective-permute-start(bf16[256,64]{1,0:T(8,128)(2,1)S(1)} %get-tuple-element.21), channel_id=1, source_target_pairs={{1,0},{2,1},{3,2},{5,4},{6,5},{7,6},{9,8},{10,9},{11,10},{13,12},{... | collective-permute-start | bytes 98312 | tf_op jit(solution)/shard_map/ppermute | solution.py:206
  14.6 6.3 %collective-permute-start.2 = (bf16[256,64]{1,0:T(8,128)(2,1)S(1)}, bf16[256,64]{1,0:T(8,128)(2,1)S(1)}, u32[]{:S(2)}, u32[]{:S(2)}) collective-permute-start(bf16[256,64]{1,0:T(8,128)(2,1)S(1)} %get-tuple-element.22), channel_id=1, source_target_pairs={{0,1},{1,2},{2,3},{4,5},{5,6},{6,7},{8,9},{9,10},{10,11},{12,13},{... | collective-permute-start | bytes 98312 | tf_op jit(solution)/shard_map/ppermute | solution.py:205
  20.9 0.7 concatenate.64
  21.7 1.3 tile.10
  23.7 0.7 pad_slice_fusion
  24.4 0.8 slice.141.refs_6_
  25.3 0.6 concatenate.66.refs_1_
  25.9 0.7 concatenate.65.refs_0_
  26.6 5.8 %shard_map.38 = f32[256,2560]{1,0:T(8,128)} custom-call(bf16[256,128]{1,0:T(8,128)(2,1)} %concatenate.65.refs_0_, bf16[256,128]{1,0:T(8,128)(2,1)} %concatenate.66.refs_1_, bf16[256,5120]{1,0:T(8,128)(2,1)} %refs_4_.1, bf16[256,5120]{1,0:T(8,128)(2,1)} %refs_4_.1, bf16[256,5120]{1,0:T(8,128)(2,1)} %refs_4_.1, bf16[128,512]{1,0:T(8,128)(2,1)} %get-tuple-element.26.refs_5_, ...), custom_call_target="tpu_custom_call" | custom-call | tf_op jit(solution)/shard_map/pallas_call | solution.py:120
  32.5 2.4 %pad_maximum_fusion.refs_2_.refs_3_.refs_4_ = bf16[264,5120]{1,0:T(8,128)(2,1)S(1)} fusion(bf16[4,5120]{1,0:T(4,128)(2,1)S(1)} %collective-permute-done.1, bf16[256,5120]{1,0:T(8,128)(2,1)} %refs_4_.1, bf16[4,5120]{1,0:T(4,128)(2,1)S(1)} %collective-permute-done), kind=kLoop, calls=%fused_computation | loop fusion | flops 8110080 | bytes 5406720 | tf_op jit(solution)/shard_map/concatenate | solution.py:216
  34.9 0.7 slice.139.refs_0_.refs_1_
  35.6 0.8 copy-done
  36.4 6.0 %shard_map.37 = f32[264,2560]{1,0:T(8,128)} custom-call(bf16[264,128]{1,0:T(8,128)(2,1)} %slice.139.refs_0_.refs_1_, bf16[264,128]{1,0:T(8,128)(2,1)} %slice.139.refs_0_.refs_1_, bf16[264,5120]{1,0:T(8,128)(2,1)} %copy-done, bf16[264,5120]{1,0:T(8,128)(2,1)} %copy-done, bf16[264,5120]{1,0:T(8,128)(2,1)} %copy-done, ...), custom_call_target="tpu_custom_call" | custom-call | tf_op jit(solution)/shard_map/pallas_call | solution.py:120
  42.5 0.9 fusion.20
  43.4 2.8 %collective-permute-start.4 = (f32[4,2560]{1,0:T(4,128)S(1)}, f32[4,2560]{1,0:T(4,128)S(1)}, u32[]{:S(2)}, u32[]{:S(2)}) collective-permute-start(f32[4,2560]{1,0:T(4,128)S(1)} %get-tuple-element.19), channel_id=1, source_target_pairs={{4,0},{8,4},{12,8},{16,12},{20,16},{24,20},{28,24},{32,28},{36,32}... | collective-permute-start | bytes 122888 | tf_op jit(solution)/shard_map/ppermute | solution.py:26
  46.2 2.5 %collective-permute-start.5 = (f32[4,2560]{1,0:T(4,128)S(1)}, f32[4,2560]{1,0:T(4,128)S(1)}, u32[]{:S(2)}, u32[]{:S(2)}) collective-permute-start(f32[4,2560]{1,0:T(4,128)S(1)} %get-tuple-element.20), channel_id=1, source_target_pairs={{0,4},{4,8},{8,12},{12,16},{16,20},{20,24},{24,28},{28,32},{32,36}... | collective-permute-start | bytes 122888 | tf_op jit(solution)/shard_map/ppermute | solution.py:23
  48.7 3.0 %subtract_convert_fusion.own_ref = bf16[256,2560]{1,0:T(8,128)(2,1)S(1)} fusion(f32[264,2560]{1,0:T(8,128)} %shard_map.37), kind=kLoop, calls=%fused_computation.5 | loop fusion | flops 1310720 | bytes 6553600 | tf_op jit(solution)/shard_map/convert_element_type | solution.py:232
  51.7 1.9 %collective-permute-start.9 = (bf16[256,2560]{1,0:T(8,128)(2,1)S(1)}, bf16[256,2560]{1,0:T(8,128)(2,1)S(1)}, u32[]{:S(2)}, u32[]{:S(2)}) collective-permute-start(bf16[256,2560]{1,0:T(8,128)(2,1)S(1)} %subtract_convert_fusion.own_ref), channel_id=1, source_target_pairs={{0,4},{4,8},{8,12},{12,16},{16,20},{20,24},{24,28},{28,32},{32,36}... | collective-permute-start | bytes 3932168 | tf_op jit(solution)/shard_map/ppermute | solution.py:34
  53.7 1.5 collective-permute-done.5
  55.5 1.9 %collective-permute-start.10 = (bf16[256,2560]{1,0:T(8,128)(2,1)S(1)}, bf16[256,2560]{1,0:T(8,128)(2,1)S(1)}, u32[]{:S(2)}, u32[]{:S(2)}) collective-permute-start(bf16[256,2560]{1,0:T(8,128)(2,1)S(1)} %fusion.1.own_ref), channel_id=1, source_target_pairs={{0,4},{4,8},{8,12},{12,16},{16,20},{20,24},{24,28},{28,32},{32,36}... | collective-permute-start | bytes 3932168 | tf_op jit(solution)/shard_map/ppermute | solution.py:34
  58.7 7.6 %collective-permute-start.11 = (bf16[128,2560]{1,0:T(8,128)(2,1)S(1)}, bf16[128,2560]{1,0:T(8,128)(2,1)S(1)}, u32[]{:S(2)}, u32[]{:S(2)}) collective-permute-start(bf16[128,2560]{1,0:T(8,128)(2,1)S(1)} %slice.144), channel_id=1, source_target_pairs={{4,0},{8,4},{12,8},{16,12},{20,16},{24,20},{28,24},{32,28},{36,32}... | collective-permute-start | bytes 1966088 | tf_op jit(solution)/shard_map/ppermute | solution.py:34
  66.3 1.9 %collective-permute-start.12 = (bf16[128,2560]{1,0:T(8,128)(2,1)S(1)}, bf16[128,2560]{1,0:T(8,128)(2,1)S(1)}, u32[]{:S(2)}, u32[]{:S(2)}) collective-permute-start(bf16[128,2560]{1,0:T(8,128)(2,1)S(1)} %slice.145), channel_id=1, source_target_pairs={{4,0},{8,4},{12,8},{16,12},{20,16},{24,20},{28,24},{32,28},{36,32}... | collective-permute-start | bytes 1966088 | tf_op jit(solution)/shard_map/ppermute | solution.py:34
  68.3 4.5 %collective-permute-start.7 = (f32[128,256]{1,0:T(8,128)S(1)}, f32[128,256]{1,0:T(8,128)S(1)}, u32[]{:S(2)}, u32[]{:S(2)}) collective-permute-start(f32[128,256]{1,0:T(8,128)S(1)} %select_add_fusion.1), channel_id=1, source_target_pairs={{0,2},{1,3},{2,0},{3,1},{4,6},{5,7},{6,4},{7,5},{8,10},{9,11},{10,... | collective-permute-start | bytes 393224 | tf_op jit(solution)/shard_map/ppermute | solution.py:192
  72.8 30.4 %collective-permute-done.7 = f32[128,256]{1,0:T(8,128)S(1)} collective-permute-done((f32[128,256]{1,0:T(8,128)S(1)}, f32[128,256]{1,0:T(8,128)S(1)}, u32[]{:S(2)}, u32[]{:S(2)}) %collective-permute-start.7) | collective-permute-done | bytes 131104 | tf_op jit(solution)/shard_map/ppermute | solution.py:192
  103.3 2.8 %collective-permute-start.8 = (f32[128,256]{1,0:T(8,128)S(1)}, f32[128,256]{1,0:T(8,128)S(1)}, u32[]{:S(2)}, u32[]{:S(2)}) collective-permute-start(f32[128,256]{1,0:T(8,128)S(1)} %add.39), channel_id=1, source_target_pairs={{0,1},{1,0},{2,3},{3,2},{4,5},{5,4},{6,7},{7,6},{8,9},{9,8},{10,11... | collective-permute-start | bytes 393224 | tf_op jit(solution)/shard_map/ppermute | solution.py:193
  106.1 1.0 collective-permute-done.8
  107.2 10.6 %collective-permute-done.10.lower_ref = bf16[256,2560]{1,0:T(8,128)(2,1)S(1)} collective-permute-done((bf16[256,2560]{1,0:T(8,128)(2,1)S(1)}, bf16[256,2560]{1,0:T(8,128)(2,1)S(1)}, u32[]{:S(2)}, u32[]{:S(2)}) %collective-permute-start.10) | collective-permute-done | bytes 1310752 | tf_op jit(solution)/shard_map/ppermute | solution.py:34
  118.8 0.5 convolution_add_fusion
  119.9 0.7 fusion.6
  121.0 0.7 fusion.14
  121.8 1.5 collective-permute-done.14
  123.3 1.1 collective-permute-start.15
  124.4 14.5 %collective-permute-done.15 = f32[448,128]{1,0:T(8,128)S(1)} collective-permute-done((f32[448,128]{1,0:T(8,128)S(1)}, f32[448,128]{1,0:T(8,128)S(1)}, u32[]{:S(2)}, u32[]{:S(2)}) %collective-permute-start.15) | collective-permute-done | bytes 229408 | tf_op jit(solution)/shard_map/ppermute | solution.py:192
  139.0 0.5 collective-permute-start.16
  139.5 1.9 %collective-permute-start.13 = (f32[256,256]{1,0:T(8,128)S(1)}, f32[256,256]{1,0:T(8,128)S(1)}, u32[]{:S(2)}, u32[]{:S(2)}) collective-permute-start(f32[256,256]{1,0:T(8,128)S(1)} %maximum_select_fusion.1), channel_id=1, source_target_pairs={{0,4},{4,8},{8,12},{12,16},{16,20},{20,24},{24,28},{28,32},{32,36}... | collective-permute-start | bytes 786440 | tf_op jit(solution)/shard_map/ppermute | solution.py:34
  141.4 8.5 %collective-permute-start.17 = (f32[128,128]{1,0:T(8,128)S(1)}, f32[128,128]{1,0:T(8,128)S(1)}, u32[]{:S(2)}, u32[]{:S(2)}) collective-permute-start(f32[128,128]{1,0:T(8,128)S(1)} %slice.152), channel_id=1, source_target_pairs={{4,0},{8,4},{12,8},{16,12},{20,16},{24,20},{28,24},{32,28},{36,32}... | collective-permute-start | bytes 196616 | tf_op jit(solution)/shard_map/ppermute | solution.py:34
  150.5 0.7 collective-permute-done.17
  151.1 3.4 %collective-permute-done.13 = f32[256,256]{1,0:T(8,128)S(1)} collective-permute-done((f32[256,256]{1,0:T(8,128)S(1)}, f32[256,256]{1,0:T(8,128)S(1)}, u32[]{:S(2)}, u32[]{:S(2)}) %collective-permute-start.13) | collective-permute-done | bytes 262176 | tf_op jit(solution)/shard_map/ppermute | solution.py:34
  154.5 1.3 fusion.12.band_ref
  155.8 17.1 %shard_map.39.basis_ref = bf16[2,16,512]{2,1,0:T(8,128)(2,1)} custom-call(f32[640,640]{1,0:T(8,128)} %fusion.12.band_ref, f32[16,512]{1,0:T(8,128)} %bitcast.23), custom_call_target="tpu_custom_call" | custom-call | tf_op jit(solution)/shard_map/pallas_call | solution.py:87
  172.9 0.7 slice.153
  173.6 0.7 copy.13
  174.4 5.9 %shard_map.40.rest_0_ = bf16[256,5120]{1,0:T(8,128)(2,1)} custom-call(bf16[256,2560]{1,0:T(8,128)(2,1)} %copy-done.4, bf16[256,2560]{1,0:T(8,128)(2,1)} %copy-done.1, bf16[128,2560]{1,0:T(8,128)(2,1)} %copy-done.7, bf16[2,16,512]{2,1,0:T(8,128)(2,1)} %shard_map.39.basis_ref, bf16[2,128,16]{2,1,0:T(8,128)(2,1)} %bitcast.21), custom_call_target="tpu_custom_call" | custom-call | tf_op jit(solution)/shard_map/pallas_call | solution.py:164
  180.3 5.9 %shard_map.41 = bf16[256,5120]{1,0:T(8,128)(2,1)} custom-call(bf16[256,2560]{1,0:T(8,128)(2,1)} %copy-done.5, bf16[256,2560]{1,0:T(8,128)(2,1)} %copy-done.2, bf16[128,2560]{1,0:T(8,128)(2,1)} %copy-done.6, bf16[2,16,512]{2,1,0:T(8,128)(2,1)} %shard_map.39.basis_ref, bf16[2,128,16]{2,1,0:T(8,128)(2,1)} %bitcast.22, ...), custom_call_target="tpu_custom_call", output_to_operand_aliasing={{}: (5, {})} | custom-call | tf_op jit(solution)/shard_map/pallas_call | solution.py:164
  (58 shorter events, 5.1 us)
Async XLA Ops:
  1.0 31.5 %collective-permute-start = (bf16[4,5120]{1,0:T(4,128)(2,1)S(1)}, bf16[4,5120]{1,0:T(4,128)(2,1)S(1)}, u32[]{:S(2)}, u32[]{:S(2)}) collective-permute-start(bf16[4,5120]{1,0:T(4,128)(2,1)S(1)} %get-tuple-element.23), channel_id=1, source_target_pairs={{0,4},{4,8},{8,12},{12,16},{16,20},{20,24},{24,28},{28,32},{32,36}... | collective-permute-start | bytes 122888 | tf_op jit(solution)/shard_map/ppermute | solution.py:34
  4.1 28.4 %collective-permute-start.1 = (bf16[4,5120]{1,0:T(4,128)(2,1)S(1)}, bf16[4,5120]{1,0:T(4,128)(2,1)S(1)}, u32[]{:S(2)}, u32[]{:S(2)}) collective-permute-start(bf16[4,5120]{1,0:T(4,128)(2,1)S(1)} %get-tuple-element.24), channel_id=1, source_target_pairs={{4,0},{8,4},{12,8},{16,12},{20,16},{24,20},{28,24},{32,28},{36,32}... | collective-permute-start | bytes 122888 | tf_op jit(solution)/shard_map/ppermute | solution.py:34
  11.4 13.8 %collective-permute-start.3 = (bf16[256,64]{1,0:T(8,128)(2,1)S(1)}, bf16[256,64]{1,0:T(8,128)(2,1)S(1)}, u32[]{:S(2)}, u32[]{:S(2)}) collective-permute-start(bf16[256,64]{1,0:T(8,128)(2,1)S(1)} %get-tuple-element.21), channel_id=1, source_target_pairs={{1,0},{2,1},{3,2},{5,4},{6,5},{7,6},{9,8},{10,9},{11,10},{13,12},{... | collective-permute-start | bytes 98312 | tf_op jit(solution)/shard_map/ppermute | solution.py:206
  14.6 11.3 %collective-permute-start.2 = (bf16[256,64]{1,0:T(8,128)(2,1)S(1)}, bf16[256,64]{1,0:T(8,128)(2,1)S(1)}, u32[]{:S(2)}, u32[]{:S(2)}) collective-permute-start(bf16[256,64]{1,0:T(8,128)(2,1)S(1)} %get-tuple-element.22), channel_id=1, source_target_pairs={{0,1},{1,2},{2,3},{4,5},{5,6},{6,7},{8,9},{9,10},{10,11},{12,13},{... | collective-permute-start | bytes 98312 | tf_op jit(solution)/shard_map/ppermute | solution.py:205
  34.9 1.5 copy-start
  43.4 10.2 %collective-permute-start.4 = (f32[4,2560]{1,0:T(4,128)S(1)}, f32[4,2560]{1,0:T(4,128)S(1)}, u32[]{:S(2)}, u32[]{:S(2)}) collective-permute-start(f32[4,2560]{1,0:T(4,128)S(1)} %get-tuple-element.19), channel_id=1, source_target_pairs={{4,0},{8,4},{12,8},{16,12},{20,16},{24,20},{28,24},{32,28},{36,32}... | collective-permute-start | bytes 122888 | tf_op jit(solution)/shard_map/ppermute | solution.py:26
  46.2 9.0 %collective-permute-start.5 = (f32[4,2560]{1,0:T(4,128)S(1)}, f32[4,2560]{1,0:T(4,128)S(1)}, u32[]{:S(2)}, u32[]{:S(2)}) collective-permute-start(f32[4,2560]{1,0:T(4,128)S(1)} %get-tuple-element.20), channel_id=1, source_target_pairs={{0,4},{4,8},{8,12},{12,16},{16,20},{20,24},{24,28},{28,32},{32,36}... | collective-permute-start | bytes 122888 | tf_op jit(solution)/shard_map/ppermute | solution.py:23
  48.7 6.4 %copy-start.3 = (f32[256,2560]{1,0:T(8,128)S(1)}, f32[256,2560]{1,0:T(8,128)}, u32[]{:S(2)}) copy-start(f32[256,2560]{1,0:T(8,128)} %shard_map.38) | copy-start | bytes 7864324
  51.7 68.9 %copy-start.1 = (bf16[256,2560]{1,0:T(8,128)(2,1)}, bf16[256,2560]{1,0:T(8,128)(2,1)S(1)}, u32[]{:S(2)}) copy-start(bf16[256,2560]{1,0:T(8,128)(2,1)S(1)} %subtract_convert_fusion.own_ref) | copy-start | bytes 3932164
  51.7 55.4 %collective-permute-start.9 = (bf16[256,2560]{1,0:T(8,128)(2,1)S(1)}, bf16[256,2560]{1,0:T(8,128)(2,1)S(1)}, u32[]{:S(2)}, u32[]{:S(2)}) collective-permute-start(bf16[256,2560]{1,0:T(8,128)(2,1)S(1)} %subtract_convert_fusion.own_ref), channel_id=1, source_target_pairs={{0,4},{4,8},{8,12},{12,16},{16,20},{20,24},{24,28},{28,32},{32,36}... | collective-permute-start | bytes 3932168 | tf_op jit(solution)/shard_map/ppermute | solution.py:34
  55.5 63.9 %copy-start.2 = (bf16[256,2560]{1,0:T(8,128)(2,1)}, bf16[256,2560]{1,0:T(8,128)(2,1)S(1)}, u32[]{:S(2)}) copy-start(bf16[256,2560]{1,0:T(8,128)(2,1)S(1)} %fusion.1.own_ref) | copy-start | bytes 3932164
  55.5 62.3 %collective-permute-start.10 = (bf16[256,2560]{1,0:T(8,128)(2,1)S(1)}, bf16[256,2560]{1,0:T(8,128)(2,1)S(1)}, u32[]{:S(2)}, u32[]{:S(2)}) collective-permute-start(bf16[256,2560]{1,0:T(8,128)(2,1)S(1)} %fusion.1.own_ref), channel_id=1, source_target_pairs={{0,4},{4,8},{8,12},{12,16},{16,20},{20,24},{24,28},{28,32},{32,36}... | collective-permute-start | bytes 3932168 | tf_op jit(solution)/shard_map/ppermute | solution.py:34
  58.5 9.7 %collective-permute-start.6 = (f32[128,256]{1,0:T(8,128)S(1)}, f32[128,256]{1,0:T(8,128)S(1)}, u32[]{:S(2)}, u32[]{:S(2)}) collective-permute-start(f32[128,256]{1,0:T(8,128)S(1)} %slice_select_fusion), channel_id=1, source_target_pairs={{0,1},{1,0},{2,3},{3,2},{4,5},{5,4},{6,7},{7,6},{8,9},{9,8},{10,11... | collective-permute-start | bytes 393224 | tf_op jit(solution)/shard_map/ppermute | solution.py:191
  58.7 48.4 %collective-permute-start.11 = (bf16[128,2560]{1,0:T(8,128)(2,1)S(1)}, bf16[128,2560]{1,0:T(8,128)(2,1)S(1)}, u32[]{:S(2)}, u32[]{:S(2)}) collective-permute-start(bf16[128,2560]{1,0:T(8,128)(2,1)S(1)} %slice.144), channel_id=1, source_target_pairs={{4,0},{8,4},{12,8},{16,12},{20,16},{24,20},{28,24},{32,28},{36,32}... | collective-permute-start | bytes 1966088 | tf_op jit(solution)/shard_map/ppermute | solution.py:34
  66.3 40.8 %collective-permute-start.12 = (bf16[128,2560]{1,0:T(8,128)(2,1)S(1)}, bf16[128,2560]{1,0:T(8,128)(2,1)S(1)}, u32[]{:S(2)}, u32[]{:S(2)}) collective-permute-start(bf16[128,2560]{1,0:T(8,128)(2,1)S(1)} %slice.145), channel_id=1, source_target_pairs={{4,0},{8,4},{12,8},{16,12},{20,16},{24,20},{28,24},{32,28},{36,32}... | collective-permute-start | bytes 1966088 | tf_op jit(solution)/shard_map/ppermute | solution.py:34
  68.3 34.9 %collective-permute-start.7 = (f32[128,256]{1,0:T(8,128)S(1)}, f32[128,256]{1,0:T(8,128)S(1)}, u32[]{:S(2)}, u32[]{:S(2)}) collective-permute-start(f32[128,256]{1,0:T(8,128)S(1)} %select_add_fusion.1), channel_id=1, source_target_pairs={{0,2},{1,3},{2,0},{3,1},{4,6},{5,7},{6,4},{7,5},{8,10},{9,11},{10,... | collective-permute-start | bytes 393224 | tf_op jit(solution)/shard_map/ppermute | solution.py:192
  103.3 3.8 %collective-permute-start.8 = (f32[128,256]{1,0:T(8,128)S(1)}, f32[128,256]{1,0:T(8,128)S(1)}, u32[]{:S(2)}, u32[]{:S(2)}) collective-permute-start(f32[128,256]{1,0:T(8,128)S(1)} %add.39), channel_id=1, source_target_pairs={{0,1},{1,0},{2,3},{3,2},{4,5},{5,4},{6,7},{7,6},{8,9},{9,8},{10,11... | collective-permute-start | bytes 393224 | tf_op jit(solution)/shard_map/ppermute | solution.py:193
  107.1 13.5 %copy-start.7 = (bf16[128,2560]{1,0:T(8,128)(2,1)}, bf16[128,2560]{1,0:T(8,128)(2,1)S(1)}, u32[]{:S(2)}) copy-start(bf16[128,2560]{1,0:T(8,128)(2,1)S(1)} %collective-permute-done.11.upper_ref) | copy-start | bytes 1966084
  107.1 12.3 %copy-start.6 = (bf16[128,2560]{1,0:T(8,128)(2,1)}, bf16[128,2560]{1,0:T(8,128)(2,1)S(1)}, u32[]{:S(2)}) copy-start(bf16[128,2560]{1,0:T(8,128)(2,1)S(1)} %collective-permute-done.12.upper_ref) | copy-start | bytes 1966084
  107.2 11.7 %copy-start.4 = (bf16[256,2560]{1,0:T(8,128)(2,1)}, bf16[256,2560]{1,0:T(8,128)(2,1)S(1)}, u32[]{:S(2)}) copy-start(bf16[256,2560]{1,0:T(8,128)(2,1)S(1)} %collective-permute-done.9.lower_ref) | copy-start | bytes 3932164
  117.8 1.1 copy-start.5
  118.8 1.1 slice-start.1
  119.9 1.1 slice-start
  121.7 1.6 collective-permute-start.14
  123.3 15.6 %collective-permute-start.15 = (f32[448,128]{1,0:T(8,128)S(1)}, f32[448,128]{1,0:T(8,128)S(1)}, u32[]{:S(2)}, u32[]{:S(2)}) collective-permute-start(f32[448,128]{1,0:T(8,128)S(1)} %select_add_fusion), channel_id=1, source_target_pairs={{0,2},{1,3},{2,0},{3,1},{4,6},{5,7},{6,4},{7,5},{8,10},{9,11},{10,... | collective-permute-start | bytes 688136 | tf_op jit(solution)/shard_map/ppermute | solution.py:192
  139.0 11.0 %collective-permute-start.16 = (f32[448,128]{1,0:T(8,128)S(1)}, f32[448,128]{1,0:T(8,128)S(1)}, u32[]{:S(2)}, u32[]{:S(2)}) collective-permute-start(f32[448,128]{1,0:T(8,128)S(1)} %add.43), channel_id=1, source_target_pairs={{0,1},{1,0},{2,3},{3,2},{4,5},{5,4},{6,7},{7,6},{8,9},{9,8},{10,11... | collective-permute-start | bytes 688136 | tf_op jit(solution)/shard_map/ppermute | solution.py:193
  139.5 15.0 %collective-permute-start.13 = (f32[256,256]{1,0:T(8,128)S(1)}, f32[256,256]{1,0:T(8,128)S(1)}, u32[]{:S(2)}, u32[]{:S(2)}) collective-permute-start(f32[256,256]{1,0:T(8,128)S(1)} %maximum_select_fusion.1), channel_id=1, source_target_pairs={{0,4},{4,8},{8,12},{12,16},{16,20},{20,24},{24,28},{28,32},{32,36}... | collective-permute-start | bytes 786440 | tf_op jit(solution)/shard_map/ppermute | solution.py:34
  141.4 9.7 %collective-permute-start.17 = (f32[128,128]{1,0:T(8,128)S(1)}, f32[128,128]{1,0:T(8,128)S(1)}, u32[]{:S(2)}, u32[]{:S(2)}) collective-permute-start(f32[128,128]{1,0:T(8,128)S(1)} %slice.152), channel_id=1, source_target_pairs={{4,0},{8,4},{12,8},{16,12},{20,16},{24,20},{28,24},{32,28},{36,32}... | collective-permute-start | bytes 196616 | tf_op jit(solution)/shard_map/ppermute | solution.py:34

commit v13 on v12

--- a/solution.py
+++ b/solution.py
@@ -216,19 +216,14 @@
     rimmed = jnp.concatenate(
         [shifted(raw[chans - GAUGE :], "ch", 1), raw, shifted(raw[:GAUGE], "ch", -1)], axis=0
     )
-    filters = []
+    source = raw
     for number in range(chunks):
         start = number * piece + width
         if number == chunks - 1:
-            filters.append(fir(raw, left, right, band, start, piece))
+            filtered = fir(source, left, right, band, start, piece)
+            extended = with_halo(filtered, (("ch", 0),), GAUGE)
         else:
-            filters.append(fir(rimmed, rimmed[:, :STRIDE], rimmed[:, :STRIDE], band, start, piece))
-    filters = lax.optimization_barrier(filters)
-    for number in range(chunks):
-        if number == chunks - 1:
-            extended = with_halo(filters[number], (("ch", 0),), GAUGE)
-        else:
-            extended = filters[number]
+            extended = fir(rimmed, rimmed[:, :STRIDE], rimmed[:, :STRIDE], band, start, piece)
         gauged = (extended[2 * GAUGE :] - extended[: -2 * GAUGE]).astype(jnp.bfloat16)
         lower_part = shifted(gauged[chans - 2 * STRIDE :], "ch", 1)
         upper_part = shifted(gauged[:STRIDE], "ch", -1)
@@ -237,6 +232,7 @@
         gaugeds.append(gauged)
         lowers.append(lower_part)
         uppers.append(upper_part)
+        source, left, right, gauged = lax.optimization_barrier((source, left, right, gauged))
 
     own = ta_sum(own)
     own_left = shifted(own[chans - 2 * STRIDE :, chans - 2 * STRIDE :], "ch", 1)

time: 187 us -> 188 us (level)
  other arithmetic: 7.26 us -> 9.9 us
    ppermute x8, waiting for transfers between devices: 14.6 us -> 10.4 us  [shifted(): lax.ppermute(value, axis, [(source, source + steps) for source in range(f...]
    ppermute x1, waiting for transfers between devices: 1.48 us -> 5.21 us  [with_halo(): lax.ppermute(lax.slice_in_dim(block, block.shape[dim] - width, None, axis...]
    convert_element_type x2, other arithmetic: 3.32 us -> 5.95 us  [per_device(): gauged = (extended[2 * GAUGE:] - extended[:-2 * GAUGE]).astype(jnp.bfloat16)]
  transfers between devices with their start and end apart: 18 -> 18, of which waited for: 8 -> 8; matrix products, arithmetic and copies ran while one was open for 6% -> 6% of each run, Pallas kernels for 3% -> 0%
where the time goes in v13:
time: 188 us; the launch traced here: 187 us
  waiting for transfers between devices  62.5 us (33%)
  starting transfers between devices  55.8 us (30%)
  Pallas kernels  41.2 us (22%)
  local copies, waits for them, and re-layouts  13.4 us (7%)
  other arithmetic  9.9 us (5%)
  matrix products  3.47 us (2%)
    ppermute x2, waiting for transfers between devices, ta_sum(): part = part + lax.ppermute(part, 'ta', across)  44.4 us
    ppermute x8, starting transfers between devices, shifted(): lax.ppermute(value, axis, [(source, source + steps) for source in range(f...  33.7 us
    pallas_call x1, Pallas kernels, subspace(): pl.pallas_call(subspace_kernel, out_shape=jax.ShapeDtypeStruct((windows,)...  17.1 us
    pallas_call x2, Pallas kernels, fir(): pl.pallas_call(kernel, grid=(length // width,), out_shape=jax.ShapeDtypeS...  12.4 us
    pallas_call x2, Pallas kernels, clean(): pl.pallas_call(clean_kernel, grid=(samples // width,), out_shape=jax.Shap...  11.8 us
    ppermute x8, waiting for transfers between devices, shifted(): lax.ppermute(value, axis, [(source, source + steps) for source in range(f...  10.4 us
    ppermute x1, starting transfers between devices, per_device(): lax.ppermute(raw[:, samples - half:], 'ta', forward)  6.33 us
    convert_element_type x2, other arithmetic, per_device(): gauged = (extended[2 * GAUGE:] - extended[:-2 * GAUGE]).astype(jnp.bfloat16)  5.95 us
  transfers between devices with their start and end apart: 18, of which 8 were waited for; matrix products, arithmetic and copies ran while one was open for 6% of the time, Pallas kernels for 0%

profile of v13, /device:TPU:97, one launch (start us, length us, event | category | flops | bytes accessed | tf_op | source)
XLA Modules:
  0.0 186.8 jit_solution(1905773173855499194)
XLA Ops:
  0.0 1.0 fusion.23
  1.0 3.1 %collective-permute-start = (bf16[4,5120]{1,0:T(4,128)(2,1)S(1)}, bf16[4,5120]{1,0:T(4,128)(2,1)S(1)}, u32[]{:S(2)}, u32[]{:S(2)}) collective-permute-start(bf16[4,5120]{1,0:T(4,128)(2,1)S(1)} %get-tuple-element.25), channel_id=1, source_target_pairs={{0,4},{4,8},{8,12},{12,16},{16,20},{20,24},{24,28},{28,32},{32,36}... | collective-permute-start | bytes 122888 | tf_op jit(solution)/shard_map/ppermute | solution.py:34
  4.1 6.4 %collective-permute-start.1 = (bf16[4,5120]{1,0:T(4,128)(2,1)S(1)}, bf16[4,5120]{1,0:T(4,128)(2,1)S(1)}, u32[]{:S(2)}, u32[]{:S(2)}) collective-permute-start(bf16[4,5120]{1,0:T(4,128)(2,1)S(1)} %get-tuple-element.26), channel_id=1, source_target_pairs={{4,0},{8,4},{12,8},{16,12},{20,16},{24,20},{28,24},{32,28},{36,32}... | collective-permute-start | bytes 122888 | tf_op jit(solution)/shard_map/ppermute | solution.py:34
  10.5 1.0 fusion.22
  11.4 3.1 %collective-permute-start.3 = (bf16[256,64]{1,0:T(8,128)(2,1)S(1)}, bf16[256,64]{1,0:T(8,128)(2,1)S(1)}, u32[]{:S(2)}, u32[]{:S(2)}) collective-permute-start(bf16[256,64]{1,0:T(8,128)(2,1)S(1)} %get-tuple-element.23), channel_id=1, source_target_pairs={{1,0},{2,1},{3,2},{5,4},{6,5},{7,6},{9,8},{10,9},{11,10},{13,12},{... | collective-permute-start | bytes 98312 | tf_op jit(solution)/shard_map/ppermute | solution.py:206
  14.6 6.3 %collective-permute-start.2 = (bf16[256,64]{1,0:T(8,128)(2,1)S(1)}, bf16[256,64]{1,0:T(8,128)(2,1)S(1)}, u32[]{:S(2)}, u32[]{:S(2)}) collective-permute-start(bf16[256,64]{1,0:T(8,128)(2,1)S(1)} %get-tuple-element.24), channel_id=1, source_target_pairs={{0,1},{1,2},{2,3},{4,5},{5,6},{6,7},{8,9},{9,10},{10,11},{12,13},{... | collective-permute-start | bytes 98312 | tf_op jit(solution)/shard_map/ppermute | solution.py:205
  20.9 0.7 concatenate.64
  21.7 1.3 tile.10
  23.7 0.7 pad_slice_fusion
  24.4 0.8 slice.141.refs_6_
  25.3 0.6 concatenate.66.refs_1_
  25.9 0.7 concatenate.65.refs_0_
  26.6 2.4 %pad_maximum_fusion.refs_2_.refs_3_.refs_4_ = bf16[264,5120]{1,0:T(8,128)(2,1)S(1)} fusion(bf16[4,5120]{1,0:T(4,128)(2,1)S(1)} %collective-permute-done.1, bf16[256,5120]{1,0:T(8,128)(2,1)} %refs_4_, bf16[4,5120]{1,0:T(4,128)(2,1)S(1)} %collective-permute-done), kind=kLoop, calls=%fused_computation | loop fusion | flops 8110080 | bytes 5406720 | tf_op jit(solution)/shard_map/concatenate | solution.py:216
  29.1 0.7 slice.139.refs_0_.refs_1_
  29.8 0.8 copy-done
  30.6 6.0 %shard_map.37 = f32[264,2560]{1,0:T(8,128)} custom-call(bf16[264,128]{1,0:T(8,128)(2,1)} %slice.139.refs_0_.refs_1_, bf16[264,128]{1,0:T(8,128)(2,1)} %slice.139.refs_0_.refs_1_, bf16[264,5120]{1,0:T(8,128)(2,1)} %copy-done, bf16[264,5120]{1,0:T(8,128)(2,1)} %copy-done, bf16[264,5120]{1,0:T(8,128)(2,1)} %copy-done, ...), custom_call_target="tpu_custom_call" | custom-call | tf_op jit(solution)/shard_map/pallas_call | solution.py:120
  36.6 2.8 %fusion.2.own_ref = bf16[256,2560]{1,0:T(8,128)(2,1)S(1)} fusion(f32[264,2560]{1,0:T(8,128)} %shard_map.37), kind=kLoop, calls=%fused_computation.6 | loop fusion | flops 1310720 | bytes 6553600 | tf_op jit(solution)/shard_map/convert_element_type | solution.py:227
  39.5 6.3 %shard_map.38 = f32[256,2560]{1,0:T(8,128)} custom-call(bf16[256,128]{1,0:T(8,128)(2,1)} %concatenate.65.refs_0_, bf16[256,128]{1,0:T(8,128)(2,1)} %concatenate.66.refs_1_, bf16[256,5120]{1,0:T(8,128)(2,1)} %refs_4_, bf16[256,5120]{1,0:T(8,128)(2,1)} %refs_4_, bf16[256,5120]{1,0:T(8,128)(2,1)} %refs_4_, bf16[128,512]{1,0:T(8,128)(2,1)} %get-tuple-element.28.refs_5_, ...), custom_call_target="tpu_custom_call" | custom-call | tf_op jit(solution)/shard_map/pallas_call | solution.py:120
  45.8 0.9 fusion.21
  46.7 2.8 %collective-permute-start.4 = (f32[4,2560]{1,0:T(4,128)S(1)}, f32[4,2560]{1,0:T(4,128)S(1)}, u32[]{:S(2)}, u32[]{:S(2)}) collective-permute-start(f32[4,2560]{1,0:T(4,128)S(1)} %get-tuple-element.21), channel_id=1, source_target_pairs={{4,0},{8,4},{12,8},{16,12},{20,16},{24,20},{28,24},{32,28},{36,32}... | collective-permute-start | bytes 122888 | tf_op jit(solution)/shard_map/ppermute | solution.py:26
  49.5 2.5 %collective-permute-start.5 = (f32[4,2560]{1,0:T(4,128)S(1)}, f32[4,2560]{1,0:T(4,128)S(1)}, u32[]{:S(2)}, u32[]{:S(2)}) collective-permute-start(f32[4,2560]{1,0:T(4,128)S(1)} %get-tuple-element.22), channel_id=1, source_target_pairs={{0,4},{4,8},{8,12},{12,16},{16,20},{20,24},{24,28},{28,32},{32,36}... | collective-permute-start | bytes 122888 | tf_op jit(solution)/shard_map/ppermute | solution.py:23
  52.0 1.9 %collective-permute-start.9 = (bf16[256,2560]{1,0:T(8,128)(2,1)S(1)}, bf16[256,2560]{1,0:T(8,128)(2,1)S(1)}, u32[]{:S(2)}, u32[]{:S(2)}) collective-permute-start(bf16[256,2560]{1,0:T(8,128)(2,1)S(1)} %fusion.2.own_ref), channel_id=1, source_target_pairs={{0,4},{4,8},{8,12},{12,16},{16,20},{20,24},{24,28},{28,32},{32,36}... | collective-permute-start | bytes 3932168 | tf_op jit(solution)/shard_map/ppermute | solution.py:34
  54.0 5.2 %collective-permute-done.5 = f32[4,2560]{1,0:T(4,128)S(1)} collective-permute-done((f32[4,2560]{1,0:T(4,128)S(1)}, f32[4,2560]{1,0:T(4,128)S(1)}, u32[]{:S(2)}, u32[]{:S(2)}) %collective-permute-start.5) | collective-permute-done | bytes 40992 | tf_op jit(solution)/shard_map/ppermute | solution.py:23
  59.2 3.1 %fusion.1.own_ref = bf16[256,2560]{1,0:T(8,128)(2,1)S(1)} fusion(f32[256,2560]{1,0:T(8,128)} %shard_map.38, f32[4,2560]{1,0:T(4,128)S(1)} %collective-permute-done.5, f32[4,2560]{1,0:T(4,128)S(1)} %collective-permute-done.4), kind=kLoop, calls=%fused_computation.3 | loop fusion | flops 2621440 | bytes 4014080 | tf_op jit(solution)/shard_map/convert_element_type | solution.py:227
  62.3 1.9 %collective-permute-start.10 = (bf16[256,2560]{1,0:T(8,128)(2,1)S(1)}, bf16[256,2560]{1,0:T(8,128)(2,1)S(1)}, u32[]{:S(2)}, u32[]{:S(2)}) collective-permute-start(bf16[256,2560]{1,0:T(8,128)(2,1)S(1)} %fusion.1.own_ref), channel_id=1, source_target_pairs={{0,4},{4,8},{8,12},{12,16},{16,20},{20,24},{24,28},{28,32},{32,36}... | collective-permute-start | bytes 3932168 | tf_op jit(solution)/shard_map/ppermute | solution.py:34
  65.5 7.6 %collective-permute-start.11 = (bf16[128,2560]{1,0:T(8,128)(2,1)S(1)}, bf16[128,2560]{1,0:T(8,128)(2,1)S(1)}, u32[]{:S(2)}, u32[]{:S(2)}) collective-permute-start(bf16[128,2560]{1,0:T(8,128)(2,1)S(1)} %slice.148), channel_id=1, source_target_pairs={{4,0},{8,4},{12,8},{16,12},{20,16},{24,20},{28,24},{32,28},{36,32}... | collective-permute-start | bytes 1966088 | tf_op jit(solution)/shard_map/ppermute | solution.py:34
  73.2 1.9 %collective-permute-start.12 = (bf16[128,2560]{1,0:T(8,128)(2,1)S(1)}, bf16[128,2560]{1,0:T(8,128)(2,1)S(1)}, u32[]{:S(2)}, u32[]{:S(2)}) collective-permute-start(bf16[128,2560]{1,0:T(8,128)(2,1)S(1)} %slice.149), channel_id=1, source_target_pairs={{4,0},{8,4},{12,8},{16,12},{20,16},{24,20},{28,24},{32,28},{36,32}... | collective-permute-start | bytes 1966088 | tf_op jit(solution)/shard_map/ppermute | solution.py:34
  75.1 4.2 %collective-permute-start.7 = (f32[128,256]{1,0:T(8,128)S(1)}, f32[128,256]{1,0:T(8,128)S(1)}, u32[]{:S(2)}, u32[]{:S(2)}) collective-permute-start(f32[128,256]{1,0:T(8,128)S(1)} %select_add_fusion.1), channel_id=1, source_target_pairs={{0,2},{1,3},{2,0},{3,1},{4,6},{5,7},{6,4},{7,5},{8,10},{9,11},{10,... | collective-permute-start | bytes 393224 | tf_op jit(solution)/shard_map/ppermute | solution.py:192
  79.3 30.5 %collective-permute-done.7 = f32[128,256]{1,0:T(8,128)S(1)} collective-permute-done((f32[128,256]{1,0:T(8,128)S(1)}, f32[128,256]{1,0:T(8,128)S(1)}, u32[]{:S(2)}, u32[]{:S(2)}) %collective-permute-start.7) | collective-permute-done | bytes 131104 | tf_op jit(solution)/shard_map/ppermute | solution.py:192
  109.8 1.3 collective-permute-start.8
  111.1 1.0 collective-permute-done.8
  112.1 6.4 %collective-permute-done.10.lower_ref = bf16[256,2560]{1,0:T(8,128)(2,1)S(1)} collective-permute-done((bf16[256,2560]{1,0:T(8,128)(2,1)S(1)}, bf16[256,2560]{1,0:T(8,128)(2,1)S(1)}, u32[]{:S(2)}, u32[]{:S(2)}) %collective-permute-start.10) | collective-permute-done | bytes 1310752 | tf_op jit(solution)/shard_map/ppermute | solution.py:34
  118.5 0.5 fusion.28
  120.7 0.7 fusion.7
  121.8 0.7 fusion.15
  122.6 1.5 collective-permute-done.14
  124.1 1.3 collective-permute-start.15
  125.4 13.9 %collective-permute-done.15 = f32[448,128]{1,0:T(8,128)S(1)} collective-permute-done((f32[448,128]{1,0:T(8,128)S(1)}, f32[448,128]{1,0:T(8,128)S(1)}, u32[]{:S(2)}, u32[]{:S(2)}) %collective-permute-start.15) | collective-permute-done | bytes 229408 | tf_op jit(solution)/shard_map/ppermute | solution.py:192
  139.8 1.9 %collective-permute-start.13 = (f32[256,256]{1,0:T(8,128)S(1)}, f32[256,256]{1,0:T(8,128)S(1)}, u32[]{:S(2)}, u32[]{:S(2)}) collective-permute-start(f32[256,256]{1,0:T(8,128)S(1)} %maximum_select_fusion.1), channel_id=1, source_target_pairs={{0,4},{4,8},{8,12},{12,16},{16,20},{20,24},{24,28},{28,32},{32,36}... | collective-permute-start | bytes 786440 | tf_op jit(solution)/shard_map/ppermute | solution.py:34
  141.8 8.9 %collective-permute-start.17 = (f32[128,128]{1,0:T(8,128)S(1)}, f32[128,128]{1,0:T(8,128)S(1)}, u32[]{:S(2)}, u32[]{:S(2)}) collective-permute-start(f32[128,128]{1,0:T(8,128)S(1)} %slice.156), channel_id=1, source_target_pairs={{4,0},{8,4},{12,8},{16,12},{20,16},{24,20},{28,24},{32,28},{36,32}... | collective-permute-start | bytes 196616 | tf_op jit(solution)/shard_map/ppermute | solution.py:34
  151.1 0.7 collective-permute-done.17
  151.8 3.4 %collective-permute-done.13 = f32[256,256]{1,0:T(8,128)S(1)} collective-permute-done((f32[256,256]{1,0:T(8,128)S(1)}, f32[256,256]{1,0:T(8,128)S(1)}, u32[]{:S(2)}, u32[]{:S(2)}) %collective-permute-start.13) | collective-permute-done | bytes 262176 | tf_op jit(solution)/shard_map/ppermute | solution.py:34
  155.2 1.3 fusion.13.band_ref
  156.5 17.1 %shard_map.39.basis_ref = bf16[2,16,512]{2,1,0:T(8,128)(2,1)} custom-call(f32[640,640]{1,0:T(8,128)} %fusion.13.band_ref, f32[16,512]{1,0:T(8,128)} %bitcast.23), custom_call_target="tpu_custom_call" | custom-call | tf_op jit(solution)/shard_map/pallas_call | solution.py:87
  173.6 0.7 slice.157
  174.3 0.7 copy.13
  175.0 5.9 %shard_map.40.rest_0_ = bf16[256,5120]{1,0:T(8,128)(2,1)} custom-call(bf16[256,2560]{1,0:T(8,128)(2,1)} %copy-done.3, bf16[256,2560]{1,0:T(8,128)(2,1)} %copy-done.1, bf16[128,2560]{1,0:T(8,128)(2,1)} %copy-done.6, bf16[2,16,512]{2,1,0:T(8,128)(2,1)} %shard_map.39.basis_ref, bf16[2,128,16]{2,1,0:T(8,128)(2,1)} %bitcast.21), custom_call_target="tpu_custom_call" | custom-call | tf_op jit(solution)/shard_map/pallas_call | solution.py:164
  180.9 5.9 %shard_map.41 = bf16[256,5120]{1,0:T(8,128)(2,1)} custom-call(bf16[256,2560]{1,0:T(8,128)(2,1)} %copy-done.4, bf16[256,2560]{1,0:T(8,128)(2,1)} %copy-done.2, bf16[128,2560]{1,0:T(8,128)(2,1)} %copy-done.5, bf16[2,16,512]{2,1,0:T(8,128)(2,1)} %shard_map.39.basis_ref, bf16[2,128,16]{2,1,0:T(8,128)(2,1)} %bitcast.22, ...), custom_call_target="tpu_custom_call", output_to_operand_aliasing={{}: (5, {})} | custom-call | tf_op jit(solution)/shard_map/pallas_call | solution.py:164
  (56 shorter events, 5.3 us)
Async XLA Ops:
  1.0 25.7 %collective-permute-start = (bf16[4,5120]{1,0:T(4,128)(2,1)S(1)}, bf16[4,5120]{1,0:T(4,128)(2,1)S(1)}, u32[]{:S(2)}, u32[]{:S(2)}) collective-permute-start(bf16[4,5120]{1,0:T(4,128)(2,1)S(1)} %get-tuple-element.25), channel_id=1, source_target_pairs={{0,4},{4,8},{8,12},{12,16},{16,20},{20,24},{24,28},{28,32},{32,36}... | collective-permute-start | bytes 122888 | tf_op jit(solution)/shard_map/ppermute | solution.py:34
  4.1 22.5 %collective-permute-start.1 = (bf16[4,5120]{1,0:T(4,128)(2,1)S(1)}, bf16[4,5120]{1,0:T(4,128)(2,1)S(1)}, u32[]{:S(2)}, u32[]{:S(2)}) collective-permute-start(bf16[4,5120]{1,0:T(4,128)(2,1)S(1)} %get-tuple-element.26), channel_id=1, source_target_pairs={{4,0},{8,4},{12,8},{16,12},{20,16},{24,20},{28,24},{32,28},{36,32}... | collective-permute-start | bytes 122888 | tf_op jit(solution)/shard_map/ppermute | solution.py:34
  11.4 13.8 %collective-permute-start.3 = (bf16[256,64]{1,0:T(8,128)(2,1)S(1)}, bf16[256,64]{1,0:T(8,128)(2,1)S(1)}, u32[]{:S(2)}, u32[]{:S(2)}) collective-permute-start(bf16[256,64]{1,0:T(8,128)(2,1)S(1)} %get-tuple-element.23), channel_id=1, source_target_pairs={{1,0},{2,1},{3,2},{5,4},{6,5},{7,6},{9,8},{10,9},{11,10},{13,12},{... | collective-permute-start | bytes 98312 | tf_op jit(solution)/shard_map/ppermute | solution.py:206
  14.6 11.3 %collective-permute-start.2 = (bf16[256,64]{1,0:T(8,128)(2,1)S(1)}, bf16[256,64]{1,0:T(8,128)(2,1)S(1)}, u32[]{:S(2)}, u32[]{:S(2)}) collective-permute-start(bf16[256,64]{1,0:T(8,128)(2,1)S(1)} %get-tuple-element.24), channel_id=1, source_target_pairs={{0,1},{1,2},{2,3},{4,5},{5,6},{6,7},{8,9},{9,10},{10,11},{12,13},{... | collective-permute-start | bytes 98312 | tf_op jit(solution)/shard_map/ppermute | solution.py:205
  29.1 1.5 copy-start
  39.5 81.9 %copy-start.1 = (bf16[256,2560]{1,0:T(8,128)(2,1)}, bf16[256,2560]{1,0:T(8,128)(2,1)S(1)}, u32[]{:S(2)}) copy-start(bf16[256,2560]{1,0:T(8,128)(2,1)S(1)} %fusion.2.own_ref) | copy-start | bytes 3932164
  46.7 7.2 %collective-permute-start.4 = (f32[4,2560]{1,0:T(4,128)S(1)}, f32[4,2560]{1,0:T(4,128)S(1)}, u32[]{:S(2)}, u32[]{:S(2)}) collective-permute-start(f32[4,2560]{1,0:T(4,128)S(1)} %get-tuple-element.21), channel_id=1, source_target_pairs={{4,0},{8,4},{12,8},{16,12},{20,16},{24,20},{28,24},{32,28},{36,32}... | collective-permute-start | bytes 122888 | tf_op jit(solution)/shard_map/ppermute | solution.py:26
  49.5 9.7 %collective-permute-start.5 = (f32[4,2560]{1,0:T(4,128)S(1)}, f32[4,2560]{1,0:T(4,128)S(1)}, u32[]{:S(2)}, u32[]{:S(2)}) collective-permute-start(f32[4,2560]{1,0:T(4,128)S(1)} %get-tuple-element.22), channel_id=1, source_target_pairs={{0,4},{4,8},{8,12},{12,16},{16,20},{20,24},{24,28},{28,32},{32,36}... | collective-permute-start | bytes 122888 | tf_op jit(solution)/shard_map/ppermute | solution.py:23
  52.0 60.1 %collective-permute-start.9 = (bf16[256,2560]{1,0:T(8,128)(2,1)S(1)}, bf16[256,2560]{1,0:T(8,128)(2,1)S(1)}, u32[]{:S(2)}, u32[]{:S(2)}) collective-permute-start(bf16[256,2560]{1,0:T(8,128)(2,1)S(1)} %fusion.2.own_ref), channel_id=1, source_target_pairs={{0,4},{4,8},{8,12},{12,16},{16,20},{20,24},{24,28},{28,32},{32,36}... | collective-permute-start | bytes 3932168 | tf_op jit(solution)/shard_map/ppermute | solution.py:34
  62.3 57.9 %copy-start.2 = (bf16[256,2560]{1,0:T(8,128)(2,1)}, bf16[256,2560]{1,0:T(8,128)(2,1)S(1)}, u32[]{:S(2)}) copy-start(bf16[256,2560]{1,0:T(8,128)(2,1)S(1)} %fusion.1.own_ref) | copy-start | bytes 3932164
  62.3 56.2 %collective-permute-start.10 = (bf16[256,2560]{1,0:T(8,128)(2,1)S(1)}, bf16[256,2560]{1,0:T(8,128)(2,1)S(1)}, u32[]{:S(2)}, u32[]{:S(2)}) collective-permute-start(bf16[256,2560]{1,0:T(8,128)(2,1)S(1)} %fusion.1.own_ref), channel_id=1, source_target_pairs={{0,4},{4,8},{8,12},{12,16},{16,20},{20,24},{24,28},{28,32},{32,36}... | collective-permute-start | bytes 3932168 | tf_op jit(solution)/shard_map/ppermute | solution.py:34
  65.4 9.7 %collective-permute-start.6 = (f32[128,256]{1,0:T(8,128)S(1)}, f32[128,256]{1,0:T(8,128)S(1)}, u32[]{:S(2)}, u32[]{:S(2)}) collective-permute-start(f32[128,256]{1,0:T(8,128)S(1)} %slice_select_fusion), channel_id=1, source_target_pairs={{0,1},{1,0},{2,3},{3,2},{4,5},{5,4},{6,7},{7,6},{8,9},{9,8},{10,11... | collective-permute-start | bytes 393224 | tf_op jit(solution)/shard_map/ppermute | solution.py:191
  65.5 46.6 %collective-permute-start.11 = (bf16[128,2560]{1,0:T(8,128)(2,1)S(1)}, bf16[128,2560]{1,0:T(8,128)(2,1)S(1)}, u32[]{:S(2)}, u32[]{:S(2)}) collective-permute-start(bf16[128,2560]{1,0:T(8,128)(2,1)S(1)} %slice.148), channel_id=1, source_target_pairs={{4,0},{8,4},{12,8},{16,12},{20,16},{24,20},{28,24},{32,28},{36,32}... | collective-permute-start | bytes 1966088 | tf_op jit(solution)/shard_map/ppermute | solution.py:34
  73.2 38.9 %collective-permute-start.12 = (bf16[128,2560]{1,0:T(8,128)(2,1)S(1)}, bf16[128,2560]{1,0:T(8,128)(2,1)S(1)}, u32[]{:S(2)}, u32[]{:S(2)}) collective-permute-start(bf16[128,2560]{1,0:T(8,128)(2,1)S(1)} %slice.149), channel_id=1, source_target_pairs={{4,0},{8,4},{12,8},{16,12},{20,16},{24,20},{28,24},{32,28},{36,32}... | collective-permute-start | bytes 1966088 | tf_op jit(solution)/shard_map/ppermute | solution.py:34
  75.1 34.6 %collective-permute-start.7 = (f32[128,256]{1,0:T(8,128)S(1)}, f32[128,256]{1,0:T(8,128)S(1)}, u32[]{:S(2)}, u32[]{:S(2)}) collective-permute-start(f32[128,256]{1,0:T(8,128)S(1)} %select_add_fusion.1), channel_id=1, source_target_pairs={{0,2},{1,3},{2,0},{3,1},{4,6},{5,7},{6,4},{7,5},{8,10},{9,11},{10,... | collective-permute-start | bytes 393224 | tf_op jit(solution)/shard_map/ppermute | solution.py:192
  109.8 2.2 %collective-permute-start.8 = (f32[128,256]{1,0:T(8,128)S(1)}, f32[128,256]{1,0:T(8,128)S(1)}, u32[]{:S(2)}, u32[]{:S(2)}) collective-permute-start(f32[128,256]{1,0:T(8,128)S(1)} %add.39), channel_id=1, source_target_pairs={{0,1},{1,0},{2,3},{3,2},{4,5},{5,4},{6,7},{7,6},{8,9},{9,8},{10,11... | collective-permute-start | bytes 393224 | tf_op jit(solution)/shard_map/ppermute | solution.py:193
  112.1 9.3 %copy-start.6 = (bf16[128,2560]{1,0:T(8,128)(2,1)}, bf16[128,2560]{1,0:T(8,128)(2,1)S(1)}, u32[]{:S(2)}) copy-start(bf16[128,2560]{1,0:T(8,128)(2,1)S(1)} %collective-permute-done.11.upper_ref) | copy-start | bytes 1966084
  112.1 8.1 %copy-start.5 = (bf16[128,2560]{1,0:T(8,128)(2,1)}, bf16[128,2560]{1,0:T(8,128)(2,1)S(1)}, u32[]{:S(2)}) copy-start(bf16[128,2560]{1,0:T(8,128)(2,1)S(1)} %collective-permute-done.12.upper_ref) | copy-start | bytes 1966084
  112.1 7.5 %copy-start.3 = (bf16[256,2560]{1,0:T(8,128)(2,1)}, bf16[256,2560]{1,0:T(8,128)(2,1)S(1)}, u32[]{:S(2)}) copy-start(bf16[256,2560]{1,0:T(8,128)(2,1)S(1)} %collective-permute-done.9.lower_ref) | copy-start | bytes 3932164
  118.5 1.1 copy-start.4
  119.6 1.1 slice-start.1
  120.7 1.1 slice-start
  122.5 1.6 collective-permute-start.14
  124.1 15.2 %collective-permute-start.15 = (f32[448,128]{1,0:T(8,128)S(1)}, f32[448,128]{1,0:T(8,128)S(1)}, u32[]{:S(2)}, u32[]{:S(2)}) collective-permute-start(f32[448,128]{1,0:T(8,128)S(1)} %select_add_fusion), channel_id=1, source_target_pairs={{0,2},{1,3},{2,0},{3,1},{4,6},{5,7},{6,4},{7,5},{8,10},{9,11},{10,... | collective-permute-start | bytes 688136 | tf_op jit(solution)/shard_map/ppermute | solution.py:192
  139.3 11.4 %collective-permute-start.16 = (f32[448,128]{1,0:T(8,128)S(1)}, f32[448,128]{1,0:T(8,128)S(1)}, u32[]{:S(2)}, u32[]{:S(2)}) collective-permute-start(f32[448,128]{1,0:T(8,128)S(1)} %add.43), channel_id=1, source_target_pairs={{0,1},{1,0},{2,3},{3,2},{4,5},{5,4},{6,7},{7,6},{8,9},{9,8},{10,11... | collective-permute-start | bytes 688136 | tf_op jit(solution)/shard_map/ppermute | solution.py:193
  139.8 15.4 %collective-permute-start.13 = (f32[256,256]{1,0:T(8,128)S(1)}, f32[256,256]{1,0:T(8,128)S(1)}, u32[]{:S(2)}, u32[]{:S(2)}) collective-permute-start(f32[256,256]{1,0:T(8,128)S(1)} %maximum_select_fusion.1), channel_id=1, source_target_pairs={{0,4},{4,8},{8,12},{12,16},{16,20},{20,24},{24,28},{28,32},{32,36}... | collective-permute-start | bytes 786440 | tf_op jit(solution)/shard_map/ppermute | solution.py:34
  141.8 10.0 %collective-permute-start.17 = (f32[128,128]{1,0:T(8,128)S(1)}, f32[128,128]{1,0:T(8,128)S(1)}, u32[]{:S(2)}, u32[]{:S(2)}) collective-permute-start(f32[128,128]{1,0:T(8,128)S(1)} %slice.156), channel_id=1, source_target_pairs={{4,0},{8,4},{12,8},{16,12},{20,16},{24,20},{28,24},{32,28},{36,32}... | collective-permute-start | bytes 196616 | tf_op jit(solution)/shard_map/ppermute | solution.py:34

commit v14 on v11

--- a/solution.py
+++ b/solution.py
@@ -229,14 +229,22 @@
     total_time = samples * lax.axis_size("ta")
     gaugeds, lowers, uppers = [], [], []
     own = cross_left = cross_right = None
+    rimmed = jnp.concatenate(
+        [shifted(raw[chans - GAUGE :], "ch", 1), raw, shifted(raw[:GAUGE], "ch", -1)], axis=0
+    )
     filters = []
     for number in range(chunks):
         start = number * piece + width
-        edges = (left, right) if number == chunks - 1 else (raw[:, :STRIDE], raw[:, :STRIDE])
-        filters.append(fir(raw, *edges, band, start, piece))
+        if number == chunks - 1:
+            filters.append(fir(raw, left, right, band, start, piece))
+        else:
+            filters.append(fir(rimmed, rimmed[:, :STRIDE], rimmed[:, :STRIDE], band, start, piece))
     filters = lax.optimization_barrier(filters)
     for number in range(chunks):
-        extended = with_halo(filters[number], (("ch", 0),), GAUGE)
+        if number == chunks - 1:
+            extended = with_halo(filters[number], (("ch", 0),), GAUGE)
+        else:
+            extended = filters[number]
         gauged = (extended[2 * GAUGE :] - extended[: -2 * GAUGE]).astype(jnp.bfloat16)
         lower_part = shifted(gauged[chans - 2 * STRIDE :], "ch", 1)
         upper_part = shifted(gauged[:STRIDE], "ch", -1)

time: 189 us -> 188 us (level)
  waiting for transfers between devices: 66.2 us -> 63.7 us
  other arithmetic: 5 us -> 7.29 us
    ppermute x2 -> x1, starting transfers between devices: 14 us -> 2.76 us  [with_halo(): lax.ppermute(lax.slice_in_dim(block, 0, width, axis=dim), axis, backward)]
    ppermute x6 -> x8, starting transfers between devices: 23.6 us -> 33.2 us  [shifted(): lax.ppermute(value, axis, [(source, source + steps) for source in range(f...]
    ppermute x6 -> x8, waiting for transfers between devices: 17.6 us -> 14.7 us  [shifted(): lax.ppermute(value, axis, [(source, source + steps) for source in range(f...]
    concatenate x0 -> x1, other arithmetic: none -> 2.42 us  [per_device(): jnp.concatenate([shifted(raw[chans - GAUGE:], 'ch', 1), raw, shifted(raw[...]
    ppermute x2 -> x1, starting transfers between devices: 4.1 us -> 2.53 us  [with_halo(): lax.ppermute(lax.slice_in_dim(block, block.shape[dim] - width, None, axis...]
  transfers between devices with their start and end apart: 18 -> 18, of which waited for: 8 -> 8; matrix products, arithmetic and copies ran while one was open for 7% -> 6% of each run, Pallas kernels for 3% -> 3%
where the time goes in v14:
time: 188 us; the launch traced here: 187 us
  waiting for transfers between devices  63.7 us (34%)
  starting transfers between devices  57 us (30%)
  Pallas kernels  39.8 us (21%)
  local copies, waits for them, and re-layouts  14.8 us (8%)
  other arithmetic  7.29 us (4%)
  matrix products  3.48 us (2%)
    ppermute x2, waiting for transfers between devices, ta_sum(): part = part + lax.ppermute(part, 'ta', across)  45.1 us
    ppermute x8, starting transfers between devices, shifted(): lax.ppermute(value, axis, [(source, source + steps) for source in range(f...  33.2 us
    pallas_call x1, Pallas kernels, subspace(): pl.pallas_call(subspace_kernel, out_shape=jax.ShapeDtypeStruct((windows,)...  17.1 us
    ppermute x8, waiting for transfers between devices, shifted(): lax.ppermute(value, axis, [(source, source + steps) for source in range(f...  14.7 us
    pallas_call x2, Pallas kernels, fir(): pl.pallas_call(kernel, grid=(length // width,), out_shape=jax.ShapeDtypeS...  11.8 us
    pallas_call x2, Pallas kernels, clean(): pl.pallas_call(clean_kernel, grid=(samples // width,), out_shape=jax.Shap...  10.8 us
    ppermute x1, starting transfers between devices, per_device(): lax.ppermute(raw[:, samples - half:], 'ta', forward)  6.33 us
    ppermute x2, starting transfers between devices, ta_sum(): part = part + lax.ppermute(part, 'ta', across)  5.53 us
  transfers between devices with their start and end apart: 18, of which 8 were waited for; matrix products, arithmetic and copies ran while one was open for 6% of the time, Pallas kernels for 3%

profile of v14, /device:TPU:97, one launch (start us, length us, event | category | flops | bytes accessed | tf_op | source)
XLA Modules:
  0.0 186.5 jit_solution(8030728321469842929)
XLA Ops:
  0.0 1.0 fusion.22
  1.0 3.1 %collective-permute-start = (bf16[4,5120]{1,0:T(4,128)(2,1)S(1)}, bf16[4,5120]{1,0:T(4,128)(2,1)S(1)}, u32[]{:S(2)}, u32[]{:S(2)}) collective-permute-start(bf16[4,5120]{1,0:T(4,128)(2,1)S(1)} %get-tuple-element.23), channel_id=1, source_target_pairs={{0,4},{4,8},{8,12},{12,16},{16,20},{20,24},{24,28},{28,32},{32,36}... | collective-permute-start | bytes 122888 | tf_op jit(solution)/shard_map/ppermute | solution.py:34
  4.1 6.4 %collective-permute-start.1 = (bf16[4,5120]{1,0:T(4,128)(2,1)S(1)}, bf16[4,5120]{1,0:T(4,128)(2,1)S(1)}, u32[]{:S(2)}, u32[]{:S(2)}) collective-permute-start(bf16[4,5120]{1,0:T(4,128)(2,1)S(1)} %get-tuple-element.24), channel_id=1, source_target_pairs={{4,0},{8,4},{12,8},{16,12},{20,16},{24,20},{28,24},{32,28},{36,32}... | collective-permute-start | bytes 122888 | tf_op jit(solution)/shard_map/ppermute | solution.py:34
  10.5 1.0 fusion.21
  11.4 3.1 %collective-permute-start.3 = (bf16[256,64]{1,0:T(8,128)(2,1)S(1)}, bf16[256,64]{1,0:T(8,128)(2,1)S(1)}, u32[]{:S(2)}, u32[]{:S(2)}) collective-permute-start(bf16[256,64]{1,0:T(8,128)(2,1)S(1)} %get-tuple-element.21), channel_id=1, source_target_pairs={{1,0},{2,1},{3,2},{5,4},{6,5},{7,6},{9,8},{10,9},{11,10},{13,12},{... | collective-permute-start | bytes 98312 | tf_op jit(solution)/shard_map/ppermute | solution.py:222
  14.6 6.3 %collective-permute-start.2 = (bf16[256,64]{1,0:T(8,128)(2,1)S(1)}, bf16[256,64]{1,0:T(8,128)(2,1)S(1)}, u32[]{:S(2)}, u32[]{:S(2)}) collective-permute-start(bf16[256,64]{1,0:T(8,128)(2,1)S(1)} %get-tuple-element.22), channel_id=1, source_target_pairs={{0,1},{1,2},{2,3},{4,5},{5,6},{6,7},{8,9},{9,10},{10,11},{12,13},{... | collective-permute-start | bytes 98312 | tf_op jit(solution)/shard_map/ppermute | solution.py:221
  20.9 0.7 concatenate.84
  21.7 1.3 tile.10
  23.7 0.7 pad_slice_fusion
  24.4 0.9 slice.181.refs_6_
  25.3 0.6 concatenate.86.refs_1_
  25.9 0.7 concatenate.85.refs_0_
  26.7 5.8 %shard_map.38 = f32[256,2560]{1,0:T(8,128)} custom-call(bf16[256,128]{1,0:T(8,128)(2,1)} %concatenate.85.refs_0_, bf16[256,128]{1,0:T(8,128)(2,1)} %concatenate.86.refs_1_, bf16[256,5120]{1,0:T(8,128)(2,1)} %refs_4_.1, bf16[256,5120]{1,0:T(8,128)(2,1)} %refs_4_.1, bf16[256,5120]{1,0:T(8,128)(2,1)} %refs_4_.1, bf16[128,512]{1,0:T(8,128)(2,1)} %get-tuple-element.26.refs_5_, ...), custom_call_target="tpu_custom_call" | custom-call | tf_op jit(solution)/shard_map/pallas_call | solution.py:120
  32.5 2.4 %pad_maximum_fusion.refs_2_.refs_3_.refs_4_ = bf16[264,5120]{1,0:T(8,128)(2,1)S(1)} fusion(bf16[4,5120]{1,0:T(4,128)(2,1)S(1)} %collective-permute-done.1, bf16[256,5120]{1,0:T(8,128)(2,1)} %refs_4_.1, bf16[4,5120]{1,0:T(4,128)(2,1)S(1)} %collective-permute-done), kind=kLoop, calls=%fused_computation | loop fusion | flops 8110080 | bytes 5406720 | tf_op jit(solution)/shard_map/concatenate | solution.py:232
  34.9 0.7 slice.179.refs_0_.refs_1_
  35.6 0.8 copy-done
  36.4 6.0 %shard_map.37 = f32[264,2560]{1,0:T(8,128)} custom-call(bf16[264,128]{1,0:T(8,128)(2,1)} %slice.179.refs_0_.refs_1_, bf16[264,128]{1,0:T(8,128)(2,1)} %slice.179.refs_0_.refs_1_, bf16[264,5120]{1,0:T(8,128)(2,1)} %copy-done, bf16[264,5120]{1,0:T(8,128)(2,1)} %copy-done, bf16[264,5120]{1,0:T(8,128)(2,1)} %copy-done, ...), custom_call_target="tpu_custom_call" | custom-call | tf_op jit(solution)/shard_map/pallas_call | solution.py:120
  42.5 0.9 fusion.20
  43.4 2.8 %collective-permute-start.4 = (f32[4,2560]{1,0:T(4,128)S(1)}, f32[4,2560]{1,0:T(4,128)S(1)}, u32[]{:S(2)}, u32[]{:S(2)}) collective-permute-start(f32[4,2560]{1,0:T(4,128)S(1)} %get-tuple-element.19), channel_id=1, source_target_pairs={{4,0},{8,4},{12,8},{16,12},{20,16},{24,20},{28,24},{32,28},{36,32}... | collective-permute-start | bytes 122888 | tf_op jit(solution)/shard_map/ppermute | solution.py:26
  46.2 2.5 %collective-permute-start.5 = (f32[4,2560]{1,0:T(4,128)S(1)}, f32[4,2560]{1,0:T(4,128)S(1)}, u32[]{:S(2)}, u32[]{:S(2)}) collective-permute-start(f32[4,2560]{1,0:T(4,128)S(1)} %get-tuple-element.20), channel_id=1, source_target_pairs={{0,4},{4,8},{8,12},{12,16},{16,20},{20,24},{24,28},{28,32},{32,36}... | collective-permute-start | bytes 122888 | tf_op jit(solution)/shard_map/ppermute | solution.py:23
  48.7 3.0 %subtract_convert_fusion.own_ref = bf16[256,2560]{1,0:T(8,128)(2,1)S(1)} fusion(f32[264,2560]{1,0:T(8,128)} %shard_map.37), kind=kLoop, calls=%fused_computation.5 | loop fusion | flops 1310720 | bytes 6553600 | tf_op jit(solution)/shard_map/convert_element_type | solution.py:248
  51.7 1.9 %collective-permute-start.9 = (bf16[256,2560]{1,0:T(8,128)(2,1)S(1)}, bf16[256,2560]{1,0:T(8,128)(2,1)S(1)}, u32[]{:S(2)}, u32[]{:S(2)}) collective-permute-start(bf16[256,2560]{1,0:T(8,128)(2,1)S(1)} %subtract_convert_fusion.own_ref), channel_id=1, source_target_pairs={{0,4},{4,8},{8,12},{12,16},{16,20},{20,24},{24,28},{28,32},{32,36}... | collective-permute-start | bytes 3932168 | tf_op jit(solution)/shard_map/ppermute | solution.py:34
  53.6 1.5 collective-permute-done.5
  55.5 1.9 %collective-permute-start.10 = (bf16[256,2560]{1,0:T(8,128)(2,1)S(1)}, bf16[256,2560]{1,0:T(8,128)(2,1)S(1)}, u32[]{:S(2)}, u32[]{:S(2)}) collective-permute-start(bf16[256,2560]{1,0:T(8,128)(2,1)S(1)} %fusion.1.own_ref), channel_id=1, source_target_pairs={{0,4},{4,8},{8,12},{12,16},{16,20},{20,24},{24,28},{28,32},{32,36}... | collective-permute-start | bytes 3932168 | tf_op jit(solution)/shard_map/ppermute | solution.py:34
  58.7 7.6 %collective-permute-start.11 = (bf16[128,2560]{1,0:T(8,128)(2,1)S(1)}, bf16[128,2560]{1,0:T(8,128)(2,1)S(1)}, u32[]{:S(2)}, u32[]{:S(2)}) collective-permute-start(bf16[128,2560]{1,0:T(8,128)(2,1)S(1)} %slice.184), channel_id=1, source_target_pairs={{4,0},{8,4},{12,8},{16,12},{20,16},{24,20},{28,24},{32,28},{36,32}... | collective-permute-start | bytes 1966088 | tf_op jit(solution)/shard_map/ppermute | solution.py:34
  66.3 1.9 %collective-permute-start.12 = (bf16[128,2560]{1,0:T(8,128)(2,1)S(1)}, bf16[128,2560]{1,0:T(8,128)(2,1)S(1)}, u32[]{:S(2)}, u32[]{:S(2)}) collective-permute-start(bf16[128,2560]{1,0:T(8,128)(2,1)S(1)} %slice.185), channel_id=1, source_target_pairs={{4,0},{8,4},{12,8},{16,12},{20,16},{24,20},{28,24},{32,28},{36,32}... | collective-permute-start | bytes 1966088 | tf_op jit(solution)/shard_map/ppermute | solution.py:34
  68.3 4.5 %collective-permute-start.7 = (f32[128,256]{1,0:T(8,128)S(1)}, f32[128,256]{1,0:T(8,128)S(1)}, u32[]{:S(2)}, u32[]{:S(2)}) collective-permute-start(f32[128,256]{1,0:T(8,128)S(1)} %select_add_fusion.1), channel_id=1, source_target_pairs={{0,2},{1,3},{2,0},{3,1},{4,6},{5,7},{6,4},{7,5},{8,10},{9,11},{10,... | collective-permute-start | bytes 393224 | tf_op jit(solution)/shard_map/ppermute | solution.py:208
  72.7 30.5 %collective-permute-done.7 = f32[128,256]{1,0:T(8,128)S(1)} collective-permute-done((f32[128,256]{1,0:T(8,128)S(1)}, f32[128,256]{1,0:T(8,128)S(1)}, u32[]{:S(2)}, u32[]{:S(2)}) %collective-permute-start.7) | collective-permute-done | bytes 131104 | tf_op jit(solution)/shard_map/ppermute | solution.py:208
  103.3 2.8 %collective-permute-start.8 = (f32[128,256]{1,0:T(8,128)S(1)}, f32[128,256]{1,0:T(8,128)S(1)}, u32[]{:S(2)}, u32[]{:S(2)}) collective-permute-start(f32[128,256]{1,0:T(8,128)S(1)} %add.43), channel_id=1, source_target_pairs={{0,1},{1,0},{2,3},{3,2},{4,5},{5,4},{6,7},{7,6},{8,9},{9,8},{10,11... | collective-permute-start | bytes 393224 | tf_op jit(solution)/shard_map/ppermute | solution.py:209
  106.1 1.0 collective-permute-done.8
  107.1 10.6 %collective-permute-done.10.lower_ref = bf16[256,2560]{1,0:T(8,128)(2,1)S(1)} collective-permute-done((bf16[256,2560]{1,0:T(8,128)(2,1)S(1)}, bf16[256,2560]{1,0:T(8,128)(2,1)S(1)}, u32[]{:S(2)}, u32[]{:S(2)}) %collective-permute-start.10) | collective-permute-done | bytes 1310752 | tf_op jit(solution)/shard_map/ppermute | solution.py:34
  119.9 0.7 fusion.6
  121.0 0.7 fusion.14
  121.8 1.5 collective-permute-done.14
  123.3 1.1 collective-permute-start.15
  124.4 14.5 %collective-permute-done.15 = f32[448,128]{1,0:T(8,128)S(1)} collective-permute-done((f32[448,128]{1,0:T(8,128)S(1)}, f32[448,128]{1,0:T(8,128)S(1)}, u32[]{:S(2)}, u32[]{:S(2)}) %collective-permute-start.15) | collective-permute-done | bytes 229408 | tf_op jit(solution)/shard_map/ppermute | solution.py:208
  139.5 1.9 %collective-permute-start.13 = (f32[256,256]{1,0:T(8,128)S(1)}, f32[256,256]{1,0:T(8,128)S(1)}, u32[]{:S(2)}, u32[]{:S(2)}) collective-permute-start(f32[256,256]{1,0:T(8,128)S(1)} %maximum_select_fusion.1), channel_id=1, source_target_pairs={{0,4},{4,8},{8,12},{12,16},{16,20},{20,24},{24,28},{28,32},{32,36}... | collective-permute-start | bytes 786440 | tf_op jit(solution)/shard_map/ppermute | solution.py:34
  141.4 8.5 %collective-permute-start.17 = (f32[128,128]{1,0:T(8,128)S(1)}, f32[128,128]{1,0:T(8,128)S(1)}, u32[]{:S(2)}, u32[]{:S(2)}) collective-permute-start(f32[128,128]{1,0:T(8,128)S(1)} %slice.192), channel_id=1, source_target_pairs={{4,0},{8,4},{12,8},{16,12},{20,16},{24,20},{28,24},{32,28},{36,32}... | collective-permute-start | bytes 196616 | tf_op jit(solution)/shard_map/ppermute | solution.py:34
  150.4 0.7 collective-permute-done.17
  151.0 3.4 %collective-permute-done.13 = f32[256,256]{1,0:T(8,128)S(1)} collective-permute-done((f32[256,256]{1,0:T(8,128)S(1)}, f32[256,256]{1,0:T(8,128)S(1)}, u32[]{:S(2)}, u32[]{:S(2)}) %collective-permute-start.13) | collective-permute-done | bytes 262176 | tf_op jit(solution)/shard_map/ppermute | solution.py:34
  154.5 1.3 fusion.12.band_ref
  155.8 17.1 %shard_map.39 = bf16[2,16,512]{2,1,0:T(8,128)(2,1)} custom-call(f32[640,640]{1,0:T(8,128)} %fusion.12.band_ref, f32[16,512]{1,0:T(8,128)} %bitcast.55), custom_call_target="tpu_custom_call" | custom-call | tf_op jit(solution)/shard_map/pallas_call | solution.py:87
  172.9 0.7 slice.201
  173.6 0.7 slice_bitcast_fusion
  174.3 0.7 copy.13
  175.1 0.6 copy-done.8
  175.7 5.4 %shard_map.40.rest_0_ = bf16[256,5120]{1,0:T(8,128)(2,1)} custom-call(bf16[256,2560]{1,0:T(8,128)(2,1)} %copy-done.5, bf16[256,2560]{1,0:T(8,128)(2,1)} %copy-done.1, bf16[128,2560]{1,0:T(8,128)(2,1)} %copy-done.7, bf16[5,32,128]{2,1,0:T(8,128)(2,1)} %copy-done.8, bf16[2,128,16]{2,1,0:T(8,128)(2,1)} %bitcast.53), custom_call_target="tpu_custom_call" | custom-call | tf_op jit(solution)/shard_map/pallas_call | solution.py:180
  181.1 5.4 %shard_map.41 = bf16[256,5120]{1,0:T(8,128)(2,1)} custom-call(bf16[256,2560]{1,0:T(8,128)(2,1)} %copy-done.4, bf16[256,2560]{1,0:T(8,128)(2,1)} %copy-done.2, bf16[128,2560]{1,0:T(8,128)(2,1)} %copy-done.6, bf16[5,32,128]{2,1,0:T(8,128)(2,1)} %copy-done.8, bf16[2,128,16]{2,1,0:T(8,128)(2,1)} %bitcast.54, ...), custom_call_target="tpu_custom_call", output_to_operand_aliasing={{}: (5, {})} | custom-call | tf_op jit(solution)/shard_map/pallas_call | solution.py:180
  (66 shorter events, 6.2 us)
Async XLA Ops:
  1.0 31.5 %collective-permute-start = (bf16[4,5120]{1,0:T(4,128)(2,1)S(1)}, bf16[4,5120]{1,0:T(4,128)(2,1)S(1)}, u32[]{:S(2)}, u32[]{:S(2)}) collective-permute-start(bf16[4,5120]{1,0:T(4,128)(2,1)S(1)} %get-tuple-element.23), channel_id=1, source_target_pairs={{0,4},{4,8},{8,12},{12,16},{16,20},{20,24},{24,28},{28,32},{32,36}... | collective-permute-start | bytes 122888 | tf_op jit(solution)/shard_map/ppermute | solution.py:34
  4.1 28.4 %collective-permute-start.1 = (bf16[4,5120]{1,0:T(4,128)(2,1)S(1)}, bf16[4,5120]{1,0:T(4,128)(2,1)S(1)}, u32[]{:S(2)}, u32[]{:S(2)}) collective-permute-start(bf16[4,5120]{1,0:T(4,128)(2,1)S(1)} %get-tuple-element.24), channel_id=1, source_target_pairs={{4,0},{8,4},{12,8},{16,12},{20,16},{24,20},{28,24},{32,28},{36,32}... | collective-permute-start | bytes 122888 | tf_op jit(solution)/shard_map/ppermute | solution.py:34
  11.4 13.8 %collective-permute-start.3 = (bf16[256,64]{1,0:T(8,128)(2,1)S(1)}, bf16[256,64]{1,0:T(8,128)(2,1)S(1)}, u32[]{:S(2)}, u32[]{:S(2)}) collective-permute-start(bf16[256,64]{1,0:T(8,128)(2,1)S(1)} %get-tuple-element.21), channel_id=1, source_target_pairs={{1,0},{2,1},{3,2},{5,4},{6,5},{7,6},{9,8},{10,9},{11,10},{13,12},{... | collective-permute-start | bytes 98312 | tf_op jit(solution)/shard_map/ppermute | solution.py:222
  14.6 11.3 %collective-permute-start.2 = (bf16[256,64]{1,0:T(8,128)(2,1)S(1)}, bf16[256,64]{1,0:T(8,128)(2,1)S(1)}, u32[]{:S(2)}, u32[]{:S(2)}) collective-permute-start(bf16[256,64]{1,0:T(8,128)(2,1)S(1)} %get-tuple-element.22), channel_id=1, source_target_pairs={{0,1},{1,2},{2,3},{4,5},{5,6},{6,7},{8,9},{9,10},{10,11},{12,13},{... | collective-permute-start | bytes 98312 | tf_op jit(solution)/shard_map/ppermute | solution.py:221
  34.9 1.5 copy-start
  43.4 10.2 %collective-permute-start.4 = (f32[4,2560]{1,0:T(4,128)S(1)}, f32[4,2560]{1,0:T(4,128)S(1)}, u32[]{:S(2)}, u32[]{:S(2)}) collective-permute-start(f32[4,2560]{1,0:T(4,128)S(1)} %get-tuple-element.19), channel_id=1, source_target_pairs={{4,0},{8,4},{12,8},{16,12},{20,16},{24,20},{28,24},{32,28},{36,32}... | collective-permute-start | bytes 122888 | tf_op jit(solution)/shard_map/ppermute | solution.py:26
  46.2 9.0 %collective-permute-start.5 = (f32[4,2560]{1,0:T(4,128)S(1)}, f32[4,2560]{1,0:T(4,128)S(1)}, u32[]{:S(2)}, u32[]{:S(2)}) collective-permute-start(f32[4,2560]{1,0:T(4,128)S(1)} %get-tuple-element.20), channel_id=1, source_target_pairs={{0,4},{4,8},{8,12},{12,16},{16,20},{20,24},{24,28},{28,32},{32,36}... | collective-permute-start | bytes 122888 | tf_op jit(solution)/shard_map/ppermute | solution.py:23
  48.7 6.4 %copy-start.3 = (f32[256,2560]{1,0:T(8,128)S(1)}, f32[256,2560]{1,0:T(8,128)}, u32[]{:S(2)}) copy-start(f32[256,2560]{1,0:T(8,128)} %shard_map.38) | copy-start | bytes 7864324
  51.7 68.9 %copy-start.1 = (bf16[256,2560]{1,0:T(8,128)(2,1)}, bf16[256,2560]{1,0:T(8,128)(2,1)S(1)}, u32[]{:S(2)}) copy-start(bf16[256,2560]{1,0:T(8,128)(2,1)S(1)} %subtract_convert_fusion.own_ref) | copy-start | bytes 3932164
  51.7 55.4 %collective-permute-start.9 = (bf16[256,2560]{1,0:T(8,128)(2,1)S(1)}, bf16[256,2560]{1,0:T(8,128)(2,1)S(1)}, u32[]{:S(2)}, u32[]{:S(2)}) collective-permute-start(bf16[256,2560]{1,0:T(8,128)(2,1)S(1)} %subtract_convert_fusion.own_ref), channel_id=1, source_target_pairs={{0,4},{4,8},{8,12},{12,16},{16,20},{20,24},{24,28},{28,32},{32,36}... | collective-permute-start | bytes 3932168 | tf_op jit(solution)/shard_map/ppermute | solution.py:34
  55.5 63.9 %copy-start.2 = (bf16[256,2560]{1,0:T(8,128)(2,1)}, bf16[256,2560]{1,0:T(8,128)(2,1)S(1)}, u32[]{:S(2)}) copy-start(bf16[256,2560]{1,0:T(8,128)(2,1)S(1)} %fusion.1.own_ref) | copy-start | bytes 3932164
  55.5 62.3 %collective-permute-start.10 = (bf16[256,2560]{1,0:T(8,128)(2,1)S(1)}, bf16[256,2560]{1,0:T(8,128)(2,1)S(1)}, u32[]{:S(2)}, u32[]{:S(2)}) collective-permute-start(bf16[256,2560]{1,0:T(8,128)(2,1)S(1)} %fusion.1.own_ref), channel_id=1, source_target_pairs={{0,4},{4,8},{8,12},{12,16},{16,20},{20,24},{24,28},{28,32},{32,36}... | collective-permute-start | bytes 3932168 | tf_op jit(solution)/shard_map/ppermute | solution.py:34
  58.5 9.7 %collective-permute-start.6 = (f32[128,256]{1,0:T(8,128)S(1)}, f32[128,256]{1,0:T(8,128)S(1)}, u32[]{:S(2)}, u32[]{:S(2)}) collective-permute-start(f32[128,256]{1,0:T(8,128)S(1)} %slice_select_fusion), channel_id=1, source_target_pairs={{0,1},{1,0},{2,3},{3,2},{4,5},{5,4},{6,7},{7,6},{8,9},{9,8},{10,11... | collective-permute-start | bytes 393224 | tf_op jit(solution)/shard_map/ppermute | solution.py:207
  58.7 48.4 %collective-permute-start.11 = (bf16[128,2560]{1,0:T(8,128)(2,1)S(1)}, bf16[128,2560]{1,0:T(8,128)(2,1)S(1)}, u32[]{:S(2)}, u32[]{:S(2)}) collective-permute-start(bf16[128,2560]{1,0:T(8,128)(2,1)S(1)} %slice.184), channel_id=1, source_target_pairs={{4,0},{8,4},{12,8},{16,12},{20,16},{24,20},{28,24},{32,28},{36,32}... | collective-permute-start | bytes 1966088 | tf_op jit(solution)/shard_map/ppermute | solution.py:34
  66.3 40.8 %collective-permute-start.12 = (bf16[128,2560]{1,0:T(8,128)(2,1)S(1)}, bf16[128,2560]{1,0:T(8,128)(2,1)S(1)}, u32[]{:S(2)}, u32[]{:S(2)}) collective-permute-start(bf16[128,2560]{1,0:T(8,128)(2,1)S(1)} %slice.185), channel_id=1, source_target_pairs={{4,0},{8,4},{12,8},{16,12},{20,16},{24,20},{28,24},{32,28},{36,32}... | collective-permute-start | bytes 1966088 | tf_op jit(solution)/shard_map/ppermute | solution.py:34
  68.3 35.0 %collective-permute-start.7 = (f32[128,256]{1,0:T(8,128)S(1)}, f32[128,256]{1,0:T(8,128)S(1)}, u32[]{:S(2)}, u32[]{:S(2)}) collective-permute-start(f32[128,256]{1,0:T(8,128)S(1)} %select_add_fusion.1), channel_id=1, source_target_pairs={{0,2},{1,3},{2,0},{3,1},{4,6},{5,7},{6,4},{7,5},{8,10},{9,11},{10,... | collective-permute-start | bytes 393224 | tf_op jit(solution)/shard_map/ppermute | solution.py:208
  103.3 3.8 %collective-permute-start.8 = (f32[128,256]{1,0:T(8,128)S(1)}, f32[128,256]{1,0:T(8,128)S(1)}, u32[]{:S(2)}, u32[]{:S(2)}) collective-permute-start(f32[128,256]{1,0:T(8,128)S(1)} %add.43), channel_id=1, source_target_pairs={{0,1},{1,0},{2,3},{3,2},{4,5},{5,4},{6,7},{7,6},{8,9},{9,8},{10,11... | collective-permute-start | bytes 393224 | tf_op jit(solution)/shard_map/ppermute | solution.py:209
  107.1 13.5 %copy-start.7 = (bf16[128,2560]{1,0:T(8,128)(2,1)}, bf16[128,2560]{1,0:T(8,128)(2,1)S(1)}, u32[]{:S(2)}) copy-start(bf16[128,2560]{1,0:T(8,128)(2,1)S(1)} %collective-permute-done.11.upper_ref) | copy-start | bytes 1966084
  107.1 12.3 %copy-start.6 = (bf16[128,2560]{1,0:T(8,128)(2,1)}, bf16[128,2560]{1,0:T(8,128)(2,1)S(1)}, u32[]{:S(2)}) copy-start(bf16[128,2560]{1,0:T(8,128)(2,1)S(1)} %collective-permute-done.12.upper_ref) | copy-start | bytes 1966084
  107.1 11.7 %copy-start.5 = (bf16[256,2560]{1,0:T(8,128)(2,1)}, bf16[256,2560]{1,0:T(8,128)(2,1)S(1)}, u32[]{:S(2)}) copy-start(bf16[256,2560]{1,0:T(8,128)(2,1)S(1)} %collective-permute-done.9.lower_ref) | copy-start | bytes 3932164
  117.7 1.1 copy-start.4
  118.8 1.1 slice-start
  119.9 1.1 slice-start.1
  121.7 1.6 collective-permute-start.14
  123.3 15.6 %collective-permute-start.15 = (f32[448,128]{1,0:T(8,128)S(1)}, f32[448,128]{1,0:T(8,128)S(1)}, u32[]{:S(2)}, u32[]{:S(2)}) collective-permute-start(f32[448,128]{1,0:T(8,128)S(1)} %select_add_fusion), channel_id=1, source_target_pairs={{0,2},{1,3},{2,0},{3,1},{4,6},{5,7},{6,4},{7,5},{8,10},{9,11},{10,... | collective-permute-start | bytes 688136 | tf_op jit(solution)/shard_map/ppermute | solution.py:208
  139.0 11.0 %collective-permute-start.16 = (f32[448,128]{1,0:T(8,128)S(1)}, f32[448,128]{1,0:T(8,128)S(1)}, u32[]{:S(2)}, u32[]{:S(2)}) collective-permute-start(f32[448,128]{1,0:T(8,128)S(1)} %add.47), channel_id=1, source_target_pairs={{0,1},{1,0},{2,3},{3,2},{4,5},{5,4},{6,7},{7,6},{8,9},{9,8},{10,11... | collective-permute-start | bytes 688136 | tf_op jit(solution)/shard_map/ppermute | solution.py:209
  139.5 14.9 %collective-permute-start.13 = (f32[256,256]{1,0:T(8,128)S(1)}, f32[256,256]{1,0:T(8,128)S(1)}, u32[]{:S(2)}, u32[]{:S(2)}) collective-permute-start(f32[256,256]{1,0:T(8,128)S(1)} %maximum_select_fusion.1), channel_id=1, source_target_pairs={{0,4},{4,8},{8,12},{12,16},{16,20},{20,24},{24,28},{28,32},{32,36}... | collective-permute-start | bytes 786440 | tf_op jit(solution)/shard_map/ppermute | solution.py:34
  141.4 9.6 %collective-permute-start.17 = (f32[128,128]{1,0:T(8,128)S(1)}, f32[128,128]{1,0:T(8,128)S(1)}, u32[]{:S(2)}, u32[]{:S(2)}) collective-permute-start(f32[128,128]{1,0:T(8,128)S(1)} %slice.192), channel_id=1, source_target_pairs={{4,0},{8,4},{12,8},{16,12},{20,16},{24,20},{28,24},{32,28},{36,32}... | collective-permute-start | bytes 196616 | tf_op jit(solution)/shard_map/ppermute | solution.py:34
  175.1 0.6 copy-start.8
